TPU v7x, 32 devices: a whole 2x2x4 slice. The times are simulated.
32 devices in a mesh: tm: 4 (over x, core), space: 8 (over z, y).
Axes of the slice: x: 2, y: 2, z: 4, core: 2. Of those that a mesh axis runs over, the one named last changes fastest.
Arguments:
- u_start: float32 [12, 64, 16, 128], P(None, 'space'), may hold values from -6 to 6
- guess: float32 [4, 3, 12, 64, 16, 128], P('tm', None, None, 'space'), may hold values from -6 to 6
- velocity: float32 [3, 12], replicated, may hold values from -1 to 1
- rates: float32 [21], replicated, may hold values from 0.5 to 5
- energies: float32 [21], replicated, may hold values from 0.5 to 4
- reactions: int32 [21, 3], replicated, may hold values from 0 to 11
Outputs:
- fine_end: float32 [4, 12, 64, 16, 128], P('tm', None, 'space')
- coarse_end: float32 [4, 12, 64, 8, 128], P('tm', None, 'space')
All inputs are finite; a program needn't handle non-finite values.
Results may differ from a plain program's by a relative error of at most 0.0001.
Values sent between devices are 32-bit elements; how exact they have to be, the bound alone decides.
No kernel may reach another device: no remote copies, remote signals or barrier semaphores. Data moves between devices by JAX's collectives and lax.ppermute only.
A program may use at most 64 MiB of HBM per device.

v0:
```python
import jax
import jax.numpy as jnp
import numpy as np
from jax import lax
from jax.experimental import pallas as pl
from jax.experimental.pallas import tpu as pltpu
from jax.sharding import PartitionSpec as P

ITERS = 2


STEP = 0.01
HIGHEST = lax.Precision.HIGHEST
FINE_NODES = np.array(
    [
        -1.0,
        -0.8717401485096066,
        -0.5917001814331423,
        -0.2092992179024789,
        0.2092992179024789,
        0.5917001814331423,
        0.8717401485096066,
        1.0,
    ]
)
COARSE_NODES = np.array([-1.0, -0.4472135954999579, 0.4472135954999579, 1.0])


def lagrange_table(source, target):
    table = np.ones((len(target), len(source)))
    for j in range(len(source)):
        for m in range(len(source)):
            if m != j:
                table[:, j] *= (target - source[m]) / (source[j] - source[m])
    return table


def derivative_table(points):
    total = len(points)
    weights = np.array(
        [
            1.0 / np.prod([points[j] - points[m] for m in range(total) if m != j])
            for j in range(total)
        ]
    )
    table = np.zeros((total, total))
    for i in range(total):
        for j in range(total):
            if i != j:
                table[i, j] = weights[j] / weights[i] / (points[i] - points[j])
        table[i, i] = -np.sum(table[i])
    return table


def element_tables(length, table, lift):
    per_element = table.shape[0]
    block = np.kron(np.eye(length // per_element), table)
    position = np.arange(length) % per_element
    identity = np.eye(length)
    before = np.roll(identity, -1, axis=1)
    after = np.roll(identity, 1, axis=1)
    first_mask = np.where(position == 0, 1.0, 0.0)
    last_mask = np.where(position == per_element - 1, 1.0, 0.0)
    upwind = lift * first_mask[:, None] * (before - identity)
    downwind = lift * last_mask[:, None] * (after - identity)
    return (block, upwind, downwind)


def widen(matrix):
    length = matrix.shape[0]
    wider = np.zeros((length, matrix.shape[1] + 2))
    wider[:, 1:-1] = matrix
    return wider


def padded_tables(length, table, lift):
    block, upwind, downwind = element_tables(length, table, lift)
    block_wide = widen(block)
    upwind_wide = widen(upwind)
    downwind_wide = widen(downwind)
    upwind_wide[0, length] = 0.0
    upwind_wide[0, 0] = lift
    downwind_wide[length - 1, 1] = 0.0
    downwind_wide[length - 1, length + 1] = lift
    return (block_wide, upwind_wide, downwind_wide)


def field_operators(speed, tables):
    block = jnp.asarray(tables[0], jnp.float32)
    upwind = jnp.asarray(tables[1], jnp.float32)
    downwind = jnp.asarray(tables[2], jnp.float32)
    speeds = speed[:, None, None]
    return (
        -speeds * block + jnp.maximum(speeds, 0.0) * upwind + jnp.maximum(-speeds, 0.0) * downwind
    )


def plane_operator(y_mats, z_local):
    depth = z_local.shape[1]
    rows = y_mats.shape[1]
    eye_z = jnp.eye(depth, dtype=jnp.float32)
    eye_y = jnp.eye(rows, dtype=jnp.float32)
    op = (
        eye_z[None, :, None, :, None] * y_mats[:, None, :, None, :]
        + z_local[:, :, None, :, None] * eye_y[None, None, :, None, :]
    )
    fields = y_mats.shape[0]
    return op.reshape(fields, depth * rows, depth * rows)


def dot(a, b):
    return jnp.dot(a, b, precision=HIGHEST, preferred_element_type=jnp.float32)


def tendency_into(out_ref, b, v_ref, prev_ref, next_ref, lop_ref, xt_ref, zc_ref, rx_ref,
                  rate_ref, en_ref, s_ref):
    fields, span = v_ref.shape[1], v_ref.shape[2]
    rows = prev_ref.shape[2]

    def field_body(f, carry):
        v = v_ref[b, f]
        out_ref[b, f] = dot(lop_ref[f], v) + dot(v, xt_ref[f])
        out_ref[b, f, pl.ds(0, rows), :] = (
            out_ref[b, f, pl.ds(0, rows), :] + zc_ref[0, f] * prev_ref[b, f]
        )
        out_ref[b, f, pl.ds(span - rows, rows), :] = (
            out_ref[b, f, pl.ds(span - rows, rows), :] + zc_ref[1, f] * next_ref[b, f]
        )
        s_ref[f] = jnp.tanh(v)
        return carry

    lax.fori_loop(0, fields, field_body, 0)
    temper = 1.5 + 0.5 * s_ref[fields - 1]

    def reaction_body(r, carry):
        first = rx_ref[r, 0]
        second = rx_ref[r, 1]
        product = rx_ref[r, 2]
        progress = rate_ref[r] * jnp.exp(-en_ref[r] / temper) * s_ref[first] * s_ref[second]
        out_ref[b, product] = out_ref[b, product] + progress
        out_ref[b, first] = out_ref[b, first] - progress
        out_ref[b, second] = out_ref[b, second] - progress
        return carry

    lax.fori_loop(0, rx_ref.shape[0], reaction_body, 0)


def vmem():
    return pl.BlockSpec(memory_space=pltpu.VMEM)


def smem():
    return pl.BlockSpec(memory_space=pltpu.SMEM)


def tendency_cost(states, fields, span, columns, reactions):
    flops = states * fields * (2 * span * span * columns + 2 * span * columns * columns) * 6
    flops += states * span * columns * (8 * reactions + 4 * fields)
    trans = states * span * columns * (fields + 2 * reactions)
    return flops, trans


def call(kernel, ins, in_kinds, outs, scratch, flops, trans):
    nbytes = sum(int(np.prod(x.shape)) * 4 for x in ins) + sum(
        int(np.prod(o.shape)) * 4 for o in outs
    )
    return pl.pallas_call(
        kernel,
        out_shape=outs,
        in_specs=[smem() if k else vmem() for k in in_kinds],
        out_specs=tuple(vmem() for _ in outs),
        scratch_shapes=scratch,
        cost_estimate=pl.CostEstimate(
            flops=int(flops), transcendentals=int(trans), bytes_accessed=int(nbytes)
        ),
    )(*ins)


def per_device(u_start, guess, velocity, rates, energies, reactions):
    fields, depth, rows, columns = u_start.shape
    coarse_rows = rows // 2
    span = depth * rows
    coarse_span = depth * coarse_rows
    reaction_count = rates.shape[0]
    fine_table = derivative_table(FINE_NODES)
    coarse_table = derivative_table(COARSE_NODES)
    x_mats = field_operators(velocity[0], element_tables(columns, fine_table, 28.0))
    xt = jnp.swapaxes(x_mats, 1, 2)
    y_fine = field_operators(velocity[1], element_tables(rows, fine_table, 28.0))
    y_coarse = field_operators(velocity[1], element_tables(coarse_rows, coarse_table, 6.0))
    z_mats = field_operators(velocity[2], padded_tables(depth, fine_table, 28.0))
    z_local = z_mats[:, :, 1:-1]
    zc = jnp.stack([z_mats[:, 0, 0], z_mats[:, depth - 1, depth + 1]])
    lop_fine = plane_operator(y_fine, z_local)
    lop_coarse = plane_operator(y_coarse, z_local)
    restrict_rows = np.kron(np.eye(rows // 8), lagrange_table(FINE_NODES, COARSE_NODES))
    prolong_rows = np.kron(np.eye(rows // 8), lagrange_table(COARSE_NODES, FINE_NODES))
    rmat = jnp.asarray(np.kron(np.eye(depth), restrict_rows), jnp.float32)
    pmat = jnp.asarray(np.kron(np.eye(depth), prolong_rows), jnp.float32)
    restrict_plane = jnp.asarray(restrict_rows, jnp.float32)
    scalars = (zc, reactions.astype(jnp.int32), rates, energies)
    scalar_kinds = (True, True, True, True)

    space_n = lax.axis_size("space")
    sections = lax.axis_size("tm")
    section = lax.axis_index("tm")
    lead = (section == 0).astype(jnp.int32).reshape(1)

    def halo(x, plane_rows):
        head = x[..., :plane_rows, :]
        tail = x[..., x.shape[-2] - plane_rows:, :]
        prev = lax.ppermute(tail, "space", [(i, (i + 1) % space_n) for i in range(space_n)])
        nxt = lax.ppermute(head, "space", [((i + 1) % space_n, i) for i in range(space_n)])
        return prev, nxt

    f32 = jnp.float32
    fine_state = jax.ShapeDtypeStruct((1, fields, span, columns), f32)
    coarse_state = jax.ShapeDtypeStruct((fields, coarse_span, columns), f32)

    def nodes_kernel(u_ref, p_ref, n_ref, l_ref, x_ref, zc_ref, rx_ref, ra_ref, en_ref,
                     f_ref, a1_ref, s_ref):
        for b in range(u_ref.shape[0]):
            tendency_into(f_ref, b, u_ref, p_ref, n_ref, l_ref, x_ref, zc_ref, rx_ref, ra_ref,
                          en_ref, s_ref)

        def body(f, carry):
            a1_ref[0, f] = u_ref[0, f] + STEP * (
                5.0 * f_ref[0, f] + 8.0 * f_ref[1, f] - f_ref[2, f]
            ) / 24.0
            return carry

        lax.fori_loop(0, fields, body, 0)

    def middle_kernel(a1_ref, p_ref, n_ref, l_ref, x_ref, zc_ref, rx_ref, ra_ref, en_ref,
                      f_ref, g1_ref, a2_ref, s_ref):
        tendency_into(g1_ref, 0, a1_ref, p_ref, n_ref, l_ref, x_ref, zc_ref, rx_ref, ra_ref,
                      en_ref, s_ref)

        def body(f, carry):
            a2_ref[0, f] = (
                a1_ref[0, f]
                + 0.5 * STEP * (g1_ref[0, f] - f_ref[1, f])
                + STEP * (-f_ref[0, f] + 8.0 * f_ref[1, f] + 5.0 * f_ref[2, f]) / 24.0
            )
            return carry

        lax.fori_loop(0, fields, body, 0)

    def ending_kernel(a2_ref, p_ref, n_ref, l_ref, x_ref, zc_ref, rx_ref, ra_ref, en_ref,
                      f_ref, g1_ref, u_ref, r_ref, rint_ref, c1_ref, c0_ref, g2_ref, s_ref):
        tendency_into(g2_ref, 0, a2_ref, p_ref, n_ref, l_ref, x_ref, zc_ref, rx_ref, ra_ref,
                      en_ref, s_ref)

        def body(f, carry):
            integral = STEP * (f_ref[0, f] + 4.0 * g1_ref[0, f] + g2_ref[0, f]) / 6.0
            rint_ref[f] = dot(r_ref[...], integral)
            c1_ref[f] = dot(r_ref[...], a2_ref[0, f])
            c0_ref[f] = dot(r_ref[...], u_ref[0, f])
            return carry

        lax.fori_loop(0, fields, body, 0)

    def base_kernel(c_ref, p_ref, n_ref, l_ref, x_ref, zc_ref, rx_ref, ra_ref, en_ref,
                    out_ref, s_ref):
        tendency_into(out_ref, 0, c_ref, p_ref, n_ref, l_ref, x_ref, zc_ref, rx_ref, ra_ref,
                      en_ref, s_ref)

    def chain_kernel(w_ref, p_ref, n_ref, l_ref, x_ref, zc_ref, rx_ref, ra_ref, en_ref,
                     base_ref, rint_ref, out_ref, g_ref, s_ref):
        tendency_into(g_ref, 0, w_ref, p_ref, n_ref, l_ref, x_ref, zc_ref, rx_ref, ra_ref,
                      en_ref, s_ref)

        def body(f, carry):
            out_ref[f] = w_ref[0, f] + STEP * (g_ref[0, f] - base_ref[f]) + rint_ref[f]
            return carry

        lax.fori_loop(0, fields, body, 0)

    def correct_kernel(a1_ref, a2_ref, c0_ref, c1_ref, w0_ref, w1_ref, prev_ref, us_ref,
                       r_ref, pm_ref, lead_ref, out_ref):
        def body(f, carry):
            first_change = w0_ref[f] - c0_ref[f]
            last_change = w1_ref[f] - c1_ref[f]
            out_ref[1, f] = a1_ref[0, f] + dot(pm_ref[...], 0.5 * (first_change + last_change))
            out_ref[2, f] = a2_ref[0, f] + dot(pm_ref[...], last_change)
            handed = prev_ref[0, f]
            fixed = handed + dot(pm_ref[...], w0_ref[f] - dot(r_ref[...], handed))
            out_ref[0, f] = jnp.where(lead_ref[0] != 0, us_ref[f], fixed)
            return carry

        lax.fori_loop(0, fields, body, 0)

    def finish_kernel(a2_ref, c1_ref, w1_ref, pm_ref, out_ref):
        def body(f, carry):
            out_ref[0, f] = a2_ref[0, f] + dot(pm_ref[...], w1_ref[f] - c1_ref[f])
            return carry

        lax.fori_loop(0, fields, body, 0)

    fine_cost = tendency_cost(1, fields, span, columns, reaction_count)
    coarse_cost = tendency_cost(1, fields, coarse_span, columns, reaction_count)

    def fine_scratch():
        return pltpu.VMEM((fields, span, columns), f32)

    def coarse_scratch():
        return pltpu.VMEM((fields, coarse_span, columns), f32)

    u_flat = u_start.reshape(fields, span, columns)
    nodes = guess[0].reshape(3, fields, span, columns)
    nodes = jnp.concatenate([jnp.where(section == 0, u_flat, nodes[0])[None], nodes[1:]], axis=0)
    coarse_start = jnp.einsum("cy,fzyx->fzcx", restrict_plane,
                              u_start, precision=HIGHEST).reshape(fields, coarse_span, columns)
    start_halo = halo(coarse_start, coarse_rows)

    def coarse_step(w, w_halo, base, rint):
        return call(
            chain_kernel,
            (w[None], w_halo[0][None], w_halo[1][None], lop_coarse, xt) + scalars + (base, rint),
            (False,) * 5 + scalar_kinds + (False, False),
            (coarse_state,),
            [pltpu.VMEM((1, fields, coarse_span, columns), f32), coarse_scratch()],
            *coarse_cost,
        )[0]

    fine_end = None
    coarse_end = None
    for iteration in range(ITERS):
        node_prev, node_next = halo(nodes, rows)
        f_all, a1 = call(
            nodes_kernel,
            (nodes, node_prev, node_next, lop_fine, xt) + scalars,
            (False,) * 5 + scalar_kinds,
            (jax.ShapeDtypeStruct((3, fields, span, columns), f32), fine_state),
            [fine_scratch()],
            fine_cost[0] * 3, fine_cost[1] * 3,
        )
        c0_prev = jnp.einsum("cy,fyx->fcx", restrict_plane, node_prev[0], precision=HIGHEST)
        c0_next = jnp.einsum("cy,fyx->fcx", restrict_plane, node_next[0], precision=HIGHEST)
        a1_prev, a1_next = halo(a1, rows)
        g1, a2 = call(
            middle_kernel,
            (a1, a1_prev, a1_next, lop_fine, xt) + scalars + (f_all,),
            (False,) * 5 + scalar_kinds + (False,),
            (fine_state, fine_state),
            [fine_scratch()],
            *fine_cost,
        )
        a2_prev, a2_next = halo(a2, rows)
        rint, c1, c0 = call(
            ending_kernel,
            (a2, a2_prev, a2_next, lop_fine, xt) + scalars + (f_all, g1, nodes, rmat),
            (False,) * 5 + scalar_kinds + (False,) * 4,
            (coarse_state, coarse_state, coarse_state),
            [pltpu.VMEM((1, fields, span, columns), f32), fine_scratch()],
            *fine_cost,
        )
        (base,) = call(
            base_kernel,
            (c0[None], c0_prev[None], c0_next[None], lop_coarse, xt) + scalars,
            (False,) * 5 + scalar_kinds,
            (jax.ShapeDtypeStruct((1, fields, coarse_span, columns), f32),),
            [coarse_scratch()],
            *coarse_cost,
        )
        gathered = lax.all_gather(jnp.stack([base[0], rint]), "tm")
        last = iteration + 1 == ITERS
        if not last:
            a2_handed = lax.ppermute(a2, "tm", [(i, i + 1) for i in range(sections - 1)])
        w = coarse_start
        w_halo = start_halo
        chain = [w]
        for n in range(sections):
            w = coarse_step(w, w_halo, gathered[n, 0], gathered[n, 1])
            chain.append(w)
            if n + 1 < sections:
                w_halo = halo(w, coarse_rows)
        chain = jnp.stack(chain)
        w0 = lax.dynamic_index_in_dim(chain, section, 0, keepdims=False)
        w1 = lax.dynamic_index_in_dim(chain, section + 1, 0, keepdims=False)
        if last:
            (fine_end,) = call(
                finish_kernel,
                (a2, c1, w1, pmat),
                (False,) * 4,
                (fine_state,),
                [],
                2 * fields * span * coarse_span * columns * 6, 0,
            )
            coarse_end = w1
        else:
            (nodes,) = call(
                correct_kernel,
                (a1, a2, c0, c1, w0, w1, a2_handed, u_flat, rmat, pmat, lead),
                (False,) * 10 + (True,),
                (jax.ShapeDtypeStruct((3, fields, span, columns), f32),),
                [],
                8 * fields * span * coarse_span * columns * 6, 0,
            )
    fine_end = fine_end.reshape(1, fields, depth, rows, columns)
    coarse_end = coarse_end.reshape(1, fields, depth, coarse_rows, columns)
    return (fine_end, coarse_end)


def solution(mesh):
    return jax.shard_map(
        per_device,
        mesh=mesh,
        in_specs=(
            P(None, "space", None, None),
            P("tm", None, None, "space", None, None),
            P(),
            P(),
            P(),
            P(),
        ),
        out_specs=(P("tm", None, "space", None, None), P("tm", None, "space", None, None)),
        check_vma=False,
    )
```

profile of v0, /device:TPU:0, one launch (start us, length us, event | category | flops | bytes accessed | tf_op | source)
XLA Modules:
  0.0 383.4 jit_solution(4611921104523426221)
XLA Ops:
  32.5 4.3 %mul.282 = f32[12,128,128]{2,1,0:T(8,128)S(1)} reshape(f32[12,8,16,8,16]{4,3,2,1,0:T(8,128)} %mul.281) | data formatting | bytes 1572864 | tf_op jit(solution)/shard_map/mul | solution.py:104
  46.5 16.4 %shard_map.212 = (f32[3,12,128,128]{3,2,1,0:T(8,128)}, f32[1,12,128,128]{3,2,1,0:T(8,128)}) custom-call(f32[3,12,128,128]{3,2,1,0:T(8,128)} %pad_maximum_fusion.u_ref, f32[3,12,16,128]{3,2,1,0:T(8,128)} %collective-permute-done.p_ref, f32[3,12,16,128]{3,2,1,0:T(8,128)} %collective-permute-done.1.n_ref, f32[12,128,128]{2,1,0:T(8,128)} %multiply_add_fusion.1.l_ref, ...), custom_call_target="tpu_custom_call" | custom-call | flops 1822556160 | bytes 7668228 | tf_op jit(solution)/shard_map/pallas_call | solution.py:167
  64.0 4.7 %collective-permute-start.3 = (f32[1,12,16,128]{3,2,1,0:T(8,128)S(1)}, f32[1,12,16,128]{3,2,1,0:T(8,128)S(1)}, u32[]{:S(2)}, u32[]{:S(2)}) collective-permute-start(f32[1,12,16,128]{3,2,1,0:T(8,128)S(1)} %get-tuple-element.60), channel_id=1, source_target_pairs={{1,0},{2,1},{3,2},{4,3},{5,4},{6,5},{7,6},{0,7},{9,8},{10,9},{11,1... | collective-permute-start | bytes 294920 | tf_op jit(solution)/shard_map/ppermute | solution.py:213
  71.9 8.0 %shard_map.213 = (f32[1,12,128,128]{3,2,1,0:T(8,128)}, f32[1,12,128,128]{3,2,1,0:T(8,128)}) custom-call(f32[1,12,128,128]{3,2,1,0:T(8,128)} %get-tuple-element.16.a1_ref, f32[1,12,16,128]{3,2,1,0:T(8,128)} %copy-done.14, f32[1,12,16,128]{3,2,1,0:T(8,128)} %copy-done.16, f32[12,128,128]{2,1,0:T(8,128)} %multiply_add_fusion.1.l_ref, ...), custom_call_target="tpu_custom_call" | custom-call | flops 607518720 | bytes 6488580 | tf_op jit(solution)/shard_map/pallas_call | solution.py:167
  81.0 4.7 %collective-permute-start.5 = (f32[1,12,16,128]{3,2,1,0:T(8,128)S(1)}, f32[1,12,16,128]{3,2,1,0:T(8,128)S(1)}, u32[]{:S(2)}, u32[]{:S(2)}) collective-permute-start(f32[1,12,16,128]{3,2,1,0:T(8,128)S(1)} %get-tuple-element.58), channel_id=1, source_target_pairs={{1,0},{2,1},{3,2},{4,3},{5,4},{6,5},{7,6},{0,7},{9,8},{10,9},{11,1... | collective-permute-start | bytes 294920 | tf_op jit(solution)/shard_map/ppermute | solution.py:213
  89.0 11.8 %shard_map.214 = (f32[12,64,128]{2,1,0:T(8,128)}, f32[12,64,128]{2,1,0:T(8,128)}, f32[12,64,128]{2,1,0:T(8,128)}) custom-call(f32[1,12,128,128]{3,2,1,0:T(8,128)} %get-tuple-element.18.a2_ref, f32[1,12,16,128]{3,2,1,0:T(8,128)} %copy-done.10, f32[1,12,16,128]{3,2,1,0:T(8,128)} %copy-done.12, f32[12,128,128]{2,1,0:T(8,128)} %multiply_add_fusion.1.l_ref, ...), custom_call_target="tpu_custom_call" | custom-call | flops 607518720 | bytes 9273860 | tf_op jit(solution)/shard_map/pallas_call | solution.py:167
  100.8 5.5 %shard_map.215 = f32[1,12,64,128]{3,2,1,0:T(8,128)} custom-call(f32[1,12,64,128]{3,2,1,0:T(8,128)} %bitcast.181, f32[1,12,8,128]{3,2,1,0:T(8,128)} %convolution_bitcast_fusion.3.p_ref, f32[1,12,8,128]{3,2,1,0:T(8,128)} %convolution_bitcast_fusion.2.n_ref, f32[12,64,64]{2,1,0:T(8,128)} %multiply_add_fusion.2.l_ref, f32[12,128,128]{2,1,0:T(8,128)} %multiply_add_fusion.x_ref, ...), custom_call_target="tpu_custom_call" | custom-call | flops 228261888 | bytes 1868292 | tf_op jit(solution)/shard_map/pallas_call | solution.py:167
  109.6 4.7 %collective-permute-start.7 = (f32[12,8,128]{2,1,0:T(8,128)}, f32[12,8,128]{2,1,0:T(8,128)}, u32[]{:S(2)}, u32[]{:S(2)}) collective-permute-start(f32[12,8,128]{2,1,0:T(8,128)} %get-tuple-element.74), channel_id=1, source_target_pairs={{1,0},{2,1},{3,2},{4,3},{5,4},{6,5},{7,6},{0,7},{9,8},{10,9},{11,1... | collective-permute-start | bytes 147464 | tf_op jit(solution)/shard_map/ppermute | solution.py:213
  117.4 25.0 %all-gather.5.cloned.1.call-done = f32[8,12,64,128]{3,2,1,0:T(8,128)} async-done(((f32[2,12,64,128]{3,2,1,0:T(8,128)}), f32[8,12,64,128]{3,2,1,0:T(8,128)}) %all-gather.5.cloned.1.call-update) | async-done | bytes 3145744 | tf_op jit(solution)/shard_map/all_gather | solution.py:366
  145.9 5.8 %shard_map.216 = f32[12,64,128]{2,1,0:T(8,128)} custom-call(f32[1,12,64,128]{3,2,1,0:T(8,128)} %bitcast.176, f32[1,12,8,128]{3,2,1,0:T(8,128)} %bitcast.17.p_ref, f32[1,12,8,128]{3,2,1,0:T(8,128)} %bitcast.19.n_ref, f32[12,64,64]{2,1,0:T(8,128)} %multiply_add_fusion.2.l_ref, f32[12,128,128]{2,1,0:T(8,128)} %multiply_add_fusion.x_ref, ...), custom_call_target="tpu_custom_call" | custom-call | flops 228261888 | bytes 2654724 | tf_op jit(solution)/shard_map/pallas_call | solution.py:167
  152.9 4.8 %collective-permute-start.9 = (f32[12,8,128]{2,1,0:T(8,128)S(1)}, f32[12,8,128]{2,1,0:T(8,128)S(1)}, u32[]{:S(2)}, u32[]{:S(2)}) collective-permute-start(f32[12,8,128]{2,1,0:T(8,128)S(1)} %get-tuple-element.72), channel_id=1, source_target_pairs={{1,0},{2,1},{3,2},{4,3},{5,4},{6,5},{7,6},{0,7},{9,8},{10,9},{11,1... | collective-permute-start | bytes 147464 | tf_op jit(solution)/shard_map/ppermute | solution.py:213
  160.9 5.7 %shard_map.217 = f32[12,64,128]{2,1,0:T(8,128)} custom-call(f32[1,12,64,128]{3,2,1,0:T(8,128)} %bitcast.174, f32[1,12,8,128]{3,2,1,0:T(8,128)} %bitcast.189, f32[1,12,8,128]{3,2,1,0:T(8,128)} %bitcast.194, f32[12,64,64]{2,1,0:T(8,128)} %multiply_add_fusion.2.l_ref, f32[12,128,128]{2,1,0:T(8,128)} %multiply_add_fusion.x_ref, ...), custom_call_target="tpu_custom_call" | custom-call | flops 228261888 | bytes 2654724 | tf_op jit(solution)/shard_map/pallas_call | solution.py:167
  167.6 4.7 %collective-permute-start.11 = (f32[12,8,128]{2,1,0:T(8,128)S(1)}, f32[12,8,128]{2,1,0:T(8,128)S(1)}, u32[]{:S(2)}, u32[]{:S(2)}) collective-permute-start(f32[12,8,128]{2,1,0:T(8,128)S(1)} %get-tuple-element.70), channel_id=1, source_target_pairs={{1,0},{2,1},{3,2},{4,3},{5,4},{6,5},{7,6},{0,7},{9,8},{10,9},{11,1... | collective-permute-start | bytes 147464 | tf_op jit(solution)/shard_map/ppermute | solution.py:213
  175.6 5.7 %shard_map.218 = f32[12,64,128]{2,1,0:T(8,128)} custom-call(f32[1,12,64,128]{3,2,1,0:T(8,128)} %bitcast.171, f32[1,12,8,128]{3,2,1,0:T(8,128)} %bitcast.190, f32[1,12,8,128]{3,2,1,0:T(8,128)} %bitcast.195, f32[12,64,64]{2,1,0:T(8,128)} %multiply_add_fusion.2.l_ref, f32[12,128,128]{2,1,0:T(8,128)} %multiply_add_fusion.x_ref, ...), custom_call_target="tpu_custom_call" | custom-call | flops 228261888 | bytes 2654724 | tf_op jit(solution)/shard_map/pallas_call | solution.py:167
  182.4 4.7 %collective-permute-start.13 = (f32[12,8,128]{2,1,0:T(8,128)S(1)}, f32[12,8,128]{2,1,0:T(8,128)S(1)}, u32[]{:S(2)}, u32[]{:S(2)}) collective-permute-start(f32[12,8,128]{2,1,0:T(8,128)S(1)} %get-tuple-element.68), channel_id=1, source_target_pairs={{1,0},{2,1},{3,2},{4,3},{5,4},{6,5},{7,6},{0,7},{9,8},{10,9},{11,1... | collective-permute-start | bytes 147464 | tf_op jit(solution)/shard_map/ppermute | solution.py:213
  190.4 5.8 %shard_map.219 = f32[12,64,128]{2,1,0:T(8,128)} custom-call(f32[1,12,64,128]{3,2,1,0:T(8,128)} %bitcast.170, f32[1,12,8,128]{3,2,1,0:T(8,128)} %bitcast.187, f32[1,12,8,128]{3,2,1,0:T(8,128)} %bitcast.193, f32[12,64,64]{2,1,0:T(8,128)} %multiply_add_fusion.2.l_ref, f32[12,128,128]{2,1,0:T(8,128)} %multiply_add_fusion.x_ref, ...), custom_call_target="tpu_custom_call" | custom-call | flops 228261888 | bytes 2654724 | tf_op jit(solution)/shard_map/pallas_call | solution.py:167
  199.1 10.3 %shard_map.220.u_ref = f32[3,12,128,128]{3,2,1,0:T(8,128)} custom-call(f32[1,12,128,128]{3,2,1,0:T(8,128)} %get-tuple-element.16.a1_ref, f32[1,12,128,128]{3,2,1,0:T(8,128)} %get-tuple-element.18.a2_ref, f32[12,64,128]{2,1,0:T(8,128)} %get-tuple-element.20.c0_ref, f32[12,64,128]{2,1,0:T(8,128)} %get-tuple-element.21.c1_ref, ...), custom_call_target="tpu_custom_call" | custom-call | flops 603979776 | bytes 7143428 | tf_op jit(solution)/shard_map/pallas_call | solution.py:167
  210.6 4.7 %collective-permute-start.16 = (f32[3,12,16,128]{3,2,1,0:T(8,128)S(1)}, f32[3,12,16,128]{3,2,1,0:T(8,128)S(1)}, u32[]{:S(2)}, u32[]{:S(2)}) collective-permute-start(f32[3,12,16,128]{3,2,1,0:T(8,128)S(1)} %get-tuple-element.46), channel_id=1, source_target_pairs={{1,0},{2,1},{3,2},{4,3},{5,4},{6,5},{7,6},{0,7},{9,8},{10,9},{11,1... | collective-permute-start | bytes 884744 | tf_op jit(solution)/shard_map/ppermute | solution.py:213
  215.3 4.8 %collective-permute-done.15.p_ref = f32[3,12,16,128]{3,2,1,0:T(8,128)S(1)} collective-permute-done((f32[3,12,16,128]{3,2,1,0:T(8,128)S(1)}, f32[3,12,16,128]{3,2,1,0:T(8,128)S(1)}, u32[]{:S(2)}, u32[]{:S(2)}) %collective-permute-start.15) | collective-permute-done | bytes 294944 | tf_op jit(solution)/shard_map/ppermute | solution.py:212
  223.5 16.4 %shard_map.221 = (f32[3,12,128,128]{3,2,1,0:T(8,128)}, f32[1,12,128,128]{3,2,1,0:T(8,128)}) custom-call(f32[3,12,128,128]{3,2,1,0:T(8,128)} %shard_map.220.u_ref, f32[3,12,16,128]{3,2,1,0:T(8,128)} %copy-done.33, f32[3,12,16,128]{3,2,1,0:T(8,128)} %copy-done.34, f32[12,128,128]{2,1,0:T(8,128)} %multiply_add_fusion.1.l_ref, ...), custom_call_target="tpu_custom_call" | custom-call | flops 1822556160 | bytes 7668228 | tf_op jit(solution)/shard_map/pallas_call | solution.py:167
  240.9 4.7 %collective-permute-start.18 = (f32[1,12,16,128]{3,2,1,0:T(8,128)S(1)}, f32[1,12,16,128]{3,2,1,0:T(8,128)S(1)}, u32[]{:S(2)}, u32[]{:S(2)}) collective-permute-start(f32[1,12,16,128]{3,2,1,0:T(8,128)S(1)} %get-tuple-element.56), channel_id=1, source_target_pairs={{1,0},{2,1},{3,2},{4,3},{5,4},{6,5},{7,6},{0,7},{9,8},{10,9},{11,1... | collective-permute-start | bytes 294920 | tf_op jit(solution)/shard_map/ppermute | solution.py:213
  248.9 8.1 %shard_map.222 = (f32[1,12,128,128]{3,2,1,0:T(8,128)}, f32[1,12,128,128]{3,2,1,0:T(8,128)}) custom-call(f32[1,12,128,128]{3,2,1,0:T(8,128)} %get-tuple-element.23.a1_ref, f32[1,12,16,128]{3,2,1,0:T(8,128)} %copy-done.13, f32[1,12,16,128]{3,2,1,0:T(8,128)} %copy-done.15, f32[12,128,128]{2,1,0:T(8,128)} %multiply_add_fusion.1.l_ref, ...), custom_call_target="tpu_custom_call" | custom-call | flops 607518720 | bytes 6488580 | tf_op jit(solution)/shard_map/pallas_call | solution.py:167
  258.0 4.7 %collective-permute-start.20 = (f32[1,12,16,128]{3,2,1,0:T(8,128)S(1)}, f32[1,12,16,128]{3,2,1,0:T(8,128)S(1)}, u32[]{:S(2)}, u32[]{:S(2)}) collective-permute-start(f32[1,12,16,128]{3,2,1,0:T(8,128)S(1)} %get-tuple-element.54), channel_id=1, source_target_pairs={{1,0},{2,1},{3,2},{4,3},{5,4},{6,5},{7,6},{0,7},{9,8},{10,9},{11,1... | collective-permute-start | bytes 294920 | tf_op jit(solution)/shard_map/ppermute | solution.py:213
  265.9 11.8 %shard_map.223 = (f32[12,64,128]{2,1,0:T(8,128)}, f32[12,64,128]{2,1,0:T(8,128)}, f32[12,64,128]{2,1,0:T(8,128)}) custom-call(f32[1,12,128,128]{3,2,1,0:T(8,128)} %get-tuple-element.25.a2_ref, f32[1,12,16,128]{3,2,1,0:T(8,128)} %copy-done.9, f32[1,12,16,128]{3,2,1,0:T(8,128)} %copy-done.11, f32[12,128,128]{2,1,0:T(8,128)} %multiply_add_fusion.1.l_ref, ...), custom_call_target="tpu_custom_call" | custom-call | flops 607518720 | bytes 9273860 | tf_op jit(solution)/shard_map/pallas_call | solution.py:167
  277.7 5.5 %shard_map.224 = f32[1,12,64,128]{3,2,1,0:T(8,128)} custom-call(f32[1,12,64,128]{3,2,1,0:T(8,128)} %bitcast.183, f32[1,12,8,128]{3,2,1,0:T(8,128)} %convolution_bitcast_fusion.1.p_ref, f32[1,12,8,128]{3,2,1,0:T(8,128)} %convolution_bitcast_fusion.n_ref, f32[12,64,64]{2,1,0:T(8,128)} %multiply_add_fusion.2.l_ref, f32[12,128,128]{2,1,0:T(8,128)} %multiply_add_fusion.x_ref, ...), custom_call_target="tpu_custom_call" | custom-call | flops 228261888 | bytes 1868292 | tf_op jit(solution)/shard_map/pallas_call | solution.py:167
  285.2 33.3 %all-gather.7.cloned.1.call-done = f32[8,12,64,128]{3,2,1,0:T(8,128)} async-done(((f32[2,12,64,128]{3,2,1,0:T(8,128)}), f32[8,12,64,128]{3,2,1,0:T(8,128)}) %all-gather.7.cloned.1.call-update) | async-done | bytes 3145744 | tf_op jit(solution)/shard_map/all_gather | solution.py:366
  322.0 5.9 %shard_map.225 = f32[12,64,128]{2,1,0:T(8,128)} custom-call(f32[1,12,64,128]{3,2,1,0:T(8,128)} %bitcast.177, f32[1,12,8,128]{3,2,1,0:T(8,128)} %bitcast.17.p_ref, f32[1,12,8,128]{3,2,1,0:T(8,128)} %bitcast.19.n_ref, f32[12,64,64]{2,1,0:T(8,128)} %multiply_add_fusion.2.l_ref, f32[12,128,128]{2,1,0:T(8,128)} %multiply_add_fusion.x_ref, ...), custom_call_target="tpu_custom_call" | custom-call | flops 228261888 | bytes 2654724 | tf_op jit(solution)/shard_map/pallas_call | solution.py:167
  336.2 5.7 %shard_map.226 = f32[12,64,128]{2,1,0:T(8,128)} custom-call(f32[1,12,64,128]{3,2,1,0:T(8,128)} %bitcast.172, f32[1,12,8,128]{3,2,1,0:T(8,128)} %bitcast.191, f32[1,12,8,128]{3,2,1,0:T(8,128)} %bitcast.196, f32[12,64,64]{2,1,0:T(8,128)} %multiply_add_fusion.2.l_ref, f32[12,128,128]{2,1,0:T(8,128)} %multiply_add_fusion.x_ref, ...), custom_call_target="tpu_custom_call" | custom-call | flops 228261888 | bytes 2654724 | tf_op jit(solution)/shard_map/pallas_call | solution.py:167
  350.2 5.7 %shard_map.227 = f32[12,64,128]{2,1,0:T(8,128)} custom-call(f32[1,12,64,128]{3,2,1,0:T(8,128)} %bitcast.173, f32[1,12,8,128]{3,2,1,0:T(8,128)} %bitcast.192, f32[1,12,8,128]{3,2,1,0:T(8,128)} %bitcast.197, f32[12,64,64]{2,1,0:T(8,128)} %multiply_add_fusion.2.l_ref, f32[12,128,128]{2,1,0:T(8,128)} %multiply_add_fusion.x_ref, ...), custom_call_target="tpu_custom_call" | custom-call | flops 228261888 | bytes 2654724 | tf_op jit(solution)/shard_map/pallas_call | solution.py:167
  357.0 4.6 %collective-permute-start.26 = (f32[12,8,128]{2,1,0:T(8,128)S(1)}, f32[12,8,128]{2,1,0:T(8,128)S(1)}, u32[]{:S(2)}, u32[]{:S(2)}) collective-permute-start(f32[12,8,128]{2,1,0:T(8,128)S(1)} %get-tuple-element.62), channel_id=1, source_target_pairs={{1,0},{2,1},{3,2},{4,3},{5,4},{6,5},{7,6},{0,7},{9,8},{10,9},{11,1... | collective-permute-start | bytes 147464 | tf_op jit(solution)/shard_map/ppermute | solution.py:213
  364.3 5.7 %shard_map.228 = f32[12,64,128]{2,1,0:T(8,128)} custom-call(f32[1,12,64,128]{3,2,1,0:T(8,128)} %bitcast.169, f32[1,12,8,128]{3,2,1,0:T(8,128)} %bitcast.186, f32[1,12,8,128]{3,2,1,0:T(8,128)} %bitcast.188, f32[12,64,64]{2,1,0:T(8,128)} %multiply_add_fusion.2.l_ref, f32[12,128,128]{2,1,0:T(8,128)} %multiply_add_fusion.x_ref, ...), custom_call_target="tpu_custom_call" | custom-call | flops 228261888 | bytes 2654724 | tf_op jit(solution)/shard_map/pallas_call | solution.py:167
  372.0 4.6 %shard_map.229 = f32[1,12,128,128]{3,2,1,0:T(8,128)} custom-call(f32[1,12,128,128]{3,2,1,0:T(8,128)} %get-tuple-element.25.a2_ref, f32[12,64,128]{2,1,0:T(8,128)} %get-tuple-element.27.c1_ref, f32[12,64,128]{2,1,0:T(8,128)} %get-tuple-element.51.w1_ref, f32[128,64]{1,0:T(8,128)} %constant.65.clone.pm_ref), custom_call_target="tpu_custom_call" | custom-call | flops 150994944 | bytes 2392064 | tf_op jit(solution)/shard_map/pallas_call | solution.py:167
  (217 shorter events, 109.8 us)
Async XLA Ops:
  7.2 135.2 %all-gather.5.cloned.1.call-start = ((), (), s32[]{:S(2)}) async-start(), calls=%async_computation | async-start | bytes 3932160 | tf_op jit(solution)/shard_map/all_gather | solution.py:366
  9.2 8.0 %copy-start.39 = (f32[8,10]{1,0:T(8,128)S(1)}, f32[8,10]{1,0:T(8,128)}, u32[]{:S(2)}) copy-start(f32[8,10]{1,0:T(8,128)} %constant.61.clone) | copy-start | bytes 964
  10.1 36.4 %collective-permute-start = (f32[3,12,16,128]{3,2,1,0:T(8,128)}, f32[3,12,16,128]{3,2,1,0:T(8,128)}, u32[]{:S(2)}, u32[]{:S(2)}) collective-permute-start(f32[3,12,16,128]{3,2,1,0:T(8,128)} %get-tuple-element.49), channel_id=1, source_target_pairs={{0,1},{1,2},{2,3},{3,4},{4,5},{5,6},{6,7},{7,0},{8,9},{9,10},{10,1... | collective-permute-start | bytes 884744 | tf_op jit(solution)/shard_map/ppermute | solution.py:212
  13.1 33.5 %collective-permute-start.1 = (f32[3,12,16,128]{3,2,1,0:T(8,128)}, f32[3,12,16,128]{3,2,1,0:T(8,128)}, u32[]{:S(2)}, u32[]{:S(2)}) collective-permute-start(f32[3,12,16,128]{3,2,1,0:T(8,128)} %get-tuple-element.48), channel_id=1, source_target_pairs={{1,0},{2,1},{3,2},{4,3},{5,4},{6,5},{7,6},{0,7},{9,8},{10,9},{11,1... | collective-permute-start | bytes 884744 | tf_op jit(solution)/shard_map/ppermute | solution.py:213
  46.5 22.1 %copy-start.20 = (f32[8,16,1]{1,0,2:T(8,128)S(1)}, f32[8,16,1]{1,0,2:T(8,128)}, u32[]{:S(2)}) copy-start(f32[8,16,1]{1,0,2:T(8,128)} %constant.72) | copy-start | bytes 1540
  63.9 7.4 %collective-permute-start.2 = (f32[1,12,16,128]{3,2,1,0:T(8,128)S(1)}, f32[1,12,16,128]{3,2,1,0:T(8,128)S(1)}, u32[]{:S(2)}, u32[]{:S(2)}) collective-permute-start(f32[1,12,16,128]{3,2,1,0:T(8,128)S(1)} %get-tuple-element.61), channel_id=1, source_target_pairs={{0,1},{1,2},{2,3},{3,4},{4,5},{5,6},{6,7},{7,0},{8,9},{9,10},{10,1... | collective-permute-start | bytes 294920 | tf_op jit(solution)/shard_map/ppermute | solution.py:212
  64.0 7.3 %collective-permute-start.3 = (f32[1,12,16,128]{3,2,1,0:T(8,128)S(1)}, f32[1,12,16,128]{3,2,1,0:T(8,128)S(1)}, u32[]{:S(2)}, u32[]{:S(2)}) collective-permute-start(f32[1,12,16,128]{3,2,1,0:T(8,128)S(1)} %get-tuple-element.60), channel_id=1, source_target_pairs={{1,0},{2,1},{3,2},{4,3},{5,4},{6,5},{7,6},{0,7},{9,8},{10,9},{11,1... | collective-permute-start | bytes 294920 | tf_op jit(solution)/shard_map/ppermute | solution.py:213
  80.9 7.4 %collective-permute-start.4 = (f32[1,12,16,128]{3,2,1,0:T(8,128)S(1)}, f32[1,12,16,128]{3,2,1,0:T(8,128)S(1)}, u32[]{:S(2)}, u32[]{:S(2)}) collective-permute-start(f32[1,12,16,128]{3,2,1,0:T(8,128)S(1)} %get-tuple-element.59), channel_id=1, source_target_pairs={{0,1},{1,2},{2,3},{3,4},{4,5},{5,6},{6,7},{7,0},{8,9},{9,10},{10,1... | collective-permute-start | bytes 294920 | tf_op jit(solution)/shard_map/ppermute | solution.py:212
  81.0 7.3 %collective-permute-start.5 = (f32[1,12,16,128]{3,2,1,0:T(8,128)S(1)}, f32[1,12,16,128]{3,2,1,0:T(8,128)S(1)}, u32[]{:S(2)}, u32[]{:S(2)}) collective-permute-start(f32[1,12,16,128]{3,2,1,0:T(8,128)S(1)} %get-tuple-element.58), channel_id=1, source_target_pairs={{1,0},{2,1},{3,2},{4,3},{5,4},{6,5},{7,6},{0,7},{9,8},{10,9},{11,1... | collective-permute-start | bytes 294920 | tf_op jit(solution)/shard_map/ppermute | solution.py:213
  108.3 210.1 %all-gather.7.cloned.1.call-start = ((), (), s32[]{:S(2)}) async-start(), calls=%async_computation.1 | async-start | bytes 3932160 | tf_op jit(solution)/shard_map/all_gather | solution.py:366
  109.6 36.3 %collective-permute-start.6 = (f32[12,8,128]{2,1,0:T(8,128)}, f32[12,8,128]{2,1,0:T(8,128)}, u32[]{:S(2)}, u32[]{:S(2)}) collective-permute-start(f32[12,8,128]{2,1,0:T(8,128)} %get-tuple-element.75), channel_id=1, source_target_pairs={{0,1},{1,2},{2,3},{3,4},{4,5},{5,6},{6,7},{7,0},{8,9},{9,10},{10,1... | collective-permute-start | bytes 147464 | tf_op jit(solution)/shard_map/ppermute | solution.py:212
  109.6 36.3 %collective-permute-start.7 = (f32[12,8,128]{2,1,0:T(8,128)}, f32[12,8,128]{2,1,0:T(8,128)}, u32[]{:S(2)}, u32[]{:S(2)}) collective-permute-start(f32[12,8,128]{2,1,0:T(8,128)} %get-tuple-element.74), channel_id=1, source_target_pairs={{1,0},{2,1},{3,2},{4,3},{5,4},{6,5},{7,6},{0,7},{9,8},{10,9},{11,1... | collective-permute-start | bytes 147464 | tf_op jit(solution)/shard_map/ppermute | solution.py:213
  116.0 82.2 %collective-permute-start.14 = (f32[1,12,128,128]{3,2,1,0:T(8,128)S(1)}, f32[1,12,128,128]{3,2,1,0:T(8,128)S(1)}, u32[]{:S(2)}, u32[]{:S(2)}) collective-permute-start(f32[1,12,128,128]{3,2,1,0:T(8,128)S(1)} %copy-done.3), channel_id=1, source_target_pairs={{0,8},{8,16},{16,24},{1,9},{9,17},{17,25},{2,10},{10,18},{18,26},{... | collective-permute-start | bytes 2359304 | tf_op jit(solution)/shard_map/ppermute | solution.py:369
  152.5 7.2 %collective-permute-start.8 = (f32[12,8,128]{2,1,0:T(8,128)S(1)}, f32[12,8,128]{2,1,0:T(8,128)S(1)}, u32[]{:S(2)}, u32[]{:S(2)}) collective-permute-start(f32[12,8,128]{2,1,0:T(8,128)S(1)} %get-tuple-element.73), channel_id=1, source_target_pairs={{0,1},{1,2},{2,3},{3,4},{4,5},{5,6},{6,7},{7,0},{8,9},{9,10},{10,1... | collective-permute-start | bytes 147464 | tf_op jit(solution)/shard_map/ppermute | solution.py:212
  152.9 6.8 %collective-permute-start.9 = (f32[12,8,128]{2,1,0:T(8,128)S(1)}, f32[12,8,128]{2,1,0:T(8,128)S(1)}, u32[]{:S(2)}, u32[]{:S(2)}) collective-permute-start(f32[12,8,128]{2,1,0:T(8,128)S(1)} %get-tuple-element.72), channel_id=1, source_target_pairs={{1,0},{2,1},{3,2},{4,3},{5,4},{6,5},{7,6},{0,7},{9,8},{10,9},{11,1... | collective-permute-start | bytes 147464 | tf_op jit(solution)/shard_map/ppermute | solution.py:213
  167.5 6.8 %collective-permute-start.10 = (f32[12,8,128]{2,1,0:T(8,128)S(1)}, f32[12,8,128]{2,1,0:T(8,128)S(1)}, u32[]{:S(2)}, u32[]{:S(2)}) collective-permute-start(f32[12,8,128]{2,1,0:T(8,128)S(1)} %get-tuple-element.71), channel_id=1, source_target_pairs={{0,1},{1,2},{2,3},{3,4},{4,5},{5,6},{6,7},{7,0},{8,9},{9,10},{10,1... | collective-permute-start | bytes 147464 | tf_op jit(solution)/shard_map/ppermute | solution.py:212
  167.6 6.8 %collective-permute-start.11 = (f32[12,8,128]{2,1,0:T(8,128)S(1)}, f32[12,8,128]{2,1,0:T(8,128)S(1)}, u32[]{:S(2)}, u32[]{:S(2)}) collective-permute-start(f32[12,8,128]{2,1,0:T(8,128)S(1)} %get-tuple-element.70), channel_id=1, source_target_pairs={{1,0},{2,1},{3,2},{4,3},{5,4},{6,5},{7,6},{0,7},{9,8},{10,9},{11,1... | collective-permute-start | bytes 147464 | tf_op jit(solution)/shard_map/ppermute | solution.py:213
  182.2 7.0 %collective-permute-start.12 = (f32[12,8,128]{2,1,0:T(8,128)S(1)}, f32[12,8,128]{2,1,0:T(8,128)S(1)}, u32[]{:S(2)}, u32[]{:S(2)}) collective-permute-start(f32[12,8,128]{2,1,0:T(8,128)S(1)} %get-tuple-element.69), channel_id=1, source_target_pairs={{0,1},{1,2},{2,3},{3,4},{4,5},{5,6},{6,7},{7,0},{8,9},{9,10},{10,1... | collective-permute-start | bytes 147464 | tf_op jit(solution)/shard_map/ppermute | solution.py:212
  182.4 6.8 %collective-permute-start.13 = (f32[12,8,128]{2,1,0:T(8,128)S(1)}, f32[12,8,128]{2,1,0:T(8,128)S(1)}, u32[]{:S(2)}, u32[]{:S(2)}) collective-permute-start(f32[12,8,128]{2,1,0:T(8,128)S(1)} %get-tuple-element.68), channel_id=1, source_target_pairs={{1,0},{2,1},{3,2},{4,3},{5,4},{6,5},{7,6},{0,7},{9,8},{10,9},{11,1... | collective-permute-start | bytes 147464 | tf_op jit(solution)/shard_map/ppermute | solution.py:213
  210.5 9.6 %collective-permute-start.15 = (f32[3,12,16,128]{3,2,1,0:T(8,128)S(1)}, f32[3,12,16,128]{3,2,1,0:T(8,128)S(1)}, u32[]{:S(2)}, u32[]{:S(2)}) collective-permute-start(f32[3,12,16,128]{3,2,1,0:T(8,128)S(1)} %get-tuple-element.47), channel_id=1, source_target_pairs={{0,1},{1,2},{2,3},{3,4},{4,5},{5,6},{6,7},{7,0},{8,9},{9,10},{10,1... | collective-permute-start | bytes 884744 | tf_op jit(solution)/shard_map/ppermute | solution.py:212
  210.6 12.1 %collective-permute-start.16 = (f32[3,12,16,128]{3,2,1,0:T(8,128)S(1)}, f32[3,12,16,128]{3,2,1,0:T(8,128)S(1)}, u32[]{:S(2)}, u32[]{:S(2)}) collective-permute-start(f32[3,12,16,128]{3,2,1,0:T(8,128)S(1)} %get-tuple-element.46), channel_id=1, source_target_pairs={{1,0},{2,1},{3,2},{4,3},{5,4},{6,5},{7,6},{0,7},{9,8},{10,9},{11,1... | collective-permute-start | bytes 884744 | tf_op jit(solution)/shard_map/ppermute | solution.py:213
  240.8 7.4 %collective-permute-start.17 = (f32[1,12,16,128]{3,2,1,0:T(8,128)S(1)}, f32[1,12,16,128]{3,2,1,0:T(8,128)S(1)}, u32[]{:S(2)}, u32[]{:S(2)}) collective-permute-start(f32[1,12,16,128]{3,2,1,0:T(8,128)S(1)} %get-tuple-element.57), channel_id=1, source_target_pairs={{0,1},{1,2},{2,3},{3,4},{4,5},{5,6},{6,7},{7,0},{8,9},{9,10},{10,1... | collective-permute-start | bytes 294920 | tf_op jit(solution)/shard_map/ppermute | solution.py:212
  240.9 7.3 %collective-permute-start.18 = (f32[1,12,16,128]{3,2,1,0:T(8,128)S(1)}, f32[1,12,16,128]{3,2,1,0:T(8,128)S(1)}, u32[]{:S(2)}, u32[]{:S(2)}) collective-permute-start(f32[1,12,16,128]{3,2,1,0:T(8,128)S(1)} %get-tuple-element.56), channel_id=1, source_target_pairs={{1,0},{2,1},{3,2},{4,3},{5,4},{6,5},{7,6},{0,7},{9,8},{10,9},{11,1... | collective-permute-start | bytes 294920 | tf_op jit(solution)/shard_map/ppermute | solution.py:213
  257.9 7.4 %collective-permute-start.19 = (f32[1,12,16,128]{3,2,1,0:T(8,128)S(1)}, f32[1,12,16,128]{3,2,1,0:T(8,128)S(1)}, u32[]{:S(2)}, u32[]{:S(2)}) collective-permute-start(f32[1,12,16,128]{3,2,1,0:T(8,128)S(1)} %get-tuple-element.55), channel_id=1, source_target_pairs={{0,1},{1,2},{2,3},{3,4},{4,5},{5,6},{6,7},{7,0},{8,9},{9,10},{10,1... | collective-permute-start | bytes 294920 | tf_op jit(solution)/shard_map/ppermute | solution.py:212
  258.0 7.3 %collective-permute-start.20 = (f32[1,12,16,128]{3,2,1,0:T(8,128)S(1)}, f32[1,12,16,128]{3,2,1,0:T(8,128)S(1)}, u32[]{:S(2)}, u32[]{:S(2)}) collective-permute-start(f32[1,12,16,128]{3,2,1,0:T(8,128)S(1)} %get-tuple-element.54), channel_id=1, source_target_pairs={{1,0},{2,1},{3,2},{4,3},{5,4},{6,5},{7,6},{0,7},{9,8},{10,9},{11,1... | collective-permute-start | bytes 294920 | tf_op jit(solution)/shard_map/ppermute | solution.py:213
  322.0 11.5 %copy-start.4 = (f32[5,12,64,128]{3,2,1,0:T(8,128)S(1)}, f32[5,12,64,128]{3,2,1,0:T(8,128)}, u32[]{:S(2)}) copy-start(f32[5,12,64,128]{3,2,1,0:T(8,128)} %copy.82) | copy-start | bytes 5898244
  328.7 6.8 %collective-permute-start.21 = (f32[12,8,128]{2,1,0:T(8,128)S(1)}, f32[12,8,128]{2,1,0:T(8,128)S(1)}, u32[]{:S(2)}, u32[]{:S(2)}) collective-permute-start(f32[12,8,128]{2,1,0:T(8,128)S(1)} %get-tuple-element.67), channel_id=1, source_target_pairs={{0,1},{1,2},{2,3},{3,4},{4,5},{5,6},{6,7},{7,0},{8,9},{9,10},{10,1... | collective-permute-start | bytes 147464 | tf_op jit(solution)/shard_map/ppermute | solution.py:212
  330.2 5.3 %collective-permute-start.22 = (f32[12,8,128]{2,1,0:T(8,128)S(1)}, f32[12,8,128]{2,1,0:T(8,128)S(1)}, u32[]{:S(2)}, u32[]{:S(2)}) collective-permute-start(f32[12,8,128]{2,1,0:T(8,128)S(1)} %get-tuple-element.66), channel_id=1, source_target_pairs={{1,0},{2,1},{3,2},{4,3},{5,4},{6,5},{7,6},{0,7},{9,8},{10,9},{11,1... | collective-permute-start | bytes 147464 | tf_op jit(solution)/shard_map/ppermute | solution.py:213
  342.7 6.8 %collective-permute-start.23 = (f32[12,8,128]{2,1,0:T(8,128)S(1)}, f32[12,8,128]{2,1,0:T(8,128)S(1)}, u32[]{:S(2)}, u32[]{:S(2)}) collective-permute-start(f32[12,8,128]{2,1,0:T(8,128)S(1)} %get-tuple-element.65), channel_id=1, source_target_pairs={{0,1},{1,2},{2,3},{3,4},{4,5},{5,6},{6,7},{7,0},{8,9},{9,10},{10,1... | collective-permute-start | bytes 147464 | tf_op jit(solution)/shard_map/ppermute | solution.py:212
  343.9 5.7 %collective-permute-start.24 = (f32[12,8,128]{2,1,0:T(8,128)S(1)}, f32[12,8,128]{2,1,0:T(8,128)S(1)}, u32[]{:S(2)}, u32[]{:S(2)}) collective-permute-start(f32[12,8,128]{2,1,0:T(8,128)S(1)} %get-tuple-element.64), channel_id=1, source_target_pairs={{1,0},{2,1},{3,2},{4,3},{5,4},{6,5},{7,6},{0,7},{9,8},{10,9},{11,1... | collective-permute-start | bytes 147464 | tf_op jit(solution)/shard_map/ppermute | solution.py:213
  356.8 6.9 %collective-permute-start.25 = (f32[12,8,128]{2,1,0:T(8,128)S(1)}, f32[12,8,128]{2,1,0:T(8,128)S(1)}, u32[]{:S(2)}, u32[]{:S(2)}) collective-permute-start(f32[12,8,128]{2,1,0:T(8,128)S(1)} %get-tuple-element.63), channel_id=1, source_target_pairs={{0,1},{1,2},{2,3},{3,4},{4,5},{5,6},{6,7},{7,0},{8,9},{9,10},{10,1... | collective-permute-start | bytes 147464 | tf_op jit(solution)/shard_map/ppermute | solution.py:212
  357.0 6.7 %collective-permute-start.26 = (f32[12,8,128]{2,1,0:T(8,128)S(1)}, f32[12,8,128]{2,1,0:T(8,128)S(1)}, u32[]{:S(2)}, u32[]{:S(2)}) collective-permute-start(f32[12,8,128]{2,1,0:T(8,128)S(1)} %get-tuple-element.62), channel_id=1, source_target_pairs={{1,0},{2,1},{3,2},{4,3},{5,4},{6,5},{7,6},{0,7},{9,8},{10,9},{11,1... | collective-permute-start | bytes 147464 | tf_op jit(solution)/shard_map/ppermute | solution.py:213
  (49 other events, 124.1 us)
Sparse Core Ops, SparseCore 0:
  108.4 33.9 all-gather.4
  285.3 33.1 all-gather.6
where the time goes:
time: 385 us; the launch traced here: 383 us
  Pallas kernels  144 us (37%)
  waiting for transfers between devices  75.5 us (20%)
  starting transfers between devices  65.3 us (17%)
  local copies, waits for them, and re-layouts  63.2 us (16%)
  between operations  14.6 us (4%)
  other arithmetic  13.2 us (3%)
  matrix products  7.23 us (2%)
    pallas_call x18, Pallas kernels, call(): pl.pallas_call(kernel, out_shape=outs, in_specs=[smem() if k else vmem()...  144 us
    all_gather x2, waiting for transfers between devices, per_device(): gathered = lax.all_gather(jnp.stack([base[0], rint]), 'tm')  58.4 us
    ppermute x13, starting transfers between devices, halo(): lax.ppermute(head, 'space', [((i + 1) % space_n, i) for i in range(space_...  57.1 us
    unnamed x110, local copies, waits for them, and re-layouts  18.7 us
    ppermute x13, waiting for transfers between devices, halo(): lax.ppermute(tail, 'space', [(i, (i + 1) % space_n) for i in range(space_...  14.4 us
    slice x12, local copies, waits for them, and re-layouts, halo(): head = x[..., :plane_rows, :]  10.6 us
    mul x8, local copies, waits for them, and re-layouts, plane_operator(): z_local[:, :, None, :, None] * eye_y[None, None, :, None, :]  10.3 us
    mul x8, local copies, waits for them, and re-layouts, plane_operator(): eye_z[None, :, None, :, None] * y_mats[:, None, :, None, :]  9.35 us
  transfers between devices with their start and end apart: 29, of which 14 were waited for; matrix products, arithmetic and copies ran while one was open for 14% of the time, Pallas kernels for 6%

commit v1 on v0

--- a/solution.py
+++ b/solution.py
@@ -95,17 +95,14 @@
     )
 
 
-def plane_operator(y_mats, z_local):
-    depth = z_local.shape[1]
-    rows = y_mats.shape[1]
-    eye_z = jnp.eye(depth, dtype=jnp.float32)
-    eye_y = jnp.eye(rows, dtype=jnp.float32)
-    op = (
-        eye_z[None, :, None, :, None] * y_mats[:, None, :, None, :]
-        + z_local[:, :, None, :, None] * eye_y[None, None, :, None, :]
+def speed_combination(speed, tables):
+    block = jnp.asarray(tables[0], jnp.float32)[None]
+    upwind = jnp.asarray(tables[1], jnp.float32)[None]
+    downwind = jnp.asarray(tables[2], jnp.float32)[None]
+    speeds = speed[:, None, None]
+    return (
+        -speeds * block + jnp.maximum(speeds, 0.0) * upwind + jnp.maximum(-speeds, 0.0) * downwind
     )
-    fields = y_mats.shape[0]
-    return op.reshape(fields, depth * rows, depth * rows)
 
 
 def dot(a, b):
@@ -130,13 +127,13 @@
         return carry
 
     lax.fori_loop(0, fields, field_body, 0)
-    temper = 1.5 + 0.5 * s_ref[fields - 1]
+    cooling = 1.0 / (1.5 + 0.5 * s_ref[fields - 1])
 
     def reaction_body(r, carry):
         first = rx_ref[r, 0]
         second = rx_ref[r, 1]
         product = rx_ref[r, 2]
-        progress = rate_ref[r] * jnp.exp(-en_ref[r] / temper) * s_ref[first] * s_ref[second]
+        progress = rate_ref[r] * jnp.exp(-en_ref[r] * cooling) * s_ref[first] * s_ref[second]
         out_ref[b, product] = out_ref[b, product] + progress
         out_ref[b, first] = out_ref[b, first] - progress
         out_ref[b, second] = out_ref[b, second] - progress
@@ -184,15 +181,26 @@
     reaction_count = rates.shape[0]
     fine_table = derivative_table(FINE_NODES)
     coarse_table = derivative_table(COARSE_NODES)
-    x_mats = field_operators(velocity[0], element_tables(columns, fine_table, 28.0))
-    xt = jnp.swapaxes(x_mats, 1, 2)
-    y_fine = field_operators(velocity[1], element_tables(rows, fine_table, 28.0))
-    y_coarse = field_operators(velocity[1], element_tables(coarse_rows, coarse_table, 6.0))
-    z_mats = field_operators(velocity[2], padded_tables(depth, fine_table, 28.0))
-    z_local = z_mats[:, :, 1:-1]
+    x_tables = element_tables(columns, fine_table, 28.0)
+    xt = speed_combination(velocity[0], [t.T for t in x_tables])
+    y_fine_tables = element_tables(rows, fine_table, 28.0)
+    y_coarse_tables = element_tables(coarse_rows, coarse_table, 6.0)
+    z_tables = padded_tables(depth, fine_table, 28.0)
+    z_local = [t[:, 1:-1] for t in z_tables]
+    z_mats = field_operators(velocity[2], z_tables)
     zc = jnp.stack([z_mats[:, 0, 0], z_mats[:, depth - 1, depth + 1]])
-    lop_fine = plane_operator(y_fine, z_local)
-    lop_coarse = plane_operator(y_coarse, z_local)
+
+    def plane_operator(y_tables, plane_rows):
+        along_y = speed_combination(
+            velocity[1], [np.kron(np.eye(depth), t) for t in y_tables]
+        )
+        along_z = speed_combination(
+            velocity[2], [np.kron(t, np.eye(plane_rows)) for t in z_local]
+        )
+        return along_y + along_z
+
+    lop_fine = plane_operator(y_fine_tables, rows)
+    lop_coarse = plane_operator(y_coarse_tables, coarse_rows)
     restrict_rows = np.kron(np.eye(rows // 8), lagrange_table(FINE_NODES, COARSE_NODES))
     prolong_rows = np.kron(np.eye(rows // 8), lagrange_table(COARSE_NODES, FINE_NODES))
     rmat = jnp.asarray(np.kron(np.eye(depth), restrict_rows), jnp.float32)
@@ -265,13 +273,26 @@
         tendency_into(out_ref, 0, c_ref, p_ref, n_ref, l_ref, x_ref, zc_ref, rx_ref, ra_ref,
                       en_ref, s_ref)
 
-    def chain_kernel(w_ref, p_ref, n_ref, l_ref, x_ref, zc_ref, rx_ref, ra_ref, en_ref,
-                     base_ref, rint_ref, out_ref, g_ref, s_ref):
-        tendency_into(g_ref, 0, w_ref, p_ref, n_ref, l_ref, x_ref, zc_ref, rx_ref, ra_ref,
+    def chain_kernel(lead_ref, w_ref, p_ref, n_ref, ws_ref, ps_ref, ns_ref, l_ref, x_ref,
+                     zc_ref, rx_ref, ra_ref, en_ref, base_ref, rint_ref, out_ref, begin_ref,
+                     bp_ref, bn_ref, g_ref, s_ref):
+        @pl.when(lead_ref[0] != 0)
+        def _():
+            begin_ref[...] = ws_ref[...]
+            bp_ref[...] = ps_ref[...]
+            bn_ref[...] = ns_ref[...]
+
+        @pl.when(lead_ref[0] == 0)
+        def _():
+            begin_ref[...] = w_ref[...]
+            bp_ref[...] = p_ref[...]
+            bn_ref[...] = n_ref[...]
+
+        tendency_into(g_ref, 0, begin_ref, bp_ref, bn_ref, l_ref, x_ref, zc_ref, rx_ref, ra_ref,
                       en_ref, s_ref)
 
         def body(f, carry):
-            out_ref[f] = w_ref[0, f] + STEP * (g_ref[0, f] - base_ref[f]) + rint_ref[f]
+            out_ref[0, f] = begin_ref[0, f] + STEP * (g_ref[0, f] - base_ref[0, f]) + rint_ref[0, f]
             return carry
 
         lax.fori_loop(0, fields, body, 0)
@@ -313,15 +334,32 @@
                               u_start, precision=HIGHEST).reshape(fields, coarse_span, columns)
     start_halo = halo(coarse_start, coarse_rows)
 
-    def coarse_step(w, w_halo, base, rint):
+    coarse_one = jax.ShapeDtypeStruct((1, fields, coarse_span, columns), f32)
+    plane_one = jax.ShapeDtypeStruct((1, fields, coarse_rows, columns), f32)
+
+    def coarse_step(flag, w, w_halo, base, rint):
         return call(
             chain_kernel,
-            (w[None], w_halo[0][None], w_halo[1][None], lop_coarse, xt) + scalars + (base, rint),
-            (False,) * 5 + scalar_kinds + (False, False),
-            (coarse_state,),
+            (flag, w, w_halo[0], w_halo[1], coarse_start[None], start_halo[0][None],
+             start_halo[1][None], lop_coarse, xt) + scalars + (base, rint),
+            (True,) + (False,) * 8 + scalar_kinds + (False, False),
+            (coarse_one, coarse_one, plane_one, plane_one),
             [pltpu.VMEM((1, fields, coarse_span, columns), f32), coarse_scratch()],
             *coarse_cost,
-        )[0]
+        )
+
+    tm_n = sections
+    both = ("tm", "space")
+    hop_pairs = [(d, d + 1) for d in range(tm_n - 1)]
+    prev_pairs = [
+        (d * space_n + s, (d + 1) * space_n + (s + 1) % space_n)
+        for d in range(tm_n - 1) for s in range(space_n)
+    ]
+    next_pairs = [
+        (d * space_n + s, (d + 1) * space_n + (s - 1) % space_n)
+        for d in range(tm_n - 1) for s in range(space_n)
+    ]
+    always = jnp.ones((1,), jnp.int32)
 
     fine_end = None
     coarse_end = None
@@ -363,21 +401,23 @@
             [coarse_scratch()],
             *coarse_cost,
         )
-        gathered = lax.all_gather(jnp.stack([base[0], rint]), "tm")
         last = iteration + 1 == ITERS
         if not last:
-            a2_handed = lax.ppermute(a2, "tm", [(i, i + 1) for i in range(sections - 1)])
-        w = coarse_start
-        w_halo = start_halo
-        chain = [w]
+            a2_handed = lax.ppermute(a2, "tm", hop_pairs)
+        begin = coarse_start[None]
+        begin_halo = (start_halo[0][None], start_halo[1][None])
+        flag = always
         for n in range(sections):
-            w = coarse_step(w, w_halo, gathered[n, 0], gathered[n, 1])
-            chain.append(w)
+            finish, w0, _, _ = coarse_step(flag, begin, begin_halo, base, rint[None])
             if n + 1 < sections:
-                w_halo = halo(w, coarse_rows)
-        chain = jnp.stack(chain)
-        w0 = lax.dynamic_index_in_dim(chain, section, 0, keepdims=False)
-        w1 = lax.dynamic_index_in_dim(chain, section + 1, 0, keepdims=False)
+                begin = lax.ppermute(finish, "tm", hop_pairs)
+                tail = finish[:, :, coarse_span - coarse_rows:, :]
+                head = finish[:, :, :coarse_rows, :]
+                begin_halo = (lax.ppermute(tail, both, prev_pairs),
+                              lax.ppermute(head, both, next_pairs))
+                flag = lead
+        w0 = w0[0]
+        w1 = finish[0]
         if last:
             (fine_end,) = call(
                 finish_kernel,

time: 385 us -> 320 us (0.83)
  waiting for transfers between devices: 75.5 us -> 27.2 us
  starting transfers between devices: 65.3 us -> 106 us
  local copies, waits for them, and re-layouts: 63.2 us -> 25.1 us
  between operations: 14.6 us -> 1.32 us
  other arithmetic: 13.2 us -> 5.81 us
    ppermute x1 -> x19, starting transfers between devices: 1.33 us -> 70.7 us  [the longest x6 38 us: per_device(): lax.ppermute(head, both, next_pairs)]
    all_gather x2 -> x0, waiting for transfers between devices: 58.4 us -> none  [per_device(): gathered = lax.all_gather(jnp.stack([base[0], rint]), 'tm')]
    ppermute x13 -> x7, starting transfers between devices: 57.1 us -> 29.1 us  [halo(): lax.ppermute(head, 'space', [((i + 1) % space_n, i) for i in range(space_...]
    mul x16 -> x0, local copies, waits for them, and re-layouts: 19.7 us -> none  [the longest x8 10.3 us: plane_operator(): z_local[:, :, None, :, None] * eye_y[None, None, :, None, :]]
    ppermute x1 -> x19, waiting for transfers between devices: 0.01 us -> 10.3 us  [the longest x6 8.98 us: per_device(): lax.ppermute(head, both, next_pairs)]
    squeeze x3 -> x0, local copies, waits for them, and re-layouts: 8.03 us -> none  [the longest x2 7.02 us: per_device(): w = coarse_step(w, w_halo, gathered[n, 0], gathered[n, 1])]
    slice x12 -> x6, local copies, waits for them, and re-layouts: 10.6 us -> 4.93 us  [halo(): head = x[..., :plane_rows, :]]
    unnamed x110 -> x115, local copies, waits for them, and re-layouts: 18.7 us -> 13.4 us
  transfers between devices with their start and end apart: 29 -> 33, of which waited for: 14 -> 14; matrix products, arithmetic and copies ran while one was open for 14% -> 6% of each run, Pallas kernels for 6% -> 17%
where the time goes in v1:
time: 320 us; the launch traced here: 319 us
  Pallas kernels  147 us (46%)
  starting transfers between devices  106 us (33%)
  waiting for transfers between devices  27.2 us (8%)
  local copies, waits for them, and re-layouts  25.1 us (8%)
  matrix products  7.24 us (2%)
  other arithmetic  5.81 us (2%)
    pallas_call x18, Pallas kernels, call(): pl.pallas_call(kernel, out_shape=outs, in_specs=[smem() if k else vmem()...  147 us
    ppermute x6, starting transfers between devices, per_device(): lax.ppermute(head, both, next_pairs)  38 us
    ppermute x7, starting transfers between devices, halo(): lax.ppermute(head, 'space', [((i + 1) % space_n, i) for i in range(space_...  29.1 us
    ppermute x6, starting transfers between devices, per_device(): begin = lax.ppermute(finish, 'tm', hop_pairs)  18.9 us
    unnamed x115, local copies, waits for them, and re-layouts  13.4 us
    ppermute x7, waiting for transfers between devices, halo(): lax.ppermute(tail, 'space', [(i, (i + 1) % space_n) for i in range(space_...  12.8 us
    ppermute x6, starting transfers between devices, per_device(): lax.ppermute(tail, both, prev_pairs)  11.9 us
    ppermute x6, waiting for transfers between devices, per_device(): lax.ppermute(head, both, next_pairs)  8.98 us
  transfers between devices with their start and end apart: 33, of which 14 were waited for; matrix products, arithmetic and copies ran while one was open for 6% of the time, Pallas kernels for 17%

profile of v1, /device:TPU:0, one launch (start us, length us, event | category | flops | bytes accessed | tf_op | source)
XLA Modules:
  0.0 318.7 jit_solution(532739561121372240)
XLA Ops:
  9.4 4.7 %collective-permute-start.7 = (f32[12,8,128]{2,1,0:T(8,128)S(1)}, f32[12,8,128]{2,1,0:T(8,128)S(1)}, u32[]{:S(2)}, u32[]{:S(2)}) collective-permute-start(f32[12,8,128]{2,1,0:T(8,128)S(1)} %get-tuple-element.72), channel_id=1, source_target_pairs={{1,0},{2,1},{3,2},{4,3},{5,4},{6,5},{7,6},{0,7},{9,8},{10,9},{11,1... | collective-permute-start | bytes 147464 | tf_op jit(solution)/shard_map/ppermute | solution.py:221
  22.1 16.2 %shard_map.266 = (f32[3,12,128,128]{3,2,1,0:T(8,128)}, f32[1,12,128,128]{3,2,1,0:T(8,128)}) custom-call(f32[3,12,128,128]{3,2,1,0:T(8,128)} %pad_maximum_fusion.u_ref, f32[3,12,16,128]{3,2,1,0:T(8,128)} %copy-done.48, f32[3,12,16,128]{3,2,1,0:T(8,128)} %collective-permute-done.1.n_ref, f32[12,128,128]{2,1,0:T(8,128)} %add_add_fusion.l_ref, ...), custom_call_target="tpu_custom_call" | custom-call | flops 1822556160 | bytes 7668228 | tf_op jit(solution)/shard_map/pallas_call | solution.py:164
  40.3 3.8 %collective-permute-start.3 = (f32[1,12,16,128]{3,2,1,0:T(8,128)S(1)}, f32[1,12,16,128]{3,2,1,0:T(8,128)S(1)}, u32[]{:S(2)}, u32[]{:S(2)}) collective-permute-start(f32[1,12,16,128]{3,2,1,0:T(8,128)S(1)} %get-tuple-element.58), channel_id=1, source_target_pairs={{1,0},{2,1},{3,2},{4,3},{5,4},{6,5},{7,6},{0,7},{9,8},{10,9},{11,1... | collective-permute-start | bytes 294920 | tf_op jit(solution)/shard_map/ppermute | solution.py:221
  47.4 8.1 %shard_map.267 = (f32[1,12,128,128]{3,2,1,0:T(8,128)}, f32[1,12,128,128]{3,2,1,0:T(8,128)}) custom-call(f32[1,12,128,128]{3,2,1,0:T(8,128)} %get-tuple-element.25.a1_ref, f32[1,12,16,128]{3,2,1,0:T(8,128)} %copy-done.17, f32[1,12,16,128]{3,2,1,0:T(8,128)} %copy-done.19, f32[12,128,128]{2,1,0:T(8,128)} %add_add_fusion.l_ref, ...), custom_call_target="tpu_custom_call" | custom-call | flops 607518720 | bytes 6488580 | tf_op jit(solution)/shard_map/pallas_call | solution.py:164
  56.9 4.3 %collective-permute-start.5 = (f32[1,12,16,128]{3,2,1,0:T(8,128)S(1)}, f32[1,12,16,128]{3,2,1,0:T(8,128)S(1)}, u32[]{:S(2)}, u32[]{:S(2)}) collective-permute-start(f32[1,12,16,128]{3,2,1,0:T(8,128)S(1)} %get-tuple-element.56), channel_id=1, source_target_pairs={{1,0},{2,1},{3,2},{4,3},{5,4},{6,5},{7,6},{0,7},{9,8},{10,9},{11,1... | collective-permute-start | bytes 294920 | tf_op jit(solution)/shard_map/ppermute | solution.py:221
  64.5 11.7 %shard_map.268 = (f32[12,64,128]{2,1,0:T(8,128)}, f32[12,64,128]{2,1,0:T(8,128)}, f32[12,64,128]{2,1,0:T(8,128)}) custom-call(f32[1,12,128,128]{3,2,1,0:T(8,128)} %get-tuple-element.27.a2_ref, f32[1,12,16,128]{3,2,1,0:T(8,128)} %copy-done.13, f32[1,12,16,128]{3,2,1,0:T(8,128)} %copy-done.15, f32[12,128,128]{2,1,0:T(8,128)} %add_add_fusion.l_ref, ...), custom_call_target="tpu_custom_call" | custom-call | flops 607518720 | bytes 9273860 | tf_op jit(solution)/shard_map/pallas_call | solution.py:164
  76.2 5.4 %shard_map.269.base_ref = f32[1,12,64,128]{3,2,1,0:T(8,128)} custom-call(f32[1,12,64,128]{3,2,1,0:T(8,128)} %bitcast.125, f32[1,12,8,128]{3,2,1,0:T(8,128)} %convolution_bitcast_fusion.3.p_ref, f32[1,12,8,128]{3,2,1,0:T(8,128)} %convolution_bitcast_fusion.2.n_ref, f32[12,64,64]{2,1,0:T(8,128)} %add_add_fusion.1.l_ref, ...), custom_call_target="tpu_custom_call" | custom-call | flops 228261888 | bytes 1868292 | tf_op jit(solution)/shard_map/pallas_call | solution.py:164
  82.2 6.1 %shard_map.270 = (f32[1,12,64,128]{3,2,1,0:T(8,128)}, f32[1,12,64,128]{3,2,1,0:T(8,128)}, f32[1,12,8,128]{3,2,1,0:T(8,128)}, f32[1,12,8,128]{3,2,1,0:T(8,128)}) custom-call(s32[1]{0:T(128)} %constant.52.clone.1.lead_ref, f32[1,12,64,128]{3,2,1,0:T(8,128)} %bitcast.82, f32[1,12,8,128]{3,2,1,0:T(8,128)} %bitcast.104, f32[1,12,8,128]{3,2,1,0:T(8,128)} %bitcast.114, ...), custom_call_target="tpu_custom_call" | custom-call | flops 228261888 | bytes 3637768 | tf_op jit(solution)/shard_map/pallas_call | solution.py:164
  90.5 8.4 %collective-permute-start.10 = (f32[1,12,8,128]{3,2,1,0:T(8,128)S(1)}, f32[1,12,8,128]{3,2,1,0:T(8,128)S(1)}, u32[]{:S(2)}, u32[]{:S(2)}) collective-permute-start(f32[1,12,8,128]{3,2,1,0:T(8,128)S(1)} %get-tuple-element.70), channel_id=1, source_target_pairs={{0,15},{1,8},{2,9},{3,10},{4,11},{5,12},{6,13},{7,14},{8,23},{9,16... | collective-permute-start | bytes 147464 | tf_op jit(solution)/shard_map/ppermute | solution.py:417
  102.8 6.1 %shard_map.271 = (f32[1,12,64,128]{3,2,1,0:T(8,128)}, f32[1,12,64,128]{3,2,1,0:T(8,128)}, f32[1,12,8,128]{3,2,1,0:T(8,128)}, f32[1,12,8,128]{3,2,1,0:T(8,128)}) custom-call(s32[1]{0:T(128)} %bitcast.11.lead_ref, f32[1,12,64,128]{3,2,1,0:T(8,128)} %copy-done.8, f32[1,12,8,128]{3,2,1,0:T(8,128)} %copy-done.37, f32[1,12,8,128]{3,2,1,0:T(8,128)} %copy-done.32, ...), custom_call_target="tpu_custom_call" | custom-call | flops 228261888 | bytes 3637768 | tf_op jit(solution)/shard_map/pallas_call | solution.py:164
  108.9 6.8 %collective-permute-start.11 = (f32[1,12,64,128]{3,2,1,0:T(8,128)}, f32[1,12,64,128]{3,2,1,0:T(8,128)S(1)}, u32[]{:S(2)}, u32[]{:S(2)}) collective-permute-start(f32[1,12,64,128]{3,2,1,0:T(8,128)} %get-tuple-element.33), channel_id=1, source_target_pairs={{0,8},{8,16},{16,24},{1,9},{9,17},{17,25},{2,10},{10,18},{18,26},{... | collective-permute-start | bytes 1179656 | tf_op jit(solution)/shard_map/ppermute | solution.py:413
  126.5 6.1 %shard_map.272 = (f32[1,12,64,128]{3,2,1,0:T(8,128)}, f32[1,12,64,128]{3,2,1,0:T(8,128)}, f32[1,12,8,128]{3,2,1,0:T(8,128)}, f32[1,12,8,128]{3,2,1,0:T(8,128)}) custom-call(s32[1]{0:T(128)} %bitcast.11.lead_ref, f32[1,12,64,128]{3,2,1,0:T(8,128)} %copy-done.7, f32[1,12,8,128]{3,2,1,0:T(8,128)} %copy-done.34, f32[1,12,8,128]{3,2,1,0:T(8,128)} %copy-done.39, ...), custom_call_target="tpu_custom_call" | custom-call | flops 228261888 | bytes 3637768 | tf_op jit(solution)/shard_map/pallas_call | solution.py:164
  132.6 6.9 %collective-permute-start.14 = (f32[1,12,64,128]{3,2,1,0:T(8,128)}, f32[1,12,64,128]{3,2,1,0:T(8,128)S(1)}, u32[]{:S(2)}, u32[]{:S(2)}) collective-permute-start(f32[1,12,64,128]{3,2,1,0:T(8,128)} %get-tuple-element.34), channel_id=1, source_target_pairs={{0,8},{8,16},{16,24},{1,9},{9,17},{17,25},{2,10},{10,18},{18,26},{... | collective-permute-start | bytes 1179656 | tf_op jit(solution)/shard_map/ppermute | solution.py:413
  140.3 5.4 %collective-permute-start.15 = (f32[1,12,8,128]{3,2,1,0:T(8,128)S(1)}, f32[1,12,8,128]{3,2,1,0:T(8,128)S(1)}, u32[]{:S(2)}, u32[]{:S(2)}) collective-permute-start(f32[1,12,8,128]{3,2,1,0:T(8,128)S(1)} %get-tuple-element.67), channel_id=1, source_target_pairs={{0,9},{1,10},{2,11},{3,12},{4,13},{5,14},{6,15},{7,8},{8,17},{9,18... | collective-permute-start | bytes 147464 | tf_op jit(solution)/shard_map/ppermute | solution.py:416
  151.7 6.1 %shard_map.273 = (f32[1,12,64,128]{3,2,1,0:T(8,128)}, f32[1,12,64,128]{3,2,1,0:T(8,128)}, f32[1,12,8,128]{3,2,1,0:T(8,128)}, f32[1,12,8,128]{3,2,1,0:T(8,128)}) custom-call(s32[1]{0:T(128)} %bitcast.11.lead_ref, f32[1,12,64,128]{3,2,1,0:T(8,128)} %copy-done.9, f32[1,12,8,128]{3,2,1,0:T(8,128)} %copy-done.33, f32[1,12,8,128]{3,2,1,0:T(8,128)} %copy-done.38, ...), custom_call_target="tpu_custom_call" | custom-call | flops 228261888 | bytes 3637768 | tf_op jit(solution)/shard_map/pallas_call | solution.py:164
  158.7 10.3 %shard_map.274.u_ref = f32[3,12,128,128]{3,2,1,0:T(8,128)} custom-call(f32[1,12,128,128]{3,2,1,0:T(8,128)} %get-tuple-element.25.a1_ref, f32[1,12,128,128]{3,2,1,0:T(8,128)} %get-tuple-element.27.a2_ref, f32[12,64,128]{2,1,0:T(8,128)} %get-tuple-element.29.c0_ref, f32[12,64,128]{2,1,0:T(8,128)} %get-tuple-element.30.c1_ref, f32[12,64,128]{2,1,0:T(8,128)} %bitcast.128, ...), custom_call_target="tpu_custom_call" | custom-call | flops 603979776 | bytes 7143428 | tf_op jit(solution)/shard_map/pallas_call | solution.py:164
  170.7 4.1 %collective-permute-start.19 = (f32[3,12,16,128]{3,2,1,0:T(8,128)S(1)}, f32[3,12,16,128]{3,2,1,0:T(8,128)S(1)}, u32[]{:S(2)}, u32[]{:S(2)}) collective-permute-start(f32[3,12,16,128]{3,2,1,0:T(8,128)S(1)} %get-tuple-element.48), channel_id=1, source_target_pairs={{1,0},{2,1},{3,2},{4,3},{5,4},{6,5},{7,6},{0,7},{9,8},{10,9},{11,1... | collective-permute-start | bytes 884744 | tf_op jit(solution)/shard_map/ppermute | solution.py:221
  174.9 9.0 %collective-permute-done.18.p_ref = f32[3,12,16,128]{3,2,1,0:T(8,128)S(1)} collective-permute-done((f32[3,12,16,128]{3,2,1,0:T(8,128)S(1)}, f32[3,12,16,128]{3,2,1,0:T(8,128)S(1)}, u32[]{:S(2)}, u32[]{:S(2)}) %collective-permute-start.18) | collective-permute-done | bytes 294944 | tf_op jit(solution)/shard_map/ppermute | solution.py:220
  187.4 16.3 %shard_map.275 = (f32[3,12,128,128]{3,2,1,0:T(8,128)}, f32[1,12,128,128]{3,2,1,0:T(8,128)}) custom-call(f32[3,12,128,128]{3,2,1,0:T(8,128)} %shard_map.274.u_ref, f32[3,12,16,128]{3,2,1,0:T(8,128)} %copy-done.49, f32[3,12,16,128]{3,2,1,0:T(8,128)} %copy-done.50, f32[12,128,128]{2,1,0:T(8,128)} %add_add_fusion.l_ref, f32[12,128,128]{2,1,0:T(8,128)} %multiply_add_fusion.x_ref, ...), custom_call_target="tpu_custom_call" | custom-call | flops 1822556160 | bytes 7668228 | tf_op jit(solution)/shard_map/pallas_call | solution.py:164
  205.1 4.3 %collective-permute-start.21 = (f32[1,12,16,128]{3,2,1,0:T(8,128)S(1)}, f32[1,12,16,128]{3,2,1,0:T(8,128)S(1)}, u32[]{:S(2)}, u32[]{:S(2)}) collective-permute-start(f32[1,12,16,128]{3,2,1,0:T(8,128)S(1)} %get-tuple-element.54), channel_id=1, source_target_pairs={{1,0},{2,1},{3,2},{4,3},{5,4},{6,5},{7,6},{0,7},{9,8},{10,9},{11,1... | collective-permute-start | bytes 294920 | tf_op jit(solution)/shard_map/ppermute | solution.py:221
  212.9 8.1 %shard_map.276 = (f32[1,12,128,128]{3,2,1,0:T(8,128)}, f32[1,12,128,128]{3,2,1,0:T(8,128)}) custom-call(f32[1,12,128,128]{3,2,1,0:T(8,128)} %get-tuple-element.37.a1_ref, f32[1,12,16,128]{3,2,1,0:T(8,128)} %copy-done.16, f32[1,12,16,128]{3,2,1,0:T(8,128)} %copy-done.18, f32[12,128,128]{2,1,0:T(8,128)} %add_add_fusion.l_ref, ...), custom_call_target="tpu_custom_call" | custom-call | flops 607518720 | bytes 6488580 | tf_op jit(solution)/shard_map/pallas_call | solution.py:164
  222.0 4.6 %collective-permute-start.23 = (f32[1,12,16,128]{3,2,1,0:T(8,128)S(1)}, f32[1,12,16,128]{3,2,1,0:T(8,128)S(1)}, u32[]{:S(2)}, u32[]{:S(2)}) collective-permute-start(f32[1,12,16,128]{3,2,1,0:T(8,128)S(1)} %get-tuple-element.52), channel_id=1, source_target_pairs={{1,0},{2,1},{3,2},{4,3},{5,4},{6,5},{7,6},{0,7},{9,8},{10,9},{11,1... | collective-permute-start | bytes 294920 | tf_op jit(solution)/shard_map/ppermute | solution.py:221
  229.9 11.7 %shard_map.277 = (f32[12,64,128]{2,1,0:T(8,128)}, f32[12,64,128]{2,1,0:T(8,128)}, f32[12,64,128]{2,1,0:T(8,128)}) custom-call(f32[1,12,128,128]{3,2,1,0:T(8,128)} %get-tuple-element.39.a2_ref, f32[1,12,16,128]{3,2,1,0:T(8,128)} %copy-done.12, f32[1,12,16,128]{3,2,1,0:T(8,128)} %copy-done.14, f32[12,128,128]{2,1,0:T(8,128)} %add_add_fusion.l_ref, ...), custom_call_target="tpu_custom_call" | custom-call | flops 607518720 | bytes 9273860 | tf_op jit(solution)/shard_map/pallas_call | solution.py:164
  241.7 5.3 %shard_map.278.base_ref = f32[1,12,64,128]{3,2,1,0:T(8,128)} custom-call(f32[1,12,64,128]{3,2,1,0:T(8,128)} %bitcast.131, f32[1,12,8,128]{3,2,1,0:T(8,128)} %convolution_bitcast_fusion.1.p_ref, f32[1,12,8,128]{3,2,1,0:T(8,128)} %convolution_bitcast_fusion.n_ref, f32[12,64,64]{2,1,0:T(8,128)} %add_add_fusion.1.l_ref, f32[12,128,128]{2,1,0:T(8,128)} %multiply_add_fusion.x_ref, ...), custom_call_target="tpu_custom_call" | custom-call | flops 228261888 | bytes 1868292 | tf_op jit(solution)/shard_map/pallas_call | solution.py:164
  247.0 6.0 %shard_map.279 = (f32[1,12,64,128]{3,2,1,0:T(8,128)}, f32[1,12,64,128]{3,2,1,0:T(8,128)}, f32[1,12,8,128]{3,2,1,0:T(8,128)}, f32[1,12,8,128]{3,2,1,0:T(8,128)}) custom-call(s32[1]{0:T(128)} %constant.52.clone.1.lead_ref, f32[1,12,64,128]{3,2,1,0:T(8,128)} %bitcast.87, f32[1,12,8,128]{3,2,1,0:T(8,128)} %bitcast.109, f32[1,12,8,128]{3,2,1,0:T(8,128)} %bitcast.119, ...), custom_call_target="tpu_custom_call" | custom-call | flops 228261888 | bytes 3637768 | tf_op jit(solution)/shard_map/pallas_call | solution.py:164
  256.5 6.2 %collective-permute-start.26 = (f32[1,12,8,128]{3,2,1,0:T(8,128)S(1)}, f32[1,12,8,128]{3,2,1,0:T(8,128)S(1)}, u32[]{:S(2)}, u32[]{:S(2)}) collective-permute-start(f32[1,12,8,128]{3,2,1,0:T(8,128)S(1)} %get-tuple-element.64), channel_id=1, source_target_pairs={{0,15},{1,8},{2,9},{3,10},{4,11},{5,12},{6,13},{7,14},{8,23},{9,16... | collective-permute-start | bytes 147464 | tf_op jit(solution)/shard_map/ppermute | solution.py:417
  265.7 6.2 %shard_map.280 = (f32[1,12,64,128]{3,2,1,0:T(8,128)}, f32[1,12,64,128]{3,2,1,0:T(8,128)}, f32[1,12,8,128]{3,2,1,0:T(8,128)}, f32[1,12,8,128]{3,2,1,0:T(8,128)}) custom-call(s32[1]{0:T(128)} %bitcast.11.lead_ref, f32[1,12,64,128]{3,2,1,0:T(8,128)} %copy-done.10, f32[1,12,8,128]{3,2,1,0:T(8,128)} %copy-done.35, f32[1,12,8,128]{3,2,1,0:T(8,128)} %copy-done.40, ...), custom_call_target="tpu_custom_call" | custom-call | flops 228261888 | bytes 3637768 | tf_op jit(solution)/shard_map/pallas_call | solution.py:164
  275.4 8.5 %collective-permute-start.29 = (f32[1,12,8,128]{3,2,1,0:T(8,128)S(1)}, f32[1,12,8,128]{3,2,1,0:T(8,128)S(1)}, u32[]{:S(2)}, u32[]{:S(2)}) collective-permute-start(f32[1,12,8,128]{3,2,1,0:T(8,128)S(1)} %get-tuple-element.62), channel_id=1, source_target_pairs={{0,15},{1,8},{2,9},{3,10},{4,11},{5,12},{6,13},{7,14},{8,23},{9,16... | collective-permute-start | bytes 147464 | tf_op jit(solution)/shard_map/ppermute | solution.py:417
  286.9 6.1 %shard_map.281 = (f32[1,12,64,128]{3,2,1,0:T(8,128)}, f32[1,12,64,128]{3,2,1,0:T(8,128)}, f32[1,12,8,128]{3,2,1,0:T(8,128)}, f32[1,12,8,128]{3,2,1,0:T(8,128)}) custom-call(s32[1]{0:T(128)} %bitcast.11.lead_ref, f32[1,12,64,128]{3,2,1,0:T(8,128)} %copy-done.11, f32[1,12,8,128]{3,2,1,0:T(8,128)} %copy-done.36, f32[1,12,8,128]{3,2,1,0:T(8,128)} %copy-done.41, ...), custom_call_target="tpu_custom_call" | custom-call | flops 228261888 | bytes 3637768 | tf_op jit(solution)/shard_map/pallas_call | solution.py:164
  296.5 8.5 %collective-permute-start.32 = (f32[1,12,8,128]{3,2,1,0:T(8,128)S(1)}, f32[1,12,8,128]{3,2,1,0:T(8,128)S(1)}, u32[]{:S(2)}, u32[]{:S(2)}) collective-permute-start(f32[1,12,8,128]{3,2,1,0:T(8,128)S(1)} %get-tuple-element.60), channel_id=1, source_target_pairs={{0,15},{1,8},{2,9},{3,10},{4,11},{5,12},{6,13},{7,14},{8,23},{9,16... | collective-permute-start | bytes 147464 | tf_op jit(solution)/shard_map/ppermute | solution.py:417
  308.1 6.0 %shard_map.282 = (f32[1,12,64,128]{3,2,1,0:T(8,128)}, f32[1,12,64,128]{3,2,1,0:T(8,128)}, f32[1,12,8,128]{3,2,1,0:T(8,128)}, f32[1,12,8,128]{3,2,1,0:T(8,128)}) custom-call(s32[1]{0:T(128)} %bitcast.11.lead_ref, f32[1,12,64,128]{3,2,1,0:T(8,128)} %copy-done.6, f32[1,12,8,128]{3,2,1,0:T(8,128)} %copy-done.30, f32[1,12,8,128]{3,2,1,0:T(8,128)} %copy-done.31, ...), custom_call_target="tpu_custom_call" | custom-call | flops 228261888 | bytes 3637768 | tf_op jit(solution)/shard_map/pallas_call | solution.py:164
  314.2 4.6 %shard_map.283 = f32[1,12,128,128]{3,2,1,0:T(8,128)} custom-call(f32[1,12,128,128]{3,2,1,0:T(8,128)} %get-tuple-element.39.a2_ref, f32[12,64,128]{2,1,0:T(8,128)} %get-tuple-element.41.c1_ref, f32[12,64,128]{2,1,0:T(8,128)} %bitcast.129, f32[128,64]{1,0:T(8,128)} %constant.72.clone.pm_ref), custom_call_target="tpu_custom_call" | custom-call | flops 150994944 | bytes 2392064 | tf_op jit(solution)/shard_map/pallas_call | solution.py:164
  (198 shorter events, 85.2 us)
Async XLA Ops:
  2.6 18.2 %collective-permute-start = (f32[3,12,16,128]{3,2,1,0:T(8,128)S(1)}, f32[3,12,16,128]{3,2,1,0:T(8,128)S(1)}, u32[]{:S(2)}, u32[]{:S(2)}) collective-permute-start(f32[3,12,16,128]{3,2,1,0:T(8,128)S(1)} %get-tuple-element.51), channel_id=1, source_target_pairs={{0,1},{1,2},{2,3},{3,4},{4,5},{5,6},{6,7},{7,0},{8,9},{9,10},{10,1... | collective-permute-start | bytes 884744 | tf_op jit(solution)/shard_map/ppermute | solution.py:220
  5.7 16.5 %collective-permute-start.1 = (f32[3,12,16,128]{3,2,1,0:T(8,128)S(1)}, f32[3,12,16,128]{3,2,1,0:T(8,128)}, u32[]{:S(2)}, u32[]{:S(2)}) collective-permute-start(f32[3,12,16,128]{3,2,1,0:T(8,128)S(1)} %get-tuple-element.50), channel_id=1, source_target_pairs={{1,0},{2,1},{3,2},{4,3},{5,4},{6,5},{7,6},{0,7},{9,8},{10,9},{11,1... | collective-permute-start | bytes 884744 | tf_op jit(solution)/shard_map/ppermute | solution.py:221
  9.3 72.3 %collective-permute-start.6 = (f32[12,8,128]{2,1,0:T(8,128)S(1)}, f32[12,8,128]{2,1,0:T(8,128)S(1)}, u32[]{:S(2)}, u32[]{:S(2)}) collective-permute-start(f32[12,8,128]{2,1,0:T(8,128)S(1)} %get-tuple-element.73), channel_id=1, source_target_pairs={{0,1},{1,2},{2,3},{3,4},{4,5},{5,6},{6,7},{7,0},{8,9},{9,10},{10,1... | collective-permute-start | bytes 147464 | tf_op jit(solution)/shard_map/ppermute | solution.py:220
  9.4 72.2 %collective-permute-start.7 = (f32[12,8,128]{2,1,0:T(8,128)S(1)}, f32[12,8,128]{2,1,0:T(8,128)S(1)}, u32[]{:S(2)}, u32[]{:S(2)}) collective-permute-start(f32[12,8,128]{2,1,0:T(8,128)S(1)} %get-tuple-element.72), channel_id=1, source_target_pairs={{1,0},{2,1},{3,2},{4,3},{5,4},{6,5},{7,6},{0,7},{9,8},{10,9},{11,1... | collective-permute-start | bytes 147464 | tf_op jit(solution)/shard_map/ppermute | solution.py:221
  39.3 7.4 %collective-permute-start.2 = (f32[1,12,16,128]{3,2,1,0:T(8,128)S(1)}, f32[1,12,16,128]{3,2,1,0:T(8,128)S(1)}, u32[]{:S(2)}, u32[]{:S(2)}) collective-permute-start(f32[1,12,16,128]{3,2,1,0:T(8,128)S(1)} %get-tuple-element.59), channel_id=1, source_target_pairs={{0,1},{1,2},{2,3},{3,4},{4,5},{5,6},{6,7},{7,0},{8,9},{9,10},{10,1... | collective-permute-start | bytes 294920 | tf_op jit(solution)/shard_map/ppermute | solution.py:220
  40.3 6.4 %collective-permute-start.3 = (f32[1,12,16,128]{3,2,1,0:T(8,128)S(1)}, f32[1,12,16,128]{3,2,1,0:T(8,128)S(1)}, u32[]{:S(2)}, u32[]{:S(2)}) collective-permute-start(f32[1,12,16,128]{3,2,1,0:T(8,128)S(1)} %get-tuple-element.58), channel_id=1, source_target_pairs={{1,0},{2,1},{3,2},{4,3},{5,4},{6,5},{7,6},{0,7},{9,8},{10,9},{11,1... | collective-permute-start | bytes 294920 | tf_op jit(solution)/shard_map/ppermute | solution.py:221
  56.4 7.4 %collective-permute-start.4 = (f32[1,12,16,128]{3,2,1,0:T(8,128)S(1)}, f32[1,12,16,128]{3,2,1,0:T(8,128)S(1)}, u32[]{:S(2)}, u32[]{:S(2)}) collective-permute-start(f32[1,12,16,128]{3,2,1,0:T(8,128)S(1)} %get-tuple-element.57), channel_id=1, source_target_pairs={{0,1},{1,2},{2,3},{3,4},{4,5},{5,6},{6,7},{7,0},{8,9},{9,10},{10,1... | collective-permute-start | bytes 294920 | tf_op jit(solution)/shard_map/ppermute | solution.py:220
  56.9 6.9 %collective-permute-start.5 = (f32[1,12,16,128]{3,2,1,0:T(8,128)S(1)}, f32[1,12,16,128]{3,2,1,0:T(8,128)S(1)}, u32[]{:S(2)}, u32[]{:S(2)}) collective-permute-start(f32[1,12,16,128]{3,2,1,0:T(8,128)S(1)} %get-tuple-element.56), channel_id=1, source_target_pairs={{1,0},{2,1},{3,2},{4,3},{5,4},{6,5},{7,6},{0,7},{9,8},{10,9},{11,1... | collective-permute-start | bytes 294920 | tf_op jit(solution)/shard_map/ppermute | solution.py:221
  88.4 13.6 %collective-permute-start.8 = (f32[1,12,64,128]{3,2,1,0:T(8,128)}, f32[1,12,64,128]{3,2,1,0:T(8,128)S(1)}, u32[]{:S(2)}, u32[]{:S(2)}) collective-permute-start(f32[1,12,64,128]{3,2,1,0:T(8,128)} %get-tuple-element.32), channel_id=1, source_target_pairs={{0,8},{8,16},{16,24},{1,9},{9,17},{17,25},{2,10},{10,18},{18,26},{... | collective-permute-start | bytes 1179656 | tf_op jit(solution)/shard_map/ppermute | solution.py:413
  90.5 10.2 %collective-permute-start.10 = (f32[1,12,8,128]{3,2,1,0:T(8,128)S(1)}, f32[1,12,8,128]{3,2,1,0:T(8,128)S(1)}, u32[]{:S(2)}, u32[]{:S(2)}) collective-permute-start(f32[1,12,8,128]{3,2,1,0:T(8,128)S(1)} %get-tuple-element.70), channel_id=1, source_target_pairs={{0,15},{1,8},{2,9},{3,10},{4,11},{5,12},{6,13},{7,14},{8,23},{9,16... | collective-permute-start | bytes 147464 | tf_op jit(solution)/shard_map/ppermute | solution.py:417
  108.9 16.2 %collective-permute-start.11 = (f32[1,12,64,128]{3,2,1,0:T(8,128)}, f32[1,12,64,128]{3,2,1,0:T(8,128)S(1)}, u32[]{:S(2)}, u32[]{:S(2)}) collective-permute-start(f32[1,12,64,128]{3,2,1,0:T(8,128)} %get-tuple-element.33), channel_id=1, source_target_pairs={{0,8},{8,16},{16,24},{1,9},{9,17},{17,25},{2,10},{10,18},{18,26},{... | collective-permute-start | bytes 1179656 | tf_op jit(solution)/shard_map/ppermute | solution.py:413
  115.7 42.1 %collective-permute-start.17 = (f32[1,12,128,128]{3,2,1,0:T(8,128)S(1)}, f32[1,12,128,128]{3,2,1,0:T(8,128)S(1)}, u32[]{:S(2)}, u32[]{:S(2)}) collective-permute-start(f32[1,12,128,128]{3,2,1,0:T(8,128)S(1)} %copy-done.4), channel_id=1, source_target_pairs={{0,8},{8,16},{16,24},{1,9},{9,17},{17,25},{2,10},{10,18},{18,26},{... | collective-permute-start | bytes 2359304 | tf_op jit(solution)/shard_map/ppermute | solution.py:406
  118.5 4.9 %collective-permute-start.12 = (f32[1,12,8,128]{3,2,1,0:T(8,128)S(1)}, f32[1,12,8,128]{3,2,1,0:T(8,128)S(1)}, u32[]{:S(2)}, u32[]{:S(2)}) collective-permute-start(f32[1,12,8,128]{3,2,1,0:T(8,128)S(1)} %get-tuple-element.69), channel_id=1, source_target_pairs={{0,9},{1,10},{2,11},{3,12},{4,13},{5,14},{6,15},{7,8},{8,17},{9,18... | collective-permute-start | bytes 147464 | tf_op jit(solution)/shard_map/ppermute | solution.py:416
  119.8 5.3 %collective-permute-start.13 = (f32[1,12,8,128]{3,2,1,0:T(8,128)S(1)}, f32[1,12,8,128]{3,2,1,0:T(8,128)S(1)}, u32[]{:S(2)}, u32[]{:S(2)}) collective-permute-start(f32[1,12,8,128]{3,2,1,0:T(8,128)S(1)} %get-tuple-element.68), channel_id=1, source_target_pairs={{0,15},{1,8},{2,9},{3,10},{4,11},{5,12},{6,13},{7,14},{8,23},{9,16... | collective-permute-start | bytes 147464 | tf_op jit(solution)/shard_map/ppermute | solution.py:417
  132.6 17.7 %collective-permute-start.14 = (f32[1,12,64,128]{3,2,1,0:T(8,128)}, f32[1,12,64,128]{3,2,1,0:T(8,128)S(1)}, u32[]{:S(2)}, u32[]{:S(2)}) collective-permute-start(f32[1,12,64,128]{3,2,1,0:T(8,128)} %get-tuple-element.34), channel_id=1, source_target_pairs={{0,8},{8,16},{16,24},{1,9},{9,17},{17,25},{2,10},{10,18},{18,26},{... | collective-permute-start | bytes 1179656 | tf_op jit(solution)/shard_map/ppermute | solution.py:413
  140.3 8.2 %collective-permute-start.15 = (f32[1,12,8,128]{3,2,1,0:T(8,128)S(1)}, f32[1,12,8,128]{3,2,1,0:T(8,128)S(1)}, u32[]{:S(2)}, u32[]{:S(2)}) collective-permute-start(f32[1,12,8,128]{3,2,1,0:T(8,128)S(1)} %get-tuple-element.67), channel_id=1, source_target_pairs={{0,9},{1,10},{2,11},{3,12},{4,13},{5,14},{6,15},{7,8},{8,17},{9,18... | collective-permute-start | bytes 147464 | tf_op jit(solution)/shard_map/ppermute | solution.py:416
  145.8 4.5 %collective-permute-start.16 = (f32[1,12,8,128]{3,2,1,0:T(8,128)S(1)}, f32[1,12,8,128]{3,2,1,0:T(8,128)S(1)}, u32[]{:S(2)}, u32[]{:S(2)}) collective-permute-start(f32[1,12,8,128]{3,2,1,0:T(8,128)S(1)} %get-tuple-element.66), channel_id=1, source_target_pairs={{0,15},{1,8},{2,9},{3,10},{4,11},{5,12},{6,13},{7,14},{8,23},{9,16... | collective-permute-start | bytes 147464 | tf_op jit(solution)/shard_map/ppermute | solution.py:417
  170.1 13.8 %collective-permute-start.18 = (f32[3,12,16,128]{3,2,1,0:T(8,128)S(1)}, f32[3,12,16,128]{3,2,1,0:T(8,128)S(1)}, u32[]{:S(2)}, u32[]{:S(2)}) collective-permute-start(f32[3,12,16,128]{3,2,1,0:T(8,128)S(1)} %get-tuple-element.49), channel_id=1, source_target_pairs={{0,1},{1,2},{2,3},{3,4},{4,5},{5,6},{6,7},{7,0},{8,9},{9,10},{10,1... | collective-permute-start | bytes 884744 | tf_op jit(solution)/shard_map/ppermute | solution.py:220
  170.7 15.9 %collective-permute-start.19 = (f32[3,12,16,128]{3,2,1,0:T(8,128)S(1)}, f32[3,12,16,128]{3,2,1,0:T(8,128)S(1)}, u32[]{:S(2)}, u32[]{:S(2)}) collective-permute-start(f32[3,12,16,128]{3,2,1,0:T(8,128)S(1)} %get-tuple-element.48), channel_id=1, source_target_pairs={{1,0},{2,1},{3,2},{4,3},{5,4},{6,5},{7,6},{0,7},{9,8},{10,9},{11,1... | collective-permute-start | bytes 884744 | tf_op jit(solution)/shard_map/ppermute | solution.py:221
  204.6 7.5 %collective-permute-start.20 = (f32[1,12,16,128]{3,2,1,0:T(8,128)S(1)}, f32[1,12,16,128]{3,2,1,0:T(8,128)S(1)}, u32[]{:S(2)}, u32[]{:S(2)}) collective-permute-start(f32[1,12,16,128]{3,2,1,0:T(8,128)S(1)} %get-tuple-element.55), channel_id=1, source_target_pairs={{0,1},{1,2},{2,3},{3,4},{4,5},{5,6},{6,7},{7,0},{8,9},{9,10},{10,1... | collective-permute-start | bytes 294920 | tf_op jit(solution)/shard_map/ppermute | solution.py:220
  205.1 7.1 %collective-permute-start.21 = (f32[1,12,16,128]{3,2,1,0:T(8,128)S(1)}, f32[1,12,16,128]{3,2,1,0:T(8,128)S(1)}, u32[]{:S(2)}, u32[]{:S(2)}) collective-permute-start(f32[1,12,16,128]{3,2,1,0:T(8,128)S(1)} %get-tuple-element.54), channel_id=1, source_target_pairs={{1,0},{2,1},{3,2},{4,3},{5,4},{6,5},{7,6},{0,7},{9,8},{10,9},{11,1... | collective-permute-start | bytes 294920 | tf_op jit(solution)/shard_map/ppermute | solution.py:221
  221.9 7.4 %collective-permute-start.22 = (f32[1,12,16,128]{3,2,1,0:T(8,128)S(1)}, f32[1,12,16,128]{3,2,1,0:T(8,128)S(1)}, u32[]{:S(2)}, u32[]{:S(2)}) collective-permute-start(f32[1,12,16,128]{3,2,1,0:T(8,128)S(1)} %get-tuple-element.53), channel_id=1, source_target_pairs={{0,1},{1,2},{2,3},{3,4},{4,5},{5,6},{6,7},{7,0},{8,9},{9,10},{10,1... | collective-permute-start | bytes 294920 | tf_op jit(solution)/shard_map/ppermute | solution.py:220
  222.0 7.2 %collective-permute-start.23 = (f32[1,12,16,128]{3,2,1,0:T(8,128)S(1)}, f32[1,12,16,128]{3,2,1,0:T(8,128)S(1)}, u32[]{:S(2)}, u32[]{:S(2)}) collective-permute-start(f32[1,12,16,128]{3,2,1,0:T(8,128)S(1)} %get-tuple-element.52), channel_id=1, source_target_pairs={{1,0},{2,1},{3,2},{4,3},{5,4},{6,5},{7,6},{0,7},{9,8},{10,9},{11,1... | collective-permute-start | bytes 294920 | tf_op jit(solution)/shard_map/ppermute | solution.py:221
  253.0 11.4 %collective-permute-start.24 = (f32[1,12,64,128]{3,2,1,0:T(8,128)}, f32[1,12,64,128]{3,2,1,0:T(8,128)S(1)}, u32[]{:S(2)}, u32[]{:S(2)}) collective-permute-start(f32[1,12,64,128]{3,2,1,0:T(8,128)} %get-tuple-element.44), channel_id=1, source_target_pairs={{0,8},{8,16},{16,24},{1,9},{9,17},{17,25},{2,10},{10,18},{18,26},{... | collective-permute-start | bytes 1179656 | tf_op jit(solution)/shard_map/ppermute | solution.py:413
  255.2 7.5 %collective-permute-start.25 = (f32[1,12,8,128]{3,2,1,0:T(8,128)S(1)}, f32[1,12,8,128]{3,2,1,0:T(8,128)S(1)}, u32[]{:S(2)}, u32[]{:S(2)}) collective-permute-start(f32[1,12,8,128]{3,2,1,0:T(8,128)S(1)} %get-tuple-element.65), channel_id=1, source_target_pairs={{0,9},{1,10},{2,11},{3,12},{4,13},{5,14},{6,15},{7,8},{8,17},{9,18... | collective-permute-start | bytes 147464 | tf_op jit(solution)/shard_map/ppermute | solution.py:416
  256.5 7.9 %collective-permute-start.26 = (f32[1,12,8,128]{3,2,1,0:T(8,128)S(1)}, f32[1,12,8,128]{3,2,1,0:T(8,128)S(1)}, u32[]{:S(2)}, u32[]{:S(2)}) collective-permute-start(f32[1,12,8,128]{3,2,1,0:T(8,128)S(1)} %get-tuple-element.64), channel_id=1, source_target_pairs={{0,15},{1,8},{2,9},{3,10},{4,11},{5,12},{6,13},{7,14},{8,23},{9,16... | collective-permute-start | bytes 147464 | tf_op jit(solution)/shard_map/ppermute | solution.py:417
  271.9 13.7 %collective-permute-start.27 = (f32[1,12,64,128]{3,2,1,0:T(8,128)}, f32[1,12,64,128]{3,2,1,0:T(8,128)S(1)}, u32[]{:S(2)}, u32[]{:S(2)}) collective-permute-start(f32[1,12,64,128]{3,2,1,0:T(8,128)} %get-tuple-element.45), channel_id=1, source_target_pairs={{0,8},{8,16},{16,24},{1,9},{9,17},{17,25},{2,10},{10,18},{18,26},{... | collective-permute-start | bytes 1179656 | tf_op jit(solution)/shard_map/ppermute | solution.py:413
  274.0 9.8 %collective-permute-start.28 = (f32[1,12,8,128]{3,2,1,0:T(8,128)S(1)}, f32[1,12,8,128]{3,2,1,0:T(8,128)S(1)}, u32[]{:S(2)}, u32[]{:S(2)}) collective-permute-start(f32[1,12,8,128]{3,2,1,0:T(8,128)S(1)} %get-tuple-element.63), channel_id=1, source_target_pairs={{0,9},{1,10},{2,11},{3,12},{4,13},{5,14},{6,15},{7,8},{8,17},{9,18... | collective-permute-start | bytes 147464 | tf_op jit(solution)/shard_map/ppermute | solution.py:416
  275.4 10.2 %collective-permute-start.29 = (f32[1,12,8,128]{3,2,1,0:T(8,128)S(1)}, f32[1,12,8,128]{3,2,1,0:T(8,128)S(1)}, u32[]{:S(2)}, u32[]{:S(2)}) collective-permute-start(f32[1,12,8,128]{3,2,1,0:T(8,128)S(1)} %get-tuple-element.62), channel_id=1, source_target_pairs={{0,15},{1,8},{2,9},{3,10},{4,11},{5,12},{6,13},{7,14},{8,23},{9,16... | collective-permute-start | bytes 147464 | tf_op jit(solution)/shard_map/ppermute | solution.py:417
  293.1 13.7 %collective-permute-start.30 = (f32[1,12,64,128]{3,2,1,0:T(8,128)}, f32[1,12,64,128]{3,2,1,0:T(8,128)S(1)}, u32[]{:S(2)}, u32[]{:S(2)}) collective-permute-start(f32[1,12,64,128]{3,2,1,0:T(8,128)} %get-tuple-element.46), channel_id=1, source_target_pairs={{0,8},{8,16},{16,24},{1,9},{9,17},{17,25},{2,10},{10,18},{18,26},{... | collective-permute-start | bytes 1179656 | tf_op jit(solution)/shard_map/ppermute | solution.py:413
  295.2 9.8 %collective-permute-start.31 = (f32[1,12,8,128]{3,2,1,0:T(8,128)S(1)}, f32[1,12,8,128]{3,2,1,0:T(8,128)S(1)}, u32[]{:S(2)}, u32[]{:S(2)}) collective-permute-start(f32[1,12,8,128]{3,2,1,0:T(8,128)S(1)} %get-tuple-element.61), channel_id=1, source_target_pairs={{0,9},{1,10},{2,11},{3,12},{4,13},{5,14},{6,15},{7,8},{8,17},{9,18... | collective-permute-start | bytes 147464 | tf_op jit(solution)/shard_map/ppermute | solution.py:416
  296.5 10.2 %collective-permute-start.32 = (f32[1,12,8,128]{3,2,1,0:T(8,128)S(1)}, f32[1,12,8,128]{3,2,1,0:T(8,128)S(1)}, u32[]{:S(2)}, u32[]{:S(2)}) collective-permute-start(f32[1,12,8,128]{3,2,1,0:T(8,128)S(1)} %get-tuple-element.60), channel_id=1, source_target_pairs={{0,15},{1,8},{2,9},{3,10},{4,11},{5,12},{6,13},{7,14},{8,23},{9,16... | collective-permute-start | bytes 147464 | tf_op jit(solution)/shard_map/ppermute | solution.py:417
  (59 other events, 183.1 us)

commit v2 on v1

--- a/solution.py
+++ b/solution.py
@@ -109,6 +109,18 @@
     return jnp.dot(a, b, precision=HIGHEST, preferred_element_type=jnp.float32)
 
 
+def tdot(a, b):
+    return jnp.dot(a, b, precision=lax.Precision.HIGH, preferred_element_type=jnp.float32)
+
+
+def lanes(parts):
+    return jnp.concatenate(parts, axis=1)
+
+
+def unlanes(wide, width):
+    return [wide[:, i * width:(i + 1) * width] for i in range(wide.shape[1] // width)]
+
+
 def tendency_into(out_ref, b, v_ref, prev_ref, next_ref, lop_ref, xt_ref, zc_ref, rx_ref,
                   rate_ref, en_ref, s_ref):
     fields, span = v_ref.shape[1], v_ref.shape[2]
@@ -116,7 +128,7 @@
 
     def field_body(f, carry):
         v = v_ref[b, f]
-        out_ref[b, f] = dot(lop_ref[f], v) + dot(v, xt_ref[f])
+        out_ref[b, f] = tdot(lop_ref[f], v) + tdot(v, xt_ref[f])
         out_ref[b, f, pl.ds(0, rows), :] = (
             out_ref[b, f, pl.ds(0, rows), :] + zc_ref[0, f] * prev_ref[b, f]
         )
@@ -260,13 +272,15 @@
                       en_ref, s_ref)
 
         def body(f, carry):
-            integral = STEP * (f_ref[0, f] + 4.0 * g1_ref[0, f] + g2_ref[0, f]) / 6.0
-            rint_ref[f] = dot(r_ref[...], integral)
-            c1_ref[f] = dot(r_ref[...], a2_ref[0, f])
-            c0_ref[f] = dot(r_ref[...], u_ref[0, f])
+            g2_ref[0, f] = STEP * (f_ref[0, f] + 4.0 * g1_ref[0, f] + g2_ref[0, f]) / 6.0
             return carry
 
         lax.fori_loop(0, fields, body, 0)
+        rm = r_ref[...]
+        for dst, src_ref, lead_index in ((rint_ref, g2_ref, 0), (c1_ref, a2_ref, 0), (c0_ref, u_ref, 0)):
+            wide = dot(rm, lanes([src_ref[lead_index, f] for f in range(fields)]))
+            for f, part in enumerate(unlanes(wide, columns)):
+                dst[f] = part
 
     def base_kernel(c_ref, p_ref, n_ref, l_ref, x_ref, zc_ref, rx_ref, ra_ref, en_ref,
                     out_ref, s_ref):
@@ -299,24 +313,32 @@
 
     def correct_kernel(a1_ref, a2_ref, c0_ref, c1_ref, w0_ref, w1_ref, prev_ref, us_ref,
                        r_ref, pm_ref, lead_ref, out_ref):
-        def body(f, carry):
-            first_change = w0_ref[f] - c0_ref[f]
-            last_change = w1_ref[f] - c1_ref[f]
-            out_ref[1, f] = a1_ref[0, f] + dot(pm_ref[...], 0.5 * (first_change + last_change))
-            out_ref[2, f] = a2_ref[0, f] + dot(pm_ref[...], last_change)
-            handed = prev_ref[0, f]
-            fixed = handed + dot(pm_ref[...], w0_ref[f] - dot(r_ref[...], handed))
-            out_ref[0, f] = jnp.where(lead_ref[0] != 0, us_ref[f], fixed)
-            return carry
-
-        lax.fori_loop(0, fields, body, 0)
+        pm = pm_ref[...]
+        first_change = [w0_ref[f] - c0_ref[f] for f in range(fields)]
+        last_change = [w1_ref[f] - c1_ref[f] for f in range(fields)]
+        middle_fix = unlanes(
+            dot(pm, lanes([0.5 * (first_change[f] + last_change[f]) for f in range(fields)])),
+            columns,
+        )
+        last_fix = unlanes(dot(pm, lanes(last_change)), columns)
+        handed = lanes([prev_ref[0, f] for f in range(fields)])
+        handed_fix = unlanes(
+            dot(pm, lanes([w0_ref[f] for f in range(fields)]) - dot(r_ref[...], handed)),
+            columns,
+        )
+        for f in range(fields):
+            out_ref[1, f] = a1_ref[0, f] + middle_fix[f]
+            out_ref[2, f] = a2_ref[0, f] + last_fix[f]
+            out_ref[0, f] = jnp.where(
+                lead_ref[0] != 0, us_ref[f], prev_ref[0, f] + handed_fix[f]
+            )
 
     def finish_kernel(a2_ref, c1_ref, w1_ref, pm_ref, out_ref):
-        def body(f, carry):
-            out_ref[0, f] = a2_ref[0, f] + dot(pm_ref[...], w1_ref[f] - c1_ref[f])
-            return carry
-
-        lax.fori_loop(0, fields, body, 0)
+        fix = unlanes(
+            dot(pm_ref[...], lanes([w1_ref[f] - c1_ref[f] for f in range(fields)])), columns
+        )
+        for f in range(fields):
+            out_ref[0, f] = a2_ref[0, f] + fix[f]
 
     fine_cost = tendency_cost(1, fields, span, columns, reaction_count)
     coarse_cost = tendency_cost(1, fields, coarse_span, columns, reaction_count)

time: 320 us -> 297 us (0.928)
  Pallas kernels: 147 us -> 123 us
    pallas_call x18, Pallas kernels: 147 us -> 123 us  [call(): pl.pallas_call(kernel, out_shape=outs, in_specs=[smem() if k else vmem()...]
  transfers between devices with their start and end apart: 33 -> 33, of which waited for: 14 -> 14; matrix products, arithmetic and copies ran while one was open for 6% -> 7% of each run, Pallas kernels for 17% -> 16%
where the time goes in v2:
time: 297 us; the launch traced here: 296 us
  Pallas kernels  123 us (41%)
  starting transfers between devices  106 us (36%)
  waiting for transfers between devices  27.2 us (9%)
  local copies, waits for them, and re-layouts  25.1 us (8%)
  matrix products  7.24 us (2%)
  other arithmetic  5.81 us (2%)
    pallas_call x18, Pallas kernels, call(): pl.pallas_call(kernel, out_shape=outs, in_specs=[smem() if k else vmem()...  123 us
    ppermute x6, starting transfers between devices, per_device(): lax.ppermute(head, both, next_pairs)  38.2 us
    ppermute x7, starting transfers between devices, halo(): lax.ppermute(head, 'space', [((i + 1) % space_n, i) for i in range(space_...  29.1 us
    ppermute x6, starting transfers between devices, per_device(): begin = lax.ppermute(finish, 'tm', hop_pairs)  18.9 us
    unnamed x115, local copies, waits for them, and re-layouts  13.4 us
    ppermute x7, waiting for transfers between devices, halo(): lax.ppermute(tail, 'space', [(i, (i + 1) % space_n) for i in range(space_...  12.8 us
    ppermute x6, starting transfers between devices, per_device(): lax.ppermute(tail, both, prev_pairs)  11.9 us
    ppermute x6, waiting for transfers between devices, per_device(): lax.ppermute(head, both, next_pairs)  8.98 us
  transfers between devices with their start and end apart: 33, of which 14 were waited for; matrix products, arithmetic and copies ran while one was open for 7% of the time, Pallas kernels for 16%

profile of v2, /device:TPU:0, one launch (start us, length us, event | category | flops | bytes accessed | tf_op | source)
XLA Modules:
  0.0 295.7 jit_solution(609815010501258548)
XLA Ops:
  9.4 4.7 %collective-permute-start.7 = (f32[12,8,128]{2,1,0:T(8,128)S(1)}, f32[12,8,128]{2,1,0:T(8,128)S(1)}, u32[]{:S(2)}, u32[]{:S(2)}) collective-permute-start(f32[12,8,128]{2,1,0:T(8,128)S(1)} %get-tuple-element.72), channel_id=1, source_target_pairs={{1,0},{2,1},{3,2},{4,3},{5,4},{6,5},{7,6},{0,7},{9,8},{10,9},{11,1... | collective-permute-start | bytes 147464 | tf_op jit(solution)/shard_map/ppermute | solution.py:233
  22.1 14.0 %shard_map.266 = (f32[3,12,128,128]{3,2,1,0:T(8,128)}, f32[1,12,128,128]{3,2,1,0:T(8,128)}) custom-call(f32[3,12,128,128]{3,2,1,0:T(8,128)} %pad_maximum_fusion.u_ref, f32[3,12,16,128]{3,2,1,0:T(8,128)} %copy-done.48, f32[3,12,16,128]{3,2,1,0:T(8,128)} %collective-permute-done.1.n_ref, f32[12,128,128]{2,1,0:T(8,128)} %add_add_fusion.l_ref, ...), custom_call_target="tpu_custom_call" | custom-call | flops 1822556160 | bytes 7668228 | tf_op jit(solution)/shard_map/pallas_call | solution.py:176
  38.0 3.8 %collective-permute-start.3 = (f32[1,12,16,128]{3,2,1,0:T(8,128)S(1)}, f32[1,12,16,128]{3,2,1,0:T(8,128)S(1)}, u32[]{:S(2)}, u32[]{:S(2)}) collective-permute-start(f32[1,12,16,128]{3,2,1,0:T(8,128)S(1)} %get-tuple-element.58), channel_id=1, source_target_pairs={{1,0},{2,1},{3,2},{4,3},{5,4},{6,5},{7,6},{0,7},{9,8},{10,9},{11,1... | collective-permute-start | bytes 294920 | tf_op jit(solution)/shard_map/ppermute | solution.py:233
  45.1 7.3 %shard_map.267 = (f32[1,12,128,128]{3,2,1,0:T(8,128)}, f32[1,12,128,128]{3,2,1,0:T(8,128)}) custom-call(f32[1,12,128,128]{3,2,1,0:T(8,128)} %get-tuple-element.25.a1_ref, f32[1,12,16,128]{3,2,1,0:T(8,128)} %copy-done.17, f32[1,12,16,128]{3,2,1,0:T(8,128)} %copy-done.19, f32[12,128,128]{2,1,0:T(8,128)} %add_add_fusion.l_ref, ...), custom_call_target="tpu_custom_call" | custom-call | flops 607518720 | bytes 6488580 | tf_op jit(solution)/shard_map/pallas_call | solution.py:176
  53.9 4.3 %collective-permute-start.5 = (f32[1,12,16,128]{3,2,1,0:T(8,128)S(1)}, f32[1,12,16,128]{3,2,1,0:T(8,128)S(1)}, u32[]{:S(2)}, u32[]{:S(2)}) collective-permute-start(f32[1,12,16,128]{3,2,1,0:T(8,128)S(1)} %get-tuple-element.56), channel_id=1, source_target_pairs={{1,0},{2,1},{3,2},{4,3},{5,4},{6,5},{7,6},{0,7},{9,8},{10,9},{11,1... | collective-permute-start | bytes 294920 | tf_op jit(solution)/shard_map/ppermute | solution.py:233
  61.4 8.7 %shard_map.268 = (f32[12,64,128]{2,1,0:T(8,128)}, f32[12,64,128]{2,1,0:T(8,128)}, f32[12,64,128]{2,1,0:T(8,128)}) custom-call(f32[1,12,128,128]{3,2,1,0:T(8,128)} %get-tuple-element.27.a2_ref, f32[1,12,16,128]{3,2,1,0:T(8,128)} %copy-done.13, f32[1,12,16,128]{3,2,1,0:T(8,128)} %copy-done.15, f32[12,128,128]{2,1,0:T(8,128)} %add_add_fusion.l_ref, ...), custom_call_target="tpu_custom_call" | custom-call | flops 607518720 | bytes 9273860 | tf_op jit(solution)/shard_map/pallas_call | solution.py:176
  70.1 4.9 %shard_map.269.base_ref = f32[1,12,64,128]{3,2,1,0:T(8,128)} custom-call(f32[1,12,64,128]{3,2,1,0:T(8,128)} %bitcast.125, f32[1,12,8,128]{3,2,1,0:T(8,128)} %convolution_bitcast_fusion.3.p_ref, f32[1,12,8,128]{3,2,1,0:T(8,128)} %convolution_bitcast_fusion.2.n_ref, f32[12,64,64]{2,1,0:T(8,128)} %add_add_fusion.1.l_ref, ...), custom_call_target="tpu_custom_call" | custom-call | flops 228261888 | bytes 1868292 | tf_op jit(solution)/shard_map/pallas_call | solution.py:176
  75.6 5.6 %shard_map.270 = (f32[1,12,64,128]{3,2,1,0:T(8,128)}, f32[1,12,64,128]{3,2,1,0:T(8,128)}, f32[1,12,8,128]{3,2,1,0:T(8,128)}, f32[1,12,8,128]{3,2,1,0:T(8,128)}) custom-call(s32[1]{0:T(128)} %constant.52.clone.1.lead_ref, f32[1,12,64,128]{3,2,1,0:T(8,128)} %bitcast.82, f32[1,12,8,128]{3,2,1,0:T(8,128)} %bitcast.104, f32[1,12,8,128]{3,2,1,0:T(8,128)} %bitcast.114, ...), custom_call_target="tpu_custom_call" | custom-call | flops 228261888 | bytes 3637768 | tf_op jit(solution)/shard_map/pallas_call | solution.py:176
  83.3 8.4 %collective-permute-start.10 = (f32[1,12,8,128]{3,2,1,0:T(8,128)S(1)}, f32[1,12,8,128]{3,2,1,0:T(8,128)S(1)}, u32[]{:S(2)}, u32[]{:S(2)}) collective-permute-start(f32[1,12,8,128]{3,2,1,0:T(8,128)S(1)} %get-tuple-element.70), channel_id=1, source_target_pairs={{0,15},{1,8},{2,9},{3,10},{4,11},{5,12},{6,13},{7,14},{8,23},{9,16... | collective-permute-start | bytes 147464 | tf_op jit(solution)/shard_map/ppermute | solution.py:439
  95.6 5.5 %shard_map.271 = (f32[1,12,64,128]{3,2,1,0:T(8,128)}, f32[1,12,64,128]{3,2,1,0:T(8,128)}, f32[1,12,8,128]{3,2,1,0:T(8,128)}, f32[1,12,8,128]{3,2,1,0:T(8,128)}) custom-call(s32[1]{0:T(128)} %bitcast.11.lead_ref, f32[1,12,64,128]{3,2,1,0:T(8,128)} %copy-done.8, f32[1,12,8,128]{3,2,1,0:T(8,128)} %copy-done.37, f32[1,12,8,128]{3,2,1,0:T(8,128)} %copy-done.32, ...), custom_call_target="tpu_custom_call" | custom-call | flops 228261888 | bytes 3637768 | tf_op jit(solution)/shard_map/pallas_call | solution.py:176
  101.2 6.8 %collective-permute-start.11 = (f32[1,12,64,128]{3,2,1,0:T(8,128)}, f32[1,12,64,128]{3,2,1,0:T(8,128)S(1)}, u32[]{:S(2)}, u32[]{:S(2)}) collective-permute-start(f32[1,12,64,128]{3,2,1,0:T(8,128)} %get-tuple-element.33), channel_id=1, source_target_pairs={{0,8},{8,16},{16,24},{1,9},{9,17},{17,25},{2,10},{10,18},{18,26},{... | collective-permute-start | bytes 1179656 | tf_op jit(solution)/shard_map/ppermute | solution.py:435
  112.1 3.6 %collective-permute-start.13 = (f32[1,12,8,128]{3,2,1,0:T(8,128)S(1)}, f32[1,12,8,128]{3,2,1,0:T(8,128)S(1)}, u32[]{:S(2)}, u32[]{:S(2)}) collective-permute-start(f32[1,12,8,128]{3,2,1,0:T(8,128)S(1)} %get-tuple-element.68), channel_id=1, source_target_pairs={{0,15},{1,8},{2,9},{3,10},{4,11},{5,12},{6,13},{7,14},{8,23},{9,16... | collective-permute-start | bytes 147464 | tf_op jit(solution)/shard_map/ppermute | solution.py:439
  118.8 5.5 %shard_map.272 = (f32[1,12,64,128]{3,2,1,0:T(8,128)}, f32[1,12,64,128]{3,2,1,0:T(8,128)}, f32[1,12,8,128]{3,2,1,0:T(8,128)}, f32[1,12,8,128]{3,2,1,0:T(8,128)}) custom-call(s32[1]{0:T(128)} %bitcast.11.lead_ref, f32[1,12,64,128]{3,2,1,0:T(8,128)} %copy-done.7, f32[1,12,8,128]{3,2,1,0:T(8,128)} %copy-done.34, f32[1,12,8,128]{3,2,1,0:T(8,128)} %copy-done.39, ...), custom_call_target="tpu_custom_call" | custom-call | flops 228261888 | bytes 3637768 | tf_op jit(solution)/shard_map/pallas_call | solution.py:176
  124.4 6.9 %collective-permute-start.14 = (f32[1,12,64,128]{3,2,1,0:T(8,128)}, f32[1,12,64,128]{3,2,1,0:T(8,128)S(1)}, u32[]{:S(2)}, u32[]{:S(2)}) collective-permute-start(f32[1,12,64,128]{3,2,1,0:T(8,128)} %get-tuple-element.34), channel_id=1, source_target_pairs={{0,8},{8,16},{16,24},{1,9},{9,17},{17,25},{2,10},{10,18},{18,26},{... | collective-permute-start | bytes 1179656 | tf_op jit(solution)/shard_map/ppermute | solution.py:435
  132.1 5.4 %collective-permute-start.15 = (f32[1,12,8,128]{3,2,1,0:T(8,128)S(1)}, f32[1,12,8,128]{3,2,1,0:T(8,128)S(1)}, u32[]{:S(2)}, u32[]{:S(2)}) collective-permute-start(f32[1,12,8,128]{3,2,1,0:T(8,128)S(1)} %get-tuple-element.67), channel_id=1, source_target_pairs={{0,9},{1,10},{2,11},{3,12},{4,13},{5,14},{6,15},{7,8},{8,17},{9,18... | collective-permute-start | bytes 147464 | tf_op jit(solution)/shard_map/ppermute | solution.py:438
  143.5 5.6 %shard_map.273 = (f32[1,12,64,128]{3,2,1,0:T(8,128)}, f32[1,12,64,128]{3,2,1,0:T(8,128)}, f32[1,12,8,128]{3,2,1,0:T(8,128)}, f32[1,12,8,128]{3,2,1,0:T(8,128)}) custom-call(s32[1]{0:T(128)} %bitcast.11.lead_ref, f32[1,12,64,128]{3,2,1,0:T(8,128)} %copy-done.9, f32[1,12,8,128]{3,2,1,0:T(8,128)} %copy-done.33, f32[1,12,8,128]{3,2,1,0:T(8,128)} %copy-done.38, ...), custom_call_target="tpu_custom_call" | custom-call | flops 228261888 | bytes 3637768 | tf_op jit(solution)/shard_map/pallas_call | solution.py:176
  150.0 6.1 %shard_map.274.u_ref = f32[3,12,128,128]{3,2,1,0:T(8,128)} custom-call(f32[1,12,128,128]{3,2,1,0:T(8,128)} %get-tuple-element.25.a1_ref, f32[1,12,128,128]{3,2,1,0:T(8,128)} %get-tuple-element.27.a2_ref, f32[12,64,128]{2,1,0:T(8,128)} %get-tuple-element.29.c0_ref, f32[12,64,128]{2,1,0:T(8,128)} %get-tuple-element.30.c1_ref, f32[12,64,128]{2,1,0:T(8,128)} %bitcast.128, ...), custom_call_target="tpu_custom_call" | custom-call | flops 603979776 | bytes 7143428 | tf_op jit(solution)/shard_map/pallas_call | solution.py:176
  157.8 4.1 %collective-permute-start.19 = (f32[3,12,16,128]{3,2,1,0:T(8,128)S(1)}, f32[3,12,16,128]{3,2,1,0:T(8,128)S(1)}, u32[]{:S(2)}, u32[]{:S(2)}) collective-permute-start(f32[3,12,16,128]{3,2,1,0:T(8,128)S(1)} %get-tuple-element.48), channel_id=1, source_target_pairs={{1,0},{2,1},{3,2},{4,3},{5,4},{6,5},{7,6},{0,7},{9,8},{10,9},{11,1... | collective-permute-start | bytes 884744 | tf_op jit(solution)/shard_map/ppermute | solution.py:233
  161.9 9.0 %collective-permute-done.18.p_ref = f32[3,12,16,128]{3,2,1,0:T(8,128)S(1)} collective-permute-done((f32[3,12,16,128]{3,2,1,0:T(8,128)S(1)}, f32[3,12,16,128]{3,2,1,0:T(8,128)S(1)}, u32[]{:S(2)}, u32[]{:S(2)}) %collective-permute-start.18) | collective-permute-done | bytes 294944 | tf_op jit(solution)/shard_map/ppermute | solution.py:232
  174.4 14.0 %shard_map.275 = (f32[3,12,128,128]{3,2,1,0:T(8,128)}, f32[1,12,128,128]{3,2,1,0:T(8,128)}) custom-call(f32[3,12,128,128]{3,2,1,0:T(8,128)} %shard_map.274.u_ref, f32[3,12,16,128]{3,2,1,0:T(8,128)} %copy-done.49, f32[3,12,16,128]{3,2,1,0:T(8,128)} %copy-done.50, f32[12,128,128]{2,1,0:T(8,128)} %add_add_fusion.l_ref, f32[12,128,128]{2,1,0:T(8,128)} %multiply_add_fusion.x_ref, ...), custom_call_target="tpu_custom_call" | custom-call | flops 1822556160 | bytes 7668228 | tf_op jit(solution)/shard_map/pallas_call | solution.py:176
  189.9 4.3 %collective-permute-start.21 = (f32[1,12,16,128]{3,2,1,0:T(8,128)S(1)}, f32[1,12,16,128]{3,2,1,0:T(8,128)S(1)}, u32[]{:S(2)}, u32[]{:S(2)}) collective-permute-start(f32[1,12,16,128]{3,2,1,0:T(8,128)S(1)} %get-tuple-element.54), channel_id=1, source_target_pairs={{1,0},{2,1},{3,2},{4,3},{5,4},{6,5},{7,6},{0,7},{9,8},{10,9},{11,1... | collective-permute-start | bytes 294920 | tf_op jit(solution)/shard_map/ppermute | solution.py:233
  197.7 7.3 %shard_map.276 = (f32[1,12,128,128]{3,2,1,0:T(8,128)}, f32[1,12,128,128]{3,2,1,0:T(8,128)}) custom-call(f32[1,12,128,128]{3,2,1,0:T(8,128)} %get-tuple-element.37.a1_ref, f32[1,12,16,128]{3,2,1,0:T(8,128)} %copy-done.16, f32[1,12,16,128]{3,2,1,0:T(8,128)} %copy-done.18, f32[12,128,128]{2,1,0:T(8,128)} %add_add_fusion.l_ref, ...), custom_call_target="tpu_custom_call" | custom-call | flops 607518720 | bytes 6488580 | tf_op jit(solution)/shard_map/pallas_call | solution.py:176
  206.1 4.6 %collective-permute-start.23 = (f32[1,12,16,128]{3,2,1,0:T(8,128)S(1)}, f32[1,12,16,128]{3,2,1,0:T(8,128)S(1)}, u32[]{:S(2)}, u32[]{:S(2)}) collective-permute-start(f32[1,12,16,128]{3,2,1,0:T(8,128)S(1)} %get-tuple-element.52), channel_id=1, source_target_pairs={{1,0},{2,1},{3,2},{4,3},{5,4},{6,5},{7,6},{0,7},{9,8},{10,9},{11,1... | collective-permute-start | bytes 294920 | tf_op jit(solution)/shard_map/ppermute | solution.py:233
  214.0 8.6 %shard_map.277 = (f32[12,64,128]{2,1,0:T(8,128)}, f32[12,64,128]{2,1,0:T(8,128)}, f32[12,64,128]{2,1,0:T(8,128)}) custom-call(f32[1,12,128,128]{3,2,1,0:T(8,128)} %get-tuple-element.39.a2_ref, f32[1,12,16,128]{3,2,1,0:T(8,128)} %copy-done.12, f32[1,12,16,128]{3,2,1,0:T(8,128)} %copy-done.14, f32[12,128,128]{2,1,0:T(8,128)} %add_add_fusion.l_ref, ...), custom_call_target="tpu_custom_call" | custom-call | flops 607518720 | bytes 9273860 | tf_op jit(solution)/shard_map/pallas_call | solution.py:176
  222.6 4.8 %shard_map.278.base_ref = f32[1,12,64,128]{3,2,1,0:T(8,128)} custom-call(f32[1,12,64,128]{3,2,1,0:T(8,128)} %bitcast.131, f32[1,12,8,128]{3,2,1,0:T(8,128)} %convolution_bitcast_fusion.1.p_ref, f32[1,12,8,128]{3,2,1,0:T(8,128)} %convolution_bitcast_fusion.n_ref, f32[12,64,64]{2,1,0:T(8,128)} %add_add_fusion.1.l_ref, f32[12,128,128]{2,1,0:T(8,128)} %multiply_add_fusion.x_ref, ...), custom_call_target="tpu_custom_call" | custom-call | flops 228261888 | bytes 1868292 | tf_op jit(solution)/shard_map/pallas_call | solution.py:176
  227.4 5.5 %shard_map.279 = (f32[1,12,64,128]{3,2,1,0:T(8,128)}, f32[1,12,64,128]{3,2,1,0:T(8,128)}, f32[1,12,8,128]{3,2,1,0:T(8,128)}, f32[1,12,8,128]{3,2,1,0:T(8,128)}) custom-call(s32[1]{0:T(128)} %constant.52.clone.1.lead_ref, f32[1,12,64,128]{3,2,1,0:T(8,128)} %bitcast.87, f32[1,12,8,128]{3,2,1,0:T(8,128)} %bitcast.109, f32[1,12,8,128]{3,2,1,0:T(8,128)} %bitcast.119, ...), custom_call_target="tpu_custom_call" | custom-call | flops 228261888 | bytes 3637768 | tf_op jit(solution)/shard_map/pallas_call | solution.py:176
  236.4 6.4 %collective-permute-start.26 = (f32[1,12,8,128]{3,2,1,0:T(8,128)S(1)}, f32[1,12,8,128]{3,2,1,0:T(8,128)S(1)}, u32[]{:S(2)}, u32[]{:S(2)}) collective-permute-start(f32[1,12,8,128]{3,2,1,0:T(8,128)S(1)} %get-tuple-element.64), channel_id=1, source_target_pairs={{0,15},{1,8},{2,9},{3,10},{4,11},{5,12},{6,13},{7,14},{8,23},{9,16... | collective-permute-start | bytes 147464 | tf_op jit(solution)/shard_map/ppermute | solution.py:439
  245.8 5.6 %shard_map.280 = (f32[1,12,64,128]{3,2,1,0:T(8,128)}, f32[1,12,64,128]{3,2,1,0:T(8,128)}, f32[1,12,8,128]{3,2,1,0:T(8,128)}, f32[1,12,8,128]{3,2,1,0:T(8,128)}) custom-call(s32[1]{0:T(128)} %bitcast.11.lead_ref, f32[1,12,64,128]{3,2,1,0:T(8,128)} %copy-done.10, f32[1,12,8,128]{3,2,1,0:T(8,128)} %copy-done.35, f32[1,12,8,128]{3,2,1,0:T(8,128)} %copy-done.40, ...), custom_call_target="tpu_custom_call" | custom-call | flops 228261888 | bytes 3637768 | tf_op jit(solution)/shard_map/pallas_call | solution.py:176
  254.9 8.5 %collective-permute-start.29 = (f32[1,12,8,128]{3,2,1,0:T(8,128)S(1)}, f32[1,12,8,128]{3,2,1,0:T(8,128)S(1)}, u32[]{:S(2)}, u32[]{:S(2)}) collective-permute-start(f32[1,12,8,128]{3,2,1,0:T(8,128)S(1)} %get-tuple-element.62), channel_id=1, source_target_pairs={{0,15},{1,8},{2,9},{3,10},{4,11},{5,12},{6,13},{7,14},{8,23},{9,16... | collective-permute-start | bytes 147464 | tf_op jit(solution)/shard_map/ppermute | solution.py:439
  266.5 5.6 %shard_map.281 = (f32[1,12,64,128]{3,2,1,0:T(8,128)}, f32[1,12,64,128]{3,2,1,0:T(8,128)}, f32[1,12,8,128]{3,2,1,0:T(8,128)}, f32[1,12,8,128]{3,2,1,0:T(8,128)}) custom-call(s32[1]{0:T(128)} %bitcast.11.lead_ref, f32[1,12,64,128]{3,2,1,0:T(8,128)} %copy-done.11, f32[1,12,8,128]{3,2,1,0:T(8,128)} %copy-done.36, f32[1,12,8,128]{3,2,1,0:T(8,128)} %copy-done.41, ...), custom_call_target="tpu_custom_call" | custom-call | flops 228261888 | bytes 3637768 | tf_op jit(solution)/shard_map/pallas_call | solution.py:176
  275.5 8.5 %collective-permute-start.32 = (f32[1,12,8,128]{3,2,1,0:T(8,128)S(1)}, f32[1,12,8,128]{3,2,1,0:T(8,128)S(1)}, u32[]{:S(2)}, u32[]{:S(2)}) collective-permute-start(f32[1,12,8,128]{3,2,1,0:T(8,128)S(1)} %get-tuple-element.60), channel_id=1, source_target_pairs={{0,15},{1,8},{2,9},{3,10},{4,11},{5,12},{6,13},{7,14},{8,23},{9,16... | collective-permute-start | bytes 147464 | tf_op jit(solution)/shard_map/ppermute | solution.py:439
  287.2 5.5 %shard_map.282 = (f32[1,12,64,128]{3,2,1,0:T(8,128)}, f32[1,12,64,128]{3,2,1,0:T(8,128)}, f32[1,12,8,128]{3,2,1,0:T(8,128)}, f32[1,12,8,128]{3,2,1,0:T(8,128)}) custom-call(s32[1]{0:T(128)} %bitcast.11.lead_ref, f32[1,12,64,128]{3,2,1,0:T(8,128)} %copy-done.6, f32[1,12,8,128]{3,2,1,0:T(8,128)} %copy-done.30, f32[1,12,8,128]{3,2,1,0:T(8,128)} %copy-done.31, ...), custom_call_target="tpu_custom_call" | custom-call | flops 228261888 | bytes 3637768 | tf_op jit(solution)/shard_map/pallas_call | solution.py:176
  (198 shorter events, 84.6 us)
Async XLA Ops:
  2.6 18.2 %collective-permute-start = (f32[3,12,16,128]{3,2,1,0:T(8,128)S(1)}, f32[3,12,16,128]{3,2,1,0:T(8,128)S(1)}, u32[]{:S(2)}, u32[]{:S(2)}) collective-permute-start(f32[3,12,16,128]{3,2,1,0:T(8,128)S(1)} %get-tuple-element.51), channel_id=1, source_target_pairs={{0,1},{1,2},{2,3},{3,4},{4,5},{5,6},{6,7},{7,0},{8,9},{9,10},{10,1... | collective-permute-start | bytes 884744 | tf_op jit(solution)/shard_map/ppermute | solution.py:232
  5.7 16.5 %collective-permute-start.1 = (f32[3,12,16,128]{3,2,1,0:T(8,128)S(1)}, f32[3,12,16,128]{3,2,1,0:T(8,128)}, u32[]{:S(2)}, u32[]{:S(2)}) collective-permute-start(f32[3,12,16,128]{3,2,1,0:T(8,128)S(1)} %get-tuple-element.50), channel_id=1, source_target_pairs={{1,0},{2,1},{3,2},{4,3},{5,4},{6,5},{7,6},{0,7},{9,8},{10,9},{11,1... | collective-permute-start | bytes 884744 | tf_op jit(solution)/shard_map/ppermute | solution.py:233
  9.3 65.6 %collective-permute-start.6 = (f32[12,8,128]{2,1,0:T(8,128)S(1)}, f32[12,8,128]{2,1,0:T(8,128)S(1)}, u32[]{:S(2)}, u32[]{:S(2)}) collective-permute-start(f32[12,8,128]{2,1,0:T(8,128)S(1)} %get-tuple-element.73), channel_id=1, source_target_pairs={{0,1},{1,2},{2,3},{3,4},{4,5},{5,6},{6,7},{7,0},{8,9},{9,10},{10,1... | collective-permute-start | bytes 147464 | tf_op jit(solution)/shard_map/ppermute | solution.py:232
  9.4 65.6 %collective-permute-start.7 = (f32[12,8,128]{2,1,0:T(8,128)S(1)}, f32[12,8,128]{2,1,0:T(8,128)S(1)}, u32[]{:S(2)}, u32[]{:S(2)}) collective-permute-start(f32[12,8,128]{2,1,0:T(8,128)S(1)} %get-tuple-element.72), channel_id=1, source_target_pairs={{1,0},{2,1},{3,2},{4,3},{5,4},{6,5},{7,6},{0,7},{9,8},{10,9},{11,1... | collective-permute-start | bytes 147464 | tf_op jit(solution)/shard_map/ppermute | solution.py:233
  37.1 7.4 %collective-permute-start.2 = (f32[1,12,16,128]{3,2,1,0:T(8,128)S(1)}, f32[1,12,16,128]{3,2,1,0:T(8,128)S(1)}, u32[]{:S(2)}, u32[]{:S(2)}) collective-permute-start(f32[1,12,16,128]{3,2,1,0:T(8,128)S(1)} %get-tuple-element.59), channel_id=1, source_target_pairs={{0,1},{1,2},{2,3},{3,4},{4,5},{5,6},{6,7},{7,0},{8,9},{9,10},{10,1... | collective-permute-start | bytes 294920 | tf_op jit(solution)/shard_map/ppermute | solution.py:232
  38.0 6.4 %collective-permute-start.3 = (f32[1,12,16,128]{3,2,1,0:T(8,128)S(1)}, f32[1,12,16,128]{3,2,1,0:T(8,128)S(1)}, u32[]{:S(2)}, u32[]{:S(2)}) collective-permute-start(f32[1,12,16,128]{3,2,1,0:T(8,128)S(1)} %get-tuple-element.58), channel_id=1, source_target_pairs={{1,0},{2,1},{3,2},{4,3},{5,4},{6,5},{7,6},{0,7},{9,8},{10,9},{11,1... | collective-permute-start | bytes 294920 | tf_op jit(solution)/shard_map/ppermute | solution.py:233
  53.4 7.4 %collective-permute-start.4 = (f32[1,12,16,128]{3,2,1,0:T(8,128)S(1)}, f32[1,12,16,128]{3,2,1,0:T(8,128)S(1)}, u32[]{:S(2)}, u32[]{:S(2)}) collective-permute-start(f32[1,12,16,128]{3,2,1,0:T(8,128)S(1)} %get-tuple-element.57), channel_id=1, source_target_pairs={{0,1},{1,2},{2,3},{3,4},{4,5},{5,6},{6,7},{7,0},{8,9},{9,10},{10,1... | collective-permute-start | bytes 294920 | tf_op jit(solution)/shard_map/ppermute | solution.py:232
  53.9 6.9 %collective-permute-start.5 = (f32[1,12,16,128]{3,2,1,0:T(8,128)S(1)}, f32[1,12,16,128]{3,2,1,0:T(8,128)S(1)}, u32[]{:S(2)}, u32[]{:S(2)}) collective-permute-start(f32[1,12,16,128]{3,2,1,0:T(8,128)S(1)} %get-tuple-element.56), channel_id=1, source_target_pairs={{1,0},{2,1},{3,2},{4,3},{5,4},{6,5},{7,6},{0,7},{9,8},{10,9},{11,1... | collective-permute-start | bytes 294920 | tf_op jit(solution)/shard_map/ppermute | solution.py:233
  81.2 13.6 %collective-permute-start.8 = (f32[1,12,64,128]{3,2,1,0:T(8,128)}, f32[1,12,64,128]{3,2,1,0:T(8,128)S(1)}, u32[]{:S(2)}, u32[]{:S(2)}) collective-permute-start(f32[1,12,64,128]{3,2,1,0:T(8,128)} %get-tuple-element.32), channel_id=1, source_target_pairs={{0,8},{8,16},{16,24},{1,9},{9,17},{17,25},{2,10},{10,18},{18,26},{... | collective-permute-start | bytes 1179656 | tf_op jit(solution)/shard_map/ppermute | solution.py:435
  83.3 10.2 %collective-permute-start.10 = (f32[1,12,8,128]{3,2,1,0:T(8,128)S(1)}, f32[1,12,8,128]{3,2,1,0:T(8,128)S(1)}, u32[]{:S(2)}, u32[]{:S(2)}) collective-permute-start(f32[1,12,8,128]{3,2,1,0:T(8,128)S(1)} %get-tuple-element.70), channel_id=1, source_target_pairs={{0,15},{1,8},{2,9},{3,10},{4,11},{5,12},{6,13},{7,14},{8,23},{9,16... | collective-permute-start | bytes 147464 | tf_op jit(solution)/shard_map/ppermute | solution.py:439
  101.2 16.2 %collective-permute-start.11 = (f32[1,12,64,128]{3,2,1,0:T(8,128)}, f32[1,12,64,128]{3,2,1,0:T(8,128)S(1)}, u32[]{:S(2)}, u32[]{:S(2)}) collective-permute-start(f32[1,12,64,128]{3,2,1,0:T(8,128)} %get-tuple-element.33), channel_id=1, source_target_pairs={{0,8},{8,16},{16,24},{1,9},{9,17},{17,25},{2,10},{10,18},{18,26},{... | collective-permute-start | bytes 1179656 | tf_op jit(solution)/shard_map/ppermute | solution.py:435
  108.0 41.1 %collective-permute-start.17 = (f32[1,12,128,128]{3,2,1,0:T(8,128)S(1)}, f32[1,12,128,128]{3,2,1,0:T(8,128)S(1)}, u32[]{:S(2)}, u32[]{:S(2)}) collective-permute-start(f32[1,12,128,128]{3,2,1,0:T(8,128)S(1)} %copy-done.4), channel_id=1, source_target_pairs={{0,8},{8,16},{16,24},{1,9},{9,17},{17,25},{2,10},{10,18},{18,26},{... | collective-permute-start | bytes 2359304 | tf_op jit(solution)/shard_map/ppermute | solution.py:428
  110.8 4.9 %collective-permute-start.12 = (f32[1,12,8,128]{3,2,1,0:T(8,128)S(1)}, f32[1,12,8,128]{3,2,1,0:T(8,128)S(1)}, u32[]{:S(2)}, u32[]{:S(2)}) collective-permute-start(f32[1,12,8,128]{3,2,1,0:T(8,128)S(1)} %get-tuple-element.69), channel_id=1, source_target_pairs={{0,9},{1,10},{2,11},{3,12},{4,13},{5,14},{6,15},{7,8},{8,17},{9,18... | collective-permute-start | bytes 147464 | tf_op jit(solution)/shard_map/ppermute | solution.py:438
  112.1 5.3 %collective-permute-start.13 = (f32[1,12,8,128]{3,2,1,0:T(8,128)S(1)}, f32[1,12,8,128]{3,2,1,0:T(8,128)S(1)}, u32[]{:S(2)}, u32[]{:S(2)}) collective-permute-start(f32[1,12,8,128]{3,2,1,0:T(8,128)S(1)} %get-tuple-element.68), channel_id=1, source_target_pairs={{0,15},{1,8},{2,9},{3,10},{4,11},{5,12},{6,13},{7,14},{8,23},{9,16... | collective-permute-start | bytes 147464 | tf_op jit(solution)/shard_map/ppermute | solution.py:439
  124.4 17.7 %collective-permute-start.14 = (f32[1,12,64,128]{3,2,1,0:T(8,128)}, f32[1,12,64,128]{3,2,1,0:T(8,128)S(1)}, u32[]{:S(2)}, u32[]{:S(2)}) collective-permute-start(f32[1,12,64,128]{3,2,1,0:T(8,128)} %get-tuple-element.34), channel_id=1, source_target_pairs={{0,8},{8,16},{16,24},{1,9},{9,17},{17,25},{2,10},{10,18},{18,26},{... | collective-permute-start | bytes 1179656 | tf_op jit(solution)/shard_map/ppermute | solution.py:435
  132.1 8.2 %collective-permute-start.15 = (f32[1,12,8,128]{3,2,1,0:T(8,128)S(1)}, f32[1,12,8,128]{3,2,1,0:T(8,128)S(1)}, u32[]{:S(2)}, u32[]{:S(2)}) collective-permute-start(f32[1,12,8,128]{3,2,1,0:T(8,128)S(1)} %get-tuple-element.67), channel_id=1, source_target_pairs={{0,9},{1,10},{2,11},{3,12},{4,13},{5,14},{6,15},{7,8},{8,17},{9,18... | collective-permute-start | bytes 147464 | tf_op jit(solution)/shard_map/ppermute | solution.py:438
  137.6 4.5 %collective-permute-start.16 = (f32[1,12,8,128]{3,2,1,0:T(8,128)S(1)}, f32[1,12,8,128]{3,2,1,0:T(8,128)S(1)}, u32[]{:S(2)}, u32[]{:S(2)}) collective-permute-start(f32[1,12,8,128]{3,2,1,0:T(8,128)S(1)} %get-tuple-element.66), channel_id=1, source_target_pairs={{0,15},{1,8},{2,9},{3,10},{4,11},{5,12},{6,13},{7,14},{8,23},{9,16... | collective-permute-start | bytes 147464 | tf_op jit(solution)/shard_map/ppermute | solution.py:439
  157.2 13.8 %collective-permute-start.18 = (f32[3,12,16,128]{3,2,1,0:T(8,128)S(1)}, f32[3,12,16,128]{3,2,1,0:T(8,128)S(1)}, u32[]{:S(2)}, u32[]{:S(2)}) collective-permute-start(f32[3,12,16,128]{3,2,1,0:T(8,128)S(1)} %get-tuple-element.49), channel_id=1, source_target_pairs={{0,1},{1,2},{2,3},{3,4},{4,5},{5,6},{6,7},{7,0},{8,9},{9,10},{10,1... | collective-permute-start | bytes 884744 | tf_op jit(solution)/shard_map/ppermute | solution.py:232
  157.8 15.9 %collective-permute-start.19 = (f32[3,12,16,128]{3,2,1,0:T(8,128)S(1)}, f32[3,12,16,128]{3,2,1,0:T(8,128)S(1)}, u32[]{:S(2)}, u32[]{:S(2)}) collective-permute-start(f32[3,12,16,128]{3,2,1,0:T(8,128)S(1)} %get-tuple-element.48), channel_id=1, source_target_pairs={{1,0},{2,1},{3,2},{4,3},{5,4},{6,5},{7,6},{0,7},{9,8},{10,9},{11,1... | collective-permute-start | bytes 884744 | tf_op jit(solution)/shard_map/ppermute | solution.py:233
  189.4 7.6 %collective-permute-start.20 = (f32[1,12,16,128]{3,2,1,0:T(8,128)S(1)}, f32[1,12,16,128]{3,2,1,0:T(8,128)S(1)}, u32[]{:S(2)}, u32[]{:S(2)}) collective-permute-start(f32[1,12,16,128]{3,2,1,0:T(8,128)S(1)} %get-tuple-element.55), channel_id=1, source_target_pairs={{0,1},{1,2},{2,3},{3,4},{4,5},{5,6},{6,7},{7,0},{8,9},{9,10},{10,1... | collective-permute-start | bytes 294920 | tf_op jit(solution)/shard_map/ppermute | solution.py:232
  189.9 7.1 %collective-permute-start.21 = (f32[1,12,16,128]{3,2,1,0:T(8,128)S(1)}, f32[1,12,16,128]{3,2,1,0:T(8,128)S(1)}, u32[]{:S(2)}, u32[]{:S(2)}) collective-permute-start(f32[1,12,16,128]{3,2,1,0:T(8,128)S(1)} %get-tuple-element.54), channel_id=1, source_target_pairs={{1,0},{2,1},{3,2},{4,3},{5,4},{6,5},{7,6},{0,7},{9,8},{10,9},{11,1... | collective-permute-start | bytes 294920 | tf_op jit(solution)/shard_map/ppermute | solution.py:233
  205.9 7.4 %collective-permute-start.22 = (f32[1,12,16,128]{3,2,1,0:T(8,128)S(1)}, f32[1,12,16,128]{3,2,1,0:T(8,128)S(1)}, u32[]{:S(2)}, u32[]{:S(2)}) collective-permute-start(f32[1,12,16,128]{3,2,1,0:T(8,128)S(1)} %get-tuple-element.53), channel_id=1, source_target_pairs={{0,1},{1,2},{2,3},{3,4},{4,5},{5,6},{6,7},{7,0},{8,9},{9,10},{10,1... | collective-permute-start | bytes 294920 | tf_op jit(solution)/shard_map/ppermute | solution.py:232
  206.1 7.2 %collective-permute-start.23 = (f32[1,12,16,128]{3,2,1,0:T(8,128)S(1)}, f32[1,12,16,128]{3,2,1,0:T(8,128)S(1)}, u32[]{:S(2)}, u32[]{:S(2)}) collective-permute-start(f32[1,12,16,128]{3,2,1,0:T(8,128)S(1)} %get-tuple-element.52), channel_id=1, source_target_pairs={{1,0},{2,1},{3,2},{4,3},{5,4},{6,5},{7,6},{0,7},{9,8},{10,9},{11,1... | collective-permute-start | bytes 294920 | tf_op jit(solution)/shard_map/ppermute | solution.py:233
  233.0 11.5 %collective-permute-start.24 = (f32[1,12,64,128]{3,2,1,0:T(8,128)}, f32[1,12,64,128]{3,2,1,0:T(8,128)S(1)}, u32[]{:S(2)}, u32[]{:S(2)}) collective-permute-start(f32[1,12,64,128]{3,2,1,0:T(8,128)} %get-tuple-element.44), channel_id=1, source_target_pairs={{0,8},{8,16},{16,24},{1,9},{9,17},{17,25},{2,10},{10,18},{18,26},{... | collective-permute-start | bytes 1179656 | tf_op jit(solution)/shard_map/ppermute | solution.py:435
  235.1 7.7 %collective-permute-start.25 = (f32[1,12,8,128]{3,2,1,0:T(8,128)S(1)}, f32[1,12,8,128]{3,2,1,0:T(8,128)S(1)}, u32[]{:S(2)}, u32[]{:S(2)}) collective-permute-start(f32[1,12,8,128]{3,2,1,0:T(8,128)S(1)} %get-tuple-element.65), channel_id=1, source_target_pairs={{0,9},{1,10},{2,11},{3,12},{4,13},{5,14},{6,15},{7,8},{8,17},{9,18... | collective-permute-start | bytes 147464 | tf_op jit(solution)/shard_map/ppermute | solution.py:438
  236.4 8.1 %collective-permute-start.26 = (f32[1,12,8,128]{3,2,1,0:T(8,128)S(1)}, f32[1,12,8,128]{3,2,1,0:T(8,128)S(1)}, u32[]{:S(2)}, u32[]{:S(2)}) collective-permute-start(f32[1,12,8,128]{3,2,1,0:T(8,128)S(1)} %get-tuple-element.64), channel_id=1, source_target_pairs={{0,15},{1,8},{2,9},{3,10},{4,11},{5,12},{6,13},{7,14},{8,23},{9,16... | collective-permute-start | bytes 147464 | tf_op jit(solution)/shard_map/ppermute | solution.py:439
  251.5 13.7 %collective-permute-start.27 = (f32[1,12,64,128]{3,2,1,0:T(8,128)}, f32[1,12,64,128]{3,2,1,0:T(8,128)S(1)}, u32[]{:S(2)}, u32[]{:S(2)}) collective-permute-start(f32[1,12,64,128]{3,2,1,0:T(8,128)} %get-tuple-element.45), channel_id=1, source_target_pairs={{0,8},{8,16},{16,24},{1,9},{9,17},{17,25},{2,10},{10,18},{18,26},{... | collective-permute-start | bytes 1179656 | tf_op jit(solution)/shard_map/ppermute | solution.py:435
  253.6 9.8 %collective-permute-start.28 = (f32[1,12,8,128]{3,2,1,0:T(8,128)S(1)}, f32[1,12,8,128]{3,2,1,0:T(8,128)S(1)}, u32[]{:S(2)}, u32[]{:S(2)}) collective-permute-start(f32[1,12,8,128]{3,2,1,0:T(8,128)S(1)} %get-tuple-element.63), channel_id=1, source_target_pairs={{0,9},{1,10},{2,11},{3,12},{4,13},{5,14},{6,15},{7,8},{8,17},{9,18... | collective-permute-start | bytes 147464 | tf_op jit(solution)/shard_map/ppermute | solution.py:438
  254.9 10.2 %collective-permute-start.29 = (f32[1,12,8,128]{3,2,1,0:T(8,128)S(1)}, f32[1,12,8,128]{3,2,1,0:T(8,128)S(1)}, u32[]{:S(2)}, u32[]{:S(2)}) collective-permute-start(f32[1,12,8,128]{3,2,1,0:T(8,128)S(1)} %get-tuple-element.62), channel_id=1, source_target_pairs={{0,15},{1,8},{2,9},{3,10},{4,11},{5,12},{6,13},{7,14},{8,23},{9,16... | collective-permute-start | bytes 147464 | tf_op jit(solution)/shard_map/ppermute | solution.py:439
  272.1 13.7 %collective-permute-start.30 = (f32[1,12,64,128]{3,2,1,0:T(8,128)}, f32[1,12,64,128]{3,2,1,0:T(8,128)S(1)}, u32[]{:S(2)}, u32[]{:S(2)}) collective-permute-start(f32[1,12,64,128]{3,2,1,0:T(8,128)} %get-tuple-element.46), channel_id=1, source_target_pairs={{0,8},{8,16},{16,24},{1,9},{9,17},{17,25},{2,10},{10,18},{18,26},{... | collective-permute-start | bytes 1179656 | tf_op jit(solution)/shard_map/ppermute | solution.py:435
  274.3 9.8 %collective-permute-start.31 = (f32[1,12,8,128]{3,2,1,0:T(8,128)S(1)}, f32[1,12,8,128]{3,2,1,0:T(8,128)S(1)}, u32[]{:S(2)}, u32[]{:S(2)}) collective-permute-start(f32[1,12,8,128]{3,2,1,0:T(8,128)S(1)} %get-tuple-element.61), channel_id=1, source_target_pairs={{0,9},{1,10},{2,11},{3,12},{4,13},{5,14},{6,15},{7,8},{8,17},{9,18... | collective-permute-start | bytes 147464 | tf_op jit(solution)/shard_map/ppermute | solution.py:438
  275.5 10.2 %collective-permute-start.32 = (f32[1,12,8,128]{3,2,1,0:T(8,128)S(1)}, f32[1,12,8,128]{3,2,1,0:T(8,128)S(1)}, u32[]{:S(2)}, u32[]{:S(2)}) collective-permute-start(f32[1,12,8,128]{3,2,1,0:T(8,128)S(1)} %get-tuple-element.60), channel_id=1, source_target_pairs={{0,15},{1,8},{2,9},{3,10},{4,11},{5,12},{6,13},{7,14},{8,23},{9,16... | collective-permute-start | bytes 147464 | tf_op jit(solution)/shard_map/ppermute | solution.py:439
  (59 other events, 179.8 us)

commit v3 on v2

--- a/solution.py
+++ b/solution.py
@@ -121,37 +121,43 @@
     return [wide[:, i * width:(i + 1) * width] for i in range(wide.shape[1] // width)]
 
 
-def tendency_into(out_ref, b, v_ref, prev_ref, next_ref, lop_ref, xt_ref, zc_ref, rx_ref,
+def tendency_into(out_ref, v_ref, prev_ref, next_ref, lop_ref, xt_ref, zc_ref, rx_ref,
                   rate_ref, en_ref, s_ref):
-    fields, span = v_ref.shape[1], v_ref.shape[2]
+    states, fields, span, columns = v_ref.shape
     rows = prev_ref.shape[2]
 
     def field_body(f, carry):
-        v = v_ref[b, f]
-        out_ref[b, f] = tdot(lop_ref[f], v) + tdot(v, xt_ref[f])
-        out_ref[b, f, pl.ds(0, rows), :] = (
-            out_ref[b, f, pl.ds(0, rows), :] + zc_ref[0, f] * prev_ref[b, f]
-        )
-        out_ref[b, f, pl.ds(span - rows, rows), :] = (
-            out_ref[b, f, pl.ds(span - rows, rows), :] + zc_ref[1, f] * next_ref[b, f]
-        )
-        s_ref[f] = jnp.tanh(v)
+        parts = [v_ref[b, f] for b in range(states)]
+        left = unlanes(tdot(lop_ref[f], lanes(parts)), columns)
+        right = tdot(jnp.concatenate(parts, axis=0), xt_ref[f])
+        for b in range(states):
+            out_ref[b, f] = left[b] + right[b * span:(b + 1) * span]
+            out_ref[b, f, pl.ds(0, rows), :] = (
+                out_ref[b, f, pl.ds(0, rows), :] + zc_ref[0, f] * prev_ref[b, f]
+            )
+            out_ref[b, f, pl.ds(span - rows, rows), :] = (
+                out_ref[b, f, pl.ds(span - rows, rows), :] + zc_ref[1, f] * next_ref[b, f]
+            )
+            s_ref[b, f] = jnp.tanh(parts[b])
         return carry
 
     lax.fori_loop(0, fields, field_body, 0)
-    cooling = 1.0 / (1.5 + 0.5 * s_ref[fields - 1])
-
-    def reaction_body(r, carry):
-        first = rx_ref[r, 0]
-        second = rx_ref[r, 1]
-        product = rx_ref[r, 2]
-        progress = rate_ref[r] * jnp.exp(-en_ref[r] * cooling) * s_ref[first] * s_ref[second]
-        out_ref[b, product] = out_ref[b, product] + progress
-        out_ref[b, first] = out_ref[b, first] - progress
-        out_ref[b, second] = out_ref[b, second] - progress
-        return carry
-
-    lax.fori_loop(0, rx_ref.shape[0], reaction_body, 0)
+    for b in range(states):
+        cooling = 1.0 / (1.5 + 0.5 * s_ref[b, fields - 1])
+
+        def reaction_body(r, carry):
+            first = rx_ref[r, 0]
+            second = rx_ref[r, 1]
+            product = rx_ref[r, 2]
+            progress = (
+                rate_ref[r] * jnp.exp(-en_ref[r] * cooling) * s_ref[b, first] * s_ref[b, second]
+            )
+            out_ref[b, product] = out_ref[b, product] + progress
+            out_ref[b, first] = out_ref[b, first] - progress
+            out_ref[b, second] = out_ref[b, second] - progress
+            return carry
+
+        lax.fori_loop(0, rx_ref.shape[0], reaction_body, 0)
 
 
 def vmem():
@@ -239,9 +245,8 @@
 
     def nodes_kernel(u_ref, p_ref, n_ref, l_ref, x_ref, zc_ref, rx_ref, ra_ref, en_ref,
                      f_ref, a1_ref, s_ref):
-        for b in range(u_ref.shape[0]):
-            tendency_into(f_ref, b, u_ref, p_ref, n_ref, l_ref, x_ref, zc_ref, rx_ref, ra_ref,
-                          en_ref, s_ref)
+        tendency_into(f_ref, u_ref, p_ref, n_ref, l_ref, x_ref, zc_ref, rx_ref, ra_ref, en_ref,
+                      s_ref)
 
         def body(f, carry):
             a1_ref[0, f] = u_ref[0, f] + STEP * (
@@ -253,7 +258,7 @@
 
     def middle_kernel(a1_ref, p_ref, n_ref, l_ref, x_ref, zc_ref, rx_ref, ra_ref, en_ref,
                       f_ref, g1_ref, a2_ref, s_ref):
-        tendency_into(g1_ref, 0, a1_ref, p_ref, n_ref, l_ref, x_ref, zc_ref, rx_ref, ra_ref,
+        tendency_into(g1_ref, a1_ref, p_ref, n_ref, l_ref, x_ref, zc_ref, rx_ref, ra_ref,
                       en_ref, s_ref)
 
         def body(f, carry):
@@ -268,7 +273,7 @@
 
     def ending_kernel(a2_ref, p_ref, n_ref, l_ref, x_ref, zc_ref, rx_ref, ra_ref, en_ref,
                       f_ref, g1_ref, u_ref, r_ref, rint_ref, c1_ref, c0_ref, g2_ref, s_ref):
-        tendency_into(g2_ref, 0, a2_ref, p_ref, n_ref, l_ref, x_ref, zc_ref, rx_ref, ra_ref,
+        tendency_into(g2_ref, a2_ref, p_ref, n_ref, l_ref, x_ref, zc_ref, rx_ref, ra_ref,
                       en_ref, s_ref)
 
         def body(f, carry):
@@ -282,9 +287,14 @@
             for f, part in enumerate(unlanes(wide, columns)):
                 dst[f] = part
 
-    def base_kernel(c_ref, p_ref, n_ref, l_ref, x_ref, zc_ref, rx_ref, ra_ref, en_ref,
-                    out_ref, s_ref):
-        tendency_into(out_ref, 0, c_ref, p_ref, n_ref, l_ref, x_ref, zc_ref, rx_ref, ra_ref,
+    def base_kernel(c_ref, p_ref, n_ref, r_ref, l_ref, x_ref, zc_ref, rx_ref, ra_ref, en_ref,
+                    out_ref, bp_ref, bn_ref, s_ref):
+        rm = r_ref[...]
+        for dst, src_ref in ((bp_ref, p_ref), (bn_ref, n_ref)):
+            wide = dot(rm, lanes([src_ref[0, f] for f in range(fields)]))
+            for f, part in enumerate(unlanes(wide, columns)):
+                dst[0, f] = part
+        tendency_into(out_ref, c_ref, bp_ref, bn_ref, l_ref, x_ref, zc_ref, rx_ref, ra_ref,
                       en_ref, s_ref)
 
     def chain_kernel(lead_ref, w_ref, p_ref, n_ref, ws_ref, ps_ref, ns_ref, l_ref, x_ref,
@@ -302,7 +312,7 @@
             bp_ref[...] = p_ref[...]
             bn_ref[...] = n_ref[...]
 
-        tendency_into(g_ref, 0, begin_ref, bp_ref, bn_ref, l_ref, x_ref, zc_ref, rx_ref, ra_ref,
+        tendency_into(g_ref, begin_ref, bp_ref, bn_ref, l_ref, x_ref, zc_ref, rx_ref, ra_ref,
                       en_ref, s_ref)
 
         def body(f, carry):
@@ -343,11 +353,11 @@
     fine_cost = tendency_cost(1, fields, span, columns, reaction_count)
     coarse_cost = tendency_cost(1, fields, coarse_span, columns, reaction_count)
 
-    def fine_scratch():
-        return pltpu.VMEM((fields, span, columns), f32)
-
-    def coarse_scratch():
-        return pltpu.VMEM((fields, coarse_span, columns), f32)
+    def fine_scratch(states):
+        return pltpu.VMEM((states, fields, span, columns), f32)
+
+    def coarse_scratch(states):
+        return pltpu.VMEM((states, fields, coarse_span, columns), f32)
 
     u_flat = u_start.reshape(fields, span, columns)
     nodes = guess[0].reshape(3, fields, span, columns)
@@ -366,7 +376,7 @@
              start_halo[1][None], lop_coarse, xt) + scalars + (base, rint),
             (True,) + (False,) * 8 + scalar_kinds + (False, False),
             (coarse_one, coarse_one, plane_one, plane_one),
-            [pltpu.VMEM((1, fields, coarse_span, columns), f32), coarse_scratch()],
+            [pltpu.VMEM((1, fields, coarse_span, columns), f32), coarse_scratch(1)],
             *coarse_cost,
         )
 
@@ -392,18 +402,16 @@
             (nodes, node_prev, node_next, lop_fine, xt) + scalars,
             (False,) * 5 + scalar_kinds,
             (jax.ShapeDtypeStruct((3, fields, span, columns), f32), fine_state),
-            [fine_scratch()],
+            [fine_scratch(3)],
             fine_cost[0] * 3, fine_cost[1] * 3,
         )
-        c0_prev = jnp.einsum("cy,fyx->fcx", restrict_plane, node_prev[0], precision=HIGHEST)
-        c0_next = jnp.einsum("cy,fyx->fcx", restrict_plane, node_next[0], precision=HIGHEST)
         a1_prev, a1_next = halo(a1, rows)
         g1, a2 = call(
             middle_kernel,
             (a1, a1_prev, a1_next, lop_fine, xt) + scalars + (f_all,),
             (False,) * 5 + scalar_kinds + (False,),
             (fine_state, fine_state),
-            [fine_scratch()],
+            [fine_scratch(1)],
             *fine_cost,
         )
         a2_prev, a2_next = halo(a2, rows)
@@ -412,15 +420,16 @@
             (a2, a2_prev, a2_next, lop_fine, xt) + scalars + (f_all, g1, nodes, rmat),
             (False,) * 5 + scalar_kinds + (False,) * 4,
             (coarse_state, coarse_state, coarse_state),
-            [pltpu.VMEM((1, fields, span, columns), f32), fine_scratch()],
+            [pltpu.VMEM((1, fields, span, columns), f32), fine_scratch(1)],
             *fine_cost,
         )
         (base,) = call(
             base_kernel,
-            (c0[None], c0_prev[None], c0_next[None], lop_coarse, xt) + scalars,
-            (False,) * 5 + scalar_kinds,
+            (c0[None], node_prev, node_next, restrict_plane, lop_coarse, xt) + scalars,
+            (False,) * 6 + scalar_kinds,
             (jax.ShapeDtypeStruct((1, fields, coarse_span, columns), f32),),
-            [coarse_scratch()],
+            [pltpu.VMEM((1, fields, coarse_rows, columns), f32),
+             pltpu.VMEM((1, fields, coarse_rows, columns), f32), coarse_scratch(1)],
             *coarse_cost,
         )
         last = iteration + 1 == ITERS

time: 297 us -> 293 us (0.987)
  matrix products: 7.24 us -> 1.18 us
  waiting for transfers between devices: 27.2 us -> 33.2 us
  Pallas kernels: 123 us -> 117 us
    dot_general x4 -> x0, matrix products: 6.74 us -> none  [the longest x2 3.38 us: per_device(): jnp.einsum('cy,fyx->fcx', restrict_plane, node_next[0], precision=HIGHEST)]
    pallas_call x18, Pallas kernels: 123 us -> 117 us  [call(): pl.pallas_call(kernel, out_shape=outs, in_specs=[smem() if k else vmem()...]
    ppermute x7, waiting for transfers between devices: 12.8 us -> 17.9 us  [halo(): lax.ppermute(tail, 'space', [(i, (i + 1) % space_n) for i in range(space_...]
    unnamed x115 -> x119, local copies, waits for them, and re-layouts: 13.4 us -> 14.7 us
  transfers between devices with their start and end apart: 33 -> 33, of which waited for: 14 -> 14; matrix products, arithmetic and copies ran while one was open for 7% -> 5% of each run, Pallas kernels for 16% -> 11%
where the time goes in v3:
time: 293 us; the launch traced here: 291 us
  Pallas kernels  117 us (40%)
  starting transfers between devices  106 us (36%)
  waiting for transfers between devices  33.2 us (11%)
  local copies, waits for them, and re-layouts  26.5 us (9%)
  other arithmetic  5.82 us (2%)
    pallas_call x18, Pallas kernels, call(): pl.pallas_call(kernel, out_shape=outs, in_specs=[smem() if k else vmem()...  117 us
    ppermute x6, starting transfers between devices, per_device(): lax.ppermute(head, both, next_pairs)  38.1 us
    ppermute x7, starting transfers between devices, halo(): lax.ppermute(head, 'space', [((i + 1) % space_n, i) for i in range(space_...  29.3 us
    ppermute x6, starting transfers between devices, per_device(): begin = lax.ppermute(finish, 'tm', hop_pairs)  18.9 us
    ppermute x7, waiting for transfers between devices, halo(): lax.ppermute(tail, 'space', [(i, (i + 1) % space_n) for i in range(space_...  17.9 us
    unnamed x119, local copies, waits for them, and re-layouts  14.7 us
    ppermute x6, starting transfers between devices, per_device(): lax.ppermute(tail, both, prev_pairs)  11.9 us
    ppermute x6, waiting for transfers between devices, per_device(): lax.ppermute(head, both, next_pairs)  8.98 us
  transfers between devices with their start and end apart: 33, of which 14 were waited for; matrix products, arithmetic and copies ran while one was open for 5% of the time, Pallas kernels for 11%

profile of v3, /device:TPU:0, one launch (start us, length us, event | category | flops | bytes accessed | tf_op | source)
XLA Modules:
  0.0 291.0 jit_solution(1193145298254334618)
XLA Ops:
  21.1 10.5 %shard_map.266 = (f32[3,12,128,128]{3,2,1,0:T(8,128)}, f32[1,12,128,128]{3,2,1,0:T(8,128)}) custom-call(f32[3,12,128,128]{3,2,1,0:T(8,128)} %pad_maximum_fusion.u_ref, f32[3,12,16,128]{3,2,1,0:T(8,128)} %copy-done.12, f32[3,12,16,128]{3,2,1,0:T(8,128)} %copy-done.13, f32[12,128,128]{2,1,0:T(8,128)} %add_add_fusion.l_ref, ...), custom_call_target="tpu_custom_call" | custom-call | flops 1822556160 | bytes 7668228 | tf_op jit(solution)/shard_map/pallas_call | solution.py:182
  33.7 3.7 %collective-permute-start.3 = (f32[1,12,16,128]{3,2,1,0:T(8,128)S(1)}, f32[1,12,16,128]{3,2,1,0:T(8,128)S(1)}, u32[]{:S(2)}, u32[]{:S(2)}) collective-permute-start(f32[1,12,16,128]{3,2,1,0:T(8,128)S(1)} %get-tuple-element.58), channel_id=1, source_target_pairs={{1,0},{2,1},{3,2},{4,3},{5,4},{6,5},{7,6},{0,7},{9,8},{10,9},{11,1... | collective-permute-start | bytes 294920 | tf_op jit(solution)/shard_map/ppermute | solution.py:239
  37.5 4.7 %collective-permute-start.7 = (f32[12,8,128]{2,1,0:T(8,128)S(1)}, f32[12,8,128]{2,1,0:T(8,128)S(1)}, u32[]{:S(2)}, u32[]{:S(2)}) collective-permute-start(f32[12,8,128]{2,1,0:T(8,128)S(1)} %get-tuple-element.72), channel_id=1, source_target_pairs={{1,0},{2,1},{3,2},{4,3},{5,4},{6,5},{7,6},{0,7},{9,8},{10,9},{11,1... | collective-permute-start | bytes 147464 | tf_op jit(solution)/shard_map/ppermute | solution.py:239
  42.9 7.4 %shard_map.267 = (f32[1,12,128,128]{3,2,1,0:T(8,128)}, f32[1,12,128,128]{3,2,1,0:T(8,128)}) custom-call(f32[1,12,128,128]{3,2,1,0:T(8,128)} %get-tuple-element.25.a1_ref, f32[1,12,16,128]{3,2,1,0:T(8,128)} %copy-done.20, f32[1,12,16,128]{3,2,1,0:T(8,128)} %copy-done.21, f32[12,128,128]{2,1,0:T(8,128)} %add_add_fusion.l_ref, ...), custom_call_target="tpu_custom_call" | custom-call | flops 607518720 | bytes 6488580 | tf_op jit(solution)/shard_map/pallas_call | solution.py:182
  51.3 4.7 %collective-permute-start.5 = (f32[1,12,16,128]{3,2,1,0:T(8,128)S(1)}, f32[1,12,16,128]{3,2,1,0:T(8,128)S(1)}, u32[]{:S(2)}, u32[]{:S(2)}) collective-permute-start(f32[1,12,16,128]{3,2,1,0:T(8,128)S(1)} %get-tuple-element.56), channel_id=1, source_target_pairs={{1,0},{2,1},{3,2},{4,3},{5,4},{6,5},{7,6},{0,7},{9,8},{10,9},{11,1... | collective-permute-start | bytes 294920 | tf_op jit(solution)/shard_map/ppermute | solution.py:239
  59.3 8.7 %shard_map.268 = (f32[12,64,128]{2,1,0:T(8,128)}, f32[12,64,128]{2,1,0:T(8,128)}, f32[12,64,128]{2,1,0:T(8,128)}) custom-call(f32[1,12,128,128]{3,2,1,0:T(8,128)} %get-tuple-element.27.a2_ref, f32[1,12,16,128]{3,2,1,0:T(8,128)} %copy-done.16, f32[1,12,16,128]{3,2,1,0:T(8,128)} %copy-done.17, f32[12,128,128]{2,1,0:T(8,128)} %add_add_fusion.l_ref, ...), custom_call_target="tpu_custom_call" | custom-call | flops 607518720 | bytes 9273860 | tf_op jit(solution)/shard_map/pallas_call | solution.py:182
  68.0 5.3 %shard_map.269.base_ref = f32[1,12,64,128]{3,2,1,0:T(8,128)} custom-call(f32[1,12,64,128]{3,2,1,0:T(8,128)} %bitcast.92, f32[3,12,16,128]{3,2,1,0:T(8,128)} %copy-done.12, f32[3,12,16,128]{3,2,1,0:T(8,128)} %copy-done.13, f32[8,16]{1,0:T(8,128)} %constant.73.clone.r_ref, f32[12,64,64]{2,1,0:T(8,128)} %add_add_fusion.1.l_ref, ...), custom_call_target="tpu_custom_call" | custom-call | flops 228261888 | bytes 2360324 | tf_op jit(solution)/shard_map/pallas_call | solution.py:182
  73.9 5.6 %shard_map.270 = (f32[1,12,64,128]{3,2,1,0:T(8,128)}, f32[1,12,64,128]{3,2,1,0:T(8,128)}, f32[1,12,8,128]{3,2,1,0:T(8,128)}, f32[1,12,8,128]{3,2,1,0:T(8,128)}) custom-call(s32[1]{0:T(128)} %constant.52.clone.1.lead_ref, f32[1,12,64,128]{3,2,1,0:T(8,128)} %bitcast.49, f32[1,12,8,128]{3,2,1,0:T(8,128)} %bitcast.71, f32[1,12,8,128]{3,2,1,0:T(8,128)} %bitcast.81, ...), custom_call_target="tpu_custom_call" | custom-call | flops 228261888 | bytes 3637768 | tf_op jit(solution)/shard_map/pallas_call | solution.py:182
  81.7 8.4 %collective-permute-start.10 = (f32[1,12,8,128]{3,2,1,0:T(8,128)S(1)}, f32[1,12,8,128]{3,2,1,0:T(8,128)S(1)}, u32[]{:S(2)}, u32[]{:S(2)}) collective-permute-start(f32[1,12,8,128]{3,2,1,0:T(8,128)S(1)} %get-tuple-element.70), channel_id=1, source_target_pairs={{0,15},{1,8},{2,9},{3,10},{4,11},{5,12},{6,13},{7,14},{8,23},{9,16... | collective-permute-start | bytes 147464 | tf_op jit(solution)/shard_map/ppermute | solution.py:448
  93.9 5.6 %shard_map.271 = (f32[1,12,64,128]{3,2,1,0:T(8,128)}, f32[1,12,64,128]{3,2,1,0:T(8,128)}, f32[1,12,8,128]{3,2,1,0:T(8,128)}, f32[1,12,8,128]{3,2,1,0:T(8,128)}) custom-call(s32[1]{0:T(128)} %bitcast.11.lead_ref, f32[1,12,64,128]{3,2,1,0:T(8,128)} %copy-done.8, f32[1,12,8,128]{3,2,1,0:T(8,128)} %copy-done.40, f32[1,12,8,128]{3,2,1,0:T(8,128)} %copy-done.35, ...), custom_call_target="tpu_custom_call" | custom-call | flops 228261888 | bytes 3637768 | tf_op jit(solution)/shard_map/pallas_call | solution.py:182
  99.5 6.8 %collective-permute-start.11 = (f32[1,12,64,128]{3,2,1,0:T(8,128)}, f32[1,12,64,128]{3,2,1,0:T(8,128)S(1)}, u32[]{:S(2)}, u32[]{:S(2)}) collective-permute-start(f32[1,12,64,128]{3,2,1,0:T(8,128)} %get-tuple-element.33), channel_id=1, source_target_pairs={{0,8},{8,16},{16,24},{1,9},{9,17},{17,25},{2,10},{10,18},{18,26},{... | collective-permute-start | bytes 1179656 | tf_op jit(solution)/shard_map/ppermute | solution.py:444
  110.4 3.6 %collective-permute-start.13 = (f32[1,12,8,128]{3,2,1,0:T(8,128)S(1)}, f32[1,12,8,128]{3,2,1,0:T(8,128)S(1)}, u32[]{:S(2)}, u32[]{:S(2)}) collective-permute-start(f32[1,12,8,128]{3,2,1,0:T(8,128)S(1)} %get-tuple-element.68), channel_id=1, source_target_pairs={{0,15},{1,8},{2,9},{3,10},{4,11},{5,12},{6,13},{7,14},{8,23},{9,16... | collective-permute-start | bytes 147464 | tf_op jit(solution)/shard_map/ppermute | solution.py:448
  117.1 5.6 %shard_map.272 = (f32[1,12,64,128]{3,2,1,0:T(8,128)}, f32[1,12,64,128]{3,2,1,0:T(8,128)}, f32[1,12,8,128]{3,2,1,0:T(8,128)}, f32[1,12,8,128]{3,2,1,0:T(8,128)}) custom-call(s32[1]{0:T(128)} %bitcast.11.lead_ref, f32[1,12,64,128]{3,2,1,0:T(8,128)} %copy-done.7, f32[1,12,8,128]{3,2,1,0:T(8,128)} %copy-done.37, f32[1,12,8,128]{3,2,1,0:T(8,128)} %copy-done.42, ...), custom_call_target="tpu_custom_call" | custom-call | flops 228261888 | bytes 3637768 | tf_op jit(solution)/shard_map/pallas_call | solution.py:182
  122.7 6.9 %collective-permute-start.14 = (f32[1,12,64,128]{3,2,1,0:T(8,128)}, f32[1,12,64,128]{3,2,1,0:T(8,128)S(1)}, u32[]{:S(2)}, u32[]{:S(2)}) collective-permute-start(f32[1,12,64,128]{3,2,1,0:T(8,128)} %get-tuple-element.34), channel_id=1, source_target_pairs={{0,8},{8,16},{16,24},{1,9},{9,17},{17,25},{2,10},{10,18},{18,26},{... | collective-permute-start | bytes 1179656 | tf_op jit(solution)/shard_map/ppermute | solution.py:444
  130.5 5.4 %collective-permute-start.15 = (f32[1,12,8,128]{3,2,1,0:T(8,128)S(1)}, f32[1,12,8,128]{3,2,1,0:T(8,128)S(1)}, u32[]{:S(2)}, u32[]{:S(2)}) collective-permute-start(f32[1,12,8,128]{3,2,1,0:T(8,128)S(1)} %get-tuple-element.67), channel_id=1, source_target_pairs={{0,9},{1,10},{2,11},{3,12},{4,13},{5,14},{6,15},{7,8},{8,17},{9,18... | collective-permute-start | bytes 147464 | tf_op jit(solution)/shard_map/ppermute | solution.py:447
  141.8 5.6 %shard_map.273 = (f32[1,12,64,128]{3,2,1,0:T(8,128)}, f32[1,12,64,128]{3,2,1,0:T(8,128)}, f32[1,12,8,128]{3,2,1,0:T(8,128)}, f32[1,12,8,128]{3,2,1,0:T(8,128)}) custom-call(s32[1]{0:T(128)} %bitcast.11.lead_ref, f32[1,12,64,128]{3,2,1,0:T(8,128)} %copy-done.9, f32[1,12,8,128]{3,2,1,0:T(8,128)} %copy-done.36, f32[1,12,8,128]{3,2,1,0:T(8,128)} %copy-done.41, ...), custom_call_target="tpu_custom_call" | custom-call | flops 228261888 | bytes 3637768 | tf_op jit(solution)/shard_map/pallas_call | solution.py:182
  148.2 6.1 %shard_map.274.u_ref = f32[3,12,128,128]{3,2,1,0:T(8,128)} custom-call(f32[1,12,128,128]{3,2,1,0:T(8,128)} %get-tuple-element.25.a1_ref, f32[1,12,128,128]{3,2,1,0:T(8,128)} %get-tuple-element.27.a2_ref, f32[12,64,128]{2,1,0:T(8,128)} %get-tuple-element.29.c0_ref, f32[12,64,128]{2,1,0:T(8,128)} %get-tuple-element.30.c1_ref, f32[12,64,128]{2,1,0:T(8,128)} %bitcast.95, ...), custom_call_target="tpu_custom_call" | custom-call | flops 603979776 | bytes 7143428 | tf_op jit(solution)/shard_map/pallas_call | solution.py:182
  156.1 4.1 %collective-permute-start.19 = (f32[3,12,16,128]{3,2,1,0:T(8,128)S(1)}, f32[3,12,16,128]{3,2,1,0:T(8,128)S(1)}, u32[]{:S(2)}, u32[]{:S(2)}) collective-permute-start(f32[3,12,16,128]{3,2,1,0:T(8,128)S(1)} %get-tuple-element.48), channel_id=1, source_target_pairs={{1,0},{2,1},{3,2},{4,3},{5,4},{6,5},{7,6},{0,7},{9,8},{10,9},{11,1... | collective-permute-start | bytes 884744 | tf_op jit(solution)/shard_map/ppermute | solution.py:239
  160.2 9.0 %collective-permute-done.18.p_ref = f32[3,12,16,128]{3,2,1,0:T(8,128)S(1)} collective-permute-done((f32[3,12,16,128]{3,2,1,0:T(8,128)S(1)}, f32[3,12,16,128]{3,2,1,0:T(8,128)S(1)}, u32[]{:S(2)}, u32[]{:S(2)}) %collective-permute-start.18) | collective-permute-done | bytes 294944 | tf_op jit(solution)/shard_map/ppermute | solution.py:238
  172.8 10.6 %shard_map.275 = (f32[3,12,128,128]{3,2,1,0:T(8,128)}, f32[1,12,128,128]{3,2,1,0:T(8,128)}) custom-call(f32[3,12,128,128]{3,2,1,0:T(8,128)} %shard_map.274.u_ref, f32[3,12,16,128]{3,2,1,0:T(8,128)} %copy-done.14, f32[3,12,16,128]{3,2,1,0:T(8,128)} %copy-done.15, f32[12,128,128]{2,1,0:T(8,128)} %add_add_fusion.l_ref, f32[12,128,128]{2,1,0:T(8,128)} %multiply_add_fusion.x_ref, ...), custom_call_target="tpu_custom_call" | custom-call | flops 1822556160 | bytes 7668228 | tf_op jit(solution)/shard_map/pallas_call | solution.py:182
  184.7 4.3 %collective-permute-start.21 = (f32[1,12,16,128]{3,2,1,0:T(8,128)S(1)}, f32[1,12,16,128]{3,2,1,0:T(8,128)S(1)}, u32[]{:S(2)}, u32[]{:S(2)}) collective-permute-start(f32[1,12,16,128]{3,2,1,0:T(8,128)S(1)} %get-tuple-element.54), channel_id=1, source_target_pairs={{1,0},{2,1},{3,2},{4,3},{5,4},{6,5},{7,6},{0,7},{9,8},{10,9},{11,1... | collective-permute-start | bytes 294920 | tf_op jit(solution)/shard_map/ppermute | solution.py:239
  192.5 7.3 %shard_map.276 = (f32[1,12,128,128]{3,2,1,0:T(8,128)}, f32[1,12,128,128]{3,2,1,0:T(8,128)}) custom-call(f32[1,12,128,128]{3,2,1,0:T(8,128)} %get-tuple-element.37.a1_ref, f32[1,12,16,128]{3,2,1,0:T(8,128)} %copy-done.22, f32[1,12,16,128]{3,2,1,0:T(8,128)} %copy-done.23, f32[12,128,128]{2,1,0:T(8,128)} %add_add_fusion.l_ref, ...), custom_call_target="tpu_custom_call" | custom-call | flops 607518720 | bytes 6488580 | tf_op jit(solution)/shard_map/pallas_call | solution.py:182
  200.9 4.6 %collective-permute-start.23 = (f32[1,12,16,128]{3,2,1,0:T(8,128)S(1)}, f32[1,12,16,128]{3,2,1,0:T(8,128)S(1)}, u32[]{:S(2)}, u32[]{:S(2)}) collective-permute-start(f32[1,12,16,128]{3,2,1,0:T(8,128)S(1)} %get-tuple-element.52), channel_id=1, source_target_pairs={{1,0},{2,1},{3,2},{4,3},{5,4},{6,5},{7,6},{0,7},{9,8},{10,9},{11,1... | collective-permute-start | bytes 294920 | tf_op jit(solution)/shard_map/ppermute | solution.py:239
  208.8 8.6 %shard_map.277 = (f32[12,64,128]{2,1,0:T(8,128)}, f32[12,64,128]{2,1,0:T(8,128)}, f32[12,64,128]{2,1,0:T(8,128)}) custom-call(f32[1,12,128,128]{3,2,1,0:T(8,128)} %get-tuple-element.39.a2_ref, f32[1,12,16,128]{3,2,1,0:T(8,128)} %copy-done.18, f32[1,12,16,128]{3,2,1,0:T(8,128)} %copy-done.19, f32[12,128,128]{2,1,0:T(8,128)} %add_add_fusion.l_ref, ...), custom_call_target="tpu_custom_call" | custom-call | flops 607518720 | bytes 9273860 | tf_op jit(solution)/shard_map/pallas_call | solution.py:182
  217.4 5.3 %shard_map.278.base_ref = f32[1,12,64,128]{3,2,1,0:T(8,128)} custom-call(f32[1,12,64,128]{3,2,1,0:T(8,128)} %bitcast.98, f32[3,12,16,128]{3,2,1,0:T(8,128)} %copy-done.14, f32[3,12,16,128]{3,2,1,0:T(8,128)} %copy-done.15, f32[8,16]{1,0:T(8,128)} %constant.73.clone.r_ref, f32[12,64,64]{2,1,0:T(8,128)} %add_add_fusion.1.l_ref, ...), custom_call_target="tpu_custom_call" | custom-call | flops 228261888 | bytes 2360324 | tf_op jit(solution)/shard_map/pallas_call | solution.py:182
  222.7 5.5 %shard_map.279 = (f32[1,12,64,128]{3,2,1,0:T(8,128)}, f32[1,12,64,128]{3,2,1,0:T(8,128)}, f32[1,12,8,128]{3,2,1,0:T(8,128)}, f32[1,12,8,128]{3,2,1,0:T(8,128)}) custom-call(s32[1]{0:T(128)} %constant.52.clone.1.lead_ref, f32[1,12,64,128]{3,2,1,0:T(8,128)} %bitcast.54, f32[1,12,8,128]{3,2,1,0:T(8,128)} %bitcast.76, f32[1,12,8,128]{3,2,1,0:T(8,128)} %bitcast.86, ...), custom_call_target="tpu_custom_call" | custom-call | flops 228261888 | bytes 3637768 | tf_op jit(solution)/shard_map/pallas_call | solution.py:182
  231.7 6.4 %collective-permute-start.26 = (f32[1,12,8,128]{3,2,1,0:T(8,128)S(1)}, f32[1,12,8,128]{3,2,1,0:T(8,128)S(1)}, u32[]{:S(2)}, u32[]{:S(2)}) collective-permute-start(f32[1,12,8,128]{3,2,1,0:T(8,128)S(1)} %get-tuple-element.64), channel_id=1, source_target_pairs={{0,15},{1,8},{2,9},{3,10},{4,11},{5,12},{6,13},{7,14},{8,23},{9,16... | collective-permute-start | bytes 147464 | tf_op jit(solution)/shard_map/ppermute | solution.py:448
  241.1 5.6 %shard_map.280 = (f32[1,12,64,128]{3,2,1,0:T(8,128)}, f32[1,12,64,128]{3,2,1,0:T(8,128)}, f32[1,12,8,128]{3,2,1,0:T(8,128)}, f32[1,12,8,128]{3,2,1,0:T(8,128)}) custom-call(s32[1]{0:T(128)} %bitcast.11.lead_ref, f32[1,12,64,128]{3,2,1,0:T(8,128)} %copy-done.10, f32[1,12,8,128]{3,2,1,0:T(8,128)} %copy-done.38, f32[1,12,8,128]{3,2,1,0:T(8,128)} %copy-done.43, ...), custom_call_target="tpu_custom_call" | custom-call | flops 228261888 | bytes 3637768 | tf_op jit(solution)/shard_map/pallas_call | solution.py:182
  250.2 8.5 %collective-permute-start.29 = (f32[1,12,8,128]{3,2,1,0:T(8,128)S(1)}, f32[1,12,8,128]{3,2,1,0:T(8,128)S(1)}, u32[]{:S(2)}, u32[]{:S(2)}) collective-permute-start(f32[1,12,8,128]{3,2,1,0:T(8,128)S(1)} %get-tuple-element.62), channel_id=1, source_target_pairs={{0,15},{1,8},{2,9},{3,10},{4,11},{5,12},{6,13},{7,14},{8,23},{9,16... | collective-permute-start | bytes 147464 | tf_op jit(solution)/shard_map/ppermute | solution.py:448
  261.8 5.6 %shard_map.281 = (f32[1,12,64,128]{3,2,1,0:T(8,128)}, f32[1,12,64,128]{3,2,1,0:T(8,128)}, f32[1,12,8,128]{3,2,1,0:T(8,128)}, f32[1,12,8,128]{3,2,1,0:T(8,128)}) custom-call(s32[1]{0:T(128)} %bitcast.11.lead_ref, f32[1,12,64,128]{3,2,1,0:T(8,128)} %copy-done.11, f32[1,12,8,128]{3,2,1,0:T(8,128)} %copy-done.39, f32[1,12,8,128]{3,2,1,0:T(8,128)} %copy-done.44, ...), custom_call_target="tpu_custom_call" | custom-call | flops 228261888 | bytes 3637768 | tf_op jit(solution)/shard_map/pallas_call | solution.py:182
  270.8 8.5 %collective-permute-start.32 = (f32[1,12,8,128]{3,2,1,0:T(8,128)S(1)}, f32[1,12,8,128]{3,2,1,0:T(8,128)S(1)}, u32[]{:S(2)}, u32[]{:S(2)}) collective-permute-start(f32[1,12,8,128]{3,2,1,0:T(8,128)S(1)} %get-tuple-element.60), channel_id=1, source_target_pairs={{0,15},{1,8},{2,9},{3,10},{4,11},{5,12},{6,13},{7,14},{8,23},{9,16... | collective-permute-start | bytes 147464 | tf_op jit(solution)/shard_map/ppermute | solution.py:448
  282.5 5.5 %shard_map.282 = (f32[1,12,64,128]{3,2,1,0:T(8,128)}, f32[1,12,64,128]{3,2,1,0:T(8,128)}, f32[1,12,8,128]{3,2,1,0:T(8,128)}, f32[1,12,8,128]{3,2,1,0:T(8,128)}) custom-call(s32[1]{0:T(128)} %bitcast.11.lead_ref, f32[1,12,64,128]{3,2,1,0:T(8,128)} %copy-done.6, f32[1,12,8,128]{3,2,1,0:T(8,128)} %copy-done.33, f32[1,12,8,128]{3,2,1,0:T(8,128)} %copy-done.34, ...), custom_call_target="tpu_custom_call" | custom-call | flops 228261888 | bytes 3637768 | tf_op jit(solution)/shard_map/pallas_call | solution.py:182
  (198 shorter events, 85.6 us)
Async XLA Ops:
  2.6 15.6 %collective-permute-start = (f32[3,12,16,128]{3,2,1,0:T(8,128)S(1)}, f32[3,12,16,128]{3,2,1,0:T(8,128)S(1)}, u32[]{:S(2)}, u32[]{:S(2)}) collective-permute-start(f32[3,12,16,128]{3,2,1,0:T(8,128)S(1)} %get-tuple-element.51), channel_id=1, source_target_pairs={{0,1},{1,2},{2,3},{3,4},{4,5},{5,6},{6,7},{7,0},{8,9},{9,10},{10,1... | collective-permute-start | bytes 884744 | tf_op jit(solution)/shard_map/ppermute | solution.py:238
  5.7 14.8 %collective-permute-start.1 = (f32[3,12,16,128]{3,2,1,0:T(8,128)S(1)}, f32[3,12,16,128]{3,2,1,0:T(8,128)S(1)}, u32[]{:S(2)}, u32[]{:S(2)}) collective-permute-start(f32[3,12,16,128]{3,2,1,0:T(8,128)S(1)} %get-tuple-element.50), channel_id=1, source_target_pairs={{1,0},{2,1},{3,2},{4,3},{5,4},{6,5},{7,6},{0,7},{9,8},{10,9},{11,1... | collective-permute-start | bytes 884744 | tf_op jit(solution)/shard_map/ppermute | solution.py:239
  32.6 9.6 %collective-permute-start.2 = (f32[1,12,16,128]{3,2,1,0:T(8,128)S(1)}, f32[1,12,16,128]{3,2,1,0:T(8,128)S(1)}, u32[]{:S(2)}, u32[]{:S(2)}) collective-permute-start(f32[1,12,16,128]{3,2,1,0:T(8,128)S(1)} %get-tuple-element.59), channel_id=1, source_target_pairs={{0,1},{1,2},{2,3},{3,4},{4,5},{5,6},{6,7},{7,0},{8,9},{9,10},{10,1... | collective-permute-start | bytes 294920 | tf_op jit(solution)/shard_map/ppermute | solution.py:238
  33.7 8.5 %collective-permute-start.3 = (f32[1,12,16,128]{3,2,1,0:T(8,128)S(1)}, f32[1,12,16,128]{3,2,1,0:T(8,128)S(1)}, u32[]{:S(2)}, u32[]{:S(2)}) collective-permute-start(f32[1,12,16,128]{3,2,1,0:T(8,128)S(1)} %get-tuple-element.58), channel_id=1, source_target_pairs={{1,0},{2,1},{3,2},{4,3},{5,4},{6,5},{7,6},{0,7},{9,8},{10,9},{11,1... | collective-permute-start | bytes 294920 | tf_op jit(solution)/shard_map/ppermute | solution.py:239
  37.4 35.9 %collective-permute-start.6 = (f32[12,8,128]{2,1,0:T(8,128)S(1)}, f32[12,8,128]{2,1,0:T(8,128)S(1)}, u32[]{:S(2)}, u32[]{:S(2)}) collective-permute-start(f32[12,8,128]{2,1,0:T(8,128)S(1)} %get-tuple-element.73), channel_id=1, source_target_pairs={{0,1},{1,2},{2,3},{3,4},{4,5},{5,6},{6,7},{7,0},{8,9},{9,10},{10,1... | collective-permute-start | bytes 147464 | tf_op jit(solution)/shard_map/ppermute | solution.py:238
  37.5 35.8 %collective-permute-start.7 = (f32[12,8,128]{2,1,0:T(8,128)S(1)}, f32[12,8,128]{2,1,0:T(8,128)S(1)}, u32[]{:S(2)}, u32[]{:S(2)}) collective-permute-start(f32[12,8,128]{2,1,0:T(8,128)S(1)} %get-tuple-element.72), channel_id=1, source_target_pairs={{1,0},{2,1},{3,2},{4,3},{5,4},{6,5},{7,6},{0,7},{9,8},{10,9},{11,1... | collective-permute-start | bytes 147464 | tf_op jit(solution)/shard_map/ppermute | solution.py:239
  51.3 7.4 %collective-permute-start.4 = (f32[1,12,16,128]{3,2,1,0:T(8,128)S(1)}, f32[1,12,16,128]{3,2,1,0:T(8,128)S(1)}, u32[]{:S(2)}, u32[]{:S(2)}) collective-permute-start(f32[1,12,16,128]{3,2,1,0:T(8,128)S(1)} %get-tuple-element.57), channel_id=1, source_target_pairs={{0,1},{1,2},{2,3},{3,4},{4,5},{5,6},{6,7},{7,0},{8,9},{9,10},{10,1... | collective-permute-start | bytes 294920 | tf_op jit(solution)/shard_map/ppermute | solution.py:238
  51.3 7.3 %collective-permute-start.5 = (f32[1,12,16,128]{3,2,1,0:T(8,128)S(1)}, f32[1,12,16,128]{3,2,1,0:T(8,128)S(1)}, u32[]{:S(2)}, u32[]{:S(2)}) collective-permute-start(f32[1,12,16,128]{3,2,1,0:T(8,128)S(1)} %get-tuple-element.56), channel_id=1, source_target_pairs={{1,0},{2,1},{3,2},{4,3},{5,4},{6,5},{7,6},{0,7},{9,8},{10,9},{11,1... | collective-permute-start | bytes 294920 | tf_op jit(solution)/shard_map/ppermute | solution.py:239
  79.5 13.6 %collective-permute-start.8 = (f32[1,12,64,128]{3,2,1,0:T(8,128)}, f32[1,12,64,128]{3,2,1,0:T(8,128)S(1)}, u32[]{:S(2)}, u32[]{:S(2)}) collective-permute-start(f32[1,12,64,128]{3,2,1,0:T(8,128)} %get-tuple-element.32), channel_id=1, source_target_pairs={{0,8},{8,16},{16,24},{1,9},{9,17},{17,25},{2,10},{10,18},{18,26},{... | collective-permute-start | bytes 1179656 | tf_op jit(solution)/shard_map/ppermute | solution.py:444
  81.7 10.1 %collective-permute-start.10 = (f32[1,12,8,128]{3,2,1,0:T(8,128)S(1)}, f32[1,12,8,128]{3,2,1,0:T(8,128)S(1)}, u32[]{:S(2)}, u32[]{:S(2)}) collective-permute-start(f32[1,12,8,128]{3,2,1,0:T(8,128)S(1)} %get-tuple-element.70), channel_id=1, source_target_pairs={{0,15},{1,8},{2,9},{3,10},{4,11},{5,12},{6,13},{7,14},{8,23},{9,16... | collective-permute-start | bytes 147464 | tf_op jit(solution)/shard_map/ppermute | solution.py:448
  99.5 16.2 %collective-permute-start.11 = (f32[1,12,64,128]{3,2,1,0:T(8,128)}, f32[1,12,64,128]{3,2,1,0:T(8,128)S(1)}, u32[]{:S(2)}, u32[]{:S(2)}) collective-permute-start(f32[1,12,64,128]{3,2,1,0:T(8,128)} %get-tuple-element.33), channel_id=1, source_target_pairs={{0,8},{8,16},{16,24},{1,9},{9,17},{17,25},{2,10},{10,18},{18,26},{... | collective-permute-start | bytes 1179656 | tf_op jit(solution)/shard_map/ppermute | solution.py:444
  106.3 41.0 %collective-permute-start.17 = (f32[1,12,128,128]{3,2,1,0:T(8,128)S(1)}, f32[1,12,128,128]{3,2,1,0:T(8,128)S(1)}, u32[]{:S(2)}, u32[]{:S(2)}) collective-permute-start(f32[1,12,128,128]{3,2,1,0:T(8,128)S(1)} %copy-done.4), channel_id=1, source_target_pairs={{0,8},{8,16},{16,24},{1,9},{9,17},{17,25},{2,10},{10,18},{18,26},{... | collective-permute-start | bytes 2359304 | tf_op jit(solution)/shard_map/ppermute | solution.py:437
  109.1 4.9 %collective-permute-start.12 = (f32[1,12,8,128]{3,2,1,0:T(8,128)S(1)}, f32[1,12,8,128]{3,2,1,0:T(8,128)S(1)}, u32[]{:S(2)}, u32[]{:S(2)}) collective-permute-start(f32[1,12,8,128]{3,2,1,0:T(8,128)S(1)} %get-tuple-element.69), channel_id=1, source_target_pairs={{0,9},{1,10},{2,11},{3,12},{4,13},{5,14},{6,15},{7,8},{8,17},{9,18... | collective-permute-start | bytes 147464 | tf_op jit(solution)/shard_map/ppermute | solution.py:447
  110.4 5.3 %collective-permute-start.13 = (f32[1,12,8,128]{3,2,1,0:T(8,128)S(1)}, f32[1,12,8,128]{3,2,1,0:T(8,128)S(1)}, u32[]{:S(2)}, u32[]{:S(2)}) collective-permute-start(f32[1,12,8,128]{3,2,1,0:T(8,128)S(1)} %get-tuple-element.68), channel_id=1, source_target_pairs={{0,15},{1,8},{2,9},{3,10},{4,11},{5,12},{6,13},{7,14},{8,23},{9,16... | collective-permute-start | bytes 147464 | tf_op jit(solution)/shard_map/ppermute | solution.py:448
  122.7 17.7 %collective-permute-start.14 = (f32[1,12,64,128]{3,2,1,0:T(8,128)}, f32[1,12,64,128]{3,2,1,0:T(8,128)S(1)}, u32[]{:S(2)}, u32[]{:S(2)}) collective-permute-start(f32[1,12,64,128]{3,2,1,0:T(8,128)} %get-tuple-element.34), channel_id=1, source_target_pairs={{0,8},{8,16},{16,24},{1,9},{9,17},{17,25},{2,10},{10,18},{18,26},{... | collective-permute-start | bytes 1179656 | tf_op jit(solution)/shard_map/ppermute | solution.py:444
  130.5 8.2 %collective-permute-start.15 = (f32[1,12,8,128]{3,2,1,0:T(8,128)S(1)}, f32[1,12,8,128]{3,2,1,0:T(8,128)S(1)}, u32[]{:S(2)}, u32[]{:S(2)}) collective-permute-start(f32[1,12,8,128]{3,2,1,0:T(8,128)S(1)} %get-tuple-element.67), channel_id=1, source_target_pairs={{0,9},{1,10},{2,11},{3,12},{4,13},{5,14},{6,15},{7,8},{8,17},{9,18... | collective-permute-start | bytes 147464 | tf_op jit(solution)/shard_map/ppermute | solution.py:447
  135.9 4.5 %collective-permute-start.16 = (f32[1,12,8,128]{3,2,1,0:T(8,128)S(1)}, f32[1,12,8,128]{3,2,1,0:T(8,128)S(1)}, u32[]{:S(2)}, u32[]{:S(2)}) collective-permute-start(f32[1,12,8,128]{3,2,1,0:T(8,128)S(1)} %get-tuple-element.66), channel_id=1, source_target_pairs={{0,15},{1,8},{2,9},{3,10},{4,11},{5,12},{6,13},{7,14},{8,23},{9,16... | collective-permute-start | bytes 147464 | tf_op jit(solution)/shard_map/ppermute | solution.py:448
  155.4 13.8 %collective-permute-start.18 = (f32[3,12,16,128]{3,2,1,0:T(8,128)S(1)}, f32[3,12,16,128]{3,2,1,0:T(8,128)S(1)}, u32[]{:S(2)}, u32[]{:S(2)}) collective-permute-start(f32[3,12,16,128]{3,2,1,0:T(8,128)S(1)} %get-tuple-element.49), channel_id=1, source_target_pairs={{0,1},{1,2},{2,3},{3,4},{4,5},{5,6},{6,7},{7,0},{8,9},{9,10},{10,1... | collective-permute-start | bytes 884744 | tf_op jit(solution)/shard_map/ppermute | solution.py:238
  156.1 15.9 %collective-permute-start.19 = (f32[3,12,16,128]{3,2,1,0:T(8,128)S(1)}, f32[3,12,16,128]{3,2,1,0:T(8,128)S(1)}, u32[]{:S(2)}, u32[]{:S(2)}) collective-permute-start(f32[3,12,16,128]{3,2,1,0:T(8,128)S(1)} %get-tuple-element.48), channel_id=1, source_target_pairs={{1,0},{2,1},{3,2},{4,3},{5,4},{6,5},{7,6},{0,7},{9,8},{10,9},{11,1... | collective-permute-start | bytes 884744 | tf_op jit(solution)/shard_map/ppermute | solution.py:239
  184.3 7.6 %collective-permute-start.20 = (f32[1,12,16,128]{3,2,1,0:T(8,128)S(1)}, f32[1,12,16,128]{3,2,1,0:T(8,128)S(1)}, u32[]{:S(2)}, u32[]{:S(2)}) collective-permute-start(f32[1,12,16,128]{3,2,1,0:T(8,128)S(1)} %get-tuple-element.55), channel_id=1, source_target_pairs={{0,1},{1,2},{2,3},{3,4},{4,5},{5,6},{6,7},{7,0},{8,9},{9,10},{10,1... | collective-permute-start | bytes 294920 | tf_op jit(solution)/shard_map/ppermute | solution.py:238
  184.7 7.1 %collective-permute-start.21 = (f32[1,12,16,128]{3,2,1,0:T(8,128)S(1)}, f32[1,12,16,128]{3,2,1,0:T(8,128)S(1)}, u32[]{:S(2)}, u32[]{:S(2)}) collective-permute-start(f32[1,12,16,128]{3,2,1,0:T(8,128)S(1)} %get-tuple-element.54), channel_id=1, source_target_pairs={{1,0},{2,1},{3,2},{4,3},{5,4},{6,5},{7,6},{0,7},{9,8},{10,9},{11,1... | collective-permute-start | bytes 294920 | tf_op jit(solution)/shard_map/ppermute | solution.py:239
  200.7 7.4 %collective-permute-start.22 = (f32[1,12,16,128]{3,2,1,0:T(8,128)S(1)}, f32[1,12,16,128]{3,2,1,0:T(8,128)S(1)}, u32[]{:S(2)}, u32[]{:S(2)}) collective-permute-start(f32[1,12,16,128]{3,2,1,0:T(8,128)S(1)} %get-tuple-element.53), channel_id=1, source_target_pairs={{0,1},{1,2},{2,3},{3,4},{4,5},{5,6},{6,7},{7,0},{8,9},{9,10},{10,1... | collective-permute-start | bytes 294920 | tf_op jit(solution)/shard_map/ppermute | solution.py:238
  200.9 7.2 %collective-permute-start.23 = (f32[1,12,16,128]{3,2,1,0:T(8,128)S(1)}, f32[1,12,16,128]{3,2,1,0:T(8,128)S(1)}, u32[]{:S(2)}, u32[]{:S(2)}) collective-permute-start(f32[1,12,16,128]{3,2,1,0:T(8,128)S(1)} %get-tuple-element.52), channel_id=1, source_target_pairs={{1,0},{2,1},{3,2},{4,3},{5,4},{6,5},{7,6},{0,7},{9,8},{10,9},{11,1... | collective-permute-start | bytes 294920 | tf_op jit(solution)/shard_map/ppermute | solution.py:239
  228.2 11.5 %collective-permute-start.24 = (f32[1,12,64,128]{3,2,1,0:T(8,128)}, f32[1,12,64,128]{3,2,1,0:T(8,128)S(1)}, u32[]{:S(2)}, u32[]{:S(2)}) collective-permute-start(f32[1,12,64,128]{3,2,1,0:T(8,128)} %get-tuple-element.44), channel_id=1, source_target_pairs={{0,8},{8,16},{16,24},{1,9},{9,17},{17,25},{2,10},{10,18},{18,26},{... | collective-permute-start | bytes 1179656 | tf_op jit(solution)/shard_map/ppermute | solution.py:444
  230.4 7.7 %collective-permute-start.25 = (f32[1,12,8,128]{3,2,1,0:T(8,128)S(1)}, f32[1,12,8,128]{3,2,1,0:T(8,128)S(1)}, u32[]{:S(2)}, u32[]{:S(2)}) collective-permute-start(f32[1,12,8,128]{3,2,1,0:T(8,128)S(1)} %get-tuple-element.65), channel_id=1, source_target_pairs={{0,9},{1,10},{2,11},{3,12},{4,13},{5,14},{6,15},{7,8},{8,17},{9,18... | collective-permute-start | bytes 147464 | tf_op jit(solution)/shard_map/ppermute | solution.py:447
  231.7 8.1 %collective-permute-start.26 = (f32[1,12,8,128]{3,2,1,0:T(8,128)S(1)}, f32[1,12,8,128]{3,2,1,0:T(8,128)S(1)}, u32[]{:S(2)}, u32[]{:S(2)}) collective-permute-start(f32[1,12,8,128]{3,2,1,0:T(8,128)S(1)} %get-tuple-element.64), channel_id=1, source_target_pairs={{0,15},{1,8},{2,9},{3,10},{4,11},{5,12},{6,13},{7,14},{8,23},{9,16... | collective-permute-start | bytes 147464 | tf_op jit(solution)/shard_map/ppermute | solution.py:448
  246.7 13.7 %collective-permute-start.27 = (f32[1,12,64,128]{3,2,1,0:T(8,128)}, f32[1,12,64,128]{3,2,1,0:T(8,128)S(1)}, u32[]{:S(2)}, u32[]{:S(2)}) collective-permute-start(f32[1,12,64,128]{3,2,1,0:T(8,128)} %get-tuple-element.45), channel_id=1, source_target_pairs={{0,8},{8,16},{16,24},{1,9},{9,17},{17,25},{2,10},{10,18},{18,26},{... | collective-permute-start | bytes 1179656 | tf_op jit(solution)/shard_map/ppermute | solution.py:444
  248.9 9.8 %collective-permute-start.28 = (f32[1,12,8,128]{3,2,1,0:T(8,128)S(1)}, f32[1,12,8,128]{3,2,1,0:T(8,128)S(1)}, u32[]{:S(2)}, u32[]{:S(2)}) collective-permute-start(f32[1,12,8,128]{3,2,1,0:T(8,128)S(1)} %get-tuple-element.63), channel_id=1, source_target_pairs={{0,9},{1,10},{2,11},{3,12},{4,13},{5,14},{6,15},{7,8},{8,17},{9,18... | collective-permute-start | bytes 147464 | tf_op jit(solution)/shard_map/ppermute | solution.py:447
  250.2 10.2 %collective-permute-start.29 = (f32[1,12,8,128]{3,2,1,0:T(8,128)S(1)}, f32[1,12,8,128]{3,2,1,0:T(8,128)S(1)}, u32[]{:S(2)}, u32[]{:S(2)}) collective-permute-start(f32[1,12,8,128]{3,2,1,0:T(8,128)S(1)} %get-tuple-element.62), channel_id=1, source_target_pairs={{0,15},{1,8},{2,9},{3,10},{4,11},{5,12},{6,13},{7,14},{8,23},{9,16... | collective-permute-start | bytes 147464 | tf_op jit(solution)/shard_map/ppermute | solution.py:448
  267.4 13.7 %collective-permute-start.30 = (f32[1,12,64,128]{3,2,1,0:T(8,128)}, f32[1,12,64,128]{3,2,1,0:T(8,128)S(1)}, u32[]{:S(2)}, u32[]{:S(2)}) collective-permute-start(f32[1,12,64,128]{3,2,1,0:T(8,128)} %get-tuple-element.46), channel_id=1, source_target_pairs={{0,8},{8,16},{16,24},{1,9},{9,17},{17,25},{2,10},{10,18},{18,26},{... | collective-permute-start | bytes 1179656 | tf_op jit(solution)/shard_map/ppermute | solution.py:444
  269.5 9.8 %collective-permute-start.31 = (f32[1,12,8,128]{3,2,1,0:T(8,128)S(1)}, f32[1,12,8,128]{3,2,1,0:T(8,128)S(1)}, u32[]{:S(2)}, u32[]{:S(2)}) collective-permute-start(f32[1,12,8,128]{3,2,1,0:T(8,128)S(1)} %get-tuple-element.61), channel_id=1, source_target_pairs={{0,9},{1,10},{2,11},{3,12},{4,13},{5,14},{6,15},{7,8},{8,17},{9,18... | collective-permute-start | bytes 147464 | tf_op jit(solution)/shard_map/ppermute | solution.py:447
  270.8 10.2 %collective-permute-start.32 = (f32[1,12,8,128]{3,2,1,0:T(8,128)S(1)}, f32[1,12,8,128]{3,2,1,0:T(8,128)S(1)}, u32[]{:S(2)}, u32[]{:S(2)}) collective-permute-start(f32[1,12,8,128]{3,2,1,0:T(8,128)S(1)} %get-tuple-element.60), channel_id=1, source_target_pairs={{0,15},{1,8},{2,9},{3,10},{4,11},{5,12},{6,13},{7,14},{8,23},{9,16... | collective-permute-start | bytes 147464 | tf_op jit(solution)/shard_map/ppermute | solution.py:448
  (61 other events, 237.9 us)

commit v4 on v3

--- a/solution.py
+++ b/solution.py
@@ -235,6 +235,9 @@
     def halo(x, plane_rows):
         head = x[..., :plane_rows, :]
         tail = x[..., x.shape[-2] - plane_rows:, :]
+        return swap(head, tail)
+
+    def swap(head, tail):
         prev = lax.ppermute(tail, "space", [(i, (i + 1) % space_n) for i in range(space_n)])
         nxt = lax.ppermute(head, "space", [((i + 1) % space_n, i) for i in range(space_n)])
         return prev, nxt
@@ -244,29 +247,35 @@
     coarse_state = jax.ShapeDtypeStruct((fields, coarse_span, columns), f32)
 
     def nodes_kernel(u_ref, p_ref, n_ref, l_ref, x_ref, zc_ref, rx_ref, ra_ref, en_ref,
-                     f_ref, a1_ref, s_ref):
+                     f_ref, a1_ref, h_ref, t_ref, s_ref):
         tendency_into(f_ref, u_ref, p_ref, n_ref, l_ref, x_ref, zc_ref, rx_ref, ra_ref, en_ref,
                       s_ref)
 
         def body(f, carry):
-            a1_ref[0, f] = u_ref[0, f] + STEP * (
+            value = u_ref[0, f] + STEP * (
                 5.0 * f_ref[0, f] + 8.0 * f_ref[1, f] - f_ref[2, f]
             ) / 24.0
+            a1_ref[0, f] = value
+            h_ref[0, f] = value[:rows]
+            t_ref[0, f] = value[span - rows:]
             return carry
 
         lax.fori_loop(0, fields, body, 0)
 
     def middle_kernel(a1_ref, p_ref, n_ref, l_ref, x_ref, zc_ref, rx_ref, ra_ref, en_ref,
-                      f_ref, g1_ref, a2_ref, s_ref):
+                      f_ref, g1_ref, a2_ref, h_ref, t_ref, s_ref):
         tendency_into(g1_ref, a1_ref, p_ref, n_ref, l_ref, x_ref, zc_ref, rx_ref, ra_ref,
                       en_ref, s_ref)
 
         def body(f, carry):
-            a2_ref[0, f] = (
+            value = (
                 a1_ref[0, f]
                 + 0.5 * STEP * (g1_ref[0, f] - f_ref[1, f])
                 + STEP * (-f_ref[0, f] + 8.0 * f_ref[1, f] + 5.0 * f_ref[2, f]) / 24.0
             )
+            a2_ref[0, f] = value
+            h_ref[0, f] = value[:rows]
+            t_ref[0, f] = value[span - rows:]
             return carry
 
         lax.fori_loop(0, fields, body, 0)
@@ -299,7 +308,7 @@
 
     def chain_kernel(lead_ref, w_ref, p_ref, n_ref, ws_ref, ps_ref, ns_ref, l_ref, x_ref,
                      zc_ref, rx_ref, ra_ref, en_ref, base_ref, rint_ref, out_ref, begin_ref,
-                     bp_ref, bn_ref, g_ref, s_ref):
+                     bp_ref, bn_ref, h_ref, t_ref, g_ref, s_ref):
         @pl.when(lead_ref[0] != 0)
         def _():
             begin_ref[...] = ws_ref[...]
@@ -316,13 +325,16 @@
                       en_ref, s_ref)
 
         def body(f, carry):
-            out_ref[0, f] = begin_ref[0, f] + STEP * (g_ref[0, f] - base_ref[0, f]) + rint_ref[0, f]
+            value = begin_ref[0, f] + STEP * (g_ref[0, f] - base_ref[0, f]) + rint_ref[0, f]
+            out_ref[0, f] = value
+            h_ref[0, f] = value[:coarse_rows]
+            t_ref[0, f] = value[coarse_span - coarse_rows:]
             return carry
 
         lax.fori_loop(0, fields, body, 0)
 
     def correct_kernel(a1_ref, a2_ref, c0_ref, c1_ref, w0_ref, w1_ref, prev_ref, us_ref,
-                       r_ref, pm_ref, lead_ref, out_ref):
+                       r_ref, pm_ref, lead_ref, out_ref, h_ref, t_ref):
         pm = pm_ref[...]
         first_change = [w0_ref[f] - c0_ref[f] for f in range(fields)]
         last_change = [w1_ref[f] - c1_ref[f] for f in range(fields)]
@@ -337,11 +349,15 @@
             columns,
         )
         for f in range(fields):
-            out_ref[1, f] = a1_ref[0, f] + middle_fix[f]
-            out_ref[2, f] = a2_ref[0, f] + last_fix[f]
-            out_ref[0, f] = jnp.where(
-                lead_ref[0] != 0, us_ref[f], prev_ref[0, f] + handed_fix[f]
-            )
+            values = (
+                jnp.where(lead_ref[0] != 0, us_ref[f], prev_ref[0, f] + handed_fix[f]),
+                a1_ref[0, f] + middle_fix[f],
+                a2_ref[0, f] + last_fix[f],
+            )
+            for b, value in enumerate(values):
+                out_ref[b, f] = value
+                h_ref[b, f] = value[:rows]
+                t_ref[b, f] = value[span - rows:]
 
     def finish_kernel(a2_ref, c1_ref, w1_ref, pm_ref, out_ref):
         fix = unlanes(
@@ -368,6 +384,8 @@
 
     coarse_one = jax.ShapeDtypeStruct((1, fields, coarse_span, columns), f32)
     plane_one = jax.ShapeDtypeStruct((1, fields, coarse_rows, columns), f32)
+    fine_plane = jax.ShapeDtypeStruct((1, fields, rows, columns), f32)
+    node_planes = jax.ShapeDtypeStruct((3, fields, rows, columns), f32)
 
     def coarse_step(flag, w, w_halo, base, rint):
         return call(
@@ -375,7 +393,7 @@
             (flag, w, w_halo[0], w_halo[1], coarse_start[None], start_halo[0][None],
              start_halo[1][None], lop_coarse, xt) + scalars + (base, rint),
             (True,) + (False,) * 8 + scalar_kinds + (False, False),
-            (coarse_one, coarse_one, plane_one, plane_one),
+            (coarse_one, coarse_one, plane_one, plane_one, plane_one, plane_one),
             [pltpu.VMEM((1, fields, coarse_span, columns), f32), coarse_scratch(1)],
             *coarse_cost,
         )
@@ -396,25 +414,29 @@
     fine_end = None
     coarse_end = None
     for iteration in range(ITERS):
-        node_prev, node_next = halo(nodes, rows)
-        f_all, a1 = call(
+        if iteration == 0:
+            node_prev, node_next = halo(nodes, rows)
+        else:
+            node_prev, node_next = swap(node_head, node_tail)
+        f_all, a1, a1_head, a1_tail = call(
             nodes_kernel,
             (nodes, node_prev, node_next, lop_fine, xt) + scalars,
             (False,) * 5 + scalar_kinds,
-            (jax.ShapeDtypeStruct((3, fields, span, columns), f32), fine_state),
+            (jax.ShapeDtypeStruct((3, fields, span, columns), f32), fine_state, fine_plane,
+             fine_plane),
             [fine_scratch(3)],
             fine_cost[0] * 3, fine_cost[1] * 3,
         )
-        a1_prev, a1_next = halo(a1, rows)
-        g1, a2 = call(
+        a1_prev, a1_next = swap(a1_head, a1_tail)
+        g1, a2, a2_head, a2_tail = call(
             middle_kernel,
             (a1, a1_prev, a1_next, lop_fine, xt) + scalars + (f_all,),
             (False,) * 5 + scalar_kinds + (False,),
-            (fine_state, fine_state),
+            (fine_state, fine_state, fine_plane, fine_plane),
             [fine_scratch(1)],
             *fine_cost,
         )
-        a2_prev, a2_next = halo(a2, rows)
+        a2_prev, a2_next = swap(a2_head, a2_tail)
         rint, c1, c0 = call(
             ending_kernel,
             (a2, a2_prev, a2_next, lop_fine, xt) + scalars + (f_all, g1, nodes, rmat),
@@ -439,11 +461,9 @@
         begin_halo = (start_halo[0][None], start_halo[1][None])
         flag = always
         for n in range(sections):
-            finish, w0, _, _ = coarse_step(flag, begin, begin_halo, base, rint[None])
+            finish, w0, _, _, head, tail = coarse_step(flag, begin, begin_halo, base, rint[None])
             if n + 1 < sections:
                 begin = lax.ppermute(finish, "tm", hop_pairs)
-                tail = finish[:, :, coarse_span - coarse_rows:, :]
-                head = finish[:, :, :coarse_rows, :]
                 begin_halo = (lax.ppermute(tail, both, prev_pairs),
                               lax.ppermute(head, both, next_pairs))
                 flag = lead
@@ -460,11 +480,12 @@
             )
             coarse_end = w1
         else:
-            (nodes,) = call(
+            nodes, node_head, node_tail = call(
                 correct_kernel,
                 (a1, a2, c0, c1, w0, w1, a2_handed, u_flat, rmat, pmat, lead),
                 (False,) * 10 + (True,),
-                (jax.ShapeDtypeStruct((3, fields, span, columns), f32),),
+                (jax.ShapeDtypeStruct((3, fields, span, columns), f32), node_planes,
+                 node_planes),
                 [],
                 8 * fields * span * coarse_span * columns * 6, 0,
             )

time: 293 us -> 285 us (0.973)
  local copies, waits for them, and re-layouts: 26.5 us -> 16.5 us
    slice x6 -> x0, local copies, waits for them, and re-layouts: 5 us -> none  [per_device(): head = finish[:, :, :coarse_rows, :]]
    slice x6 -> x1, local copies, waits for them, and re-layouts: 4.93 us -> 0.01 us  [halo(): head = x[..., :plane_rows, :]]
  transfers between devices with their start and end apart: 33 -> 33, of which waited for: 14 -> 14; matrix products, arithmetic and copies ran while one was open for 5% -> 3% of each run, Pallas kernels for 11% -> 11%
where the time goes in v4:
time: 285 us; the launch traced here: 284 us
  Pallas kernels  118 us (41%)
  starting transfers between devices  105 us (37%)
  waiting for transfers between devices  36 us (13%)
  local copies, waits for them, and re-layouts  16.5 us (6%)
  other arithmetic  5.82 us (2%)
    pallas_call x18, Pallas kernels, call(): pl.pallas_call(kernel, out_shape=outs, in_specs=[smem() if k else vmem()...  118 us
    ppermute x6, starting transfers between devices, per_device(): lax.ppermute(head, both, next_pairs)  37.2 us
    ppermute x7, starting transfers between devices, swap(): lax.ppermute(head, 'space', [((i + 1) % space_n, i) for i in range(space_...  29.9 us
    ppermute x6, starting transfers between devices, per_device(): begin = lax.ppermute(finish, 'tm', hop_pairs)  19.5 us
    ppermute x7, waiting for transfers between devices, swap(): lax.ppermute(tail, 'space', [(i, (i + 1) % space_n) for i in range(space_...  19 us
    unnamed x119, local copies, waits for them, and re-layouts  14.7 us
    ppermute x6, starting transfers between devices, per_device(): lax.ppermute(tail, both, prev_pairs)  12.2 us
    ppermute x6, waiting for transfers between devices, per_device(): lax.ppermute(head, both, next_pairs)  10.9 us
  transfers between devices with their start and end apart: 33, of which 14 were waited for; matrix products, arithmetic and copies ran while one was open for 3% of the time, Pallas kernels for 11%

profile of v4, /device:TPU:0, one launch (start us, length us, event | category | flops | bytes accessed | tf_op | source)
XLA Modules:
  0.0 284.2 jit_solution(10734481452256591544)
XLA Ops:
  21.1 10.6 %shard_map.266 = (f32[3,12,128,128]{3,2,1,0:T(8,128)}, f32[1,12,128,128]{3,2,1,0:T(8,128)}, f32[1,12,16,128]{3,2,1,0:T(8,128)}, f32[1,12,16,128]{3,2,1,0:T(8,128)}) custom-call(f32[3,12,128,128]{3,2,1,0:T(8,128)} %pad_maximum_fusion.u_ref, f32[3,12,16,128]{3,2,1,0:T(8,128)} %copy-done.12, f32[3,12,16,128]{3,2,1,0:T(8,128)} %copy-done.13, ...), custom_call_target="tpu_custom_call" | custom-call | flops 1822556160 | bytes 7864836 | tf_op jit(solution)/shard_map/pallas_call | solution.py:182
  32.7 3.7 %collective-permute-start.3 = (f32[1,12,16,128]{3,2,1,0:T(8,128)}, f32[1,12,16,128]{3,2,1,0:T(8,128)S(1)}, u32[]{:S(2)}, u32[]{:S(2)}) collective-permute-start(f32[1,12,16,128]{3,2,1,0:T(8,128)} %get-tuple-element.50), channel_id=1, source_target_pairs={{1,0},{2,1},{3,2},{4,3},{5,4},{6,5},{7,6},{0,7},{9,8},{10,9},{11,1... | collective-permute-start | bytes 294920 | tf_op jit(solution)/shard_map/ppermute | solution.py:242
  36.6 4.7 %collective-permute-start.7 = (f32[12,8,128]{2,1,0:T(8,128)S(1)}, f32[12,8,128]{2,1,0:T(8,128)S(1)}, u32[]{:S(2)}, u32[]{:S(2)}) collective-permute-start(f32[12,8,128]{2,1,0:T(8,128)S(1)} %get-tuple-element.96), channel_id=1, source_target_pairs={{1,0},{2,1},{3,2},{4,3},{5,4},{6,5},{7,6},{0,7},{9,8},{10,9},{11,1... | collective-permute-start | bytes 147464 | tf_op jit(solution)/shard_map/ppermute | solution.py:242
  42.0 7.4 %shard_map.267 = (f32[1,12,128,128]{3,2,1,0:T(8,128)}, f32[1,12,128,128]{3,2,1,0:T(8,128)}, f32[1,12,16,128]{3,2,1,0:T(8,128)}, f32[1,12,16,128]{3,2,1,0:T(8,128)}) custom-call(f32[1,12,128,128]{3,2,1,0:T(8,128)} %get-tuple-element.48.a1_ref, f32[1,12,16,128]{3,2,1,0:T(8,128)} %copy-done.20, f32[1,12,16,128]{3,2,1,0:T(8,128)} %copy-done.21, ...), custom_call_target="tpu_custom_call" | custom-call | flops 607518720 | bytes 6685188 | tf_op jit(solution)/shard_map/pallas_call | solution.py:182
  49.4 4.7 %collective-permute-start.5 = (f32[1,12,16,128]{3,2,1,0:T(8,128)}, f32[1,12,16,128]{3,2,1,0:T(8,128)S(1)}, u32[]{:S(2)}, u32[]{:S(2)}) collective-permute-start(f32[1,12,16,128]{3,2,1,0:T(8,128)} %get-tuple-element.54), channel_id=1, source_target_pairs={{1,0},{2,1},{3,2},{4,3},{5,4},{6,5},{7,6},{0,7},{9,8},{10,9},{11,1... | collective-permute-start | bytes 294920 | tf_op jit(solution)/shard_map/ppermute | solution.py:242
  57.6 8.7 %shard_map.268 = (f32[12,64,128]{2,1,0:T(8,128)}, f32[12,64,128]{2,1,0:T(8,128)}, f32[12,64,128]{2,1,0:T(8,128)}) custom-call(f32[1,12,128,128]{3,2,1,0:T(8,128)} %get-tuple-element.52.a2_ref, f32[1,12,16,128]{3,2,1,0:T(8,128)} %copy-done.16, f32[1,12,16,128]{3,2,1,0:T(8,128)} %copy-done.17, f32[12,128,128]{2,1,0:T(8,128)} %add_add_fusion.l_ref, ...), custom_call_target="tpu_custom_call" | custom-call | flops 607518720 | bytes 9273860 | tf_op jit(solution)/shard_map/pallas_call | solution.py:182
  66.3 5.3 %shard_map.269.base_ref = f32[1,12,64,128]{3,2,1,0:T(8,128)} custom-call(f32[1,12,64,128]{3,2,1,0:T(8,128)} %bitcast.92, f32[3,12,16,128]{3,2,1,0:T(8,128)} %copy-done.12, f32[3,12,16,128]{3,2,1,0:T(8,128)} %copy-done.13, f32[8,16]{1,0:T(8,128)} %constant.73.clone.r_ref, f32[12,64,64]{2,1,0:T(8,128)} %add_add_fusion.1.l_ref, ...), custom_call_target="tpu_custom_call" | custom-call | flops 228261888 | bytes 2360324 | tf_op jit(solution)/shard_map/pallas_call | solution.py:182
  72.2 5.7 %shard_map.270 = (f32[1,12,64,128]{3,2,1,0:T(8,128)}, f32[1,12,64,128]{3,2,1,0:T(8,128)}, f32[1,12,8,128]{3,2,1,0:T(8,128)}, f32[1,12,8,128]{3,2,1,0:T(8,128)}, ...) custom-call(s32[1]{0:T(128)} %constant.52.clone.1.lead_ref, f32[1,12,64,128]{3,2,1,0:T(8,128)} %bitcast.49, ...), custom_call_target="tpu_custom_call" | custom-call | flops 228261888 | bytes 3736072 | tf_op jit(solution)/shard_map/pallas_call | solution.py:182
  79.2 8.4 %collective-permute-start.10 = (f32[1,12,8,128]{3,2,1,0:T(8,128)}, f32[1,12,8,128]{3,2,1,0:T(8,128)S(1)}, u32[]{:S(2)}, u32[]{:S(2)}) collective-permute-start(f32[1,12,8,128]{3,2,1,0:T(8,128)} %get-tuple-element.61), channel_id=1, source_target_pairs={{0,15},{1,8},{2,9},{3,10},{4,11},{5,12},{6,13},{7,14},{8,23},{9,16... | collective-permute-start | bytes 147464 | tf_op jit(solution)/shard_map/ppermute | solution.py:468
  91.7 5.6 %shard_map.271 = (f32[1,12,64,128]{3,2,1,0:T(8,128)}, f32[1,12,64,128]{3,2,1,0:T(8,128)}, f32[1,12,8,128]{3,2,1,0:T(8,128)}, f32[1,12,8,128]{3,2,1,0:T(8,128)}, ...) custom-call(s32[1]{0:T(128)} %bitcast.11.lead_ref, f32[1,12,64,128]{3,2,1,0:T(8,128)} %copy-done.8, ...), custom_call_target="tpu_custom_call" | custom-call | flops 228261888 | bytes 3736072 | tf_op jit(solution)/shard_map/pallas_call | solution.py:182
  97.3 6.7 %collective-permute-start.11 = (f32[1,12,64,128]{3,2,1,0:T(8,128)}, f32[1,12,64,128]{3,2,1,0:T(8,128)S(1)}, u32[]{:S(2)}, u32[]{:S(2)}) collective-permute-start(f32[1,12,64,128]{3,2,1,0:T(8,128)} %get-tuple-element.62), channel_id=1, source_target_pairs={{0,8},{8,16},{16,24},{1,9},{9,17},{17,25},{2,10},{10,18},{18,26},{... | collective-permute-start | bytes 1179656 | tf_op jit(solution)/shard_map/ppermute | solution.py:466
  107.3 3.6 %collective-permute-start.13 = (f32[1,12,8,128]{3,2,1,0:T(8,128)}, f32[1,12,8,128]{3,2,1,0:T(8,128)S(1)}, u32[]{:S(2)}, u32[]{:S(2)}) collective-permute-start(f32[1,12,8,128]{3,2,1,0:T(8,128)} %get-tuple-element.64), channel_id=1, source_target_pairs={{0,15},{1,8},{2,9},{3,10},{4,11},{5,12},{6,13},{7,14},{8,23},{9,16... | collective-permute-start | bytes 147464 | tf_op jit(solution)/shard_map/ppermute | solution.py:468
  114.3 5.6 %shard_map.272 = (f32[1,12,64,128]{3,2,1,0:T(8,128)}, f32[1,12,64,128]{3,2,1,0:T(8,128)}, f32[1,12,8,128]{3,2,1,0:T(8,128)}, f32[1,12,8,128]{3,2,1,0:T(8,128)}, ...) custom-call(s32[1]{0:T(128)} %bitcast.11.lead_ref, f32[1,12,64,128]{3,2,1,0:T(8,128)} %copy-done.7, ...), custom_call_target="tpu_custom_call" | custom-call | flops 228261888 | bytes 3736072 | tf_op jit(solution)/shard_map/pallas_call | solution.py:182
  119.9 7.5 %collective-permute-start.14 = (f32[1,12,64,128]{3,2,1,0:T(8,128)}, f32[1,12,64,128]{3,2,1,0:T(8,128)S(1)}, u32[]{:S(2)}, u32[]{:S(2)}) collective-permute-start(f32[1,12,64,128]{3,2,1,0:T(8,128)} %get-tuple-element.65), channel_id=1, source_target_pairs={{0,8},{8,16},{16,24},{1,9},{9,17},{17,25},{2,10},{10,18},{18,26},{... | collective-permute-start | bytes 1179656 | tf_op jit(solution)/shard_map/ppermute | solution.py:466
  127.4 5.3 %collective-permute-start.15 = (f32[1,12,8,128]{3,2,1,0:T(8,128)}, f32[1,12,8,128]{3,2,1,0:T(8,128)S(1)}, u32[]{:S(2)}, u32[]{:S(2)}) collective-permute-start(f32[1,12,8,128]{3,2,1,0:T(8,128)} %get-tuple-element.66), channel_id=1, source_target_pairs={{0,9},{1,10},{2,11},{3,12},{4,13},{5,14},{6,15},{7,8},{8,17},{9,18... | collective-permute-start | bytes 147464 | tf_op jit(solution)/shard_map/ppermute | solution.py:467
  139.0 5.6 %shard_map.273 = (f32[1,12,64,128]{3,2,1,0:T(8,128)}, f32[1,12,64,128]{3,2,1,0:T(8,128)}, f32[1,12,8,128]{3,2,1,0:T(8,128)}, f32[1,12,8,128]{3,2,1,0:T(8,128)}, ...) custom-call(s32[1]{0:T(128)} %bitcast.11.lead_ref, f32[1,12,64,128]{3,2,1,0:T(8,128)} %copy-done.9, ...), custom_call_target="tpu_custom_call" | custom-call | flops 228261888 | bytes 3736072 | tf_op jit(solution)/shard_map/pallas_call | solution.py:182
  145.5 6.3 %shard_map.274 = (f32[3,12,128,128]{3,2,1,0:T(8,128)}, f32[3,12,16,128]{3,2,1,0:T(8,128)}, f32[3,12,16,128]{3,2,1,0:T(8,128)}) custom-call(f32[1,12,128,128]{3,2,1,0:T(8,128)} %get-tuple-element.48.a1_ref, f32[1,12,128,128]{3,2,1,0:T(8,128)} %get-tuple-element.52.a2_ref, f32[12,64,128]{2,1,0:T(8,128)} %get-tuple-element.56.c0_ref, ...), custom_call_target="tpu_custom_call" | custom-call | flops 603979776 | bytes 7733252 | tf_op jit(solution)/shard_map/pallas_call | solution.py:182
  152.4 4.1 %collective-permute-start.19 = (f32[3,12,16,128]{3,2,1,0:T(8,128)}, f32[3,12,16,128]{3,2,1,0:T(8,128)S(1)}, u32[]{:S(2)}, u32[]{:S(2)}) collective-permute-start(f32[3,12,16,128]{3,2,1,0:T(8,128)} %get-tuple-element.72), channel_id=1, source_target_pairs={{1,0},{2,1},{3,2},{4,3},{5,4},{6,5},{7,6},{0,7},{9,8},{10,9},{11,1... | collective-permute-start | bytes 884744 | tf_op jit(solution)/shard_map/ppermute | solution.py:242
  156.5 9.4 %collective-permute-done.18.p_ref = f32[3,12,16,128]{3,2,1,0:T(8,128)S(1)} collective-permute-done((f32[3,12,16,128]{3,2,1,0:T(8,128)}, f32[3,12,16,128]{3,2,1,0:T(8,128)S(1)}, u32[]{:S(2)}, u32[]{:S(2)}) %collective-permute-start.18) | collective-permute-done | bytes 294944 | tf_op jit(solution)/shard_map/ppermute | solution.py:241
  169.2 10.6 %shard_map.275 = (f32[3,12,128,128]{3,2,1,0:T(8,128)}, f32[1,12,128,128]{3,2,1,0:T(8,128)}, f32[1,12,16,128]{3,2,1,0:T(8,128)}, f32[1,12,16,128]{3,2,1,0:T(8,128)}) custom-call(f32[3,12,128,128]{3,2,1,0:T(8,128)} %get-tuple-element.70.u_ref, f32[3,12,16,128]{3,2,1,0:T(8,128)} %copy-done.14, f32[3,12,16,128]{3,2,1,0:T(8,128)} %copy-done.15, ...), custom_call_target="tpu_custom_call" | custom-call | flops 1822556160 | bytes 7864836 | tf_op jit(solution)/shard_map/pallas_call | solution.py:182
  179.9 4.7 %collective-permute-start.21 = (f32[1,12,16,128]{3,2,1,0:T(8,128)}, f32[1,12,16,128]{3,2,1,0:T(8,128)S(1)}, u32[]{:S(2)}, u32[]{:S(2)}) collective-permute-start(f32[1,12,16,128]{3,2,1,0:T(8,128)} %get-tuple-element.75), channel_id=1, source_target_pairs={{1,0},{2,1},{3,2},{4,3},{5,4},{6,5},{7,6},{0,7},{9,8},{10,9},{11,1... | collective-permute-start | bytes 294920 | tf_op jit(solution)/shard_map/ppermute | solution.py:242
  188.3 7.4 %shard_map.276 = (f32[1,12,128,128]{3,2,1,0:T(8,128)}, f32[1,12,128,128]{3,2,1,0:T(8,128)}, f32[1,12,16,128]{3,2,1,0:T(8,128)}, f32[1,12,16,128]{3,2,1,0:T(8,128)}) custom-call(f32[1,12,128,128]{3,2,1,0:T(8,128)} %get-tuple-element.73.a1_ref, f32[1,12,16,128]{3,2,1,0:T(8,128)} %copy-done.22, f32[1,12,16,128]{3,2,1,0:T(8,128)} %copy-done.23, ...), custom_call_target="tpu_custom_call" | custom-call | flops 607518720 | bytes 6685188 | tf_op jit(solution)/shard_map/pallas_call | solution.py:182
  195.6 4.7 %collective-permute-start.23 = (f32[1,12,16,128]{3,2,1,0:T(8,128)}, f32[1,12,16,128]{3,2,1,0:T(8,128)S(1)}, u32[]{:S(2)}, u32[]{:S(2)}) collective-permute-start(f32[1,12,16,128]{3,2,1,0:T(8,128)} %get-tuple-element.79), channel_id=1, source_target_pairs={{1,0},{2,1},{3,2},{4,3},{5,4},{6,5},{7,6},{0,7},{9,8},{10,9},{11,1... | collective-permute-start | bytes 294920 | tf_op jit(solution)/shard_map/ppermute | solution.py:242
  203.8 8.6 %shard_map.277 = (f32[12,64,128]{2,1,0:T(8,128)}, f32[12,64,128]{2,1,0:T(8,128)}, f32[12,64,128]{2,1,0:T(8,128)}) custom-call(f32[1,12,128,128]{3,2,1,0:T(8,128)} %get-tuple-element.77.a2_ref, f32[1,12,16,128]{3,2,1,0:T(8,128)} %copy-done.18, f32[1,12,16,128]{3,2,1,0:T(8,128)} %copy-done.19, f32[12,128,128]{2,1,0:T(8,128)} %add_add_fusion.l_ref, ...), custom_call_target="tpu_custom_call" | custom-call | flops 607518720 | bytes 9273860 | tf_op jit(solution)/shard_map/pallas_call | solution.py:182
  212.5 5.3 %shard_map.278.base_ref = f32[1,12,64,128]{3,2,1,0:T(8,128)} custom-call(f32[1,12,64,128]{3,2,1,0:T(8,128)} %bitcast.98, f32[3,12,16,128]{3,2,1,0:T(8,128)} %copy-done.14, f32[3,12,16,128]{3,2,1,0:T(8,128)} %copy-done.15, f32[8,16]{1,0:T(8,128)} %constant.73.clone.r_ref, f32[12,64,64]{2,1,0:T(8,128)} %add_add_fusion.1.l_ref, ...), custom_call_target="tpu_custom_call" | custom-call | flops 228261888 | bytes 2360324 | tf_op jit(solution)/shard_map/pallas_call | solution.py:182
  217.8 5.5 %shard_map.279 = (f32[1,12,64,128]{3,2,1,0:T(8,128)}, f32[1,12,64,128]{3,2,1,0:T(8,128)}, f32[1,12,8,128]{3,2,1,0:T(8,128)}, f32[1,12,8,128]{3,2,1,0:T(8,128)}, ...) custom-call(s32[1]{0:T(128)} %constant.52.clone.1.lead_ref, f32[1,12,64,128]{3,2,1,0:T(8,128)} %bitcast.54, ...), custom_call_target="tpu_custom_call" | custom-call | flops 228261888 | bytes 3736072 | tf_op jit(solution)/shard_map/pallas_call | solution.py:182
  225.9 6.1 %collective-permute-start.26 = (f32[1,12,8,128]{3,2,1,0:T(8,128)}, f32[1,12,8,128]{3,2,1,0:T(8,128)S(1)}, u32[]{:S(2)}, u32[]{:S(2)}) collective-permute-start(f32[1,12,8,128]{3,2,1,0:T(8,128)} %get-tuple-element.86), channel_id=1, source_target_pairs={{0,15},{1,8},{2,9},{3,10},{4,11},{5,12},{6,13},{7,14},{8,23},{9,16... | collective-permute-start | bytes 147464 | tf_op jit(solution)/shard_map/ppermute | solution.py:468
  235.5 5.7 %shard_map.280 = (f32[1,12,64,128]{3,2,1,0:T(8,128)}, f32[1,12,64,128]{3,2,1,0:T(8,128)}, f32[1,12,8,128]{3,2,1,0:T(8,128)}, f32[1,12,8,128]{3,2,1,0:T(8,128)}, ...) custom-call(s32[1]{0:T(128)} %bitcast.11.lead_ref, f32[1,12,64,128]{3,2,1,0:T(8,128)} %copy-done.10, ...), custom_call_target="tpu_custom_call" | custom-call | flops 228261888 | bytes 3736072 | tf_op jit(solution)/shard_map/pallas_call | solution.py:182
  244.1 8.0 %collective-permute-start.29 = (f32[1,12,8,128]{3,2,1,0:T(8,128)}, f32[1,12,8,128]{3,2,1,0:T(8,128)S(1)}, u32[]{:S(2)}, u32[]{:S(2)}) collective-permute-start(f32[1,12,8,128]{3,2,1,0:T(8,128)} %get-tuple-element.89), channel_id=1, source_target_pairs={{0,15},{1,8},{2,9},{3,10},{4,11},{5,12},{6,13},{7,14},{8,23},{9,16... | collective-permute-start | bytes 147464 | tf_op jit(solution)/shard_map/ppermute | solution.py:468
  255.5 5.7 %shard_map.281 = (f32[1,12,64,128]{3,2,1,0:T(8,128)}, f32[1,12,64,128]{3,2,1,0:T(8,128)}, f32[1,12,8,128]{3,2,1,0:T(8,128)}, f32[1,12,8,128]{3,2,1,0:T(8,128)}, ...) custom-call(s32[1]{0:T(128)} %bitcast.11.lead_ref, f32[1,12,64,128]{3,2,1,0:T(8,128)} %copy-done.11, ...), custom_call_target="tpu_custom_call" | custom-call | flops 228261888 | bytes 3736072 | tf_op jit(solution)/shard_map/pallas_call | solution.py:182
  263.8 8.4 %collective-permute-start.32 = (f32[1,12,8,128]{3,2,1,0:T(8,128)}, f32[1,12,8,128]{3,2,1,0:T(8,128)S(1)}, u32[]{:S(2)}, u32[]{:S(2)}) collective-permute-start(f32[1,12,8,128]{3,2,1,0:T(8,128)} %get-tuple-element.92), channel_id=1, source_target_pairs={{0,15},{1,8},{2,9},{3,10},{4,11},{5,12},{6,13},{7,14},{8,23},{9,16... | collective-permute-start | bytes 147464 | tf_op jit(solution)/shard_map/ppermute | solution.py:468
  275.7 5.5 %shard_map.282 = (f32[1,12,64,128]{3,2,1,0:T(8,128)}, f32[1,12,64,128]{3,2,1,0:T(8,128)}, f32[1,12,8,128]{3,2,1,0:T(8,128)}, f32[1,12,8,128]{3,2,1,0:T(8,128)}, ...) custom-call(s32[1]{0:T(128)} %bitcast.11.lead_ref, f32[1,12,64,128]{3,2,1,0:T(8,128)} %copy-done.6, ...), custom_call_target="tpu_custom_call" | custom-call | flops 228261888 | bytes 3736072 | tf_op jit(solution)/shard_map/pallas_call | solution.py:182
  (187 shorter events, 77.6 us)
Async XLA Ops:
  2.6 15.6 %collective-permute-start = (f32[3,12,16,128]{3,2,1,0:T(8,128)S(1)}, f32[3,12,16,128]{3,2,1,0:T(8,128)S(1)}, u32[]{:S(2)}, u32[]{:S(2)}) collective-permute-start(f32[3,12,16,128]{3,2,1,0:T(8,128)S(1)} %get-tuple-element.95), channel_id=1, source_target_pairs={{0,1},{1,2},{2,3},{3,4},{4,5},{5,6},{6,7},{7,0},{8,9},{9,10},{10,1... | collective-permute-start | bytes 884744 | tf_op jit(solution)/shard_map/ppermute | solution.py:241
  5.7 14.8 %collective-permute-start.1 = (f32[3,12,16,128]{3,2,1,0:T(8,128)S(1)}, f32[3,12,16,128]{3,2,1,0:T(8,128)S(1)}, u32[]{:S(2)}, u32[]{:S(2)}) collective-permute-start(f32[3,12,16,128]{3,2,1,0:T(8,128)S(1)} %get-tuple-element.94), channel_id=1, source_target_pairs={{1,0},{2,1},{3,2},{4,3},{5,4},{6,5},{7,6},{0,7},{9,8},{10,9},{11,1... | collective-permute-start | bytes 884744 | tf_op jit(solution)/shard_map/ppermute | solution.py:242
  31.8 9.5 %collective-permute-start.2 = (f32[1,12,16,128]{3,2,1,0:T(8,128)}, f32[1,12,16,128]{3,2,1,0:T(8,128)S(1)}, u32[]{:S(2)}, u32[]{:S(2)}) collective-permute-start(f32[1,12,16,128]{3,2,1,0:T(8,128)} %get-tuple-element.49), channel_id=1, source_target_pairs={{0,1},{1,2},{2,3},{3,4},{4,5},{5,6},{6,7},{7,0},{8,9},{9,10},{10,1... | collective-permute-start | bytes 294920 | tf_op jit(solution)/shard_map/ppermute | solution.py:241
  32.7 8.5 %collective-permute-start.3 = (f32[1,12,16,128]{3,2,1,0:T(8,128)}, f32[1,12,16,128]{3,2,1,0:T(8,128)S(1)}, u32[]{:S(2)}, u32[]{:S(2)}) collective-permute-start(f32[1,12,16,128]{3,2,1,0:T(8,128)} %get-tuple-element.50), channel_id=1, source_target_pairs={{1,0},{2,1},{3,2},{4,3},{5,4},{6,5},{7,6},{0,7},{9,8},{10,9},{11,1... | collective-permute-start | bytes 294920 | tf_op jit(solution)/shard_map/ppermute | solution.py:242
  36.5 35.1 %collective-permute-start.6 = (f32[12,8,128]{2,1,0:T(8,128)S(1)}, f32[12,8,128]{2,1,0:T(8,128)S(1)}, u32[]{:S(2)}, u32[]{:S(2)}) collective-permute-start(f32[12,8,128]{2,1,0:T(8,128)S(1)} %get-tuple-element.97), channel_id=1, source_target_pairs={{0,1},{1,2},{2,3},{3,4},{4,5},{5,6},{6,7},{7,0},{8,9},{9,10},{10,1... | collective-permute-start | bytes 147464 | tf_op jit(solution)/shard_map/ppermute | solution.py:241
  36.6 35.0 %collective-permute-start.7 = (f32[12,8,128]{2,1,0:T(8,128)S(1)}, f32[12,8,128]{2,1,0:T(8,128)S(1)}, u32[]{:S(2)}, u32[]{:S(2)}) collective-permute-start(f32[12,8,128]{2,1,0:T(8,128)S(1)} %get-tuple-element.96), channel_id=1, source_target_pairs={{1,0},{2,1},{3,2},{4,3},{5,4},{6,5},{7,6},{0,7},{9,8},{10,9},{11,1... | collective-permute-start | bytes 147464 | tf_op jit(solution)/shard_map/ppermute | solution.py:242
  49.4 7.5 %collective-permute-start.4 = (f32[1,12,16,128]{3,2,1,0:T(8,128)}, f32[1,12,16,128]{3,2,1,0:T(8,128)S(1)}, u32[]{:S(2)}, u32[]{:S(2)}) collective-permute-start(f32[1,12,16,128]{3,2,1,0:T(8,128)} %get-tuple-element.53), channel_id=1, source_target_pairs={{0,1},{1,2},{2,3},{3,4},{4,5},{5,6},{6,7},{7,0},{8,9},{9,10},{10,1... | collective-permute-start | bytes 294920 | tf_op jit(solution)/shard_map/ppermute | solution.py:241
  49.4 7.5 %collective-permute-start.5 = (f32[1,12,16,128]{3,2,1,0:T(8,128)}, f32[1,12,16,128]{3,2,1,0:T(8,128)S(1)}, u32[]{:S(2)}, u32[]{:S(2)}) collective-permute-start(f32[1,12,16,128]{3,2,1,0:T(8,128)} %get-tuple-element.54), channel_id=1, source_target_pairs={{1,0},{2,1},{3,2},{4,3},{5,4},{6,5},{7,6},{0,7},{9,8},{10,9},{11,1... | collective-permute-start | bytes 294920 | tf_op jit(solution)/shard_map/ppermute | solution.py:242
  77.9 13.0 %collective-permute-start.8 = (f32[1,12,64,128]{3,2,1,0:T(8,128)}, f32[1,12,64,128]{3,2,1,0:T(8,128)S(1)}, u32[]{:S(2)}, u32[]{:S(2)}) collective-permute-start(f32[1,12,64,128]{3,2,1,0:T(8,128)} %get-tuple-element.59), channel_id=1, source_target_pairs={{0,8},{8,16},{16,24},{1,9},{9,17},{17,25},{2,10},{10,18},{18,26},{... | collective-permute-start | bytes 1179656 | tf_op jit(solution)/shard_map/ppermute | solution.py:466
  79.2 10.4 %collective-permute-start.10 = (f32[1,12,8,128]{3,2,1,0:T(8,128)}, f32[1,12,8,128]{3,2,1,0:T(8,128)S(1)}, u32[]{:S(2)}, u32[]{:S(2)}) collective-permute-start(f32[1,12,8,128]{3,2,1,0:T(8,128)} %get-tuple-element.61), channel_id=1, source_target_pairs={{0,15},{1,8},{2,9},{3,10},{4,11},{5,12},{6,13},{7,14},{8,23},{9,16... | collective-permute-start | bytes 147464 | tf_op jit(solution)/shard_map/ppermute | solution.py:468
  97.3 15.6 %collective-permute-start.11 = (f32[1,12,64,128]{3,2,1,0:T(8,128)}, f32[1,12,64,128]{3,2,1,0:T(8,128)S(1)}, u32[]{:S(2)}, u32[]{:S(2)}) collective-permute-start(f32[1,12,64,128]{3,2,1,0:T(8,128)} %get-tuple-element.62), channel_id=1, source_target_pairs={{0,8},{8,16},{16,24},{1,9},{9,17},{17,25},{2,10},{10,18},{18,26},{... | collective-permute-start | bytes 1179656 | tf_op jit(solution)/shard_map/ppermute | solution.py:466
  104.0 40.5 %collective-permute-start.17 = (f32[1,12,128,128]{3,2,1,0:T(8,128)S(1)}, f32[1,12,128,128]{3,2,1,0:T(8,128)S(1)}, u32[]{:S(2)}, u32[]{:S(2)}) collective-permute-start(f32[1,12,128,128]{3,2,1,0:T(8,128)S(1)} %copy-done.4), channel_id=1, source_target_pairs={{0,8},{8,16},{16,24},{1,9},{9,17},{17,25},{2,10},{10,18},{18,26},{... | collective-permute-start | bytes 2359304 | tf_op jit(solution)/shard_map/ppermute | solution.py:459
  106.0 4.9 %collective-permute-start.12 = (f32[1,12,8,128]{3,2,1,0:T(8,128)}, f32[1,12,8,128]{3,2,1,0:T(8,128)S(1)}, u32[]{:S(2)}, u32[]{:S(2)}) collective-permute-start(f32[1,12,8,128]{3,2,1,0:T(8,128)} %get-tuple-element.63), channel_id=1, source_target_pairs={{0,9},{1,10},{2,11},{3,12},{4,13},{5,14},{6,15},{7,8},{8,17},{9,18... | collective-permute-start | bytes 147464 | tf_op jit(solution)/shard_map/ppermute | solution.py:467
  107.3 5.6 %collective-permute-start.13 = (f32[1,12,8,128]{3,2,1,0:T(8,128)}, f32[1,12,8,128]{3,2,1,0:T(8,128)S(1)}, u32[]{:S(2)}, u32[]{:S(2)}) collective-permute-start(f32[1,12,8,128]{3,2,1,0:T(8,128)} %get-tuple-element.64), channel_id=1, source_target_pairs={{0,15},{1,8},{2,9},{3,10},{4,11},{5,12},{6,13},{7,14},{8,23},{9,16... | collective-permute-start | bytes 147464 | tf_op jit(solution)/shard_map/ppermute | solution.py:468
  119.9 17.7 %collective-permute-start.14 = (f32[1,12,64,128]{3,2,1,0:T(8,128)}, f32[1,12,64,128]{3,2,1,0:T(8,128)S(1)}, u32[]{:S(2)}, u32[]{:S(2)}) collective-permute-start(f32[1,12,64,128]{3,2,1,0:T(8,128)} %get-tuple-element.65), channel_id=1, source_target_pairs={{0,8},{8,16},{16,24},{1,9},{9,17},{17,25},{2,10},{10,18},{18,26},{... | collective-permute-start | bytes 1179656 | tf_op jit(solution)/shard_map/ppermute | solution.py:466
  127.4 8.1 %collective-permute-start.15 = (f32[1,12,8,128]{3,2,1,0:T(8,128)}, f32[1,12,8,128]{3,2,1,0:T(8,128)S(1)}, u32[]{:S(2)}, u32[]{:S(2)}) collective-permute-start(f32[1,12,8,128]{3,2,1,0:T(8,128)} %get-tuple-element.66), channel_id=1, source_target_pairs={{0,9},{1,10},{2,11},{3,12},{4,13},{5,14},{6,15},{7,8},{8,17},{9,18... | collective-permute-start | bytes 147464 | tf_op jit(solution)/shard_map/ppermute | solution.py:467
  132.8 4.9 %collective-permute-start.16 = (f32[1,12,8,128]{3,2,1,0:T(8,128)}, f32[1,12,8,128]{3,2,1,0:T(8,128)S(1)}, u32[]{:S(2)}, u32[]{:S(2)}) collective-permute-start(f32[1,12,8,128]{3,2,1,0:T(8,128)} %get-tuple-element.67), channel_id=1, source_target_pairs={{0,15},{1,8},{2,9},{3,10},{4,11},{5,12},{6,13},{7,14},{8,23},{9,16... | collective-permute-start | bytes 147464 | tf_op jit(solution)/shard_map/ppermute | solution.py:468
  151.8 14.2 %collective-permute-start.18 = (f32[3,12,16,128]{3,2,1,0:T(8,128)}, f32[3,12,16,128]{3,2,1,0:T(8,128)S(1)}, u32[]{:S(2)}, u32[]{:S(2)}) collective-permute-start(f32[3,12,16,128]{3,2,1,0:T(8,128)} %get-tuple-element.71), channel_id=1, source_target_pairs={{0,1},{1,2},{2,3},{3,4},{4,5},{5,6},{6,7},{7,0},{8,9},{9,10},{10,1... | collective-permute-start | bytes 884744 | tf_op jit(solution)/shard_map/ppermute | solution.py:241
  152.4 16.2 %collective-permute-start.19 = (f32[3,12,16,128]{3,2,1,0:T(8,128)}, f32[3,12,16,128]{3,2,1,0:T(8,128)S(1)}, u32[]{:S(2)}, u32[]{:S(2)}) collective-permute-start(f32[3,12,16,128]{3,2,1,0:T(8,128)} %get-tuple-element.72), channel_id=1, source_target_pairs={{1,0},{2,1},{3,2},{4,3},{5,4},{6,5},{7,6},{0,7},{9,8},{10,9},{11,1... | collective-permute-start | bytes 884744 | tf_op jit(solution)/shard_map/ppermute | solution.py:242
  179.9 7.7 %collective-permute-start.20 = (f32[1,12,16,128]{3,2,1,0:T(8,128)}, f32[1,12,16,128]{3,2,1,0:T(8,128)S(1)}, u32[]{:S(2)}, u32[]{:S(2)}) collective-permute-start(f32[1,12,16,128]{3,2,1,0:T(8,128)} %get-tuple-element.74), channel_id=1, source_target_pairs={{0,1},{1,2},{2,3},{3,4},{4,5},{5,6},{6,7},{7,0},{8,9},{9,10},{10,1... | collective-permute-start | bytes 294920 | tf_op jit(solution)/shard_map/ppermute | solution.py:241
  179.9 7.7 %collective-permute-start.21 = (f32[1,12,16,128]{3,2,1,0:T(8,128)}, f32[1,12,16,128]{3,2,1,0:T(8,128)S(1)}, u32[]{:S(2)}, u32[]{:S(2)}) collective-permute-start(f32[1,12,16,128]{3,2,1,0:T(8,128)} %get-tuple-element.75), channel_id=1, source_target_pairs={{1,0},{2,1},{3,2},{4,3},{5,4},{6,5},{7,6},{0,7},{9,8},{10,9},{11,1... | collective-permute-start | bytes 294920 | tf_op jit(solution)/shard_map/ppermute | solution.py:242
  195.6 7.5 %collective-permute-start.22 = (f32[1,12,16,128]{3,2,1,0:T(8,128)}, f32[1,12,16,128]{3,2,1,0:T(8,128)S(1)}, u32[]{:S(2)}, u32[]{:S(2)}) collective-permute-start(f32[1,12,16,128]{3,2,1,0:T(8,128)} %get-tuple-element.78), channel_id=1, source_target_pairs={{0,1},{1,2},{2,3},{3,4},{4,5},{5,6},{6,7},{7,0},{8,9},{9,10},{10,1... | collective-permute-start | bytes 294920 | tf_op jit(solution)/shard_map/ppermute | solution.py:241
  195.6 7.5 %collective-permute-start.23 = (f32[1,12,16,128]{3,2,1,0:T(8,128)}, f32[1,12,16,128]{3,2,1,0:T(8,128)S(1)}, u32[]{:S(2)}, u32[]{:S(2)}) collective-permute-start(f32[1,12,16,128]{3,2,1,0:T(8,128)} %get-tuple-element.79), channel_id=1, source_target_pairs={{1,0},{2,1},{3,2},{4,3},{5,4},{6,5},{7,6},{0,7},{9,8},{10,9},{11,1... | collective-permute-start | bytes 294920 | tf_op jit(solution)/shard_map/ppermute | solution.py:242
  223.3 10.8 %collective-permute-start.24 = (f32[1,12,64,128]{3,2,1,0:T(8,128)}, f32[1,12,64,128]{3,2,1,0:T(8,128)S(1)}, u32[]{:S(2)}, u32[]{:S(2)}) collective-permute-start(f32[1,12,64,128]{3,2,1,0:T(8,128)} %get-tuple-element.84), channel_id=1, source_target_pairs={{0,8},{8,16},{16,24},{1,9},{9,17},{17,25},{2,10},{10,18},{18,26},{... | collective-permute-start | bytes 1179656 | tf_op jit(solution)/shard_map/ppermute | solution.py:466
  224.6 7.4 %collective-permute-start.25 = (f32[1,12,8,128]{3,2,1,0:T(8,128)}, f32[1,12,8,128]{3,2,1,0:T(8,128)S(1)}, u32[]{:S(2)}, u32[]{:S(2)}) collective-permute-start(f32[1,12,8,128]{3,2,1,0:T(8,128)} %get-tuple-element.85), channel_id=1, source_target_pairs={{0,9},{1,10},{2,11},{3,12},{4,13},{5,14},{6,15},{7,8},{8,17},{9,18... | collective-permute-start | bytes 147464 | tf_op jit(solution)/shard_map/ppermute | solution.py:467
  225.9 8.2 %collective-permute-start.26 = (f32[1,12,8,128]{3,2,1,0:T(8,128)}, f32[1,12,8,128]{3,2,1,0:T(8,128)S(1)}, u32[]{:S(2)}, u32[]{:S(2)}) collective-permute-start(f32[1,12,8,128]{3,2,1,0:T(8,128)} %get-tuple-element.86), channel_id=1, source_target_pairs={{0,15},{1,8},{2,9},{3,10},{4,11},{5,12},{6,13},{7,14},{8,23},{9,16... | collective-permute-start | bytes 147464 | tf_op jit(solution)/shard_map/ppermute | solution.py:468
  241.1 13.1 %collective-permute-start.27 = (f32[1,12,64,128]{3,2,1,0:T(8,128)}, f32[1,12,64,128]{3,2,1,0:T(8,128)S(1)}, u32[]{:S(2)}, u32[]{:S(2)}) collective-permute-start(f32[1,12,64,128]{3,2,1,0:T(8,128)} %get-tuple-element.87), channel_id=1, source_target_pairs={{0,8},{8,16},{16,24},{1,9},{9,17},{17,25},{2,10},{10,18},{18,26},{... | collective-permute-start | bytes 1179656 | tf_op jit(solution)/shard_map/ppermute | solution.py:466
  242.4 9.7 %collective-permute-start.28 = (f32[1,12,8,128]{3,2,1,0:T(8,128)}, f32[1,12,8,128]{3,2,1,0:T(8,128)S(1)}, u32[]{:S(2)}, u32[]{:S(2)}) collective-permute-start(f32[1,12,8,128]{3,2,1,0:T(8,128)} %get-tuple-element.88), channel_id=1, source_target_pairs={{0,9},{1,10},{2,11},{3,12},{4,13},{5,14},{6,15},{7,8},{8,17},{9,18... | collective-permute-start | bytes 147464 | tf_op jit(solution)/shard_map/ppermute | solution.py:467
  244.1 10.1 %collective-permute-start.29 = (f32[1,12,8,128]{3,2,1,0:T(8,128)}, f32[1,12,8,128]{3,2,1,0:T(8,128)S(1)}, u32[]{:S(2)}, u32[]{:S(2)}) collective-permute-start(f32[1,12,8,128]{3,2,1,0:T(8,128)} %get-tuple-element.89), channel_id=1, source_target_pairs={{0,15},{1,8},{2,9},{3,10},{4,11},{5,12},{6,13},{7,14},{8,23},{9,16... | collective-permute-start | bytes 147464 | tf_op jit(solution)/shard_map/ppermute | solution.py:468
  261.2 13.1 %collective-permute-start.30 = (f32[1,12,64,128]{3,2,1,0:T(8,128)}, f32[1,12,64,128]{3,2,1,0:T(8,128)S(1)}, u32[]{:S(2)}, u32[]{:S(2)}) collective-permute-start(f32[1,12,64,128]{3,2,1,0:T(8,128)} %get-tuple-element.90), channel_id=1, source_target_pairs={{0,8},{8,16},{16,24},{1,9},{9,17},{17,25},{2,10},{10,18},{18,26},{... | collective-permute-start | bytes 1179656 | tf_op jit(solution)/shard_map/ppermute | solution.py:466
  262.5 9.7 %collective-permute-start.31 = (f32[1,12,8,128]{3,2,1,0:T(8,128)}, f32[1,12,8,128]{3,2,1,0:T(8,128)S(1)}, u32[]{:S(2)}, u32[]{:S(2)}) collective-permute-start(f32[1,12,8,128]{3,2,1,0:T(8,128)} %get-tuple-element.91), channel_id=1, source_target_pairs={{0,9},{1,10},{2,11},{3,12},{4,13},{5,14},{6,15},{7,8},{8,17},{9,18... | collective-permute-start | bytes 147464 | tf_op jit(solution)/shard_map/ppermute | solution.py:467
  263.8 10.5 %collective-permute-start.32 = (f32[1,12,8,128]{3,2,1,0:T(8,128)}, f32[1,12,8,128]{3,2,1,0:T(8,128)S(1)}, u32[]{:S(2)}, u32[]{:S(2)}) collective-permute-start(f32[1,12,8,128]{3,2,1,0:T(8,128)} %get-tuple-element.92), channel_id=1, source_target_pairs={{0,15},{1,8},{2,9},{3,10},{4,11},{5,12},{6,13},{7,14},{8,23},{9,16... | collective-permute-start | bytes 147464 | tf_op jit(solution)/shard_map/ppermute | solution.py:468
  (61 other events, 230.0 us)

commit v5 on v4

--- a/solution.py
+++ b/solution.py
@@ -121,27 +121,62 @@
     return [wide[:, i * width:(i + 1) * width] for i in range(wide.shape[1] // width)]
 
 
-def tendency_into(out_ref, v_ref, prev_ref, next_ref, lop_ref, xt_ref, zc_ref, rx_ref,
-                  rate_ref, en_ref, s_ref):
+def tendency_into(out_ref, v_ref, prev_ref, next_ref, k_ref, d_ref, cf_ref, rx_ref,
+                  rate_ref, en_ref, s_ref, y_elem):
     states, fields, span, columns = v_ref.shape
     rows = prev_ref.shape[2]
-
-    def field_body(f, carry):
-        parts = [v_ref[b, f] for b in range(states)]
-        left = unlanes(tdot(lop_ref[f], lanes(parts)), columns)
-        right = tdot(jnp.concatenate(parts, axis=0), xt_ref[f])
+    planes = span // rows
+    f32 = jnp.float32
+    row = lax.broadcasted_iota(jnp.int32, (span, columns), 0)
+    lane = lax.broadcasted_iota(jnp.int32, (span, columns), 1)
+    yy = row % rows
+    zz = row // rows
+    x_first = lane % 8 == 0
+    x_last = lane % 8 == 7
+    y_first = yy % y_elem == 0
+    y_last = yy % y_elem == y_elem - 1
+    z_first = zz % 8 == 0
+    z_last = zz % 8 == 7
+
+    def scoped(xd_ref, yz_ref):
         for b in range(states):
-            out_ref[b, f] = left[b] + right[b * span:(b + 1) * span]
-            out_ref[b, f, pl.ds(0, rows), :] = (
-                out_ref[b, f, pl.ds(0, rows), :] + zc_ref[0, f] * prev_ref[b, f]
-            )
-            out_ref[b, f, pl.ds(span - rows, rows), :] = (
-                out_ref[b, f, pl.ds(span - rows, rows), :] + zc_ref[1, f] * next_ref[b, f]
-            )
-            s_ref[b, f] = jnp.tanh(parts[b])
-        return carry
-
-    lax.fori_loop(0, fields, field_body, 0)
+            xd_ref[b] = tdot(v_ref[b].reshape(fields * span, columns), d_ref[...]).reshape(
+                fields, span, columns)
+            yz_ref[b] = tdot(k_ref[...], lanes([v_ref[b, f] for f in range(fields)]))
+        for b in range(states):
+            for f in range(fields):
+                v = v_ref[b, f]
+                cols = slice(f * columns, (f + 1) * columns)
+                t = (cf_ref[0, f] * xd_ref[b, f] + cf_ref[1, f] * yz_ref[b, :span, cols]
+                     + cf_ref[2, f] * yz_ref[b, span:, cols])
+                before_x = pltpu.roll(v, 1, 1)
+                after_x = pltpu.roll(v, columns - 1, 1)
+                t = t + jnp.where(x_first, cf_ref[3, f] * (before_x - v), 0.0)
+                t = t + jnp.where(x_last, cf_ref[4, f] * (after_x - v), 0.0)
+                before_y = jnp.where(yy == 0, pltpu.roll(v, span - rows + 1, 0),
+                                     pltpu.roll(v, 1, 0))
+                after_y = jnp.where(yy == rows - 1, pltpu.roll(v, rows - 1, 0),
+                                    pltpu.roll(v, span - 1, 0))
+                t = t + jnp.where(y_first, cf_ref[5, f] * (before_y - v), 0.0)
+                t = t + jnp.where(y_last, cf_ref[6, f] * (after_y - v), 0.0)
+                if planes > 8:
+                    before_z = pltpu.roll(v, rows, 0)
+                    after_z = pltpu.roll(v, span - rows, 0)
+                    t = t + jnp.where(z_first & (zz > 0), cf_ref[7, f] * before_z, 0.0)
+                    t = t + jnp.where(z_last & (zz < planes - 1), cf_ref[8, f] * after_z, 0.0)
+                t = t - jnp.where(z_first, cf_ref[7, f] * v, 0.0)
+                t = t - jnp.where(z_last, cf_ref[8, f] * v, 0.0)
+                out_ref[b, f] = t
+                out_ref[b, f, pl.ds(0, rows), :] = (
+                    out_ref[b, f, pl.ds(0, rows), :] + cf_ref[7, f] * prev_ref[b, f]
+                )
+                out_ref[b, f, pl.ds(span - rows, rows), :] = (
+                    out_ref[b, f, pl.ds(span - rows, rows), :] + cf_ref[8, f] * next_ref[b, f]
+                )
+                s_ref[b, f] = jnp.tanh(v)
+
+    pl.run_scoped(scoped, pltpu.VMEM((states, fields, span, columns), f32),
+                  pltpu.VMEM((states, 2 * span, fields * columns), f32))
     for b in range(states):
         cooling = 1.0 / (1.5 + 0.5 * s_ref[b, fields - 1])
 
@@ -199,32 +234,40 @@
     reaction_count = rates.shape[0]
     fine_table = derivative_table(FINE_NODES)
     coarse_table = derivative_table(COARSE_NODES)
-    x_tables = element_tables(columns, fine_table, 28.0)
-    xt = speed_combination(velocity[0], [t.T for t in x_tables])
-    y_fine_tables = element_tables(rows, fine_table, 28.0)
-    y_coarse_tables = element_tables(coarse_rows, coarse_table, 6.0)
-    z_tables = padded_tables(depth, fine_table, 28.0)
-    z_local = [t[:, 1:-1] for t in z_tables]
-    z_mats = field_operators(velocity[2], z_tables)
-    zc = jnp.stack([z_mats[:, 0, 0], z_mats[:, depth - 1, depth + 1]])
-
-    def plane_operator(y_tables, plane_rows):
-        along_y = speed_combination(
-            velocity[1], [np.kron(np.eye(depth), t) for t in y_tables]
-        )
-        along_z = speed_combination(
-            velocity[2], [np.kron(t, np.eye(plane_rows)) for t in z_local]
-        )
-        return along_y + along_z
-
-    lop_fine = plane_operator(y_fine_tables, rows)
-    lop_coarse = plane_operator(y_coarse_tables, coarse_rows)
+    fine_elem = len(FINE_NODES)
+    coarse_elem = len(COARSE_NODES)
+    xt = jnp.asarray(np.kron(np.eye(columns // fine_elem), fine_table).T, jnp.float32)
+    z_block = np.kron(np.eye(depth // fine_elem), fine_table)
+
+    def plane_operator(y_table, plane_rows):
+        y_block = np.kron(np.eye(plane_rows // y_table.shape[0]), y_table)
+        return jnp.asarray(
+            np.concatenate([np.kron(np.eye(depth), y_block), np.kron(z_block, np.eye(plane_rows))]),
+            jnp.float32,
+        )
+
+    lop_fine = plane_operator(fine_table, rows)
+    lop_coarse = plane_operator(coarse_table, coarse_rows)
+
+    def coefficients(y_lift):
+        up = jnp.maximum(velocity, 0.0)
+        down = jnp.maximum(-velocity, 0.0)
+        return jnp.concatenate([
+            -velocity,
+            28.0 * up[0:1], 28.0 * down[0:1],
+            y_lift * up[1:2], y_lift * down[1:2],
+            28.0 * up[2:3], 28.0 * down[2:3],
+        ])
+
+    cf_fine = coefficients(28.0)
+    cf_coarse = coefficients(6.0)
     restrict_rows = np.kron(np.eye(rows // 8), lagrange_table(FINE_NODES, COARSE_NODES))
     prolong_rows = np.kron(np.eye(rows // 8), lagrange_table(COARSE_NODES, FINE_NODES))
     rmat = jnp.asarray(np.kron(np.eye(depth), restrict_rows), jnp.float32)
     pmat = jnp.asarray(np.kron(np.eye(depth), prolong_rows), jnp.float32)
     restrict_plane = jnp.asarray(restrict_rows, jnp.float32)
-    scalars = (zc, reactions.astype(jnp.int32), rates, energies)
+    scalars = (cf_fine, reactions.astype(jnp.int32), rates, energies)
+    coarse_scalars = (cf_coarse, reactions.astype(jnp.int32), rates, energies)
     scalar_kinds = (True, True, True, True)
 
     space_n = lax.axis_size("space")
@@ -249,7 +292,7 @@
     def nodes_kernel(u_ref, p_ref, n_ref, l_ref, x_ref, zc_ref, rx_ref, ra_ref, en_ref,
                      f_ref, a1_ref, h_ref, t_ref, s_ref):
         tendency_into(f_ref, u_ref, p_ref, n_ref, l_ref, x_ref, zc_ref, rx_ref, ra_ref, en_ref,
-                      s_ref)
+                      s_ref, fine_elem)
 
         def body(f, carry):
             value = u_ref[0, f] + STEP * (
@@ -265,7 +308,7 @@
     def middle_kernel(a1_ref, p_ref, n_ref, l_ref, x_ref, zc_ref, rx_ref, ra_ref, en_ref,
                       f_ref, g1_ref, a2_ref, h_ref, t_ref, s_ref):
         tendency_into(g1_ref, a1_ref, p_ref, n_ref, l_ref, x_ref, zc_ref, rx_ref, ra_ref,
-                      en_ref, s_ref)
+                      en_ref, s_ref, fine_elem)
 
         def body(f, carry):
             value = (
@@ -283,7 +326,7 @@
     def ending_kernel(a2_ref, p_ref, n_ref, l_ref, x_ref, zc_ref, rx_ref, ra_ref, en_ref,
                       f_ref, g1_ref, u_ref, r_ref, rint_ref, c1_ref, c0_ref, g2_ref, s_ref):
         tendency_into(g2_ref, a2_ref, p_ref, n_ref, l_ref, x_ref, zc_ref, rx_ref, ra_ref,
-                      en_ref, s_ref)
+                      en_ref, s_ref, fine_elem)
 
         def body(f, carry):
             g2_ref[0, f] = STEP * (f_ref[0, f] + 4.0 * g1_ref[0, f] + g2_ref[0, f]) / 6.0
@@ -304,7 +347,7 @@
             for f, part in enumerate(unlanes(wide, columns)):
                 dst[0, f] = part
         tendency_into(out_ref, c_ref, bp_ref, bn_ref, l_ref, x_ref, zc_ref, rx_ref, ra_ref,
-                      en_ref, s_ref)
+                      en_ref, s_ref, coarse_elem)
 
     def chain_kernel(lead_ref, w_ref, p_ref, n_ref, ws_ref, ps_ref, ns_ref, l_ref, x_ref,
                      zc_ref, rx_ref, ra_ref, en_ref, base_ref, rint_ref, out_ref, begin_ref,
@@ -322,7 +365,7 @@
             bn_ref[...] = n_ref[...]
 
         tendency_into(g_ref, begin_ref, bp_ref, bn_ref, l_ref, x_ref, zc_ref, rx_ref, ra_ref,
-                      en_ref, s_ref)
+                      en_ref, s_ref, coarse_elem)
 
         def body(f, carry):
             value = begin_ref[0, f] + STEP * (g_ref[0, f] - base_ref[0, f]) + rint_ref[0, f]
@@ -391,7 +434,7 @@
         return call(
             chain_kernel,
             (flag, w, w_halo[0], w_halo[1], coarse_start[None], start_halo[0][None],
-             start_halo[1][None], lop_coarse, xt) + scalars + (base, rint),
+             start_halo[1][None], lop_coarse, xt) + coarse_scalars + (base, rint),
             (True,) + (False,) * 8 + scalar_kinds + (False, False),
             (coarse_one, coarse_one, plane_one, plane_one, plane_one, plane_one),
             [pltpu.VMEM((1, fields, coarse_span, columns), f32), coarse_scratch(1)],
@@ -447,7 +490,7 @@
         )
         (base,) = call(
             base_kernel,
-            (c0[None], node_prev, node_next, restrict_plane, lop_coarse, xt) + scalars,
+            (c0[None], node_prev, node_next, restrict_plane, lop_coarse, xt) + coarse_scalars,
             (False,) * 6 + scalar_kinds,
             (jax.ShapeDtypeStruct((1, fields, coarse_span, columns), f32),),
             [pltpu.VMEM((1, fields, coarse_rows, columns), f32),

time: 285 us -> 266 us (0.933)
  Pallas kernels: 118 us -> 97 us
  waiting for transfers between devices: 36 us -> 42.5 us
  other arithmetic: 5.82 us -> 2.41 us
  starting transfers between devices: 105 us -> 102 us
    pallas_call x18, Pallas kernels: 118 us -> 97 us  [call(): pl.pallas_call(kernel, out_shape=outs, in_specs=[smem() if k else vmem()...]
    ppermute x7, waiting for transfers between devices: 19 us -> 25.1 us  [swap(): lax.ppermute(tail, 'space', [(i, (i + 1) % space_n) for i in range(space_...]
    add x4 -> x0, other arithmetic: 3.55 us -> none  [the longest x2 2.28 us: plane_operator(): return along_y + along_z]
    ppermute x7, starting transfers between devices: 29.9 us -> 26.5 us  [swap(): lax.ppermute(head, 'space', [((i + 1) % space_n, i) for i in range(space_...]
    unnamed x119 -> x75, local copies, waits for them, and re-layouts: 14.7 us -> 13.2 us
  transfers between devices with their start and end apart: 33 -> 33, of which waited for: 14 -> 16; matrix products, arithmetic and copies ran while one was open for 3% -> 2% of each run, Pallas kernels for 11% -> 7%
where the time goes in v5:
time: 266 us; the launch traced here: 265 us
  starting transfers between devices  102 us (38%)
  Pallas kernels  97 us (36%)
  waiting for transfers between devices  42.5 us (16%)
  local copies, waits for them, and re-layouts  19.3 us (7%)
    pallas_call x18, Pallas kernels, call(): pl.pallas_call(kernel, out_shape=outs, in_specs=[smem() if k else vmem()...  97 us
    ppermute x6, starting transfers between devices, per_device(): lax.ppermute(head, both, next_pairs)  36.5 us
    ppermute x7, starting transfers between devices, swap(): lax.ppermute(head, 'space', [((i + 1) % space_n, i) for i in range(space_...  26.5 us
    ppermute x7, waiting for transfers between devices, swap(): lax.ppermute(tail, 'space', [(i, (i + 1) % space_n) for i in range(space_...  25.1 us
    ppermute x6, starting transfers between devices, per_device(): begin = lax.ppermute(finish, 'tm', hop_pairs)  19.6 us
    unnamed x75, local copies, waits for them, and re-layouts  13.2 us
    ppermute x6, starting transfers between devices, per_device(): lax.ppermute(tail, both, prev_pairs)  12.3 us
    ppermute x6, waiting for transfers between devices, per_device(): lax.ppermute(head, both, next_pairs)  10.9 us
  transfers between devices with their start and end apart: 33, of which 16 were waited for; matrix products, arithmetic and copies ran while one was open for 2% of the time, Pallas kernels for 7%

profile of v5, /device:TPU:0, one launch (start us, length us, event | category | flops | bytes accessed | tf_op | source)
XLA Modules:
  0.0 264.8 jit_solution(740645930930136988)
XLA Ops:
  14.7 7.5 %collective-permute-done.p_ref = f32[3,12,16,128]{3,2,1,0:T(8,128)} collective-permute-done((f32[3,12,16,128]{3,2,1,0:T(8,128)}, f32[3,12,16,128]{3,2,1,0:T(8,128)}, u32[]{:S(2)}, u32[]{:S(2)}) %collective-permute-start) | collective-permute-done | bytes 294944 | tf_op jit(solution)/shard_map/ppermute | solution.py:284
  24.2 10.5 %shard_map.131 = (f32[3,12,128,128]{3,2,1,0:T(8,128)}, f32[1,12,128,128]{3,2,1,0:T(8,128)}, f32[1,12,16,128]{3,2,1,0:T(8,128)}, f32[1,12,16,128]{3,2,1,0:T(8,128)}) custom-call(f32[3,12,128,128]{3,2,1,0:T(8,128)} %pad_maximum_fusion.u_ref, f32[3,12,16,128]{3,2,1,0:T(8,128)} %collective-permute-done.p_ref, f32[3,12,16,128]{3,2,1,0:T(8,128)} %collective-permute-done.1.n_ref, ...), custom_call_target="tpu_custom_call" | custom-call | flops 1822556160 | bytes 6488916 | tf_op jit(solution)/shard_map/pallas_call | solution.py:217
  35.2 4.2 %collective-permute-start.3 = (f32[1,12,16,128]{3,2,1,0:T(8,128)}, f32[1,12,16,128]{3,2,1,0:T(8,128)S(1)}, u32[]{:S(2)}, u32[]{:S(2)}) collective-permute-start(f32[1,12,16,128]{3,2,1,0:T(8,128)} %get-tuple-element.50), channel_id=1, source_target_pairs={{1,0},{2,1},{3,2},{4,3},{5,4},{6,5},{7,6},{0,7},{9,8},{10,9},{11,1... | collective-permute-start | bytes 294920 | tf_op jit(solution)/shard_map/ppermute | solution.py:285
  43.3 6.0 %shard_map.132 = (f32[1,12,128,128]{3,2,1,0:T(8,128)}, f32[1,12,128,128]{3,2,1,0:T(8,128)}, f32[1,12,16,128]{3,2,1,0:T(8,128)}, f32[1,12,16,128]{3,2,1,0:T(8,128)}) custom-call(f32[1,12,128,128]{3,2,1,0:T(8,128)} %get-tuple-element.48.a1_ref, f32[1,12,16,128]{3,2,1,0:T(8,128)} %copy-done.14, f32[1,12,16,128]{3,2,1,0:T(8,128)} %copy-done.16, ...), custom_call_target="tpu_custom_call" | custom-call | flops 607518720 | bytes 5309268 | tf_op jit(solution)/shard_map/pallas_call | solution.py:217
  49.9 4.1 %collective-permute-start.5 = (f32[1,12,16,128]{3,2,1,0:T(8,128)}, f32[1,12,16,128]{3,2,1,0:T(8,128)S(1)}, u32[]{:S(2)}, u32[]{:S(2)}) collective-permute-start(f32[1,12,16,128]{3,2,1,0:T(8,128)} %get-tuple-element.54), channel_id=1, source_target_pairs={{1,0},{2,1},{3,2},{4,3},{5,4},{6,5},{7,6},{0,7},{9,8},{10,9},{11,1... | collective-permute-start | bytes 294920 | tf_op jit(solution)/shard_map/ppermute | solution.py:285
  58.1 7.5 %shard_map.133 = (f32[12,64,128]{2,1,0:T(8,128)}, f32[12,64,128]{2,1,0:T(8,128)}, f32[12,64,128]{2,1,0:T(8,128)}) custom-call(f32[1,12,128,128]{3,2,1,0:T(8,128)} %get-tuple-element.52.a2_ref, f32[1,12,16,128]{3,2,1,0:T(8,128)} %copy-done.18, f32[1,12,16,128]{3,2,1,0:T(8,128)} %copy-done.19, f32[256,128]{1,0:T(8,128)} %constant.28.clone.l_ref, ...), custom_call_target="tpu_custom_call" | custom-call | flops 607518720 | bytes 7897940 | tf_op jit(solution)/shard_map/pallas_call | solution.py:217
  65.6 3.7 %shard_map.134.base_ref = f32[1,12,64,128]{3,2,1,0:T(8,128)} custom-call(f32[1,12,64,128]{3,2,1,0:T(8,128)} %bitcast.70, f32[3,12,16,128]{3,2,1,0:T(8,128)} %collective-permute-done.p_ref, f32[3,12,16,128]{3,2,1,0:T(8,128)} %collective-permute-done.1.n_ref, f32[8,16]{1,0:T(8,128)} %constant.32.clone.r_ref, f32[128,64]{1,0:T(8,128)} %constant.29.clone.l_ref, ...), custom_call_target="tpu_custom_call" | custom-call | flops 228261888 | bytes 1475924 | tf_op jit(solution)/shard_map/pallas_call | solution.py:217
  69.9 4.1 %shard_map.135 = (f32[1,12,64,128]{3,2,1,0:T(8,128)}, f32[1,12,64,128]{3,2,1,0:T(8,128)}, f32[1,12,8,128]{3,2,1,0:T(8,128)}, f32[1,12,8,128]{3,2,1,0:T(8,128)}, ...) custom-call(s32[1]{0:T(128)} %constant.11.clone.1.lead_ref, f32[1,12,64,128]{3,2,1,0:T(8,128)} %bitcast.27, ...), custom_call_target="tpu_custom_call" | custom-call | flops 228261888 | bytes 2851672 | tf_op jit(solution)/shard_map/pallas_call | solution.py:217
  75.6 7.6 %collective-permute-start.10 = (f32[1,12,8,128]{3,2,1,0:T(8,128)}, f32[1,12,8,128]{3,2,1,0:T(8,128)S(1)}, u32[]{:S(2)}, u32[]{:S(2)}) collective-permute-start(f32[1,12,8,128]{3,2,1,0:T(8,128)} %get-tuple-element.61), channel_id=1, source_target_pairs={{0,15},{1,8},{2,9},{3,10},{4,11},{5,12},{6,13},{7,14},{8,23},{9,16... | collective-permute-start | bytes 147464 | tf_op jit(solution)/shard_map/ppermute | solution.py:511
  87.3 4.0 %shard_map.136 = (f32[1,12,64,128]{3,2,1,0:T(8,128)}, f32[1,12,64,128]{3,2,1,0:T(8,128)}, f32[1,12,8,128]{3,2,1,0:T(8,128)}, f32[1,12,8,128]{3,2,1,0:T(8,128)}, ...) custom-call(s32[1]{0:T(128)} %bitcast.3.lead_ref, f32[1,12,64,128]{3,2,1,0:T(8,128)} %copy-done.8, ...), custom_call_target="tpu_custom_call" | custom-call | flops 228261888 | bytes 2851672 | tf_op jit(solution)/shard_map/pallas_call | solution.py:217
  91.4 6.7 %collective-permute-start.11 = (f32[1,12,64,128]{3,2,1,0:T(8,128)}, f32[1,12,64,128]{3,2,1,0:T(8,128)S(1)}, u32[]{:S(2)}, u32[]{:S(2)}) collective-permute-start(f32[1,12,64,128]{3,2,1,0:T(8,128)} %get-tuple-element.62), channel_id=1, source_target_pairs={{0,8},{8,16},{16,24},{1,9},{9,17},{17,25},{2,10},{10,18},{18,26},{... | collective-permute-start | bytes 1179656 | tf_op jit(solution)/shard_map/ppermute | solution.py:509
  101.4 3.8 %collective-permute-start.13 = (f32[1,12,8,128]{3,2,1,0:T(8,128)}, f32[1,12,8,128]{3,2,1,0:T(8,128)S(1)}, u32[]{:S(2)}, u32[]{:S(2)}) collective-permute-start(f32[1,12,8,128]{3,2,1,0:T(8,128)} %get-tuple-element.64), channel_id=1, source_target_pairs={{0,15},{1,8},{2,9},{3,10},{4,11},{5,12},{6,13},{7,14},{8,23},{9,16... | collective-permute-start | bytes 147464 | tf_op jit(solution)/shard_map/ppermute | solution.py:511
  108.6 4.1 %shard_map.137 = (f32[1,12,64,128]{3,2,1,0:T(8,128)}, f32[1,12,64,128]{3,2,1,0:T(8,128)}, f32[1,12,8,128]{3,2,1,0:T(8,128)}, f32[1,12,8,128]{3,2,1,0:T(8,128)}, ...) custom-call(s32[1]{0:T(128)} %bitcast.3.lead_ref, f32[1,12,64,128]{3,2,1,0:T(8,128)} %copy-done.7, ...), custom_call_target="tpu_custom_call" | custom-call | flops 228261888 | bytes 2851672 | tf_op jit(solution)/shard_map/pallas_call | solution.py:217
  112.6 7.4 %collective-permute-start.14 = (f32[1,12,64,128]{3,2,1,0:T(8,128)}, f32[1,12,64,128]{3,2,1,0:T(8,128)S(1)}, u32[]{:S(2)}, u32[]{:S(2)}) collective-permute-start(f32[1,12,64,128]{3,2,1,0:T(8,128)} %get-tuple-element.65), channel_id=1, source_target_pairs={{0,8},{8,16},{16,24},{1,9},{9,17},{17,25},{2,10},{10,18},{18,26},{... | collective-permute-start | bytes 1179656 | tf_op jit(solution)/shard_map/ppermute | solution.py:509
  120.0 5.3 %collective-permute-start.15 = (f32[1,12,8,128]{3,2,1,0:T(8,128)}, f32[1,12,8,128]{3,2,1,0:T(8,128)S(1)}, u32[]{:S(2)}, u32[]{:S(2)}) collective-permute-start(f32[1,12,8,128]{3,2,1,0:T(8,128)} %get-tuple-element.66), channel_id=1, source_target_pairs={{0,9},{1,10},{2,11},{3,12},{4,13},{5,14},{6,15},{7,8},{8,17},{9,18... | collective-permute-start | bytes 147464 | tf_op jit(solution)/shard_map/ppermute | solution.py:510
  131.5 4.0 %shard_map.138 = (f32[1,12,64,128]{3,2,1,0:T(8,128)}, f32[1,12,64,128]{3,2,1,0:T(8,128)}, f32[1,12,8,128]{3,2,1,0:T(8,128)}, f32[1,12,8,128]{3,2,1,0:T(8,128)}, ...) custom-call(s32[1]{0:T(128)} %bitcast.3.lead_ref, f32[1,12,64,128]{3,2,1,0:T(8,128)} %copy-done.9, ...), custom_call_target="tpu_custom_call" | custom-call | flops 228261888 | bytes 2851672 | tf_op jit(solution)/shard_map/pallas_call | solution.py:217
  136.5 6.3 %shard_map.139 = (f32[3,12,128,128]{3,2,1,0:T(8,128)}, f32[3,12,16,128]{3,2,1,0:T(8,128)}, f32[3,12,16,128]{3,2,1,0:T(8,128)}) custom-call(f32[1,12,128,128]{3,2,1,0:T(8,128)} %get-tuple-element.48.a1_ref, f32[1,12,128,128]{3,2,1,0:T(8,128)} %get-tuple-element.52.a2_ref, f32[12,64,128]{2,1,0:T(8,128)} %get-tuple-element.56.c0_ref, ...), custom_call_target="tpu_custom_call" | custom-call | flops 603979776 | bytes 7733252 | tf_op jit(solution)/shard_map/pallas_call | solution.py:217
  143.3 4.1 %collective-permute-start.19 = (f32[3,12,16,128]{3,2,1,0:T(8,128)}, f32[3,12,16,128]{3,2,1,0:T(8,128)S(1)}, u32[]{:S(2)}, u32[]{:S(2)}) collective-permute-start(f32[3,12,16,128]{3,2,1,0:T(8,128)} %get-tuple-element.72), channel_id=1, source_target_pairs={{1,0},{2,1},{3,2},{4,3},{5,4},{6,5},{7,6},{0,7},{9,8},{10,9},{11,1... | collective-permute-start | bytes 884744 | tf_op jit(solution)/shard_map/ppermute | solution.py:285
  147.4 9.5 %collective-permute-done.18.p_ref = f32[3,12,16,128]{3,2,1,0:T(8,128)S(1)} collective-permute-done((f32[3,12,16,128]{3,2,1,0:T(8,128)}, f32[3,12,16,128]{3,2,1,0:T(8,128)S(1)}, u32[]{:S(2)}, u32[]{:S(2)}) %collective-permute-start.18) | collective-permute-done | bytes 294944 | tf_op jit(solution)/shard_map/ppermute | solution.py:284
  160.2 10.5 %shard_map.140 = (f32[3,12,128,128]{3,2,1,0:T(8,128)}, f32[1,12,128,128]{3,2,1,0:T(8,128)}, f32[1,12,16,128]{3,2,1,0:T(8,128)}, f32[1,12,16,128]{3,2,1,0:T(8,128)}) custom-call(f32[3,12,128,128]{3,2,1,0:T(8,128)} %get-tuple-element.70.u_ref, f32[3,12,16,128]{3,2,1,0:T(8,128)} %copy-done.12, f32[3,12,16,128]{3,2,1,0:T(8,128)} %copy-done.13, ...), custom_call_target="tpu_custom_call" | custom-call | flops 1822556160 | bytes 6488916 | tf_op jit(solution)/shard_map/pallas_call | solution.py:217
  170.7 4.7 %collective-permute-start.21 = (f32[1,12,16,128]{3,2,1,0:T(8,128)}, f32[1,12,16,128]{3,2,1,0:T(8,128)S(1)}, u32[]{:S(2)}, u32[]{:S(2)}) collective-permute-start(f32[1,12,16,128]{3,2,1,0:T(8,128)} %get-tuple-element.75), channel_id=1, source_target_pairs={{1,0},{2,1},{3,2},{4,3},{5,4},{6,5},{7,6},{0,7},{9,8},{10,9},{11,1... | collective-permute-start | bytes 294920 | tf_op jit(solution)/shard_map/ppermute | solution.py:285
  179.1 6.0 %shard_map.141 = (f32[1,12,128,128]{3,2,1,0:T(8,128)}, f32[1,12,128,128]{3,2,1,0:T(8,128)}, f32[1,12,16,128]{3,2,1,0:T(8,128)}, f32[1,12,16,128]{3,2,1,0:T(8,128)}) custom-call(f32[1,12,128,128]{3,2,1,0:T(8,128)} %get-tuple-element.73.a1_ref, f32[1,12,16,128]{3,2,1,0:T(8,128)} %copy-done.15, f32[1,12,16,128]{3,2,1,0:T(8,128)} %copy-done.17, ...), custom_call_target="tpu_custom_call" | custom-call | flops 607518720 | bytes 5309268 | tf_op jit(solution)/shard_map/pallas_call | solution.py:217
  185.1 4.7 %collective-permute-start.23 = (f32[1,12,16,128]{3,2,1,0:T(8,128)}, f32[1,12,16,128]{3,2,1,0:T(8,128)S(1)}, u32[]{:S(2)}, u32[]{:S(2)}) collective-permute-start(f32[1,12,16,128]{3,2,1,0:T(8,128)} %get-tuple-element.79), channel_id=1, source_target_pairs={{1,0},{2,1},{3,2},{4,3},{5,4},{6,5},{7,6},{0,7},{9,8},{10,9},{11,1... | collective-permute-start | bytes 294920 | tf_op jit(solution)/shard_map/ppermute | solution.py:285
  193.3 7.4 %shard_map.142 = (f32[12,64,128]{2,1,0:T(8,128)}, f32[12,64,128]{2,1,0:T(8,128)}, f32[12,64,128]{2,1,0:T(8,128)}) custom-call(f32[1,12,128,128]{3,2,1,0:T(8,128)} %get-tuple-element.77.a2_ref, f32[1,12,16,128]{3,2,1,0:T(8,128)} %copy-done.20, f32[1,12,16,128]{3,2,1,0:T(8,128)} %copy-done.21, f32[256,128]{1,0:T(8,128)} %constant.28.clone.l_ref, ...), custom_call_target="tpu_custom_call" | custom-call | flops 607518720 | bytes 7897940 | tf_op jit(solution)/shard_map/pallas_call | solution.py:217
  200.7 3.6 %shard_map.143.base_ref = f32[1,12,64,128]{3,2,1,0:T(8,128)} custom-call(f32[1,12,64,128]{3,2,1,0:T(8,128)} %bitcast.76, f32[3,12,16,128]{3,2,1,0:T(8,128)} %copy-done.12, f32[3,12,16,128]{3,2,1,0:T(8,128)} %copy-done.13, f32[8,16]{1,0:T(8,128)} %constant.32.clone.r_ref, f32[128,64]{1,0:T(8,128)} %constant.29.clone.l_ref, f32[128,128]{1,0:T(8,128)} %constant.27.clone.x_ref, ...), custom_call_target="tpu_custom_call" | custom-call | flops 228261888 | bytes 1475924 | tf_op jit(solution)/shard_map/pallas_call | solution.py:217
  204.3 4.0 %shard_map.144 = (f32[1,12,64,128]{3,2,1,0:T(8,128)}, f32[1,12,64,128]{3,2,1,0:T(8,128)}, f32[1,12,8,128]{3,2,1,0:T(8,128)}, f32[1,12,8,128]{3,2,1,0:T(8,128)}, ...) custom-call(s32[1]{0:T(128)} %constant.11.clone.1.lead_ref, f32[1,12,64,128]{3,2,1,0:T(8,128)} %bitcast.32, ...), custom_call_target="tpu_custom_call" | custom-call | flops 228261888 | bytes 2851672 | tf_op jit(solution)/shard_map/pallas_call | solution.py:217
  211.0 6.1 %collective-permute-start.26 = (f32[1,12,8,128]{3,2,1,0:T(8,128)}, f32[1,12,8,128]{3,2,1,0:T(8,128)S(1)}, u32[]{:S(2)}, u32[]{:S(2)}) collective-permute-start(f32[1,12,8,128]{3,2,1,0:T(8,128)} %get-tuple-element.86), channel_id=1, source_target_pairs={{0,15},{1,8},{2,9},{3,10},{4,11},{5,12},{6,13},{7,14},{8,23},{9,16... | collective-permute-start | bytes 147464 | tf_op jit(solution)/shard_map/ppermute | solution.py:511
  220.5 4.3 %shard_map.145 = (f32[1,12,64,128]{3,2,1,0:T(8,128)}, f32[1,12,64,128]{3,2,1,0:T(8,128)}, f32[1,12,8,128]{3,2,1,0:T(8,128)}, f32[1,12,8,128]{3,2,1,0:T(8,128)}, ...) custom-call(s32[1]{0:T(128)} %bitcast.3.lead_ref, f32[1,12,64,128]{3,2,1,0:T(8,128)} %copy-done.10, ...), custom_call_target="tpu_custom_call" | custom-call | flops 228261888 | bytes 2851672 | tf_op jit(solution)/shard_map/pallas_call | solution.py:217
  228.0 7.8 %collective-permute-start.29 = (f32[1,12,8,128]{3,2,1,0:T(8,128)}, f32[1,12,8,128]{3,2,1,0:T(8,128)S(1)}, u32[]{:S(2)}, u32[]{:S(2)}) collective-permute-start(f32[1,12,8,128]{3,2,1,0:T(8,128)} %get-tuple-element.89), channel_id=1, source_target_pairs={{0,15},{1,8},{2,9},{3,10},{4,11},{5,12},{6,13},{7,14},{8,23},{9,16... | collective-permute-start | bytes 147464 | tf_op jit(solution)/shard_map/ppermute | solution.py:511
  239.3 4.1 %shard_map.146 = (f32[1,12,64,128]{3,2,1,0:T(8,128)}, f32[1,12,64,128]{3,2,1,0:T(8,128)}, f32[1,12,8,128]{3,2,1,0:T(8,128)}, f32[1,12,8,128]{3,2,1,0:T(8,128)}, ...) custom-call(s32[1]{0:T(128)} %bitcast.3.lead_ref, f32[1,12,64,128]{3,2,1,0:T(8,128)} %copy-done.11, ...), custom_call_target="tpu_custom_call" | custom-call | flops 228261888 | bytes 2851672 | tf_op jit(solution)/shard_map/pallas_call | solution.py:217
  246.0 8.4 %collective-permute-start.32 = (f32[1,12,8,128]{3,2,1,0:T(8,128)}, f32[1,12,8,128]{3,2,1,0:T(8,128)S(1)}, u32[]{:S(2)}, u32[]{:S(2)}) collective-permute-start(f32[1,12,8,128]{3,2,1,0:T(8,128)} %get-tuple-element.92), channel_id=1, source_target_pairs={{0,15},{1,8},{2,9},{3,10},{4,11},{5,12},{6,13},{7,14},{8,23},{9,16... | collective-permute-start | bytes 147464 | tf_op jit(solution)/shard_map/ppermute | solution.py:511
  257.8 4.0 %shard_map.147 = (f32[1,12,64,128]{3,2,1,0:T(8,128)}, f32[1,12,64,128]{3,2,1,0:T(8,128)}, f32[1,12,8,128]{3,2,1,0:T(8,128)}, f32[1,12,8,128]{3,2,1,0:T(8,128)}, ...) custom-call(s32[1]{0:T(128)} %bitcast.3.lead_ref, f32[1,12,64,128]{3,2,1,0:T(8,128)} %copy-done.6, ...), custom_call_target="tpu_custom_call" | custom-call | flops 228261888 | bytes 2851672 | tf_op jit(solution)/shard_map/pallas_call | solution.py:217
  (138 shorter events, 77.7 us)
Async XLA Ops:
  5.2 17.0 %collective-permute-start = (f32[3,12,16,128]{3,2,1,0:T(8,128)}, f32[3,12,16,128]{3,2,1,0:T(8,128)}, u32[]{:S(2)}, u32[]{:S(2)}) collective-permute-start(f32[3,12,16,128]{3,2,1,0:T(8,128)} %get-tuple-element.95), channel_id=1, source_target_pairs={{0,1},{1,2},{2,3},{3,4},{4,5},{5,6},{6,7},{7,0},{8,9},{9,10},{10,1... | collective-permute-start | bytes 884744 | tf_op jit(solution)/shard_map/ppermute | solution.py:284
  8.2 16.0 %collective-permute-start.1 = (f32[3,12,16,128]{3,2,1,0:T(8,128)S(1)}, f32[3,12,16,128]{3,2,1,0:T(8,128)}, u32[]{:S(2)}, u32[]{:S(2)}) collective-permute-start(f32[3,12,16,128]{3,2,1,0:T(8,128)S(1)} %get-tuple-element.94), channel_id=1, source_target_pairs={{1,0},{2,1},{3,2},{4,3},{5,4},{6,5},{7,6},{0,7},{9,8},{10,9},{11,1... | collective-permute-start | bytes 884744 | tf_op jit(solution)/shard_map/ppermute | solution.py:285
  34.7 7.6 %collective-permute-start.2 = (f32[1,12,16,128]{3,2,1,0:T(8,128)}, f32[1,12,16,128]{3,2,1,0:T(8,128)S(1)}, u32[]{:S(2)}, u32[]{:S(2)}) collective-permute-start(f32[1,12,16,128]{3,2,1,0:T(8,128)} %get-tuple-element.49), channel_id=1, source_target_pairs={{0,1},{1,2},{2,3},{3,4},{4,5},{5,6},{6,7},{7,0},{8,9},{9,10},{10,1... | collective-permute-start | bytes 294920 | tf_op jit(solution)/shard_map/ppermute | solution.py:284
  35.2 7.5 %collective-permute-start.3 = (f32[1,12,16,128]{3,2,1,0:T(8,128)}, f32[1,12,16,128]{3,2,1,0:T(8,128)S(1)}, u32[]{:S(2)}, u32[]{:S(2)}) collective-permute-start(f32[1,12,16,128]{3,2,1,0:T(8,128)} %get-tuple-element.50), channel_id=1, source_target_pairs={{1,0},{2,1},{3,2},{4,3},{5,4},{6,5},{7,6},{0,7},{9,8},{10,9},{11,1... | collective-permute-start | bytes 294920 | tf_op jit(solution)/shard_map/ppermute | solution.py:285
  49.3 8.0 %collective-permute-start.4 = (f32[1,12,16,128]{3,2,1,0:T(8,128)}, f32[1,12,16,128]{3,2,1,0:T(8,128)S(1)}, u32[]{:S(2)}, u32[]{:S(2)}) collective-permute-start(f32[1,12,16,128]{3,2,1,0:T(8,128)} %get-tuple-element.53), channel_id=1, source_target_pairs={{0,1},{1,2},{2,3},{3,4},{4,5},{5,6},{6,7},{7,0},{8,9},{9,10},{10,1... | collective-permute-start | bytes 294920 | tf_op jit(solution)/shard_map/ppermute | solution.py:284
  49.9 7.5 %collective-permute-start.5 = (f32[1,12,16,128]{3,2,1,0:T(8,128)}, f32[1,12,16,128]{3,2,1,0:T(8,128)S(1)}, u32[]{:S(2)}, u32[]{:S(2)}) collective-permute-start(f32[1,12,16,128]{3,2,1,0:T(8,128)} %get-tuple-element.54), channel_id=1, source_target_pairs={{1,0},{2,1},{3,2},{4,3},{5,4},{6,5},{7,6},{0,7},{9,8},{10,9},{11,1... | collective-permute-start | bytes 294920 | tf_op jit(solution)/shard_map/ppermute | solution.py:285
  54.0 15.2 %collective-permute-start.7 = (f32[12,8,128]{2,1,0:T(8,128)S(1)}, f32[12,8,128]{2,1,0:T(8,128)S(1)}, u32[]{:S(2)}, u32[]{:S(2)}) collective-permute-start(f32[12,8,128]{2,1,0:T(8,128)S(1)} %get-tuple-element.96), channel_id=1, source_target_pairs={{1,0},{2,1},{3,2},{4,3},{5,4},{6,5},{7,6},{0,7},{9,8},{10,9},{11,1... | collective-permute-start | bytes 147464 | tf_op jit(solution)/shard_map/ppermute | solution.py:285
  55.6 13.6 %collective-permute-start.6 = (f32[12,8,128]{2,1,0:T(8,128)S(1)}, f32[12,8,128]{2,1,0:T(8,128)S(1)}, u32[]{:S(2)}, u32[]{:S(2)}) collective-permute-start(f32[12,8,128]{2,1,0:T(8,128)S(1)} %get-tuple-element.97), channel_id=1, source_target_pairs={{0,1},{1,2},{2,3},{3,4},{4,5},{5,6},{6,7},{7,0},{8,9},{9,10},{10,1... | collective-permute-start | bytes 147464 | tf_op jit(solution)/shard_map/ppermute | solution.py:284
  74.0 12.5 %collective-permute-start.8 = (f32[1,12,64,128]{3,2,1,0:T(8,128)}, f32[1,12,64,128]{3,2,1,0:T(8,128)S(1)}, u32[]{:S(2)}, u32[]{:S(2)}) collective-permute-start(f32[1,12,64,128]{3,2,1,0:T(8,128)} %get-tuple-element.59), channel_id=1, source_target_pairs={{0,8},{8,16},{16,24},{1,9},{9,17},{17,25},{2,10},{10,18},{18,26},{... | collective-permute-start | bytes 1179656 | tf_op jit(solution)/shard_map/ppermute | solution.py:509
  75.6 9.6 %collective-permute-start.10 = (f32[1,12,8,128]{3,2,1,0:T(8,128)}, f32[1,12,8,128]{3,2,1,0:T(8,128)S(1)}, u32[]{:S(2)}, u32[]{:S(2)}) collective-permute-start(f32[1,12,8,128]{3,2,1,0:T(8,128)} %get-tuple-element.61), channel_id=1, source_target_pairs={{0,15},{1,8},{2,9},{3,10},{4,11},{5,12},{6,13},{7,14},{8,23},{9,16... | collective-permute-start | bytes 147464 | tf_op jit(solution)/shard_map/ppermute | solution.py:511
  91.4 15.8 %collective-permute-start.11 = (f32[1,12,64,128]{3,2,1,0:T(8,128)}, f32[1,12,64,128]{3,2,1,0:T(8,128)S(1)}, u32[]{:S(2)}, u32[]{:S(2)}) collective-permute-start(f32[1,12,64,128]{3,2,1,0:T(8,128)} %get-tuple-element.62), channel_id=1, source_target_pairs={{0,8},{8,16},{16,24},{1,9},{9,17},{17,25},{2,10},{10,18},{18,26},{... | collective-permute-start | bytes 1179656 | tf_op jit(solution)/shard_map/ppermute | solution.py:509
  98.1 37.5 %collective-permute-start.17 = (f32[1,12,128,128]{3,2,1,0:T(8,128)S(1)}, f32[1,12,128,128]{3,2,1,0:T(8,128)S(1)}, u32[]{:S(2)}, u32[]{:S(2)}) collective-permute-start(f32[1,12,128,128]{3,2,1,0:T(8,128)S(1)} %copy-done.4), channel_id=1, source_target_pairs={{0,8},{8,16},{16,24},{1,9},{9,17},{17,25},{2,10},{10,18},{18,26},{... | collective-permute-start | bytes 2359304 | tf_op jit(solution)/shard_map/ppermute | solution.py:502
  100.1 5.1 %collective-permute-start.12 = (f32[1,12,8,128]{3,2,1,0:T(8,128)}, f32[1,12,8,128]{3,2,1,0:T(8,128)S(1)}, u32[]{:S(2)}, u32[]{:S(2)}) collective-permute-start(f32[1,12,8,128]{3,2,1,0:T(8,128)} %get-tuple-element.63), channel_id=1, source_target_pairs={{0,9},{1,10},{2,11},{3,12},{4,13},{5,14},{6,15},{7,8},{8,17},{9,18... | collective-permute-start | bytes 147464 | tf_op jit(solution)/shard_map/ppermute | solution.py:510
  101.4 5.8 %collective-permute-start.13 = (f32[1,12,8,128]{3,2,1,0:T(8,128)}, f32[1,12,8,128]{3,2,1,0:T(8,128)S(1)}, u32[]{:S(2)}, u32[]{:S(2)}) collective-permute-start(f32[1,12,8,128]{3,2,1,0:T(8,128)} %get-tuple-element.64), channel_id=1, source_target_pairs={{0,15},{1,8},{2,9},{3,10},{4,11},{5,12},{6,13},{7,14},{8,23},{9,16... | collective-permute-start | bytes 147464 | tf_op jit(solution)/shard_map/ppermute | solution.py:511
  112.6 17.5 %collective-permute-start.14 = (f32[1,12,64,128]{3,2,1,0:T(8,128)}, f32[1,12,64,128]{3,2,1,0:T(8,128)S(1)}, u32[]{:S(2)}, u32[]{:S(2)}) collective-permute-start(f32[1,12,64,128]{3,2,1,0:T(8,128)} %get-tuple-element.65), channel_id=1, source_target_pairs={{0,8},{8,16},{16,24},{1,9},{9,17},{17,25},{2,10},{10,18},{18,26},{... | collective-permute-start | bytes 1179656 | tf_op jit(solution)/shard_map/ppermute | solution.py:509
  120.0 8.1 %collective-permute-start.15 = (f32[1,12,8,128]{3,2,1,0:T(8,128)}, f32[1,12,8,128]{3,2,1,0:T(8,128)S(1)}, u32[]{:S(2)}, u32[]{:S(2)}) collective-permute-start(f32[1,12,8,128]{3,2,1,0:T(8,128)} %get-tuple-element.66), channel_id=1, source_target_pairs={{0,9},{1,10},{2,11},{3,12},{4,13},{5,14},{6,15},{7,8},{8,17},{9,18... | collective-permute-start | bytes 147464 | tf_op jit(solution)/shard_map/ppermute | solution.py:510
  125.3 4.8 %collective-permute-start.16 = (f32[1,12,8,128]{3,2,1,0:T(8,128)}, f32[1,12,8,128]{3,2,1,0:T(8,128)S(1)}, u32[]{:S(2)}, u32[]{:S(2)}) collective-permute-start(f32[1,12,8,128]{3,2,1,0:T(8,128)} %get-tuple-element.67), channel_id=1, source_target_pairs={{0,15},{1,8},{2,9},{3,10},{4,11},{5,12},{6,13},{7,14},{8,23},{9,16... | collective-permute-start | bytes 147464 | tf_op jit(solution)/shard_map/ppermute | solution.py:511
  142.7 14.2 %collective-permute-start.18 = (f32[3,12,16,128]{3,2,1,0:T(8,128)}, f32[3,12,16,128]{3,2,1,0:T(8,128)S(1)}, u32[]{:S(2)}, u32[]{:S(2)}) collective-permute-start(f32[3,12,16,128]{3,2,1,0:T(8,128)} %get-tuple-element.71), channel_id=1, source_target_pairs={{0,1},{1,2},{2,3},{3,4},{4,5},{5,6},{6,7},{7,0},{8,9},{9,10},{10,1... | collective-permute-start | bytes 884744 | tf_op jit(solution)/shard_map/ppermute | solution.py:284
  143.3 16.2 %collective-permute-start.19 = (f32[3,12,16,128]{3,2,1,0:T(8,128)}, f32[3,12,16,128]{3,2,1,0:T(8,128)S(1)}, u32[]{:S(2)}, u32[]{:S(2)}) collective-permute-start(f32[3,12,16,128]{3,2,1,0:T(8,128)} %get-tuple-element.72), channel_id=1, source_target_pairs={{1,0},{2,1},{3,2},{4,3},{5,4},{6,5},{7,6},{0,7},{9,8},{10,9},{11,1... | collective-permute-start | bytes 884744 | tf_op jit(solution)/shard_map/ppermute | solution.py:285
  170.7 7.7 %collective-permute-start.20 = (f32[1,12,16,128]{3,2,1,0:T(8,128)}, f32[1,12,16,128]{3,2,1,0:T(8,128)S(1)}, u32[]{:S(2)}, u32[]{:S(2)}) collective-permute-start(f32[1,12,16,128]{3,2,1,0:T(8,128)} %get-tuple-element.74), channel_id=1, source_target_pairs={{0,1},{1,2},{2,3},{3,4},{4,5},{5,6},{6,7},{7,0},{8,9},{9,10},{10,1... | collective-permute-start | bytes 294920 | tf_op jit(solution)/shard_map/ppermute | solution.py:284
  170.7 7.7 %collective-permute-start.21 = (f32[1,12,16,128]{3,2,1,0:T(8,128)}, f32[1,12,16,128]{3,2,1,0:T(8,128)S(1)}, u32[]{:S(2)}, u32[]{:S(2)}) collective-permute-start(f32[1,12,16,128]{3,2,1,0:T(8,128)} %get-tuple-element.75), channel_id=1, source_target_pairs={{1,0},{2,1},{3,2},{4,3},{5,4},{6,5},{7,6},{0,7},{9,8},{10,9},{11,1... | collective-permute-start | bytes 294920 | tf_op jit(solution)/shard_map/ppermute | solution.py:285
  185.1 7.5 %collective-permute-start.22 = (f32[1,12,16,128]{3,2,1,0:T(8,128)}, f32[1,12,16,128]{3,2,1,0:T(8,128)S(1)}, u32[]{:S(2)}, u32[]{:S(2)}) collective-permute-start(f32[1,12,16,128]{3,2,1,0:T(8,128)} %get-tuple-element.78), channel_id=1, source_target_pairs={{0,1},{1,2},{2,3},{3,4},{4,5},{5,6},{6,7},{7,0},{8,9},{9,10},{10,1... | collective-permute-start | bytes 294920 | tf_op jit(solution)/shard_map/ppermute | solution.py:284
  185.1 7.5 %collective-permute-start.23 = (f32[1,12,16,128]{3,2,1,0:T(8,128)}, f32[1,12,16,128]{3,2,1,0:T(8,128)S(1)}, u32[]{:S(2)}, u32[]{:S(2)}) collective-permute-start(f32[1,12,16,128]{3,2,1,0:T(8,128)} %get-tuple-element.79), channel_id=1, source_target_pairs={{1,0},{2,1},{3,2},{4,3},{5,4},{6,5},{7,6},{0,7},{9,8},{10,9},{11,1... | collective-permute-start | bytes 294920 | tf_op jit(solution)/shard_map/ppermute | solution.py:285
  208.4 10.8 %collective-permute-start.24 = (f32[1,12,64,128]{3,2,1,0:T(8,128)}, f32[1,12,64,128]{3,2,1,0:T(8,128)S(1)}, u32[]{:S(2)}, u32[]{:S(2)}) collective-permute-start(f32[1,12,64,128]{3,2,1,0:T(8,128)} %get-tuple-element.84), channel_id=1, source_target_pairs={{0,8},{8,16},{16,24},{1,9},{9,17},{17,25},{2,10},{10,18},{18,26},{... | collective-permute-start | bytes 1179656 | tf_op jit(solution)/shard_map/ppermute | solution.py:509
  209.7 7.5 %collective-permute-start.25 = (f32[1,12,8,128]{3,2,1,0:T(8,128)}, f32[1,12,8,128]{3,2,1,0:T(8,128)S(1)}, u32[]{:S(2)}, u32[]{:S(2)}) collective-permute-start(f32[1,12,8,128]{3,2,1,0:T(8,128)} %get-tuple-element.85), channel_id=1, source_target_pairs={{0,9},{1,10},{2,11},{3,12},{4,13},{5,14},{6,15},{7,8},{8,17},{9,18... | collective-permute-start | bytes 147464 | tf_op jit(solution)/shard_map/ppermute | solution.py:510
  211.0 8.2 %collective-permute-start.26 = (f32[1,12,8,128]{3,2,1,0:T(8,128)}, f32[1,12,8,128]{3,2,1,0:T(8,128)S(1)}, u32[]{:S(2)}, u32[]{:S(2)}) collective-permute-start(f32[1,12,8,128]{3,2,1,0:T(8,128)} %get-tuple-element.86), channel_id=1, source_target_pairs={{0,15},{1,8},{2,9},{3,10},{4,11},{5,12},{6,13},{7,14},{8,23},{9,16... | collective-permute-start | bytes 147464 | tf_op jit(solution)/shard_map/ppermute | solution.py:511
  224.9 13.1 %collective-permute-start.27 = (f32[1,12,64,128]{3,2,1,0:T(8,128)}, f32[1,12,64,128]{3,2,1,0:T(8,128)S(1)}, u32[]{:S(2)}, u32[]{:S(2)}) collective-permute-start(f32[1,12,64,128]{3,2,1,0:T(8,128)} %get-tuple-element.87), channel_id=1, source_target_pairs={{0,8},{8,16},{16,24},{1,9},{9,17},{17,25},{2,10},{10,18},{18,26},{... | collective-permute-start | bytes 1179656 | tf_op jit(solution)/shard_map/ppermute | solution.py:509
  226.2 9.7 %collective-permute-start.28 = (f32[1,12,8,128]{3,2,1,0:T(8,128)}, f32[1,12,8,128]{3,2,1,0:T(8,128)S(1)}, u32[]{:S(2)}, u32[]{:S(2)}) collective-permute-start(f32[1,12,8,128]{3,2,1,0:T(8,128)} %get-tuple-element.88), channel_id=1, source_target_pairs={{0,9},{1,10},{2,11},{3,12},{4,13},{5,14},{6,15},{7,8},{8,17},{9,18... | collective-permute-start | bytes 147464 | tf_op jit(solution)/shard_map/ppermute | solution.py:510
  228.0 9.9 %collective-permute-start.29 = (f32[1,12,8,128]{3,2,1,0:T(8,128)}, f32[1,12,8,128]{3,2,1,0:T(8,128)S(1)}, u32[]{:S(2)}, u32[]{:S(2)}) collective-permute-start(f32[1,12,8,128]{3,2,1,0:T(8,128)} %get-tuple-element.89), channel_id=1, source_target_pairs={{0,15},{1,8},{2,9},{3,10},{4,11},{5,12},{6,13},{7,14},{8,23},{9,16... | collective-permute-start | bytes 147464 | tf_op jit(solution)/shard_map/ppermute | solution.py:511
  243.4 13.1 %collective-permute-start.30 = (f32[1,12,64,128]{3,2,1,0:T(8,128)}, f32[1,12,64,128]{3,2,1,0:T(8,128)S(1)}, u32[]{:S(2)}, u32[]{:S(2)}) collective-permute-start(f32[1,12,64,128]{3,2,1,0:T(8,128)} %get-tuple-element.90), channel_id=1, source_target_pairs={{0,8},{8,16},{16,24},{1,9},{9,17},{17,25},{2,10},{10,18},{18,26},{... | collective-permute-start | bytes 1179656 | tf_op jit(solution)/shard_map/ppermute | solution.py:509
  244.7 9.7 %collective-permute-start.31 = (f32[1,12,8,128]{3,2,1,0:T(8,128)}, f32[1,12,8,128]{3,2,1,0:T(8,128)S(1)}, u32[]{:S(2)}, u32[]{:S(2)}) collective-permute-start(f32[1,12,8,128]{3,2,1,0:T(8,128)} %get-tuple-element.91), channel_id=1, source_target_pairs={{0,9},{1,10},{2,11},{3,12},{4,13},{5,14},{6,15},{7,8},{8,17},{9,18... | collective-permute-start | bytes 147464 | tf_op jit(solution)/shard_map/ppermute | solution.py:510
  246.0 10.4 %collective-permute-start.32 = (f32[1,12,8,128]{3,2,1,0:T(8,128)}, f32[1,12,8,128]{3,2,1,0:T(8,128)S(1)}, u32[]{:S(2)}, u32[]{:S(2)}) collective-permute-start(f32[1,12,8,128]{3,2,1,0:T(8,128)} %get-tuple-element.92), channel_id=1, source_target_pairs={{0,15},{1,8},{2,9},{3,10},{4,11},{5,12},{6,13},{7,14},{8,23},{9,16... | collective-permute-start | bytes 147464 | tf_op jit(solution)/shard_map/ppermute | solution.py:511
  (38 other events, 134.2 us)

commit v6 on v5

--- a/solution.py
+++ b/solution.py
@@ -144,11 +144,11 @@
                 fields, span, columns)
             yz_ref[b] = tdot(k_ref[...], lanes([v_ref[b, f] for f in range(fields)]))
         for b in range(states):
-            for f in range(fields):
+            def field_body(f, carry):
                 v = v_ref[b, f]
-                cols = slice(f * columns, (f + 1) * columns)
-                t = (cf_ref[0, f] * xd_ref[b, f] + cf_ref[1, f] * yz_ref[b, :span, cols]
-                     + cf_ref[2, f] * yz_ref[b, span:, cols])
+                cols = pl.ds(pl.multiple_of(f * columns, columns), columns)
+                t = (cf_ref[0, f] * xd_ref[b, f] + cf_ref[1, f] * yz_ref[b, pl.ds(0, span), cols]
+                     + cf_ref[2, f] * yz_ref[b, pl.ds(span, span), cols])
                 before_x = pltpu.roll(v, 1, 1)
                 after_x = pltpu.roll(v, columns - 1, 1)
                 t = t + jnp.where(x_first, cf_ref[3, f] * (before_x - v), 0.0)
@@ -174,6 +174,9 @@
                     out_ref[b, f, pl.ds(span - rows, rows), :] + cf_ref[8, f] * next_ref[b, f]
                 )
                 s_ref[b, f] = jnp.tanh(v)
+                return carry
+
+            lax.fori_loop(0, fields, field_body, 0)
 
     pl.run_scoped(scoped, pltpu.VMEM((states, fields, span, columns), f32),
                   pltpu.VMEM((states, 2 * span, fields * columns), f32))

time: 266 us -> 285 us (1.071)
  Pallas kernels: 97 us -> 116 us
    pallas_call x18, Pallas kernels: 97 us -> 116 us  [call(): pl.pallas_call(kernel, out_shape=outs, in_specs=[smem() if k else vmem()...]
  transfers between devices with their start and end apart: 33 -> 33, of which waited for: 16 -> 16; matrix products, arithmetic and copies ran while one was open for 2% -> 2% of each run, Pallas kernels for 7% -> 8%
where the time goes in v6:
time: 285 us; the launch traced here: 284 us
  Pallas kernels  116 us (41%)
  starting transfers between devices  102 us (36%)
  waiting for transfers between devices  42.5 us (15%)
  local copies, waits for them, and re-layouts  19.3 us (7%)
    pallas_call x18, Pallas kernels, call(): pl.pallas_call(kernel, out_shape=outs, in_specs=[smem() if k else vmem()...  116 us
    ppermute x6, starting transfers between devices, per_device(): lax.ppermute(head, both, next_pairs)  36.8 us
    ppermute x7, starting transfers between devices, swap(): lax.ppermute(head, 'space', [((i + 1) % space_n, i) for i in range(space_...  26.5 us
    ppermute x7, waiting for transfers between devices, swap(): lax.ppermute(tail, 'space', [(i, (i + 1) % space_n) for i in range(space_...  25.1 us
    ppermute x6, starting transfers between devices, per_device(): begin = lax.ppermute(finish, 'tm', hop_pairs)  19.2 us
    unnamed x75, local copies, waits for them, and re-layouts  13.2 us
    ppermute x6, starting transfers between devices, per_device(): lax.ppermute(tail, both, prev_pairs)  12.3 us
    ppermute x6, waiting for transfers between devices, per_device(): lax.ppermute(head, both, next_pairs)  10.9 us
  transfers between devices with their start and end apart: 33, of which 16 were waited for; matrix products, arithmetic and copies ran while one was open for 2% of the time, Pallas kernels for 8%

profile of v6, /device:TPU:0, one launch (start us, length us, event | category | flops | bytes accessed | tf_op | source)
XLA Modules:
  0.0 284.0 jit_solution(16320484443976931039)
XLA Ops:
  14.7 7.5 %collective-permute-done.p_ref = f32[3,12,16,128]{3,2,1,0:T(8,128)} collective-permute-done((f32[3,12,16,128]{3,2,1,0:T(8,128)}, f32[3,12,16,128]{3,2,1,0:T(8,128)}, u32[]{:S(2)}, u32[]{:S(2)}) %collective-permute-start) | collective-permute-done | bytes 294944 | tf_op jit(solution)/shard_map/ppermute | solution.py:287
  24.2 13.4 %shard_map.131 = (f32[3,12,128,128]{3,2,1,0:T(8,128)}, f32[1,12,128,128]{3,2,1,0:T(8,128)}, f32[1,12,16,128]{3,2,1,0:T(8,128)}, f32[1,12,16,128]{3,2,1,0:T(8,128)}) custom-call(f32[3,12,128,128]{3,2,1,0:T(8,128)} %pad_maximum_fusion.u_ref, f32[3,12,16,128]{3,2,1,0:T(8,128)} %collective-permute-done.p_ref, f32[3,12,16,128]{3,2,1,0:T(8,128)} %collective-permute-done.1.n_ref, ...), custom_call_target="tpu_custom_call" | custom-call | flops 1822556160 | bytes 6488916 | tf_op jit(solution)/shard_map/pallas_call | solution.py:220
  38.1 4.2 %collective-permute-start.3 = (f32[1,12,16,128]{3,2,1,0:T(8,128)}, f32[1,12,16,128]{3,2,1,0:T(8,128)S(1)}, u32[]{:S(2)}, u32[]{:S(2)}) collective-permute-start(f32[1,12,16,128]{3,2,1,0:T(8,128)} %get-tuple-element.50), channel_id=1, source_target_pairs={{1,0},{2,1},{3,2},{4,3},{5,4},{6,5},{7,6},{0,7},{9,8},{10,9},{11,1... | collective-permute-start | bytes 294920 | tf_op jit(solution)/shard_map/ppermute | solution.py:288
  46.3 7.0 %shard_map.132 = (f32[1,12,128,128]{3,2,1,0:T(8,128)}, f32[1,12,128,128]{3,2,1,0:T(8,128)}, f32[1,12,16,128]{3,2,1,0:T(8,128)}, f32[1,12,16,128]{3,2,1,0:T(8,128)}) custom-call(f32[1,12,128,128]{3,2,1,0:T(8,128)} %get-tuple-element.48.a1_ref, f32[1,12,16,128]{3,2,1,0:T(8,128)} %copy-done.14, f32[1,12,16,128]{3,2,1,0:T(8,128)} %copy-done.16, ...), custom_call_target="tpu_custom_call" | custom-call | flops 607518720 | bytes 5309268 | tf_op jit(solution)/shard_map/pallas_call | solution.py:220
  53.9 4.1 %collective-permute-start.5 = (f32[1,12,16,128]{3,2,1,0:T(8,128)}, f32[1,12,16,128]{3,2,1,0:T(8,128)S(1)}, u32[]{:S(2)}, u32[]{:S(2)}) collective-permute-start(f32[1,12,16,128]{3,2,1,0:T(8,128)} %get-tuple-element.54), channel_id=1, source_target_pairs={{1,0},{2,1},{3,2},{4,3},{5,4},{6,5},{7,6},{0,7},{9,8},{10,9},{11,1... | collective-permute-start | bytes 294920 | tf_op jit(solution)/shard_map/ppermute | solution.py:288
  62.0 8.5 %shard_map.133 = (f32[12,64,128]{2,1,0:T(8,128)}, f32[12,64,128]{2,1,0:T(8,128)}, f32[12,64,128]{2,1,0:T(8,128)}) custom-call(f32[1,12,128,128]{3,2,1,0:T(8,128)} %get-tuple-element.52.a2_ref, f32[1,12,16,128]{3,2,1,0:T(8,128)} %copy-done.18, f32[1,12,16,128]{3,2,1,0:T(8,128)} %copy-done.19, f32[256,128]{1,0:T(8,128)} %constant.28.clone.l_ref, ...), custom_call_target="tpu_custom_call" | custom-call | flops 607518720 | bytes 7897940 | tf_op jit(solution)/shard_map/pallas_call | solution.py:220
  70.6 4.6 %shard_map.134.base_ref = f32[1,12,64,128]{3,2,1,0:T(8,128)} custom-call(f32[1,12,64,128]{3,2,1,0:T(8,128)} %bitcast.70, f32[3,12,16,128]{3,2,1,0:T(8,128)} %collective-permute-done.p_ref, f32[3,12,16,128]{3,2,1,0:T(8,128)} %collective-permute-done.1.n_ref, f32[8,16]{1,0:T(8,128)} %constant.32.clone.r_ref, f32[128,64]{1,0:T(8,128)} %constant.29.clone.l_ref, ...), custom_call_target="tpu_custom_call" | custom-call | flops 228261888 | bytes 1475924 | tf_op jit(solution)/shard_map/pallas_call | solution.py:220
  75.9 5.0 %shard_map.135 = (f32[1,12,64,128]{3,2,1,0:T(8,128)}, f32[1,12,64,128]{3,2,1,0:T(8,128)}, f32[1,12,8,128]{3,2,1,0:T(8,128)}, f32[1,12,8,128]{3,2,1,0:T(8,128)}, ...) custom-call(s32[1]{0:T(128)} %constant.11.clone.1.lead_ref, f32[1,12,64,128]{3,2,1,0:T(8,128)} %bitcast.27, ...), custom_call_target="tpu_custom_call" | custom-call | flops 228261888 | bytes 2851672 | tf_op jit(solution)/shard_map/pallas_call | solution.py:220
  82.5 7.6 %collective-permute-start.10 = (f32[1,12,8,128]{3,2,1,0:T(8,128)}, f32[1,12,8,128]{3,2,1,0:T(8,128)S(1)}, u32[]{:S(2)}, u32[]{:S(2)}) collective-permute-start(f32[1,12,8,128]{3,2,1,0:T(8,128)} %get-tuple-element.61), channel_id=1, source_target_pairs={{0,15},{1,8},{2,9},{3,10},{4,11},{5,12},{6,13},{7,14},{8,23},{9,16... | collective-permute-start | bytes 147464 | tf_op jit(solution)/shard_map/ppermute | solution.py:514
  94.2 5.0 %shard_map.136 = (f32[1,12,64,128]{3,2,1,0:T(8,128)}, f32[1,12,64,128]{3,2,1,0:T(8,128)}, f32[1,12,8,128]{3,2,1,0:T(8,128)}, f32[1,12,8,128]{3,2,1,0:T(8,128)}, ...) custom-call(s32[1]{0:T(128)} %bitcast.3.lead_ref, f32[1,12,64,128]{3,2,1,0:T(8,128)} %copy-done.8, ...), custom_call_target="tpu_custom_call" | custom-call | flops 228261888 | bytes 2851672 | tf_op jit(solution)/shard_map/pallas_call | solution.py:220
  99.1 6.7 %collective-permute-start.11 = (f32[1,12,64,128]{3,2,1,0:T(8,128)}, f32[1,12,64,128]{3,2,1,0:T(8,128)S(1)}, u32[]{:S(2)}, u32[]{:S(2)}) collective-permute-start(f32[1,12,64,128]{3,2,1,0:T(8,128)} %get-tuple-element.62), channel_id=1, source_target_pairs={{0,8},{8,16},{16,24},{1,9},{9,17},{17,25},{2,10},{10,18},{18,26},{... | collective-permute-start | bytes 1179656 | tf_op jit(solution)/shard_map/ppermute | solution.py:512
  109.2 4.2 %collective-permute-start.13 = (f32[1,12,8,128]{3,2,1,0:T(8,128)}, f32[1,12,8,128]{3,2,1,0:T(8,128)S(1)}, u32[]{:S(2)}, u32[]{:S(2)}) collective-permute-start(f32[1,12,8,128]{3,2,1,0:T(8,128)} %get-tuple-element.64), channel_id=1, source_target_pairs={{0,15},{1,8},{2,9},{3,10},{4,11},{5,12},{6,13},{7,14},{8,23},{9,16... | collective-permute-start | bytes 147464 | tf_op jit(solution)/shard_map/ppermute | solution.py:514
  116.8 5.2 %shard_map.137 = (f32[1,12,64,128]{3,2,1,0:T(8,128)}, f32[1,12,64,128]{3,2,1,0:T(8,128)}, f32[1,12,8,128]{3,2,1,0:T(8,128)}, f32[1,12,8,128]{3,2,1,0:T(8,128)}, ...) custom-call(s32[1]{0:T(128)} %bitcast.3.lead_ref, f32[1,12,64,128]{3,2,1,0:T(8,128)} %copy-done.7, ...), custom_call_target="tpu_custom_call" | custom-call | flops 228261888 | bytes 2851672 | tf_op jit(solution)/shard_map/pallas_call | solution.py:220
  122.0 6.9 %collective-permute-start.14 = (f32[1,12,64,128]{3,2,1,0:T(8,128)}, f32[1,12,64,128]{3,2,1,0:T(8,128)S(1)}, u32[]{:S(2)}, u32[]{:S(2)}) collective-permute-start(f32[1,12,64,128]{3,2,1,0:T(8,128)} %get-tuple-element.65), channel_id=1, source_target_pairs={{0,8},{8,16},{16,24},{1,9},{9,17},{17,25},{2,10},{10,18},{18,26},{... | collective-permute-start | bytes 1179656 | tf_op jit(solution)/shard_map/ppermute | solution.py:512
  128.9 5.3 %collective-permute-start.15 = (f32[1,12,8,128]{3,2,1,0:T(8,128)}, f32[1,12,8,128]{3,2,1,0:T(8,128)S(1)}, u32[]{:S(2)}, u32[]{:S(2)}) collective-permute-start(f32[1,12,8,128]{3,2,1,0:T(8,128)} %get-tuple-element.66), channel_id=1, source_target_pairs={{0,9},{1,10},{2,11},{3,12},{4,13},{5,14},{6,15},{7,8},{8,17},{9,18... | collective-permute-start | bytes 147464 | tf_op jit(solution)/shard_map/ppermute | solution.py:513
  140.4 5.0 %shard_map.138 = (f32[1,12,64,128]{3,2,1,0:T(8,128)}, f32[1,12,64,128]{3,2,1,0:T(8,128)}, f32[1,12,8,128]{3,2,1,0:T(8,128)}, f32[1,12,8,128]{3,2,1,0:T(8,128)}, ...) custom-call(s32[1]{0:T(128)} %bitcast.3.lead_ref, f32[1,12,64,128]{3,2,1,0:T(8,128)} %copy-done.9, ...), custom_call_target="tpu_custom_call" | custom-call | flops 228261888 | bytes 2851672 | tf_op jit(solution)/shard_map/pallas_call | solution.py:220
  146.3 6.3 %shard_map.139 = (f32[3,12,128,128]{3,2,1,0:T(8,128)}, f32[3,12,16,128]{3,2,1,0:T(8,128)}, f32[3,12,16,128]{3,2,1,0:T(8,128)}) custom-call(f32[1,12,128,128]{3,2,1,0:T(8,128)} %get-tuple-element.48.a1_ref, f32[1,12,128,128]{3,2,1,0:T(8,128)} %get-tuple-element.52.a2_ref, f32[12,64,128]{2,1,0:T(8,128)} %get-tuple-element.56.c0_ref, ...), custom_call_target="tpu_custom_call" | custom-call | flops 603979776 | bytes 7733252 | tf_op jit(solution)/shard_map/pallas_call | solution.py:220
  153.1 4.1 %collective-permute-start.19 = (f32[3,12,16,128]{3,2,1,0:T(8,128)}, f32[3,12,16,128]{3,2,1,0:T(8,128)S(1)}, u32[]{:S(2)}, u32[]{:S(2)}) collective-permute-start(f32[3,12,16,128]{3,2,1,0:T(8,128)} %get-tuple-element.72), channel_id=1, source_target_pairs={{1,0},{2,1},{3,2},{4,3},{5,4},{6,5},{7,6},{0,7},{9,8},{10,9},{11,1... | collective-permute-start | bytes 884744 | tf_op jit(solution)/shard_map/ppermute | solution.py:288
  157.3 9.5 %collective-permute-done.18.p_ref = f32[3,12,16,128]{3,2,1,0:T(8,128)S(1)} collective-permute-done((f32[3,12,16,128]{3,2,1,0:T(8,128)}, f32[3,12,16,128]{3,2,1,0:T(8,128)S(1)}, u32[]{:S(2)}, u32[]{:S(2)}) %collective-permute-start.18) | collective-permute-done | bytes 294944 | tf_op jit(solution)/shard_map/ppermute | solution.py:287
  170.1 13.4 %shard_map.140 = (f32[3,12,128,128]{3,2,1,0:T(8,128)}, f32[1,12,128,128]{3,2,1,0:T(8,128)}, f32[1,12,16,128]{3,2,1,0:T(8,128)}, f32[1,12,16,128]{3,2,1,0:T(8,128)}) custom-call(f32[3,12,128,128]{3,2,1,0:T(8,128)} %get-tuple-element.70.u_ref, f32[3,12,16,128]{3,2,1,0:T(8,128)} %copy-done.12, f32[3,12,16,128]{3,2,1,0:T(8,128)} %copy-done.13, ...), custom_call_target="tpu_custom_call" | custom-call | flops 1822556160 | bytes 6488916 | tf_op jit(solution)/shard_map/pallas_call | solution.py:220
  183.5 4.7 %collective-permute-start.21 = (f32[1,12,16,128]{3,2,1,0:T(8,128)}, f32[1,12,16,128]{3,2,1,0:T(8,128)S(1)}, u32[]{:S(2)}, u32[]{:S(2)}) collective-permute-start(f32[1,12,16,128]{3,2,1,0:T(8,128)} %get-tuple-element.75), channel_id=1, source_target_pairs={{1,0},{2,1},{3,2},{4,3},{5,4},{6,5},{7,6},{0,7},{9,8},{10,9},{11,1... | collective-permute-start | bytes 294920 | tf_op jit(solution)/shard_map/ppermute | solution.py:288
  191.8 7.0 %shard_map.141 = (f32[1,12,128,128]{3,2,1,0:T(8,128)}, f32[1,12,128,128]{3,2,1,0:T(8,128)}, f32[1,12,16,128]{3,2,1,0:T(8,128)}, f32[1,12,16,128]{3,2,1,0:T(8,128)}) custom-call(f32[1,12,128,128]{3,2,1,0:T(8,128)} %get-tuple-element.73.a1_ref, f32[1,12,16,128]{3,2,1,0:T(8,128)} %copy-done.15, f32[1,12,16,128]{3,2,1,0:T(8,128)} %copy-done.17, ...), custom_call_target="tpu_custom_call" | custom-call | flops 607518720 | bytes 5309268 | tf_op jit(solution)/shard_map/pallas_call | solution.py:220
  198.8 4.7 %collective-permute-start.23 = (f32[1,12,16,128]{3,2,1,0:T(8,128)}, f32[1,12,16,128]{3,2,1,0:T(8,128)S(1)}, u32[]{:S(2)}, u32[]{:S(2)}) collective-permute-start(f32[1,12,16,128]{3,2,1,0:T(8,128)} %get-tuple-element.79), channel_id=1, source_target_pairs={{1,0},{2,1},{3,2},{4,3},{5,4},{6,5},{7,6},{0,7},{9,8},{10,9},{11,1... | collective-permute-start | bytes 294920 | tf_op jit(solution)/shard_map/ppermute | solution.py:288
  207.0 8.5 %shard_map.142 = (f32[12,64,128]{2,1,0:T(8,128)}, f32[12,64,128]{2,1,0:T(8,128)}, f32[12,64,128]{2,1,0:T(8,128)}) custom-call(f32[1,12,128,128]{3,2,1,0:T(8,128)} %get-tuple-element.77.a2_ref, f32[1,12,16,128]{3,2,1,0:T(8,128)} %copy-done.20, f32[1,12,16,128]{3,2,1,0:T(8,128)} %copy-done.21, f32[256,128]{1,0:T(8,128)} %constant.28.clone.l_ref, ...), custom_call_target="tpu_custom_call" | custom-call | flops 607518720 | bytes 7897940 | tf_op jit(solution)/shard_map/pallas_call | solution.py:220
  215.5 4.5 %shard_map.143.base_ref = f32[1,12,64,128]{3,2,1,0:T(8,128)} custom-call(f32[1,12,64,128]{3,2,1,0:T(8,128)} %bitcast.76, f32[3,12,16,128]{3,2,1,0:T(8,128)} %copy-done.12, f32[3,12,16,128]{3,2,1,0:T(8,128)} %copy-done.13, f32[8,16]{1,0:T(8,128)} %constant.32.clone.r_ref, f32[128,64]{1,0:T(8,128)} %constant.29.clone.l_ref, f32[128,128]{1,0:T(8,128)} %constant.27.clone.x_ref, ...), custom_call_target="tpu_custom_call" | custom-call | flops 228261888 | bytes 1475924 | tf_op jit(solution)/shard_map/pallas_call | solution.py:220
  220.1 5.2 %shard_map.144 = (f32[1,12,64,128]{3,2,1,0:T(8,128)}, f32[1,12,64,128]{3,2,1,0:T(8,128)}, f32[1,12,8,128]{3,2,1,0:T(8,128)}, f32[1,12,8,128]{3,2,1,0:T(8,128)}, ...) custom-call(s32[1]{0:T(128)} %constant.11.clone.1.lead_ref, f32[1,12,64,128]{3,2,1,0:T(8,128)} %bitcast.32, ...), custom_call_target="tpu_custom_call" | custom-call | flops 228261888 | bytes 2851672 | tf_op jit(solution)/shard_map/pallas_call | solution.py:220
  227.9 5.9 %collective-permute-start.26 = (f32[1,12,8,128]{3,2,1,0:T(8,128)}, f32[1,12,8,128]{3,2,1,0:T(8,128)S(1)}, u32[]{:S(2)}, u32[]{:S(2)}) collective-permute-start(f32[1,12,8,128]{3,2,1,0:T(8,128)} %get-tuple-element.86), channel_id=1, source_target_pairs={{0,15},{1,8},{2,9},{3,10},{4,11},{5,12},{6,13},{7,14},{8,23},{9,16... | collective-permute-start | bytes 147464 | tf_op jit(solution)/shard_map/ppermute | solution.py:514
  237.2 5.0 %shard_map.145 = (f32[1,12,64,128]{3,2,1,0:T(8,128)}, f32[1,12,64,128]{3,2,1,0:T(8,128)}, f32[1,12,8,128]{3,2,1,0:T(8,128)}, f32[1,12,8,128]{3,2,1,0:T(8,128)}, ...) custom-call(s32[1]{0:T(128)} %bitcast.3.lead_ref, f32[1,12,64,128]{3,2,1,0:T(8,128)} %copy-done.10, ...), custom_call_target="tpu_custom_call" | custom-call | flops 228261888 | bytes 2851672 | tf_op jit(solution)/shard_map/pallas_call | solution.py:220
  245.4 7.9 %collective-permute-start.29 = (f32[1,12,8,128]{3,2,1,0:T(8,128)}, f32[1,12,8,128]{3,2,1,0:T(8,128)S(1)}, u32[]{:S(2)}, u32[]{:S(2)}) collective-permute-start(f32[1,12,8,128]{3,2,1,0:T(8,128)} %get-tuple-element.89), channel_id=1, source_target_pairs={{0,15},{1,8},{2,9},{3,10},{4,11},{5,12},{6,13},{7,14},{8,23},{9,16... | collective-permute-start | bytes 147464 | tf_op jit(solution)/shard_map/ppermute | solution.py:514
  256.7 5.0 %shard_map.146 = (f32[1,12,64,128]{3,2,1,0:T(8,128)}, f32[1,12,64,128]{3,2,1,0:T(8,128)}, f32[1,12,8,128]{3,2,1,0:T(8,128)}, f32[1,12,8,128]{3,2,1,0:T(8,128)}, ...) custom-call(s32[1]{0:T(128)} %bitcast.3.lead_ref, f32[1,12,64,128]{3,2,1,0:T(8,128)} %copy-done.11, ...), custom_call_target="tpu_custom_call" | custom-call | flops 228261888 | bytes 2851672 | tf_op jit(solution)/shard_map/pallas_call | solution.py:220
  264.3 8.4 %collective-permute-start.32 = (f32[1,12,8,128]{3,2,1,0:T(8,128)}, f32[1,12,8,128]{3,2,1,0:T(8,128)S(1)}, u32[]{:S(2)}, u32[]{:S(2)}) collective-permute-start(f32[1,12,8,128]{3,2,1,0:T(8,128)} %get-tuple-element.92), channel_id=1, source_target_pairs={{0,15},{1,8},{2,9},{3,10},{4,11},{5,12},{6,13},{7,14},{8,23},{9,16... | collective-permute-start | bytes 147464 | tf_op jit(solution)/shard_map/ppermute | solution.py:514
  276.1 4.9 %shard_map.147 = (f32[1,12,64,128]{3,2,1,0:T(8,128)}, f32[1,12,64,128]{3,2,1,0:T(8,128)}, f32[1,12,8,128]{3,2,1,0:T(8,128)}, f32[1,12,8,128]{3,2,1,0:T(8,128)}, ...) custom-call(s32[1]{0:T(128)} %bitcast.3.lead_ref, f32[1,12,64,128]{3,2,1,0:T(8,128)} %copy-done.6, ...), custom_call_target="tpu_custom_call" | custom-call | flops 228261888 | bytes 2851672 | tf_op jit(solution)/shard_map/pallas_call | solution.py:220
  (138 shorter events, 77.7 us)
Async XLA Ops:
  5.2 17.0 %collective-permute-start = (f32[3,12,16,128]{3,2,1,0:T(8,128)}, f32[3,12,16,128]{3,2,1,0:T(8,128)}, u32[]{:S(2)}, u32[]{:S(2)}) collective-permute-start(f32[3,12,16,128]{3,2,1,0:T(8,128)} %get-tuple-element.95), channel_id=1, source_target_pairs={{0,1},{1,2},{2,3},{3,4},{4,5},{5,6},{6,7},{7,0},{8,9},{9,10},{10,1... | collective-permute-start | bytes 884744 | tf_op jit(solution)/shard_map/ppermute | solution.py:287
  8.2 16.0 %collective-permute-start.1 = (f32[3,12,16,128]{3,2,1,0:T(8,128)S(1)}, f32[3,12,16,128]{3,2,1,0:T(8,128)}, u32[]{:S(2)}, u32[]{:S(2)}) collective-permute-start(f32[3,12,16,128]{3,2,1,0:T(8,128)S(1)} %get-tuple-element.94), channel_id=1, source_target_pairs={{1,0},{2,1},{3,2},{4,3},{5,4},{6,5},{7,6},{0,7},{9,8},{10,9},{11,1... | collective-permute-start | bytes 884744 | tf_op jit(solution)/shard_map/ppermute | solution.py:288
  37.6 7.6 %collective-permute-start.2 = (f32[1,12,16,128]{3,2,1,0:T(8,128)}, f32[1,12,16,128]{3,2,1,0:T(8,128)S(1)}, u32[]{:S(2)}, u32[]{:S(2)}) collective-permute-start(f32[1,12,16,128]{3,2,1,0:T(8,128)} %get-tuple-element.49), channel_id=1, source_target_pairs={{0,1},{1,2},{2,3},{3,4},{4,5},{5,6},{6,7},{7,0},{8,9},{9,10},{10,1... | collective-permute-start | bytes 294920 | tf_op jit(solution)/shard_map/ppermute | solution.py:287
  38.1 7.5 %collective-permute-start.3 = (f32[1,12,16,128]{3,2,1,0:T(8,128)}, f32[1,12,16,128]{3,2,1,0:T(8,128)S(1)}, u32[]{:S(2)}, u32[]{:S(2)}) collective-permute-start(f32[1,12,16,128]{3,2,1,0:T(8,128)} %get-tuple-element.50), channel_id=1, source_target_pairs={{1,0},{2,1},{3,2},{4,3},{5,4},{6,5},{7,6},{0,7},{9,8},{10,9},{11,1... | collective-permute-start | bytes 294920 | tf_op jit(solution)/shard_map/ppermute | solution.py:288
  53.2 8.0 %collective-permute-start.4 = (f32[1,12,16,128]{3,2,1,0:T(8,128)}, f32[1,12,16,128]{3,2,1,0:T(8,128)S(1)}, u32[]{:S(2)}, u32[]{:S(2)}) collective-permute-start(f32[1,12,16,128]{3,2,1,0:T(8,128)} %get-tuple-element.53), channel_id=1, source_target_pairs={{0,1},{1,2},{2,3},{3,4},{4,5},{5,6},{6,7},{7,0},{8,9},{9,10},{10,1... | collective-permute-start | bytes 294920 | tf_op jit(solution)/shard_map/ppermute | solution.py:287
  53.9 7.5 %collective-permute-start.5 = (f32[1,12,16,128]{3,2,1,0:T(8,128)}, f32[1,12,16,128]{3,2,1,0:T(8,128)S(1)}, u32[]{:S(2)}, u32[]{:S(2)}) collective-permute-start(f32[1,12,16,128]{3,2,1,0:T(8,128)} %get-tuple-element.54), channel_id=1, source_target_pairs={{1,0},{2,1},{3,2},{4,3},{5,4},{6,5},{7,6},{0,7},{9,8},{10,9},{11,1... | collective-permute-start | bytes 294920 | tf_op jit(solution)/shard_map/ppermute | solution.py:288
  58.0 17.2 %collective-permute-start.7 = (f32[12,8,128]{2,1,0:T(8,128)S(1)}, f32[12,8,128]{2,1,0:T(8,128)S(1)}, u32[]{:S(2)}, u32[]{:S(2)}) collective-permute-start(f32[12,8,128]{2,1,0:T(8,128)S(1)} %get-tuple-element.96), channel_id=1, source_target_pairs={{1,0},{2,1},{3,2},{4,3},{5,4},{6,5},{7,6},{0,7},{9,8},{10,9},{11,1... | collective-permute-start | bytes 147464 | tf_op jit(solution)/shard_map/ppermute | solution.py:288
  59.6 15.6 %collective-permute-start.6 = (f32[12,8,128]{2,1,0:T(8,128)S(1)}, f32[12,8,128]{2,1,0:T(8,128)S(1)}, u32[]{:S(2)}, u32[]{:S(2)}) collective-permute-start(f32[12,8,128]{2,1,0:T(8,128)S(1)} %get-tuple-element.97), channel_id=1, source_target_pairs={{0,1},{1,2},{2,3},{3,4},{4,5},{5,6},{6,7},{7,0},{8,9},{9,10},{10,1... | collective-permute-start | bytes 147464 | tf_op jit(solution)/shard_map/ppermute | solution.py:287
  80.9 12.5 %collective-permute-start.8 = (f32[1,12,64,128]{3,2,1,0:T(8,128)}, f32[1,12,64,128]{3,2,1,0:T(8,128)S(1)}, u32[]{:S(2)}, u32[]{:S(2)}) collective-permute-start(f32[1,12,64,128]{3,2,1,0:T(8,128)} %get-tuple-element.59), channel_id=1, source_target_pairs={{0,8},{8,16},{16,24},{1,9},{9,17},{17,25},{2,10},{10,18},{18,26},{... | collective-permute-start | bytes 1179656 | tf_op jit(solution)/shard_map/ppermute | solution.py:512
  82.5 9.6 %collective-permute-start.10 = (f32[1,12,8,128]{3,2,1,0:T(8,128)}, f32[1,12,8,128]{3,2,1,0:T(8,128)S(1)}, u32[]{:S(2)}, u32[]{:S(2)}) collective-permute-start(f32[1,12,8,128]{3,2,1,0:T(8,128)} %get-tuple-element.61), channel_id=1, source_target_pairs={{0,15},{1,8},{2,9},{3,10},{4,11},{5,12},{6,13},{7,14},{8,23},{9,16... | collective-permute-start | bytes 147464 | tf_op jit(solution)/shard_map/ppermute | solution.py:514
  99.1 16.3 %collective-permute-start.11 = (f32[1,12,64,128]{3,2,1,0:T(8,128)}, f32[1,12,64,128]{3,2,1,0:T(8,128)S(1)}, u32[]{:S(2)}, u32[]{:S(2)}) collective-permute-start(f32[1,12,64,128]{3,2,1,0:T(8,128)} %get-tuple-element.62), channel_id=1, source_target_pairs={{0,8},{8,16},{16,24},{1,9},{9,17},{17,25},{2,10},{10,18},{18,26},{... | collective-permute-start | bytes 1179656 | tf_op jit(solution)/shard_map/ppermute | solution.py:512
  105.9 39.5 %collective-permute-start.17 = (f32[1,12,128,128]{3,2,1,0:T(8,128)S(1)}, f32[1,12,128,128]{3,2,1,0:T(8,128)S(1)}, u32[]{:S(2)}, u32[]{:S(2)}) collective-permute-start(f32[1,12,128,128]{3,2,1,0:T(8,128)S(1)} %copy-done.4), channel_id=1, source_target_pairs={{0,8},{8,16},{16,24},{1,9},{9,17},{17,25},{2,10},{10,18},{18,26},{... | collective-permute-start | bytes 2359304 | tf_op jit(solution)/shard_map/ppermute | solution.py:505
  107.9 5.5 %collective-permute-start.12 = (f32[1,12,8,128]{3,2,1,0:T(8,128)}, f32[1,12,8,128]{3,2,1,0:T(8,128)S(1)}, u32[]{:S(2)}, u32[]{:S(2)}) collective-permute-start(f32[1,12,8,128]{3,2,1,0:T(8,128)} %get-tuple-element.63), channel_id=1, source_target_pairs={{0,9},{1,10},{2,11},{3,12},{4,13},{5,14},{6,15},{7,8},{8,17},{9,18... | collective-permute-start | bytes 147464 | tf_op jit(solution)/shard_map/ppermute | solution.py:513
  109.2 6.3 %collective-permute-start.13 = (f32[1,12,8,128]{3,2,1,0:T(8,128)}, f32[1,12,8,128]{3,2,1,0:T(8,128)S(1)}, u32[]{:S(2)}, u32[]{:S(2)}) collective-permute-start(f32[1,12,8,128]{3,2,1,0:T(8,128)} %get-tuple-element.64), channel_id=1, source_target_pairs={{0,15},{1,8},{2,9},{3,10},{4,11},{5,12},{6,13},{7,14},{8,23},{9,16... | collective-permute-start | bytes 147464 | tf_op jit(solution)/shard_map/ppermute | solution.py:514
  122.0 17.1 %collective-permute-start.14 = (f32[1,12,64,128]{3,2,1,0:T(8,128)}, f32[1,12,64,128]{3,2,1,0:T(8,128)S(1)}, u32[]{:S(2)}, u32[]{:S(2)}) collective-permute-start(f32[1,12,64,128]{3,2,1,0:T(8,128)} %get-tuple-element.65), channel_id=1, source_target_pairs={{0,8},{8,16},{16,24},{1,9},{9,17},{17,25},{2,10},{10,18},{18,26},{... | collective-permute-start | bytes 1179656 | tf_op jit(solution)/shard_map/ppermute | solution.py:512
  128.9 8.1 %collective-permute-start.15 = (f32[1,12,8,128]{3,2,1,0:T(8,128)}, f32[1,12,8,128]{3,2,1,0:T(8,128)S(1)}, u32[]{:S(2)}, u32[]{:S(2)}) collective-permute-start(f32[1,12,8,128]{3,2,1,0:T(8,128)} %get-tuple-element.66), channel_id=1, source_target_pairs={{0,9},{1,10},{2,11},{3,12},{4,13},{5,14},{6,15},{7,8},{8,17},{9,18... | collective-permute-start | bytes 147464 | tf_op jit(solution)/shard_map/ppermute | solution.py:513
  134.2 4.8 %collective-permute-start.16 = (f32[1,12,8,128]{3,2,1,0:T(8,128)}, f32[1,12,8,128]{3,2,1,0:T(8,128)S(1)}, u32[]{:S(2)}, u32[]{:S(2)}) collective-permute-start(f32[1,12,8,128]{3,2,1,0:T(8,128)} %get-tuple-element.67), channel_id=1, source_target_pairs={{0,15},{1,8},{2,9},{3,10},{4,11},{5,12},{6,13},{7,14},{8,23},{9,16... | collective-permute-start | bytes 147464 | tf_op jit(solution)/shard_map/ppermute | solution.py:514
  152.5 14.2 %collective-permute-start.18 = (f32[3,12,16,128]{3,2,1,0:T(8,128)}, f32[3,12,16,128]{3,2,1,0:T(8,128)S(1)}, u32[]{:S(2)}, u32[]{:S(2)}) collective-permute-start(f32[3,12,16,128]{3,2,1,0:T(8,128)} %get-tuple-element.71), channel_id=1, source_target_pairs={{0,1},{1,2},{2,3},{3,4},{4,5},{5,6},{6,7},{7,0},{8,9},{9,10},{10,1... | collective-permute-start | bytes 884744 | tf_op jit(solution)/shard_map/ppermute | solution.py:287
  153.1 16.2 %collective-permute-start.19 = (f32[3,12,16,128]{3,2,1,0:T(8,128)}, f32[3,12,16,128]{3,2,1,0:T(8,128)S(1)}, u32[]{:S(2)}, u32[]{:S(2)}) collective-permute-start(f32[3,12,16,128]{3,2,1,0:T(8,128)} %get-tuple-element.72), channel_id=1, source_target_pairs={{1,0},{2,1},{3,2},{4,3},{5,4},{6,5},{7,6},{0,7},{9,8},{10,9},{11,1... | collective-permute-start | bytes 884744 | tf_op jit(solution)/shard_map/ppermute | solution.py:288
  183.5 7.7 %collective-permute-start.20 = (f32[1,12,16,128]{3,2,1,0:T(8,128)}, f32[1,12,16,128]{3,2,1,0:T(8,128)S(1)}, u32[]{:S(2)}, u32[]{:S(2)}) collective-permute-start(f32[1,12,16,128]{3,2,1,0:T(8,128)} %get-tuple-element.74), channel_id=1, source_target_pairs={{0,1},{1,2},{2,3},{3,4},{4,5},{5,6},{6,7},{7,0},{8,9},{9,10},{10,1... | collective-permute-start | bytes 294920 | tf_op jit(solution)/shard_map/ppermute | solution.py:287
  183.5 7.7 %collective-permute-start.21 = (f32[1,12,16,128]{3,2,1,0:T(8,128)}, f32[1,12,16,128]{3,2,1,0:T(8,128)S(1)}, u32[]{:S(2)}, u32[]{:S(2)}) collective-permute-start(f32[1,12,16,128]{3,2,1,0:T(8,128)} %get-tuple-element.75), channel_id=1, source_target_pairs={{1,0},{2,1},{3,2},{4,3},{5,4},{6,5},{7,6},{0,7},{9,8},{10,9},{11,1... | collective-permute-start | bytes 294920 | tf_op jit(solution)/shard_map/ppermute | solution.py:288
  198.8 7.5 %collective-permute-start.22 = (f32[1,12,16,128]{3,2,1,0:T(8,128)}, f32[1,12,16,128]{3,2,1,0:T(8,128)S(1)}, u32[]{:S(2)}, u32[]{:S(2)}) collective-permute-start(f32[1,12,16,128]{3,2,1,0:T(8,128)} %get-tuple-element.78), channel_id=1, source_target_pairs={{0,1},{1,2},{2,3},{3,4},{4,5},{5,6},{6,7},{7,0},{8,9},{9,10},{10,1... | collective-permute-start | bytes 294920 | tf_op jit(solution)/shard_map/ppermute | solution.py:287
  198.8 7.5 %collective-permute-start.23 = (f32[1,12,16,128]{3,2,1,0:T(8,128)}, f32[1,12,16,128]{3,2,1,0:T(8,128)S(1)}, u32[]{:S(2)}, u32[]{:S(2)}) collective-permute-start(f32[1,12,16,128]{3,2,1,0:T(8,128)} %get-tuple-element.79), channel_id=1, source_target_pairs={{1,0},{2,1},{3,2},{4,3},{5,4},{6,5},{7,6},{0,7},{9,8},{10,9},{11,1... | collective-permute-start | bytes 294920 | tf_op jit(solution)/shard_map/ppermute | solution.py:288
  225.3 10.6 %collective-permute-start.24 = (f32[1,12,64,128]{3,2,1,0:T(8,128)}, f32[1,12,64,128]{3,2,1,0:T(8,128)S(1)}, u32[]{:S(2)}, u32[]{:S(2)}) collective-permute-start(f32[1,12,64,128]{3,2,1,0:T(8,128)} %get-tuple-element.84), channel_id=1, source_target_pairs={{0,8},{8,16},{16,24},{1,9},{9,17},{17,25},{2,10},{10,18},{18,26},{... | collective-permute-start | bytes 1179656 | tf_op jit(solution)/shard_map/ppermute | solution.py:512
  226.6 7.3 %collective-permute-start.25 = (f32[1,12,8,128]{3,2,1,0:T(8,128)}, f32[1,12,8,128]{3,2,1,0:T(8,128)S(1)}, u32[]{:S(2)}, u32[]{:S(2)}) collective-permute-start(f32[1,12,8,128]{3,2,1,0:T(8,128)} %get-tuple-element.85), channel_id=1, source_target_pairs={{0,9},{1,10},{2,11},{3,12},{4,13},{5,14},{6,15},{7,8},{8,17},{9,18... | collective-permute-start | bytes 147464 | tf_op jit(solution)/shard_map/ppermute | solution.py:513
  227.9 8.0 %collective-permute-start.26 = (f32[1,12,8,128]{3,2,1,0:T(8,128)}, f32[1,12,8,128]{3,2,1,0:T(8,128)S(1)}, u32[]{:S(2)}, u32[]{:S(2)}) collective-permute-start(f32[1,12,8,128]{3,2,1,0:T(8,128)} %get-tuple-element.86), channel_id=1, source_target_pairs={{0,15},{1,8},{2,9},{3,10},{4,11},{5,12},{6,13},{7,14},{8,23},{9,16... | collective-permute-start | bytes 147464 | tf_op jit(solution)/shard_map/ppermute | solution.py:514
  242.2 13.1 %collective-permute-start.27 = (f32[1,12,64,128]{3,2,1,0:T(8,128)}, f32[1,12,64,128]{3,2,1,0:T(8,128)S(1)}, u32[]{:S(2)}, u32[]{:S(2)}) collective-permute-start(f32[1,12,64,128]{3,2,1,0:T(8,128)} %get-tuple-element.87), channel_id=1, source_target_pairs={{0,8},{8,16},{16,24},{1,9},{9,17},{17,25},{2,10},{10,18},{18,26},{... | collective-permute-start | bytes 1179656 | tf_op jit(solution)/shard_map/ppermute | solution.py:512
  243.5 9.7 %collective-permute-start.28 = (f32[1,12,8,128]{3,2,1,0:T(8,128)}, f32[1,12,8,128]{3,2,1,0:T(8,128)S(1)}, u32[]{:S(2)}, u32[]{:S(2)}) collective-permute-start(f32[1,12,8,128]{3,2,1,0:T(8,128)} %get-tuple-element.88), channel_id=1, source_target_pairs={{0,9},{1,10},{2,11},{3,12},{4,13},{5,14},{6,15},{7,8},{8,17},{9,18... | collective-permute-start | bytes 147464 | tf_op jit(solution)/shard_map/ppermute | solution.py:513
  245.4 9.9 %collective-permute-start.29 = (f32[1,12,8,128]{3,2,1,0:T(8,128)}, f32[1,12,8,128]{3,2,1,0:T(8,128)S(1)}, u32[]{:S(2)}, u32[]{:S(2)}) collective-permute-start(f32[1,12,8,128]{3,2,1,0:T(8,128)} %get-tuple-element.89), channel_id=1, source_target_pairs={{0,15},{1,8},{2,9},{3,10},{4,11},{5,12},{6,13},{7,14},{8,23},{9,16... | collective-permute-start | bytes 147464 | tf_op jit(solution)/shard_map/ppermute | solution.py:514
  261.7 13.1 %collective-permute-start.30 = (f32[1,12,64,128]{3,2,1,0:T(8,128)}, f32[1,12,64,128]{3,2,1,0:T(8,128)S(1)}, u32[]{:S(2)}, u32[]{:S(2)}) collective-permute-start(f32[1,12,64,128]{3,2,1,0:T(8,128)} %get-tuple-element.90), channel_id=1, source_target_pairs={{0,8},{8,16},{16,24},{1,9},{9,17},{17,25},{2,10},{10,18},{18,26},{... | collective-permute-start | bytes 1179656 | tf_op jit(solution)/shard_map/ppermute | solution.py:512
  263.0 9.7 %collective-permute-start.31 = (f32[1,12,8,128]{3,2,1,0:T(8,128)}, f32[1,12,8,128]{3,2,1,0:T(8,128)S(1)}, u32[]{:S(2)}, u32[]{:S(2)}) collective-permute-start(f32[1,12,8,128]{3,2,1,0:T(8,128)} %get-tuple-element.91), channel_id=1, source_target_pairs={{0,9},{1,10},{2,11},{3,12},{4,13},{5,14},{6,15},{7,8},{8,17},{9,18... | collective-permute-start | bytes 147464 | tf_op jit(solution)/shard_map/ppermute | solution.py:513
  264.3 10.5 %collective-permute-start.32 = (f32[1,12,8,128]{3,2,1,0:T(8,128)}, f32[1,12,8,128]{3,2,1,0:T(8,128)S(1)}, u32[]{:S(2)}, u32[]{:S(2)}) collective-permute-start(f32[1,12,8,128]{3,2,1,0:T(8,128)} %get-tuple-element.92), channel_id=1, source_target_pairs={{0,15},{1,8},{2,9},{3,10},{4,11},{5,12},{6,13},{7,14},{8,23},{9,16... | collective-permute-start | bytes 147464 | tf_op jit(solution)/shard_map/ppermute | solution.py:514
  (38 other events, 142.0 us)

commit v7 on v5

--- a/solution.py
+++ b/solution.py
@@ -324,7 +324,7 @@
         lax.fori_loop(0, fields, body, 0)
 
     def ending_kernel(a2_ref, p_ref, n_ref, l_ref, x_ref, zc_ref, rx_ref, ra_ref, en_ref,
-                      f_ref, g1_ref, u_ref, r_ref, rint_ref, c1_ref, c0_ref, g2_ref, s_ref):
+                      f_ref, g1_ref, r_ref, rint_ref, c1_ref, g2_ref, s_ref):
         tendency_into(g2_ref, a2_ref, p_ref, n_ref, l_ref, x_ref, zc_ref, rx_ref, ra_ref,
                       en_ref, s_ref, fine_elem)
 
@@ -334,41 +334,28 @@
 
         lax.fori_loop(0, fields, body, 0)
         rm = r_ref[...]
-        for dst, src_ref, lead_index in ((rint_ref, g2_ref, 0), (c1_ref, a2_ref, 0), (c0_ref, u_ref, 0)):
+        for dst, src_ref, lead_index in ((rint_ref, g2_ref, 0), (c1_ref, a2_ref, 0)):
             wide = dot(rm, lanes([src_ref[lead_index, f] for f in range(fields)]))
             for f, part in enumerate(unlanes(wide, columns)):
                 dst[f] = part
 
-    def base_kernel(c_ref, p_ref, n_ref, r_ref, l_ref, x_ref, zc_ref, rx_ref, ra_ref, en_ref,
-                    out_ref, bp_ref, bn_ref, s_ref):
-        rm = r_ref[...]
-        for dst, src_ref in ((bp_ref, p_ref), (bn_ref, n_ref)):
-            wide = dot(rm, lanes([src_ref[0, f] for f in range(fields)]))
+    def base_kernel(u_ref, p_ref, n_ref, r_ref, rp_ref, l_ref, x_ref, zc_ref, rx_ref, ra_ref,
+                    en_ref, out_ref, c0_ref, bp_ref, bn_ref, s_ref):
+        for dst, src_ref, table in ((c0_ref, u_ref, r_ref), (bp_ref, p_ref, rp_ref),
+                                    (bn_ref, n_ref, rp_ref)):
+            wide = dot(table[...], lanes([src_ref[0, f] for f in range(fields)]))
             for f, part in enumerate(unlanes(wide, columns)):
                 dst[0, f] = part
-        tendency_into(out_ref, c_ref, bp_ref, bn_ref, l_ref, x_ref, zc_ref, rx_ref, ra_ref,
+        tendency_into(out_ref, c0_ref, bp_ref, bn_ref, l_ref, x_ref, zc_ref, rx_ref, ra_ref,
                       en_ref, s_ref, coarse_elem)
 
-    def chain_kernel(lead_ref, w_ref, p_ref, n_ref, ws_ref, ps_ref, ns_ref, l_ref, x_ref,
-                     zc_ref, rx_ref, ra_ref, en_ref, base_ref, rint_ref, out_ref, begin_ref,
-                     bp_ref, bn_ref, h_ref, t_ref, g_ref, s_ref):
-        @pl.when(lead_ref[0] != 0)
-        def _():
-            begin_ref[...] = ws_ref[...]
-            bp_ref[...] = ps_ref[...]
-            bn_ref[...] = ns_ref[...]
-
-        @pl.when(lead_ref[0] == 0)
-        def _():
-            begin_ref[...] = w_ref[...]
-            bp_ref[...] = p_ref[...]
-            bn_ref[...] = n_ref[...]
-
-        tendency_into(g_ref, begin_ref, bp_ref, bn_ref, l_ref, x_ref, zc_ref, rx_ref, ra_ref,
+    def chain_kernel(w_ref, p_ref, n_ref, l_ref, x_ref, zc_ref, rx_ref, ra_ref, en_ref,
+                     base_ref, rint_ref, out_ref, h_ref, t_ref, g_ref, s_ref):
+        tendency_into(g_ref, w_ref, p_ref, n_ref, l_ref, x_ref, zc_ref, rx_ref, ra_ref,
                       en_ref, s_ref, coarse_elem)
 
         def body(f, carry):
-            value = begin_ref[0, f] + STEP * (g_ref[0, f] - base_ref[0, f]) + rint_ref[0, f]
+            value = w_ref[0, f] + STEP * (g_ref[0, f] - base_ref[0, f]) + rint_ref[0, f]
             out_ref[0, f] = value
             h_ref[0, f] = value[:coarse_rows]
             t_ref[0, f] = value[coarse_span - coarse_rows:]
@@ -376,11 +363,21 @@
 
         lax.fori_loop(0, fields, body, 0)
 
-    def correct_kernel(a1_ref, a2_ref, c0_ref, c1_ref, w0_ref, w1_ref, prev_ref, us_ref,
-                       r_ref, pm_ref, lead_ref, out_ref, h_ref, t_ref):
+    def pick(sec_ref, w_refs, f, offset):
+        value = w_refs[offset][0, f]
+        for n in range(1, sections):
+            value = jnp.where(sec_ref[0] == n, w_refs[n + offset][0, f], value)
+        return value
+
+    def correct_kernel(*refs):
+        a1_ref, a2_ref, c0_ref, c1_ref = refs[:4]
+        w_refs = refs[4:5 + sections]
+        prev_ref, us_ref, r_ref, pm_ref, lead_ref, sec_ref, out_ref, h_ref, t_ref = refs[
+            5 + sections:]
         pm = pm_ref[...]
-        first_change = [w0_ref[f] - c0_ref[f] for f in range(fields)]
-        last_change = [w1_ref[f] - c1_ref[f] for f in range(fields)]
+        w0 = [pick(sec_ref, w_refs, f, 0) for f in range(fields)]
+        first_change = [w0[f] - c0_ref[0, f] for f in range(fields)]
+        last_change = [pick(sec_ref, w_refs, f, 1) - c1_ref[f] for f in range(fields)]
         middle_fix = unlanes(
             dot(pm, lanes([0.5 * (first_change[f] + last_change[f]) for f in range(fields)])),
             columns,
@@ -388,7 +385,7 @@
         last_fix = unlanes(dot(pm, lanes(last_change)), columns)
         handed = lanes([prev_ref[0, f] for f in range(fields)])
         handed_fix = unlanes(
-            dot(pm, lanes([w0_ref[f] for f in range(fields)]) - dot(r_ref[...], handed)),
+            dot(pm, lanes(w0) - dot(r_ref[...], handed)),
             columns,
         )
         for f in range(fields):
@@ -402,12 +399,17 @@
                 h_ref[b, f] = value[:rows]
                 t_ref[b, f] = value[span - rows:]
 
-    def finish_kernel(a2_ref, c1_ref, w1_ref, pm_ref, out_ref):
+    def finish_kernel(*refs):
+        a2_ref, c1_ref = refs[:2]
+        w_refs = refs[2:3 + sections]
+        pm_ref, sec_ref, out_ref, coarse_ref = refs[3 + sections:]
+        w1 = [pick(sec_ref, w_refs, f, 1) for f in range(fields)]
         fix = unlanes(
-            dot(pm_ref[...], lanes([w1_ref[f] - c1_ref[f] for f in range(fields)])), columns
+            dot(pm_ref[...], lanes([w1[f] - c1_ref[f] for f in range(fields)])), columns
         )
         for f in range(fields):
             out_ref[0, f] = a2_ref[0, f] + fix[f]
+            coarse_ref[0, f] = w1[f]
 
     fine_cost = tendency_cost(1, fields, span, columns, reaction_count)
     coarse_cost = tendency_cost(1, fields, coarse_span, columns, reaction_count)
@@ -430,29 +432,18 @@
     fine_plane = jax.ShapeDtypeStruct((1, fields, rows, columns), f32)
     node_planes = jax.ShapeDtypeStruct((3, fields, rows, columns), f32)
 
-    def coarse_step(flag, w, w_halo, base, rint):
+    def coarse_step(w, w_halo, base, rint):
         return call(
             chain_kernel,
-            (flag, w, w_halo[0], w_halo[1], coarse_start[None], start_halo[0][None],
-             start_halo[1][None], lop_coarse, xt) + coarse_scalars + (base, rint),
-            (True,) + (False,) * 8 + scalar_kinds + (False, False),
-            (coarse_one, coarse_one, plane_one, plane_one, plane_one, plane_one),
+            (w, w_halo[0], w_halo[1], lop_coarse, xt) + coarse_scalars + (base, rint),
+            (False,) * 5 + scalar_kinds + (False, False),
+            (coarse_one, plane_one, plane_one),
             [pltpu.VMEM((1, fields, coarse_span, columns), f32), coarse_scratch(1)],
             *coarse_cost,
         )
 
-    tm_n = sections
-    both = ("tm", "space")
-    hop_pairs = [(d, d + 1) for d in range(tm_n - 1)]
-    prev_pairs = [
-        (d * space_n + s, (d + 1) * space_n + (s + 1) % space_n)
-        for d in range(tm_n - 1) for s in range(space_n)
-    ]
-    next_pairs = [
-        (d * space_n + s, (d + 1) * space_n + (s - 1) % space_n)
-        for d in range(tm_n - 1) for s in range(space_n)
-    ]
-    always = jnp.ones((1,), jnp.int32)
+    hop_pairs = [(d, d + 1) for d in range(sections - 1)]
+    where_now = section.astype(jnp.int32).reshape(1)
 
     fine_end = None
     coarse_end = None
@@ -480,53 +471,50 @@
             *fine_cost,
         )
         a2_prev, a2_next = swap(a2_head, a2_tail)
-        rint, c1, c0 = call(
-            ending_kernel,
-            (a2, a2_prev, a2_next, lop_fine, xt) + scalars + (f_all, g1, nodes, rmat),
-            (False,) * 5 + scalar_kinds + (False,) * 4,
-            (coarse_state, coarse_state, coarse_state),
-            [pltpu.VMEM((1, fields, span, columns), f32), fine_scratch(1)],
-            *fine_cost,
-        )
-        (base,) = call(
+        base, c0 = call(
             base_kernel,
-            (c0[None], node_prev, node_next, restrict_plane, lop_coarse, xt) + coarse_scalars,
-            (False,) * 6 + scalar_kinds,
-            (jax.ShapeDtypeStruct((1, fields, coarse_span, columns), f32),),
+            (nodes, node_prev, node_next, rmat, restrict_plane, lop_coarse, xt) + coarse_scalars,
+            (False,) * 7 + scalar_kinds,
+            (coarse_one, coarse_one),
             [pltpu.VMEM((1, fields, coarse_rows, columns), f32),
              pltpu.VMEM((1, fields, coarse_rows, columns), f32), coarse_scratch(1)],
             *coarse_cost,
         )
+        base_all = lax.all_gather(base, "tm")
+        rint, c1 = call(
+            ending_kernel,
+            (a2, a2_prev, a2_next, lop_fine, xt) + scalars + (f_all, g1, rmat),
+            (False,) * 5 + scalar_kinds + (False,) * 3,
+            (coarse_state, coarse_state),
+            [pltpu.VMEM((1, fields, span, columns), f32), fine_scratch(1)],
+            *fine_cost,
+        )
+        rint_all = lax.all_gather(rint[None], "tm")
         last = iteration + 1 == ITERS
         if not last:
             a2_handed = lax.ppermute(a2, "tm", hop_pairs)
-        begin = coarse_start[None]
-        begin_halo = (start_halo[0][None], start_halo[1][None])
-        flag = always
+        w = coarse_start[None]
+        w_halo = (start_halo[0][None], start_halo[1][None])
+        chain = [w]
         for n in range(sections):
-            finish, w0, _, _, head, tail = coarse_step(flag, begin, begin_halo, base, rint[None])
+            w, head, tail = coarse_step(w, w_halo, base_all[n], rint_all[n])
+            chain.append(w)
             if n + 1 < sections:
-                begin = lax.ppermute(finish, "tm", hop_pairs)
-                begin_halo = (lax.ppermute(tail, both, prev_pairs),
-                              lax.ppermute(head, both, next_pairs))
-                flag = lead
-        w0 = w0[0]
-        w1 = finish[0]
+                w_halo = swap(head, tail)
         if last:
-            (fine_end,) = call(
+            fine_end, coarse_end = call(
                 finish_kernel,
-                (a2, c1, w1, pmat),
-                (False,) * 4,
-                (fine_state,),
+                (a2, c1) + tuple(chain) + (pmat, where_now),
+                (False,) * (3 + sections) + (False, True),
+                (fine_state, coarse_one),
                 [],
                 2 * fields * span * coarse_span * columns * 6, 0,
             )
-            coarse_end = w1
         else:
             nodes, node_head, node_tail = call(
                 correct_kernel,
-                (a1, a2, c0, c1, w0, w1, a2_handed, u_flat, rmat, pmat, lead),
-                (False,) * 10 + (True,),
+                (a1, a2, c0, c1) + tuple(chain) + (a2_handed, u_flat, rmat, pmat, lead, where_now),
+                (False,) * (5 + sections) + (False,) * 4 + (True, True),
                 (jax.ShapeDtypeStruct((3, fields, span, columns), f32), node_planes,
                  node_planes),
                 [],

time: 266 us -> 279 us (1.049)
  starting transfers between devices: 102 us -> 65 us
  waiting for transfers between devices: 42.5 us -> 75.8 us
  between operations: 1.05 us -> 14 us
  local copies, waits for them, and re-layouts: 19.3 us -> 25.7 us
    ppermute x18 -> x0, starting transfers between devices: 68.4 us -> none  [the longest x6 36.5 us: per_device(): lax.ppermute(head, both, next_pairs)]
    all_gather x0 -> x4, waiting for transfers between devices: none -> 33.4 us  [the longest x2 33.4 us: per_device(): rint_all = lax.all_gather(rint[None], 'tm')]
    ppermute x7 -> x13, starting transfers between devices: 26.5 us -> 53.6 us  [swap(): lax.ppermute(head, 'space', [((i + 1) % space_n, i) for i in range(space_...]
    ppermute x7 -> x13, waiting for transfers between devices: 25.1 us -> 37.4 us  [swap(): lax.ppermute(tail, 'space', [(i, (i + 1) % space_n) for i in range(space_...]
    ppermute x18 -> x0, waiting for transfers between devices: 12.2 us -> none  [the longest x6 10.9 us: per_device(): lax.ppermute(head, both, next_pairs)]
    slice x0 -> x2, local copies, waits for them, and re-layouts: none -> 5.16 us  [per_device(): w, head, tail = coarse_step(w, w_halo, base_all[n], rint_all[n])]
    squeeze x0 -> x2, local copies, waits for them, and re-layouts: none -> 5.08 us  [per_device(): w, head, tail = coarse_step(w, w_halo, base_all[n], rint_all[n])]
    ppermute x7 -> x13, starting transfers between devices: 5.17 us -> 9.57 us  [swap(): lax.ppermute(tail, 'space', [(i, (i + 1) % space_n) for i in range(space_...]
  transfers between devices with their start and end apart: 33 -> 31, of which waited for: 16 -> 19; matrix products, arithmetic and copies ran while one was open for 2% -> 5% of each run, Pallas kernels for 7% -> 22%
where the time goes in v7:
time: 279 us
  Pallas kernels  95 us (34%)
  waiting for transfers between devices  75.8 us (27%)
  starting transfers between devices  65 us (23%)
  local copies, waits for them, and re-layouts  25.7 us (9%)
  between operations  14 us (5%)
    pallas_call x18, Pallas kernels, call(): pl.pallas_call(kernel, out_shape=outs, in_specs=[smem() if k else vmem()...  95 us
    ppermute x13, starting transfers between devices, swap(): lax.ppermute(head, 'space', [((i + 1) % space_n, i) for i in range(space_...  53.6 us
    ppermute x13, waiting for transfers between devices, swap(): lax.ppermute(tail, 'space', [(i, (i + 1) % space_n) for i in range(space_...  37.4 us
    all_gather x2, waiting for transfers between devices, per_device(): rint_all = lax.all_gather(rint[None], 'tm')  33.4 us
    ppermute x13, starting transfers between devices, swap(): lax.ppermute(tail, 'space', [(i, (i + 1) % space_n) for i in range(space_...  9.57 us
    unnamed x65, local copies, waits for them, and re-layouts  9.36 us
  transfers between devices with their start and end apart: 31, of which 19 were waited for; matrix products, arithmetic and copies ran while one was open for 5% of the time, Pallas kernels for 22%

profile of v7, /device:TPU:0, one launch (start us, length us, event | category | flops | bytes accessed | tf_op | source)
XLA Modules:
  0.0 278.5 jit_solution(7683865039463791919)
XLA Ops:
  21.4 7.5 %collective-permute-done.p_ref = f32[3,12,16,128]{3,2,1,0:T(8,128)S(1)} collective-permute-done((f32[3,12,16,128]{3,2,1,0:T(8,128)}, f32[3,12,16,128]{3,2,1,0:T(8,128)S(1)}, u32[]{:S(2)}, u32[]{:S(2)}) %collective-permute-start) | collective-permute-done | bytes 294944 | tf_op jit(solution)/shard_map/ppermute | solution.py:284
  31.1 4.8 %shard_map.133 = (f32[1,12,64,128]{3,2,1,0:T(8,128)}, f32[1,12,64,128]{3,2,1,0:T(8,128)}) custom-call(f32[3,12,128,128]{3,2,1,0:T(8,128)} %pad_maximum_fusion.u_ref, f32[3,12,16,128]{3,2,1,0:T(8,128)} %copy-done.4, f32[3,12,16,128]{3,2,1,0:T(8,128)} %collective-permute-done.1.n_ref, f32[64,128]{1,0:T(8,128)} %constant.28.clone.r_ref.refs_11_, ...), custom_call_target="tpu_custom_call" | custom-call | flops 228261888 | bytes 3867988 | tf_op jit(solution)/shard_map/pallas_call | solution.py:217
  37.2 10.5 %shard_map.131 = (f32[3,12,128,128]{3,2,1,0:T(8,128)}, f32[1,12,128,128]{3,2,1,0:T(8,128)}, f32[1,12,16,128]{3,2,1,0:T(8,128)}, f32[1,12,16,128]{3,2,1,0:T(8,128)}) custom-call(f32[3,12,128,128]{3,2,1,0:T(8,128)} %pad_maximum_fusion.u_ref, f32[3,12,16,128]{3,2,1,0:T(8,128)} %copy-done.4, f32[3,12,16,128]{3,2,1,0:T(8,128)} %collective-permute-done.1.n_ref, ...), custom_call_target="tpu_custom_call" | custom-call | flops 1822556160 | bytes 6488916 | tf_op jit(solution)/shard_map/pallas_call | solution.py:217
  48.5 3.8 %collective-permute-start.3 = (f32[1,12,16,128]{3,2,1,0:T(8,128)}, f32[1,12,16,128]{3,2,1,0:T(8,128)S(1)}, u32[]{:S(2)}, u32[]{:S(2)}) collective-permute-start(f32[1,12,16,128]{3,2,1,0:T(8,128)} %get-tuple-element.52), channel_id=1, source_target_pairs={{1,0},{2,1},{3,2},{4,3},{5,4},{6,5},{7,6},{0,7},{9,8},{10,9},{11,1... | collective-permute-start | bytes 294920 | tf_op jit(solution)/shard_map/ppermute | solution.py:285
  56.1 5.9 %shard_map.132 = (f32[1,12,128,128]{3,2,1,0:T(8,128)}, f32[1,12,128,128]{3,2,1,0:T(8,128)}, f32[1,12,16,128]{3,2,1,0:T(8,128)}, f32[1,12,16,128]{3,2,1,0:T(8,128)}) custom-call(f32[1,12,128,128]{3,2,1,0:T(8,128)} %get-tuple-element.50.a1_ref.refs_0_, f32[1,12,16,128]{3,2,1,0:T(8,128)} %copy-done.10, f32[1,12,16,128]{3,2,1,0:T(8,128)} %copy-done.12, ...), custom_call_target="tpu_custom_call" | custom-call | flops 607518720 | bytes 5309268 | tf_op jit(solution)/shard_map/pallas_call | solution.py:217
  62.7 4.1 %collective-permute-start.5 = (f32[1,12,16,128]{3,2,1,0:T(8,128)}, f32[1,12,16,128]{3,2,1,0:T(8,128)S(1)}, u32[]{:S(2)}, u32[]{:S(2)}) collective-permute-start(f32[1,12,16,128]{3,2,1,0:T(8,128)} %get-tuple-element.57), channel_id=1, source_target_pairs={{1,0},{2,1},{3,2},{4,3},{5,4},{6,5},{7,6},{0,7},{9,8},{10,9},{11,1... | collective-permute-start | bytes 294920 | tf_op jit(solution)/shard_map/ppermute | solution.py:285
  70.6 6.5 %shard_map.134 = (f32[12,64,128]{2,1,0:T(8,128)}, f32[12,64,128]{2,1,0:T(8,128)}) custom-call(f32[1,12,128,128]{3,2,1,0:T(8,128)} %get-tuple-element.54.a2_ref.refs_1_, f32[1,12,16,128]{3,2,1,0:T(8,128)} %copy-done.14, f32[1,12,16,128]{3,2,1,0:T(8,128)} %copy-done.16, f32[256,128]{1,0:T(8,128)} %constant.26.clone.l_ref, f32[128,128]{1,0:T(8,128)} %constant.25.clone.x_ref, ...), custom_call_target="tpu_custom_call" | custom-call | flops 607518720 | bytes 5145428 | tf_op jit(solution)/shard_map/pallas_call | solution.py:217
  79.3 4.4 %collective-permute-start.7 = (f32[12,8,128]{2,1,0:T(8,128)S(1)}, f32[12,8,128]{2,1,0:T(8,128)S(1)}, u32[]{:S(2)}, u32[]{:S(2)}) collective-permute-start(f32[12,8,128]{2,1,0:T(8,128)S(1)} %get-tuple-element.116), channel_id=1, source_target_pairs={{1,0},{2,1},{3,2},{4,3},{5,4},{6,5},{7,6},{0,7},{9,8},{10,9},{11,1... | collective-permute-start | bytes 147464 | tf_op jit(solution)/shard_map/ppermute | solution.py:285
  86.3 12.3 %all-gather.11.cloned.1.call-done = f32[48,64,128]{2,1,0:T(8,128)} async-done(((f32[12,64,128]{2,1,0:T(8,128)}), f32[48,64,128]{2,1,0:T(8,128)}) %all-gather.11.cloned.1.call-update) | async-done | bytes 1572880 | tf_op jit(solution)/shard_map/all_gather | solution.py:492
  101.9 3.7 %shard_map.135 = (f32[1,12,64,128]{3,2,1,0:T(8,128)}, f32[1,12,8,128]{3,2,1,0:T(8,128)}, f32[1,12,8,128]{3,2,1,0:T(8,128)}) custom-call(f32[1,12,64,128]{3,2,1,0:T(8,128)} %bitcast.39, f32[1,12,8,128]{3,2,1,0:T(8,128)} %bitcast.48, f32[1,12,8,128]{3,2,1,0:T(8,128)} %bitcast.46, f32[128,64]{1,0:T(8,128)} %constant.27.clone.l_ref, ...), custom_call_target="tpu_custom_call" | custom-call | flops 228261888 | bytes 1868628 | tf_op jit(solution)/shard_map/pallas_call | solution.py:217
  106.3 3.9 %collective-permute-start.9 = (f32[1,12,8,128]{3,2,1,0:T(8,128)}, f32[1,12,8,128]{3,2,1,0:T(8,128)S(1)}, u32[]{:S(2)}, u32[]{:S(2)}) collective-permute-start(f32[1,12,8,128]{3,2,1,0:T(8,128)} %get-tuple-element.64), channel_id=1, source_target_pairs={{1,0},{2,1},{3,2},{4,3},{5,4},{6,5},{7,6},{0,7},{9,8},{10,9},{11,1... | collective-permute-start | bytes 147464 | tf_op jit(solution)/shard_map/ppermute | solution.py:285
  113.2 3.7 %shard_map.136 = (f32[1,12,64,128]{3,2,1,0:T(8,128)}, f32[1,12,8,128]{3,2,1,0:T(8,128)}, f32[1,12,8,128]{3,2,1,0:T(8,128)}) custom-call(f32[1,12,64,128]{3,2,1,0:T(8,128)} %get-tuple-element.62.w_ref.refs_5_, f32[1,12,8,128]{3,2,1,0:T(8,128)} %copy-done.21, f32[1,12,8,128]{3,2,1,0:T(8,128)} %copy-done.25, f32[128,64]{1,0:T(8,128)} %constant.27.clone.l_ref, ...), custom_call_target="tpu_custom_call" | custom-call | flops 228261888 | bytes 1868628 | tf_op jit(solution)/shard_map/pallas_call | solution.py:217
  118.1 3.6 %collective-permute-start.11 = (f32[1,12,8,128]{3,2,1,0:T(8,128)}, f32[1,12,8,128]{3,2,1,0:T(8,128)S(1)}, u32[]{:S(2)}, u32[]{:S(2)}) collective-permute-start(f32[1,12,8,128]{3,2,1,0:T(8,128)} %get-tuple-element.67), channel_id=1, source_target_pairs={{1,0},{2,1},{3,2},{4,3},{5,4},{6,5},{7,6},{0,7},{9,8},{10,9},{11,1... | collective-permute-start | bytes 147464 | tf_op jit(solution)/shard_map/ppermute | solution.py:285
  124.5 3.7 %shard_map.137 = (f32[1,12,64,128]{3,2,1,0:T(8,128)}, f32[1,12,8,128]{3,2,1,0:T(8,128)}, f32[1,12,8,128]{3,2,1,0:T(8,128)}) custom-call(f32[1,12,64,128]{3,2,1,0:T(8,128)} %get-tuple-element.65.w_ref.refs_6_, f32[1,12,8,128]{3,2,1,0:T(8,128)} %copy-done.22, f32[1,12,8,128]{3,2,1,0:T(8,128)} %copy-done.26, f32[128,64]{1,0:T(8,128)} %constant.27.clone.l_ref, ...), custom_call_target="tpu_custom_call" | custom-call | flops 228261888 | bytes 1868628 | tf_op jit(solution)/shard_map/pallas_call | solution.py:217
  128.2 4.8 %collective-permute-start.13 = (f32[1,12,8,128]{3,2,1,0:T(8,128)}, f32[1,12,8,128]{3,2,1,0:T(8,128)S(1)}, u32[]{:S(2)}, u32[]{:S(2)}) collective-permute-start(f32[1,12,8,128]{3,2,1,0:T(8,128)} %get-tuple-element.70), channel_id=1, source_target_pairs={{1,0},{2,1},{3,2},{4,3},{5,4},{6,5},{7,6},{0,7},{9,8},{10,9},{11,1... | collective-permute-start | bytes 147464 | tf_op jit(solution)/shard_map/ppermute | solution.py:285
  135.8 3.7 %shard_map.138 = (f32[1,12,64,128]{3,2,1,0:T(8,128)}, f32[1,12,8,128]{3,2,1,0:T(8,128)}, f32[1,12,8,128]{3,2,1,0:T(8,128)}) custom-call(f32[1,12,64,128]{3,2,1,0:T(8,128)} %get-tuple-element.68.w_ref.refs_7_, f32[1,12,8,128]{3,2,1,0:T(8,128)} %copy-done.18, f32[1,12,8,128]{3,2,1,0:T(8,128)} %copy-done.20, f32[128,64]{1,0:T(8,128)} %constant.27.clone.l_ref, ...), custom_call_target="tpu_custom_call" | custom-call | flops 228261888 | bytes 1868628 | tf_op jit(solution)/shard_map/pallas_call | solution.py:217
  140.4 6.7 %shard_map.139 = (f32[3,12,128,128]{3,2,1,0:T(8,128)}, f32[3,12,16,128]{3,2,1,0:T(8,128)}, f32[3,12,16,128]{3,2,1,0:T(8,128)}) custom-call(f32[1,12,128,128]{3,2,1,0:T(8,128)} %get-tuple-element.50.a1_ref.refs_0_, f32[1,12,128,128]{3,2,1,0:T(8,128)} %get-tuple-element.54.a2_ref.refs_1_, f32[1,12,64,128]{3,2,1,0:T(8,128)} %get-tuple-element.55.refs_2_, ...), custom_call_target="tpu_custom_call" | custom-call | flops 603979776 | bytes 8912904 | tf_op jit(solution)/shard_map/pallas_call | solution.py:217
  147.1 4.8 %collective-permute-start.16 = (f32[3,12,16,128]{3,2,1,0:T(8,128)}, f32[3,12,16,128]{3,2,1,0:T(8,128)S(1)}, u32[]{:S(2)}, u32[]{:S(2)}) collective-permute-start(f32[3,12,16,128]{3,2,1,0:T(8,128)} %get-tuple-element.74), channel_id=1, source_target_pairs={{1,0},{2,1},{3,2},{4,3},{5,4},{6,5},{7,6},{0,7},{9,8},{10,9},{11,1... | collective-permute-start | bytes 884744 | tf_op jit(solution)/shard_map/ppermute | solution.py:285
  151.9 5.3 %collective-permute-done.15.p_ref = f32[3,12,16,128]{3,2,1,0:T(8,128)S(1)} collective-permute-done((f32[3,12,16,128]{3,2,1,0:T(8,128)}, f32[3,12,16,128]{3,2,1,0:T(8,128)S(1)}, u32[]{:S(2)}, u32[]{:S(2)}) %collective-permute-start.15) | collective-permute-done | bytes 294944 | tf_op jit(solution)/shard_map/ppermute | solution.py:284
  160.0 4.8 %shard_map.143 = (f32[1,12,64,128]{3,2,1,0:T(8,128)}, f32[1,12,64,128]{3,2,1,0:T(8,128)}) custom-call(f32[3,12,128,128]{3,2,1,0:T(8,128)} %get-tuple-element.72.u_ref, f32[3,12,16,128]{3,2,1,0:T(8,128)} %copy-done.5, f32[3,12,16,128]{3,2,1,0:T(8,128)} %copy-done.6, f32[64,128]{1,0:T(8,128)} %constant.28.clone.r_ref.refs_11_, f32[8,16]{1,0:T(8,128)} %constant.30.clone.rp_ref, ...), custom_call_target="tpu_custom_call" | custom-call | flops 228261888 | bytes 3867988 | tf_op jit(solution)/shard_map/pallas_call | solution.py:217
  165.1 10.5 %shard_map.140 = (f32[3,12,128,128]{3,2,1,0:T(8,128)}, f32[1,12,128,128]{3,2,1,0:T(8,128)}, f32[1,12,16,128]{3,2,1,0:T(8,128)}, f32[1,12,16,128]{3,2,1,0:T(8,128)}) custom-call(f32[3,12,128,128]{3,2,1,0:T(8,128)} %get-tuple-element.72.u_ref, f32[3,12,16,128]{3,2,1,0:T(8,128)} %copy-done.5, f32[3,12,16,128]{3,2,1,0:T(8,128)} %copy-done.6, ...), custom_call_target="tpu_custom_call" | custom-call | flops 1822556160 | bytes 6488916 | tf_op jit(solution)/shard_map/pallas_call | solution.py:217
  176.0 4.3 %collective-permute-start.18 = (f32[1,12,16,128]{3,2,1,0:T(8,128)}, f32[1,12,16,128]{3,2,1,0:T(8,128)S(1)}, u32[]{:S(2)}, u32[]{:S(2)}) collective-permute-start(f32[1,12,16,128]{3,2,1,0:T(8,128)} %get-tuple-element.77), channel_id=1, source_target_pairs={{1,0},{2,1},{3,2},{4,3},{5,4},{6,5},{7,6},{0,7},{9,8},{10,9},{11,1... | collective-permute-start | bytes 294920 | tf_op jit(solution)/shard_map/ppermute | solution.py:285
  183.8 6.0 %shard_map.141 = (f32[1,12,128,128]{3,2,1,0:T(8,128)}, f32[1,12,128,128]{3,2,1,0:T(8,128)}, f32[1,12,16,128]{3,2,1,0:T(8,128)}, f32[1,12,16,128]{3,2,1,0:T(8,128)}) custom-call(f32[1,12,128,128]{3,2,1,0:T(8,128)} %get-tuple-element.75.a1_ref, f32[1,12,16,128]{3,2,1,0:T(8,128)} %copy-done.9, f32[1,12,16,128]{3,2,1,0:T(8,128)} %copy-done.11, ...), custom_call_target="tpu_custom_call" | custom-call | flops 607518720 | bytes 5309268 | tf_op jit(solution)/shard_map/pallas_call | solution.py:217
  189.8 4.8 %collective-permute-start.20 = (f32[1,12,16,128]{3,2,1,0:T(8,128)}, f32[1,12,16,128]{3,2,1,0:T(8,128)S(1)}, u32[]{:S(2)}, u32[]{:S(2)}) collective-permute-start(f32[1,12,16,128]{3,2,1,0:T(8,128)} %get-tuple-element.81), channel_id=1, source_target_pairs={{1,0},{2,1},{3,2},{4,3},{5,4},{6,5},{7,6},{0,7},{9,8},{10,9},{11,1... | collective-permute-start | bytes 294920 | tf_op jit(solution)/shard_map/ppermute | solution.py:285
  198.0 6.5 %shard_map.142 = (f32[12,64,128]{2,1,0:T(8,128)}, f32[12,64,128]{2,1,0:T(8,128)}) custom-call(f32[1,12,128,128]{3,2,1,0:T(8,128)} %get-tuple-element.79.a2_ref.refs_0_, f32[1,12,16,128]{3,2,1,0:T(8,128)} %copy-done.13, f32[1,12,16,128]{3,2,1,0:T(8,128)} %copy-done.15, f32[256,128]{1,0:T(8,128)} %constant.26.clone.l_ref, f32[128,128]{1,0:T(8,128)} %constant.25.clone.x_ref, ...), custom_call_target="tpu_custom_call" | custom-call | flops 607518720 | bytes 5145428 | tf_op jit(solution)/shard_map/pallas_call | solution.py:217
  207.1 21.0 %all-gather.15.cloned.1.call-done = f32[48,64,128]{2,1,0:T(8,128)} async-done(((f32[12,64,128]{2,1,0:T(8,128)}), f32[48,64,128]{2,1,0:T(8,128)}) %all-gather.15.cloned.1.call-update) | async-done | bytes 1572880 | tf_op jit(solution)/shard_map/all_gather | solution.py:492
  230.6 3.7 %shard_map.144 = (f32[1,12,64,128]{3,2,1,0:T(8,128)}, f32[1,12,8,128]{3,2,1,0:T(8,128)}, f32[1,12,8,128]{3,2,1,0:T(8,128)}) custom-call(f32[1,12,64,128]{3,2,1,0:T(8,128)} %bitcast.41, f32[1,12,8,128]{3,2,1,0:T(8,128)} %bitcast.49, f32[1,12,8,128]{3,2,1,0:T(8,128)} %bitcast.47, f32[128,64]{1,0:T(8,128)} %constant.27.clone.l_ref, ...), custom_call_target="tpu_custom_call" | custom-call | flops 228261888 | bytes 1868628 | tf_op jit(solution)/shard_map/pallas_call | solution.py:217
  241.9 3.7 %shard_map.145 = (f32[1,12,64,128]{3,2,1,0:T(8,128)}, f32[1,12,8,128]{3,2,1,0:T(8,128)}, f32[1,12,8,128]{3,2,1,0:T(8,128)}) custom-call(f32[1,12,64,128]{3,2,1,0:T(8,128)} %get-tuple-element.86.w_ref.refs_3_, f32[1,12,8,128]{3,2,1,0:T(8,128)} %copy-done.23, f32[1,12,8,128]{3,2,1,0:T(8,128)} %copy-done.27, f32[128,64]{1,0:T(8,128)} %constant.27.clone.l_ref, ...), custom_call_target="tpu_custom_call" | custom-call | flops 228261888 | bytes 1868628 | tf_op jit(solution)/shard_map/pallas_call | solution.py:217
  246.7 3.9 %collective-permute-start.24 = (f32[1,12,8,128]{3,2,1,0:T(8,128)}, f32[1,12,8,128]{3,2,1,0:T(8,128)S(1)}, u32[]{:S(2)}, u32[]{:S(2)}) collective-permute-start(f32[1,12,8,128]{3,2,1,0:T(8,128)} %get-tuple-element.91), channel_id=1, source_target_pairs={{1,0},{2,1},{3,2},{4,3},{5,4},{6,5},{7,6},{0,7},{9,8},{10,9},{11,1... | collective-permute-start | bytes 147464 | tf_op jit(solution)/shard_map/ppermute | solution.py:285
  253.3 3.7 %shard_map.146 = (f32[1,12,64,128]{3,2,1,0:T(8,128)}, f32[1,12,8,128]{3,2,1,0:T(8,128)}, f32[1,12,8,128]{3,2,1,0:T(8,128)}) custom-call(f32[1,12,64,128]{3,2,1,0:T(8,128)} %get-tuple-element.89.w_ref.refs_4_, f32[1,12,8,128]{3,2,1,0:T(8,128)} %copy-done.24, f32[1,12,8,128]{3,2,1,0:T(8,128)} %copy-done.28, f32[128,64]{1,0:T(8,128)} %constant.27.clone.l_ref, ...), custom_call_target="tpu_custom_call" | custom-call | flops 228261888 | bytes 1868628 | tf_op jit(solution)/shard_map/pallas_call | solution.py:217
  257.1 4.9 %collective-permute-start.26 = (f32[1,12,8,128]{3,2,1,0:T(8,128)}, f32[1,12,8,128]{3,2,1,0:T(8,128)S(1)}, u32[]{:S(2)}, u32[]{:S(2)}) collective-permute-start(f32[1,12,8,128]{3,2,1,0:T(8,128)} %get-tuple-element.94), channel_id=1, source_target_pairs={{1,0},{2,1},{3,2},{4,3},{5,4},{6,5},{7,6},{0,7},{9,8},{10,9},{11,1... | collective-permute-start | bytes 147464 | tf_op jit(solution)/shard_map/ppermute | solution.py:285
  264.8 3.7 %shard_map.147 = (f32[1,12,64,128]{3,2,1,0:T(8,128)}, f32[1,12,8,128]{3,2,1,0:T(8,128)}, f32[1,12,8,128]{3,2,1,0:T(8,128)}) custom-call(f32[1,12,64,128]{3,2,1,0:T(8,128)} %get-tuple-element.92.w_ref.refs_5_, f32[1,12,8,128]{3,2,1,0:T(8,128)} %copy-done.17, f32[1,12,8,128]{3,2,1,0:T(8,128)} %copy-done.19, f32[128,64]{1,0:T(8,128)} %constant.27.clone.l_ref, ...), custom_call_target="tpu_custom_call" | custom-call | flops 228261888 | bytes 1868628 | tf_op jit(solution)/shard_map/pallas_call | solution.py:217
  (132 shorter events, 79.6 us)
Async XLA Ops:
  7.2 76.6 %all-gather.9.cloned.1.call-start = ((), (), s32[]{:S(2)}) async-start(), calls=%async_computation | async-start | bytes 1966080 | tf_op jit(solution)/shard_map/all_gather | solution.py:483
  11.9 17.0 %collective-permute-start = (f32[3,12,16,128]{3,2,1,0:T(8,128)}, f32[3,12,16,128]{3,2,1,0:T(8,128)S(1)}, u32[]{:S(2)}, u32[]{:S(2)}) collective-permute-start(f32[3,12,16,128]{3,2,1,0:T(8,128)} %get-tuple-element.99), channel_id=1, source_target_pairs={{0,1},{1,2},{2,3},{3,4},{4,5},{5,6},{6,7},{7,0},{8,9},{9,10},{10,1... | collective-permute-start | bytes 884744 | tf_op jit(solution)/shard_map/ppermute | solution.py:284
  14.9 16.2 %collective-permute-start.1 = (f32[3,12,16,128]{3,2,1,0:T(8,128)}, f32[3,12,16,128]{3,2,1,0:T(8,128)}, u32[]{:S(2)}, u32[]{:S(2)}) collective-permute-start(f32[3,12,16,128]{3,2,1,0:T(8,128)} %get-tuple-element.98), channel_id=1, source_target_pairs={{1,0},{2,1},{3,2},{4,3},{5,4},{6,5},{7,6},{0,7},{9,8},{10,9},{11,1... | collective-permute-start | bytes 884744 | tf_op jit(solution)/shard_map/ppermute | solution.py:285
  35.9 62.7 %all-gather.11.cloned.1.call-start = ((), (), s32[]{:S(2)}) async-start(), calls=%async_computation.1 | async-start | bytes 1966080 | tf_op jit(solution)/shard_map/all_gather | solution.py:492
  47.6 7.6 %collective-permute-start.2 = (f32[1,12,16,128]{3,2,1,0:T(8,128)}, f32[1,12,16,128]{3,2,1,0:T(8,128)S(1)}, u32[]{:S(2)}, u32[]{:S(2)}) collective-permute-start(f32[1,12,16,128]{3,2,1,0:T(8,128)} %get-tuple-element.51), channel_id=1, source_target_pairs={{0,1},{1,2},{2,3},{3,4},{4,5},{5,6},{6,7},{7,0},{8,9},{9,10},{10,1... | collective-permute-start | bytes 294920 | tf_op jit(solution)/shard_map/ppermute | solution.py:284
  48.5 6.9 %collective-permute-start.3 = (f32[1,12,16,128]{3,2,1,0:T(8,128)}, f32[1,12,16,128]{3,2,1,0:T(8,128)S(1)}, u32[]{:S(2)}, u32[]{:S(2)}) collective-permute-start(f32[1,12,16,128]{3,2,1,0:T(8,128)} %get-tuple-element.52), channel_id=1, source_target_pairs={{1,0},{2,1},{3,2},{4,3},{5,4},{6,5},{7,6},{0,7},{9,8},{10,9},{11,1... | collective-permute-start | bytes 294920 | tf_op jit(solution)/shard_map/ppermute | solution.py:285
  62.1 7.6 %collective-permute-start.4 = (f32[1,12,16,128]{3,2,1,0:T(8,128)}, f32[1,12,16,128]{3,2,1,0:T(8,128)S(1)}, u32[]{:S(2)}, u32[]{:S(2)}) collective-permute-start(f32[1,12,16,128]{3,2,1,0:T(8,128)} %get-tuple-element.56), channel_id=1, source_target_pairs={{0,1},{1,2},{2,3},{3,4},{4,5},{5,6},{6,7},{7,0},{8,9},{9,10},{10,1... | collective-permute-start | bytes 294920 | tf_op jit(solution)/shard_map/ppermute | solution.py:284
  62.7 7.3 %collective-permute-start.5 = (f32[1,12,16,128]{3,2,1,0:T(8,128)}, f32[1,12,16,128]{3,2,1,0:T(8,128)S(1)}, u32[]{:S(2)}, u32[]{:S(2)}) collective-permute-start(f32[1,12,16,128]{3,2,1,0:T(8,128)} %get-tuple-element.57), channel_id=1, source_target_pairs={{1,0},{2,1},{3,2},{4,3},{5,4},{6,5},{7,6},{0,7},{9,8},{10,9},{11,1... | collective-permute-start | bytes 294920 | tf_op jit(solution)/shard_map/ppermute | solution.py:285
  77.2 127.3 %all-gather.13.cloned.1.call-start = ((), (), s32[]{:S(2)}) async-start(), calls=%async_computation.2 | async-start | bytes 1966080 | tf_op jit(solution)/shard_map/all_gather | solution.py:483
  77.9 23.3 %copy-start = (f32[8,12,8,128]{3,0,2,1:T(8,128)}, f32[8,12,8,128]{3,0,2,1:T(8,128)S(1)}, u32[]{:S(2)}) copy-start(f32[8,12,8,128]{3,0,2,1:T(8,128)S(1)} %fusion.5) | copy-start | bytes 1179652
  77.9 61.6 %collective-permute-start.14 = (f32[1,12,128,128]{3,2,1,0:T(8,128)S(1)}, f32[1,12,128,128]{3,2,1,0:T(8,128)S(1)}, u32[]{:S(2)}, u32[]{:S(2)}) collective-permute-start(f32[1,12,128,128]{3,2,1,0:T(8,128)S(1)} %copy-done.2), channel_id=1, source_target_pairs={{0,8},{8,16},{16,24},{1,9},{9,17},{17,25},{2,10},{10,18},{18,26},{... | collective-permute-start | bytes 2359304 | tf_op jit(solution)/shard_map/ppermute | solution.py:495
  79.3 21.9 %collective-permute-start.7 = (f32[12,8,128]{2,1,0:T(8,128)S(1)}, f32[12,8,128]{2,1,0:T(8,128)S(1)}, u32[]{:S(2)}, u32[]{:S(2)}) collective-permute-start(f32[12,8,128]{2,1,0:T(8,128)S(1)} %get-tuple-element.116), channel_id=1, source_target_pairs={{1,0},{2,1},{3,2},{4,3},{5,4},{6,5},{7,6},{0,7},{9,8},{10,9},{11,1... | collective-permute-start | bytes 147464 | tf_op jit(solution)/shard_map/ppermute | solution.py:285
  83.7 17.5 %collective-permute-start.6 = (f32[12,8,128]{2,1,0:T(8,128)S(1)}, f32[12,8,128]{2,1,0:T(8,128)S(1)}, u32[]{:S(2)}, u32[]{:S(2)}) collective-permute-start(f32[12,8,128]{2,1,0:T(8,128)S(1)} %get-tuple-element.117), channel_id=1, source_target_pairs={{0,1},{1,2},{2,3},{3,4},{4,5},{5,6},{6,7},{7,0},{8,9},{9,10},{10,1... | collective-permute-start | bytes 147464 | tf_op jit(solution)/shard_map/ppermute | solution.py:284
  105.5 7.0 %collective-permute-start.8 = (f32[1,12,8,128]{3,2,1,0:T(8,128)}, f32[1,12,8,128]{3,2,1,0:T(8,128)S(1)}, u32[]{:S(2)}, u32[]{:S(2)}) collective-permute-start(f32[1,12,8,128]{3,2,1,0:T(8,128)} %get-tuple-element.63), channel_id=1, source_target_pairs={{0,1},{1,2},{2,3},{3,4},{4,5},{5,6},{6,7},{7,0},{8,9},{9,10},{10,1... | collective-permute-start | bytes 147464 | tf_op jit(solution)/shard_map/ppermute | solution.py:284
  106.3 6.2 %collective-permute-start.9 = (f32[1,12,8,128]{3,2,1,0:T(8,128)}, f32[1,12,8,128]{3,2,1,0:T(8,128)S(1)}, u32[]{:S(2)}, u32[]{:S(2)}) collective-permute-start(f32[1,12,8,128]{3,2,1,0:T(8,128)} %get-tuple-element.64), channel_id=1, source_target_pairs={{1,0},{2,1},{3,2},{4,3},{5,4},{6,5},{7,6},{0,7},{9,8},{10,9},{11,1... | collective-permute-start | bytes 147464 | tf_op jit(solution)/shard_map/ppermute | solution.py:285
  116.9 7.0 %collective-permute-start.10 = (f32[1,12,8,128]{3,2,1,0:T(8,128)}, f32[1,12,8,128]{3,2,1,0:T(8,128)S(1)}, u32[]{:S(2)}, u32[]{:S(2)}) collective-permute-start(f32[1,12,8,128]{3,2,1,0:T(8,128)} %get-tuple-element.66), channel_id=1, source_target_pairs={{0,1},{1,2},{2,3},{3,4},{4,5},{5,6},{6,7},{7,0},{8,9},{9,10},{10,1... | collective-permute-start | bytes 147464 | tf_op jit(solution)/shard_map/ppermute | solution.py:284
  118.1 5.8 %collective-permute-start.11 = (f32[1,12,8,128]{3,2,1,0:T(8,128)}, f32[1,12,8,128]{3,2,1,0:T(8,128)S(1)}, u32[]{:S(2)}, u32[]{:S(2)}) collective-permute-start(f32[1,12,8,128]{3,2,1,0:T(8,128)} %get-tuple-element.67), channel_id=1, source_target_pairs={{1,0},{2,1},{3,2},{4,3},{5,4},{6,5},{7,6},{0,7},{9,8},{10,9},{11,1... | collective-permute-start | bytes 147464 | tf_op jit(solution)/shard_map/ppermute | solution.py:285
  128.2 7.0 %collective-permute-start.12 = (f32[1,12,8,128]{3,2,1,0:T(8,128)}, f32[1,12,8,128]{3,2,1,0:T(8,128)S(1)}, u32[]{:S(2)}, u32[]{:S(2)}) collective-permute-start(f32[1,12,8,128]{3,2,1,0:T(8,128)} %get-tuple-element.69), channel_id=1, source_target_pairs={{0,1},{1,2},{2,3},{3,4},{4,5},{5,6},{6,7},{7,0},{8,9},{9,10},{10,1... | collective-permute-start | bytes 147464 | tf_op jit(solution)/shard_map/ppermute | solution.py:284
  128.2 7.0 %collective-permute-start.13 = (f32[1,12,8,128]{3,2,1,0:T(8,128)}, f32[1,12,8,128]{3,2,1,0:T(8,128)S(1)}, u32[]{:S(2)}, u32[]{:S(2)}) collective-permute-start(f32[1,12,8,128]{3,2,1,0:T(8,128)} %get-tuple-element.70), channel_id=1, source_target_pairs={{1,0},{2,1},{3,2},{4,3},{5,4},{6,5},{7,6},{0,7},{9,8},{10,9},{11,1... | collective-permute-start | bytes 147464 | tf_op jit(solution)/shard_map/ppermute | solution.py:285
  147.1 10.1 %collective-permute-start.15 = (f32[3,12,16,128]{3,2,1,0:T(8,128)}, f32[3,12,16,128]{3,2,1,0:T(8,128)S(1)}, u32[]{:S(2)}, u32[]{:S(2)}) collective-permute-start(f32[3,12,16,128]{3,2,1,0:T(8,128)} %get-tuple-element.73), channel_id=1, source_target_pairs={{0,1},{1,2},{2,3},{3,4},{4,5},{5,6},{6,7},{7,0},{8,9},{9,10},{10,1... | collective-permute-start | bytes 884744 | tf_op jit(solution)/shard_map/ppermute | solution.py:284
  147.1 12.2 %collective-permute-start.16 = (f32[3,12,16,128]{3,2,1,0:T(8,128)}, f32[3,12,16,128]{3,2,1,0:T(8,128)S(1)}, u32[]{:S(2)}, u32[]{:S(2)}) collective-permute-start(f32[3,12,16,128]{3,2,1,0:T(8,128)} %get-tuple-element.74), channel_id=1, source_target_pairs={{1,0},{2,1},{3,2},{4,3},{5,4},{6,5},{7,6},{0,7},{9,8},{10,9},{11,1... | collective-permute-start | bytes 884744 | tf_op jit(solution)/shard_map/ppermute | solution.py:285
  164.8 63.3 %all-gather.15.cloned.1.call-start = ((), (), s32[]{:S(2)}) async-start(), calls=%async_computation.3 | async-start | bytes 1966080 | tf_op jit(solution)/shard_map/all_gather | solution.py:492
  175.6 7.5 %collective-permute-start.17 = (f32[1,12,16,128]{3,2,1,0:T(8,128)}, f32[1,12,16,128]{3,2,1,0:T(8,128)S(1)}, u32[]{:S(2)}, u32[]{:S(2)}) collective-permute-start(f32[1,12,16,128]{3,2,1,0:T(8,128)} %get-tuple-element.76), channel_id=1, source_target_pairs={{0,1},{1,2},{2,3},{3,4},{4,5},{5,6},{6,7},{7,0},{8,9},{9,10},{10,1... | collective-permute-start | bytes 294920 | tf_op jit(solution)/shard_map/ppermute | solution.py:284
  176.0 7.1 %collective-permute-start.18 = (f32[1,12,16,128]{3,2,1,0:T(8,128)}, f32[1,12,16,128]{3,2,1,0:T(8,128)S(1)}, u32[]{:S(2)}, u32[]{:S(2)}) collective-permute-start(f32[1,12,16,128]{3,2,1,0:T(8,128)} %get-tuple-element.77), channel_id=1, source_target_pairs={{1,0},{2,1},{3,2},{4,3},{5,4},{6,5},{7,6},{0,7},{9,8},{10,9},{11,1... | collective-permute-start | bytes 294920 | tf_op jit(solution)/shard_map/ppermute | solution.py:285
  189.8 7.5 %collective-permute-start.19 = (f32[1,12,16,128]{3,2,1,0:T(8,128)}, f32[1,12,16,128]{3,2,1,0:T(8,128)S(1)}, u32[]{:S(2)}, u32[]{:S(2)}) collective-permute-start(f32[1,12,16,128]{3,2,1,0:T(8,128)} %get-tuple-element.80), channel_id=1, source_target_pairs={{0,1},{1,2},{2,3},{3,4},{4,5},{5,6},{6,7},{7,0},{8,9},{9,10},{10,1... | collective-permute-start | bytes 294920 | tf_op jit(solution)/shard_map/ppermute | solution.py:284
  189.8 7.5 %collective-permute-start.20 = (f32[1,12,16,128]{3,2,1,0:T(8,128)}, f32[1,12,16,128]{3,2,1,0:T(8,128)S(1)}, u32[]{:S(2)}, u32[]{:S(2)}) collective-permute-start(f32[1,12,16,128]{3,2,1,0:T(8,128)} %get-tuple-element.81), channel_id=1, source_target_pairs={{1,0},{2,1},{3,2},{4,3},{5,4},{6,5},{7,6},{0,7},{9,8},{10,9},{11,1... | collective-permute-start | bytes 294920 | tf_op jit(solution)/shard_map/ppermute | solution.py:285
  234.3 7.0 %collective-permute-start.21 = (f32[1,12,8,128]{3,2,1,0:T(8,128)}, f32[1,12,8,128]{3,2,1,0:T(8,128)S(1)}, u32[]{:S(2)}, u32[]{:S(2)}) collective-permute-start(f32[1,12,8,128]{3,2,1,0:T(8,128)} %get-tuple-element.87), channel_id=1, source_target_pairs={{0,1},{1,2},{2,3},{3,4},{4,5},{5,6},{6,7},{7,0},{8,9},{9,10},{10,1... | collective-permute-start | bytes 147464 | tf_op jit(solution)/shard_map/ppermute | solution.py:284
  235.8 5.5 %collective-permute-start.22 = (f32[1,12,8,128]{3,2,1,0:T(8,128)}, f32[1,12,8,128]{3,2,1,0:T(8,128)S(1)}, u32[]{:S(2)}, u32[]{:S(2)}) collective-permute-start(f32[1,12,8,128]{3,2,1,0:T(8,128)} %get-tuple-element.88), channel_id=1, source_target_pairs={{1,0},{2,1},{3,2},{4,3},{5,4},{6,5},{7,6},{0,7},{9,8},{10,9},{11,1... | collective-permute-start | bytes 147464 | tf_op jit(solution)/shard_map/ppermute | solution.py:285
  245.6 7.0 %collective-permute-start.23 = (f32[1,12,8,128]{3,2,1,0:T(8,128)}, f32[1,12,8,128]{3,2,1,0:T(8,128)S(1)}, u32[]{:S(2)}, u32[]{:S(2)}) collective-permute-start(f32[1,12,8,128]{3,2,1,0:T(8,128)} %get-tuple-element.90), channel_id=1, source_target_pairs={{0,1},{1,2},{2,3},{3,4},{4,5},{5,6},{6,7},{7,0},{8,9},{9,10},{10,1... | collective-permute-start | bytes 147464 | tf_op jit(solution)/shard_map/ppermute | solution.py:284
  246.7 6.0 %collective-permute-start.24 = (f32[1,12,8,128]{3,2,1,0:T(8,128)}, f32[1,12,8,128]{3,2,1,0:T(8,128)S(1)}, u32[]{:S(2)}, u32[]{:S(2)}) collective-permute-start(f32[1,12,8,128]{3,2,1,0:T(8,128)} %get-tuple-element.91), channel_id=1, source_target_pairs={{1,0},{2,1},{3,2},{4,3},{5,4},{6,5},{7,6},{0,7},{9,8},{10,9},{11,1... | collective-permute-start | bytes 147464 | tf_op jit(solution)/shard_map/ppermute | solution.py:285
  257.0 7.2 %collective-permute-start.25 = (f32[1,12,8,128]{3,2,1,0:T(8,128)}, f32[1,12,8,128]{3,2,1,0:T(8,128)S(1)}, u32[]{:S(2)}, u32[]{:S(2)}) collective-permute-start(f32[1,12,8,128]{3,2,1,0:T(8,128)} %get-tuple-element.93), channel_id=1, source_target_pairs={{0,1},{1,2},{2,3},{3,4},{4,5},{5,6},{6,7},{7,0},{8,9},{9,10},{10,1... | collective-permute-start | bytes 147464 | tf_op jit(solution)/shard_map/ppermute | solution.py:284
  257.1 7.1 %collective-permute-start.26 = (f32[1,12,8,128]{3,2,1,0:T(8,128)}, f32[1,12,8,128]{3,2,1,0:T(8,128)S(1)}, u32[]{:S(2)}, u32[]{:S(2)}) collective-permute-start(f32[1,12,8,128]{3,2,1,0:T(8,128)} %get-tuple-element.94), channel_id=1, source_target_pairs={{1,0},{2,1},{3,2},{4,3},{5,4},{6,5},{7,6},{0,7},{9,8},{10,9},{11,1... | collective-permute-start | bytes 147464 | tf_op jit(solution)/shard_map/ppermute | solution.py:285
  (31 other events, 51.6 us)
Sparse Core Ops, SparseCore 0:
  36.0 20.2 all-gather.8
  77.3 21.3 all-gather.10
  165.0 23.3 all-gather.12
  204.6 23.4 all-gather.14

commit v8 on v7

--- a/solution.py
+++ b/solution.py
@@ -210,16 +210,20 @@
     return flops, trans
 
 
-def call(kernel, ins, in_kinds, outs, scratch, flops, trans):
+def call(kernel, ins, in_kinds, outs, scratch, flops, trans, blocks=None):
     nbytes = sum(int(np.prod(x.shape)) * 4 for x in ins) + sum(
         int(np.prod(o.shape)) * 4 for o in outs
     )
     return pl.pallas_call(
         kernel,
         out_shape=outs,
-        in_specs=[smem() if k else vmem() for k in in_kinds],
+        in_specs=[
+            (blocks[i] if blocks is not None and i in blocks else smem() if k else vmem())
+            for i, k in enumerate(in_kinds)
+        ],
         out_specs=tuple(vmem() for _ in outs),
         scratch_shapes=scratch,
+        grid=() if blocks is None else (1,),
         cost_estimate=pl.CostEstimate(
             flops=int(flops), transcendentals=int(trans), bytes_accessed=int(nbytes)
         ),
@@ -355,7 +359,7 @@
                       en_ref, s_ref, coarse_elem)
 
         def body(f, carry):
-            value = w_ref[0, f] + STEP * (g_ref[0, f] - base_ref[0, f]) + rint_ref[0, f]
+            value = w_ref[0, f] + STEP * (g_ref[0, f] - base_ref[0, 0, f]) + rint_ref[0, 0, f]
             out_ref[0, f] = value
             h_ref[0, f] = value[:coarse_rows]
             t_ref[0, f] = value[coarse_span - coarse_rows:]
@@ -432,14 +436,19 @@
     fine_plane = jax.ShapeDtypeStruct((1, fields, rows, columns), f32)
     node_planes = jax.ShapeDtypeStruct((3, fields, rows, columns), f32)
 
-    def coarse_step(w, w_halo, base, rint):
+    def coarse_step(w, w_halo, base_all, rint_all, n):
+        def section_block():
+            return pl.BlockSpec((1, 1, fields, coarse_span, columns), lambda i: (n, 0, 0, 0, 0),
+                                memory_space=pltpu.VMEM)
+
         return call(
             chain_kernel,
-            (w, w_halo[0], w_halo[1], lop_coarse, xt) + coarse_scalars + (base, rint),
+            (w, w_halo[0], w_halo[1], lop_coarse, xt) + coarse_scalars + (base_all, rint_all),
             (False,) * 5 + scalar_kinds + (False, False),
             (coarse_one, plane_one, plane_one),
             [pltpu.VMEM((1, fields, coarse_span, columns), f32), coarse_scratch(1)],
             *coarse_cost,
+            blocks={9: section_block(), 10: section_block()},
         )
 
     hop_pairs = [(d, d + 1) for d in range(sections - 1)]
@@ -497,7 +506,7 @@
         w_halo = (start_halo[0][None], start_halo[1][None])
         chain = [w]
         for n in range(sections):
-            w, head, tail = coarse_step(w, w_halo, base_all[n], rint_all[n])
+            w, head, tail = coarse_step(w, w_halo, base_all, rint_all, n)
             chain.append(w)
             if n + 1 < sections:
                 w_halo = swap(head, tail)

time: 279 us -> 273 us (0.978)
  local copies, waits for them, and re-layouts: 25.7 us -> 14.8 us
  waiting for transfers between devices: 75.8 us -> 80.3 us
    slice x2 -> x0, local copies, waits for them, and re-layouts: 5.16 us -> none  [per_device(): w, head, tail = coarse_step(w, w_halo, base_all[n], rint_all[n])]
    squeeze x2 -> x0, local copies, waits for them, and re-layouts: 5.08 us -> none  [per_device(): w, head, tail = coarse_step(w, w_halo, base_all[n], rint_all[n])]
    ppermute x13, waiting for transfers between devices: 37.4 us -> 42.4 us  [swap(): lax.ppermute(tail, 'space', [(i, (i + 1) % space_n) for i in range(space_...]
  transfers between devices with their start and end apart: 31 -> 31, of which waited for: 19 -> 21; matrix products, arithmetic and copies ran while one was open for 5% -> 2% of each run, Pallas kernels for 22% -> 22%
where the time goes in v8:
time: 273 us; the launch traced here: 272 us
  Pallas kernels  94.9 us (35%)
  waiting for transfers between devices  80.3 us (29%)
  starting transfers between devices  65 us (24%)
  local copies, waits for them, and re-layouts  14.8 us (5%)
  between operations  13.9 us (5%)
    pallas_call x18, Pallas kernels, call(): pl.pallas_call(kernel, out_shape=outs, in_specs=[blocks[i] if blocks is n...  94.9 us
    ppermute x13, starting transfers between devices, swap(): lax.ppermute(head, 'space', [((i + 1) % space_n, i) for i in range(space_...  53 us
    ppermute x13, waiting for transfers between devices, swap(): lax.ppermute(tail, 'space', [(i, (i + 1) % space_n) for i in range(space_...  42.4 us
    all_gather x2, waiting for transfers between devices, per_device(): rint_all = lax.all_gather(rint[None], 'tm')  31.1 us
    ppermute x13, starting transfers between devices, swap(): lax.ppermute(tail, 'space', [(i, (i + 1) % space_n) for i in range(space_...  10.1 us
    unnamed x65, local copies, waits for them, and re-layouts  8.76 us
    ppermute x13, waiting for transfers between devices, swap(): lax.ppermute(head, 'space', [((i + 1) % space_n, i) for i in range(space_...  6.67 us
  transfers between devices with their start and end apart: 31, of which 21 were waited for; matrix products, arithmetic and copies ran while one was open for 2% of the time, Pallas kernels for 22%

profile of v8, /device:TPU:0, one launch (start us, length us, event | category | flops | bytes accessed | tf_op | source)
XLA Modules:
  0.0 272.0 jit_solution(4711602365886031391)
XLA Ops:
  21.4 7.5 %collective-permute-done.p_ref = f32[3,12,16,128]{3,2,1,0:T(8,128)S(1)} collective-permute-done((f32[3,12,16,128]{3,2,1,0:T(8,128)}, f32[3,12,16,128]{3,2,1,0:T(8,128)S(1)}, u32[]{:S(2)}, u32[]{:S(2)}) %collective-permute-start) | collective-permute-done | bytes 294944 | tf_op jit(solution)/shard_map/ppermute | solution.py:288
  31.1 4.8 %shard_map.133 = (f32[1,12,64,128]{3,2,1,0:T(8,128)}, f32[1,12,64,128]{3,2,1,0:T(8,128)}) custom-call(f32[3,12,128,128]{3,2,1,0:T(8,128)} %pad_maximum_fusion.u_ref, f32[3,12,16,128]{3,2,1,0:T(8,128)} %copy-done.4, f32[3,12,16,128]{3,2,1,0:T(8,128)} %collective-permute-done.1.n_ref, f32[64,128]{1,0:T(8,128)} %constant.28.clone.r_ref.refs_11_, ...), custom_call_target="tpu_custom_call" | custom-call | flops 228261888 | bytes 3867988 | tf_op jit(solution)/shard_map/pallas_call | solution.py:217
  37.1 10.5 %shard_map.131 = (f32[3,12,128,128]{3,2,1,0:T(8,128)}, f32[1,12,128,128]{3,2,1,0:T(8,128)}, f32[1,12,16,128]{3,2,1,0:T(8,128)}, f32[1,12,16,128]{3,2,1,0:T(8,128)}) custom-call(f32[3,12,128,128]{3,2,1,0:T(8,128)} %pad_maximum_fusion.u_ref, f32[3,12,16,128]{3,2,1,0:T(8,128)} %copy-done.4, f32[3,12,16,128]{3,2,1,0:T(8,128)} %collective-permute-done.1.n_ref, ...), custom_call_target="tpu_custom_call" | custom-call | flops 1822556160 | bytes 6488916 | tf_op jit(solution)/shard_map/pallas_call | solution.py:217
  48.5 3.8 %collective-permute-start.3 = (f32[1,12,16,128]{3,2,1,0:T(8,128)}, f32[1,12,16,128]{3,2,1,0:T(8,128)S(1)}, u32[]{:S(2)}, u32[]{:S(2)}) collective-permute-start(f32[1,12,16,128]{3,2,1,0:T(8,128)} %get-tuple-element.52), channel_id=1, source_target_pairs={{1,0},{2,1},{3,2},{4,3},{5,4},{6,5},{7,6},{0,7},{9,8},{10,9},{11,1... | collective-permute-start | bytes 294920 | tf_op jit(solution)/shard_map/ppermute | solution.py:289
  56.1 5.9 %shard_map.132 = (f32[1,12,128,128]{3,2,1,0:T(8,128)}, f32[1,12,128,128]{3,2,1,0:T(8,128)}, f32[1,12,16,128]{3,2,1,0:T(8,128)}, f32[1,12,16,128]{3,2,1,0:T(8,128)}) custom-call(f32[1,12,128,128]{3,2,1,0:T(8,128)} %get-tuple-element.50.a1_ref.refs_0_, f32[1,12,16,128]{3,2,1,0:T(8,128)} %copy-done.10, f32[1,12,16,128]{3,2,1,0:T(8,128)} %copy-done.12, ...), custom_call_target="tpu_custom_call" | custom-call | flops 607518720 | bytes 5309268 | tf_op jit(solution)/shard_map/pallas_call | solution.py:217
  62.7 4.1 %collective-permute-start.5 = (f32[1,12,16,128]{3,2,1,0:T(8,128)}, f32[1,12,16,128]{3,2,1,0:T(8,128)S(1)}, u32[]{:S(2)}, u32[]{:S(2)}) collective-permute-start(f32[1,12,16,128]{3,2,1,0:T(8,128)} %get-tuple-element.57), channel_id=1, source_target_pairs={{1,0},{2,1},{3,2},{4,3},{5,4},{6,5},{7,6},{0,7},{9,8},{10,9},{11,1... | collective-permute-start | bytes 294920 | tf_op jit(solution)/shard_map/ppermute | solution.py:289
  70.6 6.5 %shard_map.134 = (f32[12,64,128]{2,1,0:T(8,128)}, f32[12,64,128]{2,1,0:T(8,128)}) custom-call(f32[1,12,128,128]{3,2,1,0:T(8,128)} %get-tuple-element.54.a2_ref.refs_1_, f32[1,12,16,128]{3,2,1,0:T(8,128)} %copy-done.14, f32[1,12,16,128]{3,2,1,0:T(8,128)} %copy-done.16, f32[256,128]{1,0:T(8,128)} %constant.26.clone.l_ref, f32[128,128]{1,0:T(8,128)} %constant.25.clone.x_ref, ...), custom_call_target="tpu_custom_call" | custom-call | flops 607518720 | bytes 5145428 | tf_op jit(solution)/shard_map/pallas_call | solution.py:217
  79.2 4.4 %collective-permute-start.7 = (f32[12,8,128]{2,1,0:T(8,128)S(1)}, f32[12,8,128]{2,1,0:T(8,128)S(1)}, u32[]{:S(2)}, u32[]{:S(2)}) collective-permute-start(f32[12,8,128]{2,1,0:T(8,128)S(1)} %get-tuple-element.100), channel_id=1, source_target_pairs={{1,0},{2,1},{3,2},{4,3},{5,4},{6,5},{7,6},{0,7},{9,8},{10,9},{11,1... | collective-permute-start | bytes 147464 | tf_op jit(solution)/shard_map/ppermute | solution.py:289
  85.4 5.0 %collective-permute-done.6 = f32[12,8,128]{2,1,0:T(8,128)S(1)} collective-permute-done((f32[12,8,128]{2,1,0:T(8,128)S(1)}, f32[12,8,128]{2,1,0:T(8,128)S(1)}, u32[]{:S(2)}, u32[]{:S(2)}) %collective-permute-start.6) | collective-permute-done | bytes 49184 | tf_op jit(solution)/shard_map/ppermute | solution.py:288
  90.4 7.5 %all-gather.11.cloned.1.call-done = f32[48,64,128]{2,1,0:T(8,128)} async-done(((f32[12,64,128]{2,1,0:T(8,128)}), f32[48,64,128]{2,1,0:T(8,128)}) %all-gather.11.cloned.1.call-update) | async-done | bytes 1572880 | tf_op jit(solution)/shard_map/all_gather | solution.py:501
  98.0 3.6 %shard_map.135 = (f32[1,12,64,128]{3,2,1,0:T(8,128)}, f32[1,12,8,128]{3,2,1,0:T(8,128)}, f32[1,12,8,128]{3,2,1,0:T(8,128)}) custom-call(f32[1,12,64,128]{3,2,1,0:T(8,128)} %bitcast.43, f32[1,12,8,128]{3,2,1,0:T(8,128)} %bitcast.52, f32[1,12,8,128]{3,2,1,0:T(8,128)} %bitcast.50, f32[128,64]{1,0:T(8,128)} %constant.27.clone.l_ref, ...), custom_call_target="tpu_custom_call" | custom-call | flops 228261888 | bytes 4227924 | tf_op jit(solution)/shard_map/pallas_call | solution.py:217
  109.2 3.7 %shard_map.136 = (f32[1,12,64,128]{3,2,1,0:T(8,128)}, f32[1,12,8,128]{3,2,1,0:T(8,128)}, f32[1,12,8,128]{3,2,1,0:T(8,128)}) custom-call(f32[1,12,64,128]{3,2,1,0:T(8,128)} %get-tuple-element.62.w_ref.refs_5_, f32[1,12,8,128]{3,2,1,0:T(8,128)} %copy-done.21, f32[1,12,8,128]{3,2,1,0:T(8,128)} %copy-done.25, f32[128,64]{1,0:T(8,128)} %constant.27.clone.l_ref, ...), custom_call_target="tpu_custom_call" | custom-call | flops 228261888 | bytes 4227924 | tf_op jit(solution)/shard_map/pallas_call | solution.py:217
  114.0 3.7 %collective-permute-start.11 = (f32[1,12,8,128]{3,2,1,0:T(8,128)}, f32[1,12,8,128]{3,2,1,0:T(8,128)S(1)}, u32[]{:S(2)}, u32[]{:S(2)}) collective-permute-start(f32[1,12,8,128]{3,2,1,0:T(8,128)} %get-tuple-element.67), channel_id=1, source_target_pairs={{1,0},{2,1},{3,2},{4,3},{5,4},{6,5},{7,6},{0,7},{9,8},{10,9},{11,1... | collective-permute-start | bytes 147464 | tf_op jit(solution)/shard_map/ppermute | solution.py:289
  120.6 3.7 %shard_map.137 = (f32[1,12,64,128]{3,2,1,0:T(8,128)}, f32[1,12,8,128]{3,2,1,0:T(8,128)}, f32[1,12,8,128]{3,2,1,0:T(8,128)}) custom-call(f32[1,12,64,128]{3,2,1,0:T(8,128)} %get-tuple-element.65.w_ref.refs_6_, f32[1,12,8,128]{3,2,1,0:T(8,128)} %copy-done.22, f32[1,12,8,128]{3,2,1,0:T(8,128)} %copy-done.26, f32[128,64]{1,0:T(8,128)} %constant.27.clone.l_ref, ...), custom_call_target="tpu_custom_call" | custom-call | flops 228261888 | bytes 4227924 | tf_op jit(solution)/shard_map/pallas_call | solution.py:217
  124.3 4.7 %collective-permute-start.13 = (f32[1,12,8,128]{3,2,1,0:T(8,128)}, f32[1,12,8,128]{3,2,1,0:T(8,128)S(1)}, u32[]{:S(2)}, u32[]{:S(2)}) collective-permute-start(f32[1,12,8,128]{3,2,1,0:T(8,128)} %get-tuple-element.70), channel_id=1, source_target_pairs={{1,0},{2,1},{3,2},{4,3},{5,4},{6,5},{7,6},{0,7},{9,8},{10,9},{11,1... | collective-permute-start | bytes 147464 | tf_op jit(solution)/shard_map/ppermute | solution.py:289
  131.9 3.7 %shard_map.138 = (f32[1,12,64,128]{3,2,1,0:T(8,128)}, f32[1,12,8,128]{3,2,1,0:T(8,128)}, f32[1,12,8,128]{3,2,1,0:T(8,128)}) custom-call(f32[1,12,64,128]{3,2,1,0:T(8,128)} %get-tuple-element.68.w_ref.refs_7_, f32[1,12,8,128]{3,2,1,0:T(8,128)} %copy-done.18, f32[1,12,8,128]{3,2,1,0:T(8,128)} %copy-done.20, f32[128,64]{1,0:T(8,128)} %constant.27.clone.l_ref, ...), custom_call_target="tpu_custom_call" | custom-call | flops 228261888 | bytes 4227924 | tf_op jit(solution)/shard_map/pallas_call | solution.py:217
  136.5 6.7 %shard_map.139 = (f32[3,12,128,128]{3,2,1,0:T(8,128)}, f32[3,12,16,128]{3,2,1,0:T(8,128)}, f32[3,12,16,128]{3,2,1,0:T(8,128)}) custom-call(f32[1,12,128,128]{3,2,1,0:T(8,128)} %get-tuple-element.50.a1_ref.refs_0_, f32[1,12,128,128]{3,2,1,0:T(8,128)} %get-tuple-element.54.a2_ref.refs_1_, f32[1,12,64,128]{3,2,1,0:T(8,128)} %get-tuple-element.55.refs_2_, ...), custom_call_target="tpu_custom_call" | custom-call | flops 603979776 | bytes 8912904 | tf_op jit(solution)/shard_map/pallas_call | solution.py:217
  143.1 4.8 %collective-permute-start.16 = (f32[3,12,16,128]{3,2,1,0:T(8,128)}, f32[3,12,16,128]{3,2,1,0:T(8,128)S(1)}, u32[]{:S(2)}, u32[]{:S(2)}) collective-permute-start(f32[3,12,16,128]{3,2,1,0:T(8,128)} %get-tuple-element.74), channel_id=1, source_target_pairs={{1,0},{2,1},{3,2},{4,3},{5,4},{6,5},{7,6},{0,7},{9,8},{10,9},{11,1... | collective-permute-start | bytes 884744 | tf_op jit(solution)/shard_map/ppermute | solution.py:289
  147.9 5.3 %collective-permute-done.15.p_ref = f32[3,12,16,128]{3,2,1,0:T(8,128)S(1)} collective-permute-done((f32[3,12,16,128]{3,2,1,0:T(8,128)}, f32[3,12,16,128]{3,2,1,0:T(8,128)S(1)}, u32[]{:S(2)}, u32[]{:S(2)}) %collective-permute-start.15) | collective-permute-done | bytes 294944 | tf_op jit(solution)/shard_map/ppermute | solution.py:288
  156.1 4.8 %shard_map.143 = (f32[1,12,64,128]{3,2,1,0:T(8,128)}, f32[1,12,64,128]{3,2,1,0:T(8,128)}) custom-call(f32[3,12,128,128]{3,2,1,0:T(8,128)} %get-tuple-element.72.u_ref, f32[3,12,16,128]{3,2,1,0:T(8,128)} %copy-done.5, f32[3,12,16,128]{3,2,1,0:T(8,128)} %copy-done.6, f32[64,128]{1,0:T(8,128)} %constant.28.clone.r_ref.refs_11_, f32[8,16]{1,0:T(8,128)} %constant.30.clone.rp_ref, ...), custom_call_target="tpu_custom_call" | custom-call | flops 228261888 | bytes 3867988 | tf_op jit(solution)/shard_map/pallas_call | solution.py:217
  161.2 10.5 %shard_map.140 = (f32[3,12,128,128]{3,2,1,0:T(8,128)}, f32[1,12,128,128]{3,2,1,0:T(8,128)}, f32[1,12,16,128]{3,2,1,0:T(8,128)}, f32[1,12,16,128]{3,2,1,0:T(8,128)}) custom-call(f32[3,12,128,128]{3,2,1,0:T(8,128)} %get-tuple-element.72.u_ref, f32[3,12,16,128]{3,2,1,0:T(8,128)} %copy-done.5, f32[3,12,16,128]{3,2,1,0:T(8,128)} %copy-done.6, ...), custom_call_target="tpu_custom_call" | custom-call | flops 1822556160 | bytes 6488916 | tf_op jit(solution)/shard_map/pallas_call | solution.py:217
  172.0 4.3 %collective-permute-start.18 = (f32[1,12,16,128]{3,2,1,0:T(8,128)}, f32[1,12,16,128]{3,2,1,0:T(8,128)S(1)}, u32[]{:S(2)}, u32[]{:S(2)}) collective-permute-start(f32[1,12,16,128]{3,2,1,0:T(8,128)} %get-tuple-element.77), channel_id=1, source_target_pairs={{1,0},{2,1},{3,2},{4,3},{5,4},{6,5},{7,6},{0,7},{9,8},{10,9},{11,1... | collective-permute-start | bytes 294920 | tf_op jit(solution)/shard_map/ppermute | solution.py:289
  179.8 6.0 %shard_map.141 = (f32[1,12,128,128]{3,2,1,0:T(8,128)}, f32[1,12,128,128]{3,2,1,0:T(8,128)}, f32[1,12,16,128]{3,2,1,0:T(8,128)}, f32[1,12,16,128]{3,2,1,0:T(8,128)}) custom-call(f32[1,12,128,128]{3,2,1,0:T(8,128)} %get-tuple-element.75.a1_ref, f32[1,12,16,128]{3,2,1,0:T(8,128)} %copy-done.9, f32[1,12,16,128]{3,2,1,0:T(8,128)} %copy-done.11, ...), custom_call_target="tpu_custom_call" | custom-call | flops 607518720 | bytes 5309268 | tf_op jit(solution)/shard_map/pallas_call | solution.py:217
  185.8 4.8 %collective-permute-start.20 = (f32[1,12,16,128]{3,2,1,0:T(8,128)}, f32[1,12,16,128]{3,2,1,0:T(8,128)S(1)}, u32[]{:S(2)}, u32[]{:S(2)}) collective-permute-start(f32[1,12,16,128]{3,2,1,0:T(8,128)} %get-tuple-element.81), channel_id=1, source_target_pairs={{1,0},{2,1},{3,2},{4,3},{5,4},{6,5},{7,6},{0,7},{9,8},{10,9},{11,1... | collective-permute-start | bytes 294920 | tf_op jit(solution)/shard_map/ppermute | solution.py:289
  194.0 6.5 %shard_map.142 = (f32[12,64,128]{2,1,0:T(8,128)}, f32[12,64,128]{2,1,0:T(8,128)}) custom-call(f32[1,12,128,128]{3,2,1,0:T(8,128)} %get-tuple-element.79.a2_ref.refs_0_, f32[1,12,16,128]{3,2,1,0:T(8,128)} %copy-done.13, f32[1,12,16,128]{3,2,1,0:T(8,128)} %copy-done.15, f32[256,128]{1,0:T(8,128)} %constant.26.clone.l_ref, f32[128,128]{1,0:T(8,128)} %constant.25.clone.x_ref, ...), custom_call_target="tpu_custom_call" | custom-call | flops 607518720 | bytes 5145428 | tf_op jit(solution)/shard_map/pallas_call | solution.py:217
  200.5 23.6 %all-gather.15.cloned.1.call-done = f32[48,64,128]{2,1,0:T(8,128)} async-done(((f32[12,64,128]{2,1,0:T(8,128)}), f32[48,64,128]{2,1,0:T(8,128)}) %all-gather.15.cloned.1.call-update) | async-done | bytes 1572880 | tf_op jit(solution)/shard_map/all_gather | solution.py:501
  224.2 3.6 %shard_map.144 = (f32[1,12,64,128]{3,2,1,0:T(8,128)}, f32[1,12,8,128]{3,2,1,0:T(8,128)}, f32[1,12,8,128]{3,2,1,0:T(8,128)}) custom-call(f32[1,12,64,128]{3,2,1,0:T(8,128)} %bitcast.45, f32[1,12,8,128]{3,2,1,0:T(8,128)} %bitcast.53, f32[1,12,8,128]{3,2,1,0:T(8,128)} %bitcast.51, f32[128,64]{1,0:T(8,128)} %constant.27.clone.l_ref, ...), custom_call_target="tpu_custom_call" | custom-call | flops 228261888 | bytes 4227924 | tf_op jit(solution)/shard_map/pallas_call | solution.py:217
  235.4 3.7 %shard_map.145 = (f32[1,12,64,128]{3,2,1,0:T(8,128)}, f32[1,12,8,128]{3,2,1,0:T(8,128)}, f32[1,12,8,128]{3,2,1,0:T(8,128)}) custom-call(f32[1,12,64,128]{3,2,1,0:T(8,128)} %get-tuple-element.86.w_ref.refs_3_, f32[1,12,8,128]{3,2,1,0:T(8,128)} %copy-done.23, f32[1,12,8,128]{3,2,1,0:T(8,128)} %copy-done.27, f32[128,64]{1,0:T(8,128)} %constant.27.clone.l_ref, ...), custom_call_target="tpu_custom_call" | custom-call | flops 228261888 | bytes 4227924 | tf_op jit(solution)/shard_map/pallas_call | solution.py:217
  240.2 3.9 %collective-permute-start.24 = (f32[1,12,8,128]{3,2,1,0:T(8,128)}, f32[1,12,8,128]{3,2,1,0:T(8,128)S(1)}, u32[]{:S(2)}, u32[]{:S(2)}) collective-permute-start(f32[1,12,8,128]{3,2,1,0:T(8,128)} %get-tuple-element.91), channel_id=1, source_target_pairs={{1,0},{2,1},{3,2},{4,3},{5,4},{6,5},{7,6},{0,7},{9,8},{10,9},{11,1... | collective-permute-start | bytes 147464 | tf_op jit(solution)/shard_map/ppermute | solution.py:289
  246.8 3.7 %shard_map.146 = (f32[1,12,64,128]{3,2,1,0:T(8,128)}, f32[1,12,8,128]{3,2,1,0:T(8,128)}, f32[1,12,8,128]{3,2,1,0:T(8,128)}) custom-call(f32[1,12,64,128]{3,2,1,0:T(8,128)} %get-tuple-element.89.w_ref.refs_4_, f32[1,12,8,128]{3,2,1,0:T(8,128)} %copy-done.24, f32[1,12,8,128]{3,2,1,0:T(8,128)} %copy-done.28, f32[128,64]{1,0:T(8,128)} %constant.27.clone.l_ref, ...), custom_call_target="tpu_custom_call" | custom-call | flops 228261888 | bytes 4227924 | tf_op jit(solution)/shard_map/pallas_call | solution.py:217
  250.6 4.9 %collective-permute-start.26 = (f32[1,12,8,128]{3,2,1,0:T(8,128)}, f32[1,12,8,128]{3,2,1,0:T(8,128)S(1)}, u32[]{:S(2)}, u32[]{:S(2)}) collective-permute-start(f32[1,12,8,128]{3,2,1,0:T(8,128)} %get-tuple-element.94), channel_id=1, source_target_pairs={{1,0},{2,1},{3,2},{4,3},{5,4},{6,5},{7,6},{0,7},{9,8},{10,9},{11,1... | collective-permute-start | bytes 147464 | tf_op jit(solution)/shard_map/ppermute | solution.py:289
  258.3 3.7 %shard_map.147 = (f32[1,12,64,128]{3,2,1,0:T(8,128)}, f32[1,12,8,128]{3,2,1,0:T(8,128)}, f32[1,12,8,128]{3,2,1,0:T(8,128)}) custom-call(f32[1,12,64,128]{3,2,1,0:T(8,128)} %get-tuple-element.92.w_ref.refs_5_, f32[1,12,8,128]{3,2,1,0:T(8,128)} %copy-done.17, f32[1,12,8,128]{3,2,1,0:T(8,128)} %copy-done.19, f32[128,64]{1,0:T(8,128)} %constant.27.clone.l_ref, ...), custom_call_target="tpu_custom_call" | custom-call | flops 228261888 | bytes 4227924 | tf_op jit(solution)/shard_map/pallas_call | solution.py:217
  (128 shorter events, 74.4 us)
Async XLA Ops:
  7.2 83.3 %all-gather.9.cloned.1.call-start = ((), (), s32[]{:S(2)}) async-start(), calls=%async_computation | async-start | bytes 1966080 | tf_op jit(solution)/shard_map/all_gather | solution.py:492
  11.9 17.0 %collective-permute-start = (f32[3,12,16,128]{3,2,1,0:T(8,128)}, f32[3,12,16,128]{3,2,1,0:T(8,128)S(1)}, u32[]{:S(2)}, u32[]{:S(2)}) collective-permute-start(f32[3,12,16,128]{3,2,1,0:T(8,128)} %get-tuple-element.99), channel_id=1, source_target_pairs={{0,1},{1,2},{2,3},{3,4},{4,5},{5,6},{6,7},{7,0},{8,9},{9,10},{10,1... | collective-permute-start | bytes 884744 | tf_op jit(solution)/shard_map/ppermute | solution.py:288
  14.9 16.2 %collective-permute-start.1 = (f32[3,12,16,128]{3,2,1,0:T(8,128)}, f32[3,12,16,128]{3,2,1,0:T(8,128)}, u32[]{:S(2)}, u32[]{:S(2)}) collective-permute-start(f32[3,12,16,128]{3,2,1,0:T(8,128)} %get-tuple-element.98), channel_id=1, source_target_pairs={{1,0},{2,1},{3,2},{4,3},{5,4},{6,5},{7,6},{0,7},{9,8},{10,9},{11,1... | collective-permute-start | bytes 884744 | tf_op jit(solution)/shard_map/ppermute | solution.py:289
  35.9 62.0 %all-gather.11.cloned.1.call-start = ((), (), s32[]{:S(2)}) async-start(), calls=%async_computation.1 | async-start | bytes 1966080 | tf_op jit(solution)/shard_map/all_gather | solution.py:501
  47.6 7.6 %collective-permute-start.2 = (f32[1,12,16,128]{3,2,1,0:T(8,128)}, f32[1,12,16,128]{3,2,1,0:T(8,128)S(1)}, u32[]{:S(2)}, u32[]{:S(2)}) collective-permute-start(f32[1,12,16,128]{3,2,1,0:T(8,128)} %get-tuple-element.51), channel_id=1, source_target_pairs={{0,1},{1,2},{2,3},{3,4},{4,5},{5,6},{6,7},{7,0},{8,9},{9,10},{10,1... | collective-permute-start | bytes 294920 | tf_op jit(solution)/shard_map/ppermute | solution.py:288
  48.5 6.9 %collective-permute-start.3 = (f32[1,12,16,128]{3,2,1,0:T(8,128)}, f32[1,12,16,128]{3,2,1,0:T(8,128)S(1)}, u32[]{:S(2)}, u32[]{:S(2)}) collective-permute-start(f32[1,12,16,128]{3,2,1,0:T(8,128)} %get-tuple-element.52), channel_id=1, source_target_pairs={{1,0},{2,1},{3,2},{4,3},{5,4},{6,5},{7,6},{0,7},{9,8},{10,9},{11,1... | collective-permute-start | bytes 294920 | tf_op jit(solution)/shard_map/ppermute | solution.py:289
  62.0 7.6 %collective-permute-start.4 = (f32[1,12,16,128]{3,2,1,0:T(8,128)}, f32[1,12,16,128]{3,2,1,0:T(8,128)S(1)}, u32[]{:S(2)}, u32[]{:S(2)}) collective-permute-start(f32[1,12,16,128]{3,2,1,0:T(8,128)} %get-tuple-element.56), channel_id=1, source_target_pairs={{0,1},{1,2},{2,3},{3,4},{4,5},{5,6},{6,7},{7,0},{8,9},{9,10},{10,1... | collective-permute-start | bytes 294920 | tf_op jit(solution)/shard_map/ppermute | solution.py:288
  62.7 7.3 %collective-permute-start.5 = (f32[1,12,16,128]{3,2,1,0:T(8,128)}, f32[1,12,16,128]{3,2,1,0:T(8,128)S(1)}, u32[]{:S(2)}, u32[]{:S(2)}) collective-permute-start(f32[1,12,16,128]{3,2,1,0:T(8,128)} %get-tuple-element.57), channel_id=1, source_target_pairs={{1,0},{2,1},{3,2},{4,3},{5,4},{6,5},{7,6},{0,7},{9,8},{10,9},{11,1... | collective-permute-start | bytes 294920 | tf_op jit(solution)/shard_map/ppermute | solution.py:289
  77.1 123.4 %all-gather.13.cloned.1.call-start = ((), (), s32[]{:S(2)}) async-start(), calls=%async_computation.2 | async-start | bytes 1966080 | tf_op jit(solution)/shard_map/all_gather | solution.py:492
  77.2 58.4 %collective-permute-start.14 = (f32[1,12,128,128]{3,2,1,0:T(8,128)S(1)}, f32[1,12,128,128]{3,2,1,0:T(8,128)S(1)}, u32[]{:S(2)}, u32[]{:S(2)}) collective-permute-start(f32[1,12,128,128]{3,2,1,0:T(8,128)S(1)} %copy-done.2), channel_id=1, source_target_pairs={{0,8},{8,16},{16,24},{1,9},{9,17},{17,25},{2,10},{10,18},{18,26},{... | collective-permute-start | bytes 2359304 | tf_op jit(solution)/shard_map/ppermute | solution.py:504
  79.2 18.7 %copy-start = (f32[8,12,8,128]{3,0,2,1:T(8,128)}, f32[8,12,8,128]{3,0,2,1:T(8,128)S(1)}, u32[]{:S(2)}) copy-start(f32[8,12,8,128]{3,0,2,1:T(8,128)S(1)} %fusion.3) | copy-start | bytes 1179652
  79.2 6.2 %collective-permute-start.7 = (f32[12,8,128]{2,1,0:T(8,128)S(1)}, f32[12,8,128]{2,1,0:T(8,128)S(1)}, u32[]{:S(2)}, u32[]{:S(2)}) collective-permute-start(f32[12,8,128]{2,1,0:T(8,128)S(1)} %get-tuple-element.100), channel_id=1, source_target_pairs={{1,0},{2,1},{3,2},{4,3},{5,4},{6,5},{7,6},{0,7},{9,8},{10,9},{11,1... | collective-permute-start | bytes 147464 | tf_op jit(solution)/shard_map/ppermute | solution.py:289
  83.6 6.8 %collective-permute-start.6 = (f32[12,8,128]{2,1,0:T(8,128)S(1)}, f32[12,8,128]{2,1,0:T(8,128)S(1)}, u32[]{:S(2)}, u32[]{:S(2)}) collective-permute-start(f32[12,8,128]{2,1,0:T(8,128)S(1)} %get-tuple-element.101), channel_id=1, source_target_pairs={{0,1},{1,2},{2,3},{3,4},{4,5},{5,6},{6,7},{7,0},{8,9},{9,10},{10,1... | collective-permute-start | bytes 147464 | tf_op jit(solution)/shard_map/ppermute | solution.py:288
  101.6 7.0 %collective-permute-start.8 = (f32[1,12,8,128]{3,2,1,0:T(8,128)}, f32[1,12,8,128]{3,2,1,0:T(8,128)S(1)}, u32[]{:S(2)}, u32[]{:S(2)}) collective-permute-start(f32[1,12,8,128]{3,2,1,0:T(8,128)} %get-tuple-element.63), channel_id=1, source_target_pairs={{0,1},{1,2},{2,3},{3,4},{4,5},{5,6},{6,7},{7,0},{8,9},{9,10},{10,1... | collective-permute-start | bytes 147464 | tf_op jit(solution)/shard_map/ppermute | solution.py:288
  103.0 5.6 %collective-permute-start.9 = (f32[1,12,8,128]{3,2,1,0:T(8,128)}, f32[1,12,8,128]{3,2,1,0:T(8,128)S(1)}, u32[]{:S(2)}, u32[]{:S(2)}) collective-permute-start(f32[1,12,8,128]{3,2,1,0:T(8,128)} %get-tuple-element.64), channel_id=1, source_target_pairs={{1,0},{2,1},{3,2},{4,3},{5,4},{6,5},{7,6},{0,7},{9,8},{10,9},{11,1... | collective-permute-start | bytes 147464 | tf_op jit(solution)/shard_map/ppermute | solution.py:289
  112.9 7.0 %collective-permute-start.10 = (f32[1,12,8,128]{3,2,1,0:T(8,128)}, f32[1,12,8,128]{3,2,1,0:T(8,128)S(1)}, u32[]{:S(2)}, u32[]{:S(2)}) collective-permute-start(f32[1,12,8,128]{3,2,1,0:T(8,128)} %get-tuple-element.66), channel_id=1, source_target_pairs={{0,1},{1,2},{2,3},{3,4},{4,5},{5,6},{6,7},{7,0},{8,9},{9,10},{10,1... | collective-permute-start | bytes 147464 | tf_op jit(solution)/shard_map/ppermute | solution.py:288
  114.0 5.9 %collective-permute-start.11 = (f32[1,12,8,128]{3,2,1,0:T(8,128)}, f32[1,12,8,128]{3,2,1,0:T(8,128)S(1)}, u32[]{:S(2)}, u32[]{:S(2)}) collective-permute-start(f32[1,12,8,128]{3,2,1,0:T(8,128)} %get-tuple-element.67), channel_id=1, source_target_pairs={{1,0},{2,1},{3,2},{4,3},{5,4},{6,5},{7,6},{0,7},{9,8},{10,9},{11,1... | collective-permute-start | bytes 147464 | tf_op jit(solution)/shard_map/ppermute | solution.py:289
  124.2 7.0 %collective-permute-start.12 = (f32[1,12,8,128]{3,2,1,0:T(8,128)}, f32[1,12,8,128]{3,2,1,0:T(8,128)S(1)}, u32[]{:S(2)}, u32[]{:S(2)}) collective-permute-start(f32[1,12,8,128]{3,2,1,0:T(8,128)} %get-tuple-element.69), channel_id=1, source_target_pairs={{0,1},{1,2},{2,3},{3,4},{4,5},{5,6},{6,7},{7,0},{8,9},{9,10},{10,1... | collective-permute-start | bytes 147464 | tf_op jit(solution)/shard_map/ppermute | solution.py:288
  124.3 7.0 %collective-permute-start.13 = (f32[1,12,8,128]{3,2,1,0:T(8,128)}, f32[1,12,8,128]{3,2,1,0:T(8,128)S(1)}, u32[]{:S(2)}, u32[]{:S(2)}) collective-permute-start(f32[1,12,8,128]{3,2,1,0:T(8,128)} %get-tuple-element.70), channel_id=1, source_target_pairs={{1,0},{2,1},{3,2},{4,3},{5,4},{6,5},{7,6},{0,7},{9,8},{10,9},{11,1... | collective-permute-start | bytes 147464 | tf_op jit(solution)/shard_map/ppermute | solution.py:289
  143.1 10.1 %collective-permute-start.15 = (f32[3,12,16,128]{3,2,1,0:T(8,128)}, f32[3,12,16,128]{3,2,1,0:T(8,128)S(1)}, u32[]{:S(2)}, u32[]{:S(2)}) collective-permute-start(f32[3,12,16,128]{3,2,1,0:T(8,128)} %get-tuple-element.73), channel_id=1, source_target_pairs={{0,1},{1,2},{2,3},{3,4},{4,5},{5,6},{6,7},{7,0},{8,9},{9,10},{10,1... | collective-permute-start | bytes 884744 | tf_op jit(solution)/shard_map/ppermute | solution.py:288
  143.1 12.2 %collective-permute-start.16 = (f32[3,12,16,128]{3,2,1,0:T(8,128)}, f32[3,12,16,128]{3,2,1,0:T(8,128)S(1)}, u32[]{:S(2)}, u32[]{:S(2)}) collective-permute-start(f32[3,12,16,128]{3,2,1,0:T(8,128)} %get-tuple-element.74), channel_id=1, source_target_pairs={{1,0},{2,1},{3,2},{4,3},{5,4},{6,5},{7,6},{0,7},{9,8},{10,9},{11,1... | collective-permute-start | bytes 884744 | tf_op jit(solution)/shard_map/ppermute | solution.py:289
  160.9 63.3 %all-gather.15.cloned.1.call-start = ((), (), s32[]{:S(2)}) async-start(), calls=%async_computation.3 | async-start | bytes 1966080 | tf_op jit(solution)/shard_map/all_gather | solution.py:501
  171.6 7.5 %collective-permute-start.17 = (f32[1,12,16,128]{3,2,1,0:T(8,128)}, f32[1,12,16,128]{3,2,1,0:T(8,128)S(1)}, u32[]{:S(2)}, u32[]{:S(2)}) collective-permute-start(f32[1,12,16,128]{3,2,1,0:T(8,128)} %get-tuple-element.76), channel_id=1, source_target_pairs={{0,1},{1,2},{2,3},{3,4},{4,5},{5,6},{6,7},{7,0},{8,9},{9,10},{10,1... | collective-permute-start | bytes 294920 | tf_op jit(solution)/shard_map/ppermute | solution.py:288
  172.0 7.1 %collective-permute-start.18 = (f32[1,12,16,128]{3,2,1,0:T(8,128)}, f32[1,12,16,128]{3,2,1,0:T(8,128)S(1)}, u32[]{:S(2)}, u32[]{:S(2)}) collective-permute-start(f32[1,12,16,128]{3,2,1,0:T(8,128)} %get-tuple-element.77), channel_id=1, source_target_pairs={{1,0},{2,1},{3,2},{4,3},{5,4},{6,5},{7,6},{0,7},{9,8},{10,9},{11,1... | collective-permute-start | bytes 294920 | tf_op jit(solution)/shard_map/ppermute | solution.py:289
  185.8 7.5 %collective-permute-start.19 = (f32[1,12,16,128]{3,2,1,0:T(8,128)}, f32[1,12,16,128]{3,2,1,0:T(8,128)S(1)}, u32[]{:S(2)}, u32[]{:S(2)}) collective-permute-start(f32[1,12,16,128]{3,2,1,0:T(8,128)} %get-tuple-element.80), channel_id=1, source_target_pairs={{0,1},{1,2},{2,3},{3,4},{4,5},{5,6},{6,7},{7,0},{8,9},{9,10},{10,1... | collective-permute-start | bytes 294920 | tf_op jit(solution)/shard_map/ppermute | solution.py:288
  185.8 7.5 %collective-permute-start.20 = (f32[1,12,16,128]{3,2,1,0:T(8,128)}, f32[1,12,16,128]{3,2,1,0:T(8,128)S(1)}, u32[]{:S(2)}, u32[]{:S(2)}) collective-permute-start(f32[1,12,16,128]{3,2,1,0:T(8,128)} %get-tuple-element.81), channel_id=1, source_target_pairs={{1,0},{2,1},{3,2},{4,3},{5,4},{6,5},{7,6},{0,7},{9,8},{10,9},{11,1... | collective-permute-start | bytes 294920 | tf_op jit(solution)/shard_map/ppermute | solution.py:289
  227.8 7.0 %collective-permute-start.21 = (f32[1,12,8,128]{3,2,1,0:T(8,128)}, f32[1,12,8,128]{3,2,1,0:T(8,128)S(1)}, u32[]{:S(2)}, u32[]{:S(2)}) collective-permute-start(f32[1,12,8,128]{3,2,1,0:T(8,128)} %get-tuple-element.87), channel_id=1, source_target_pairs={{0,1},{1,2},{2,3},{3,4},{4,5},{5,6},{6,7},{7,0},{8,9},{9,10},{10,1... | collective-permute-start | bytes 147464 | tf_op jit(solution)/shard_map/ppermute | solution.py:288
  229.3 5.5 %collective-permute-start.22 = (f32[1,12,8,128]{3,2,1,0:T(8,128)}, f32[1,12,8,128]{3,2,1,0:T(8,128)S(1)}, u32[]{:S(2)}, u32[]{:S(2)}) collective-permute-start(f32[1,12,8,128]{3,2,1,0:T(8,128)} %get-tuple-element.88), channel_id=1, source_target_pairs={{1,0},{2,1},{3,2},{4,3},{5,4},{6,5},{7,6},{0,7},{9,8},{10,9},{11,1... | collective-permute-start | bytes 147464 | tf_op jit(solution)/shard_map/ppermute | solution.py:289
  239.1 7.0 %collective-permute-start.23 = (f32[1,12,8,128]{3,2,1,0:T(8,128)}, f32[1,12,8,128]{3,2,1,0:T(8,128)S(1)}, u32[]{:S(2)}, u32[]{:S(2)}) collective-permute-start(f32[1,12,8,128]{3,2,1,0:T(8,128)} %get-tuple-element.90), channel_id=1, source_target_pairs={{0,1},{1,2},{2,3},{3,4},{4,5},{5,6},{6,7},{7,0},{8,9},{9,10},{10,1... | collective-permute-start | bytes 147464 | tf_op jit(solution)/shard_map/ppermute | solution.py:288
  240.2 5.9 %collective-permute-start.24 = (f32[1,12,8,128]{3,2,1,0:T(8,128)}, f32[1,12,8,128]{3,2,1,0:T(8,128)S(1)}, u32[]{:S(2)}, u32[]{:S(2)}) collective-permute-start(f32[1,12,8,128]{3,2,1,0:T(8,128)} %get-tuple-element.91), channel_id=1, source_target_pairs={{1,0},{2,1},{3,2},{4,3},{5,4},{6,5},{7,6},{0,7},{9,8},{10,9},{11,1... | collective-permute-start | bytes 147464 | tf_op jit(solution)/shard_map/ppermute | solution.py:289
  250.5 7.2 %collective-permute-start.25 = (f32[1,12,8,128]{3,2,1,0:T(8,128)}, f32[1,12,8,128]{3,2,1,0:T(8,128)S(1)}, u32[]{:S(2)}, u32[]{:S(2)}) collective-permute-start(f32[1,12,8,128]{3,2,1,0:T(8,128)} %get-tuple-element.93), channel_id=1, source_target_pairs={{0,1},{1,2},{2,3},{3,4},{4,5},{5,6},{6,7},{7,0},{8,9},{9,10},{10,1... | collective-permute-start | bytes 147464 | tf_op jit(solution)/shard_map/ppermute | solution.py:288
  250.6 7.1 %collective-permute-start.26 = (f32[1,12,8,128]{3,2,1,0:T(8,128)}, f32[1,12,8,128]{3,2,1,0:T(8,128)S(1)}, u32[]{:S(2)}, u32[]{:S(2)}) collective-permute-start(f32[1,12,8,128]{3,2,1,0:T(8,128)} %get-tuple-element.94), channel_id=1, source_target_pairs={{1,0},{2,1},{3,2},{4,3},{5,4},{6,5},{7,6},{0,7},{9,8},{10,9},{11,1... | collective-permute-start | bytes 147464 | tf_op jit(solution)/shard_map/ppermute | solution.py:289
  (31 other events, 71.1 us)
Sparse Core Ops, SparseCore 0:
  36.0 20.2 all-gather.8
  77.2 20.6 all-gather.10
  161.0 23.3 all-gather.12
  200.6 23.4 all-gather.14

commit v9 on v8

--- a/solution.py
+++ b/solution.py
@@ -328,7 +328,7 @@
         lax.fori_loop(0, fields, body, 0)
 
     def ending_kernel(a2_ref, p_ref, n_ref, l_ref, x_ref, zc_ref, rx_ref, ra_ref, en_ref,
-                      f_ref, g1_ref, r_ref, rint_ref, c1_ref, g2_ref, s_ref):
+                      f_ref, g1_ref, r_ref, base_ref, rint_ref, c1_ref, g2_ref, s_ref):
         tendency_into(g2_ref, a2_ref, p_ref, n_ref, l_ref, x_ref, zc_ref, rx_ref, ra_ref,
                       en_ref, s_ref, fine_elem)
 
@@ -342,6 +342,8 @@
             wide = dot(rm, lanes([src_ref[lead_index, f] for f in range(fields)]))
             for f, part in enumerate(unlanes(wide, columns)):
                 dst[f] = part
+        for f in range(fields):
+            rint_ref[f] = rint_ref[f] - STEP * base_ref[0, f]
 
     def base_kernel(u_ref, p_ref, n_ref, r_ref, rp_ref, l_ref, x_ref, zc_ref, rx_ref, ra_ref,
                     en_ref, out_ref, c0_ref, bp_ref, bn_ref, s_ref):
@@ -354,12 +356,12 @@
                       en_ref, s_ref, coarse_elem)
 
     def chain_kernel(w_ref, p_ref, n_ref, l_ref, x_ref, zc_ref, rx_ref, ra_ref, en_ref,
-                     base_ref, rint_ref, out_ref, h_ref, t_ref, g_ref, s_ref):
+                     rint_ref, out_ref, h_ref, t_ref, g_ref, s_ref):
         tendency_into(g_ref, w_ref, p_ref, n_ref, l_ref, x_ref, zc_ref, rx_ref, ra_ref,
                       en_ref, s_ref, coarse_elem)
 
         def body(f, carry):
-            value = w_ref[0, f] + STEP * (g_ref[0, f] - base_ref[0, 0, f]) + rint_ref[0, 0, f]
+            value = w_ref[0, f] + STEP * g_ref[0, f] + rint_ref[0, 0, f]
             out_ref[0, f] = value
             h_ref[0, f] = value[:coarse_rows]
             t_ref[0, f] = value[coarse_span - coarse_rows:]
@@ -436,19 +438,19 @@
     fine_plane = jax.ShapeDtypeStruct((1, fields, rows, columns), f32)
     node_planes = jax.ShapeDtypeStruct((3, fields, rows, columns), f32)
 
-    def coarse_step(w, w_halo, base_all, rint_all, n):
+    def coarse_step(w, w_halo, rint_all, n):
         def section_block():
             return pl.BlockSpec((1, 1, fields, coarse_span, columns), lambda i: (n, 0, 0, 0, 0),
                                 memory_space=pltpu.VMEM)
 
         return call(
             chain_kernel,
-            (w, w_halo[0], w_halo[1], lop_coarse, xt) + coarse_scalars + (base_all, rint_all),
-            (False,) * 5 + scalar_kinds + (False, False),
+            (w, w_halo[0], w_halo[1], lop_coarse, xt) + coarse_scalars + (rint_all,),
+            (False,) * 5 + scalar_kinds + (False,),
             (coarse_one, plane_one, plane_one),
             [pltpu.VMEM((1, fields, coarse_span, columns), f32), coarse_scratch(1)],
             *coarse_cost,
-            blocks={9: section_block(), 10: section_block()},
+            blocks={9: section_block()},
         )
 
     hop_pairs = [(d, d + 1) for d in range(sections - 1)]
@@ -489,11 +491,10 @@
              pltpu.VMEM((1, fields, coarse_rows, columns), f32), coarse_scratch(1)],
             *coarse_cost,
         )
-        base_all = lax.all_gather(base, "tm")
         rint, c1 = call(
             ending_kernel,
-            (a2, a2_prev, a2_next, lop_fine, xt) + scalars + (f_all, g1, rmat),
-            (False,) * 5 + scalar_kinds + (False,) * 3,
+            (a2, a2_prev, a2_next, lop_fine, xt) + scalars + (f_all, g1, rmat, base),
+            (False,) * 5 + scalar_kinds + (False,) * 4,
             (coarse_state, coarse_state),
             [pltpu.VMEM((1, fields, span, columns), f32), fine_scratch(1)],
             *fine_cost,
@@ -506,7 +507,7 @@
         w_halo = (start_halo[0][None], start_halo[1][None])
         chain = [w]
         for n in range(sections):
-            w, head, tail = coarse_step(w, w_halo, base_all, rint_all, n)
+            w, head, tail = coarse_step(w, w_halo, rint_all, n)
             chain.append(w)
             if n + 1 < sections:
                 w_halo = swap(head, tail)

time: 273 us -> 262 us (0.960)
  waiting for transfers between devices: 80.3 us -> 72.8 us
  starting transfers between devices: 65 us -> 62.1 us
    ppermute x13, waiting for transfers between devices: 42.4 us -> 33.5 us  [swap(): lax.ppermute(tail, 'space', [(i, (i + 1) % space_n) for i in range(space_...]
    ppermute x13, starting transfers between devices: 10.1 us -> 6.88 us  [swap(): lax.ppermute(tail, 'space', [(i, (i + 1) % space_n) for i in range(space_...]
    ppermute x13, waiting for transfers between devices: 6.67 us -> 9.42 us  [swap(): lax.ppermute(head, 'space', [((i + 1) % space_n, i) for i in range(space_...]
  transfers between devices with their start and end apart: 31 -> 29, of which waited for: 21 -> 17; matrix products, arithmetic and copies ran while one was open for 2% -> 2% of each run, Pallas kernels for 22% -> 9%
where the time goes in v9:
time: 262 us; the launch traced here: 261 us
  Pallas kernels  94 us (36%)
  waiting for transfers between devices  72.8 us (28%)
  starting transfers between devices  62.1 us (24%)
  local copies, waits for them, and re-layouts  14.8 us (6%)
  between operations  14.3 us (5%)
    pallas_call x18, Pallas kernels, call(): pl.pallas_call(kernel, out_shape=outs, in_specs=[blocks[i] if blocks is n...  94 us
    ppermute x13, starting transfers between devices, swap(): lax.ppermute(head, 'space', [((i + 1) % space_n, i) for i in range(space_...  53.6 us
    ppermute x13, waiting for transfers between devices, swap(): lax.ppermute(tail, 'space', [(i, (i + 1) % space_n) for i in range(space_...  33.5 us
    all_gather x2, waiting for transfers between devices, per_device(): rint_all = lax.all_gather(rint[None], 'tm')  29.8 us
    ppermute x13, waiting for transfers between devices, swap(): lax.ppermute(head, 'space', [((i + 1) % space_n, i) for i in range(space_...  9.42 us
    unnamed x65, local copies, waits for them, and re-layouts  8.75 us
    ppermute x13, starting transfers between devices, swap(): lax.ppermute(tail, 'space', [(i, (i + 1) % space_n) for i in range(space_...  6.88 us
  transfers between devices with their start and end apart: 29, of which 17 were waited for; matrix products, arithmetic and copies ran while one was open for 2% of the time, Pallas kernels for 9%

profile of v9, /device:TPU:0, one launch (start us, length us, event | category | flops | bytes accessed | tf_op | source)
XLA Modules:
  0.0 261.0 jit_solution(9876037293676328519)
XLA Ops:
  11.9 6.0 %collective-permute-start.1 = (f32[3,12,16,128]{3,2,1,0:T(8,128)}, f32[3,12,16,128]{3,2,1,0:T(8,128)S(1)}, u32[]{:S(2)}, u32[]{:S(2)}) collective-permute-start(f32[3,12,16,128]{3,2,1,0:T(8,128)} %get-tuple-element.98), channel_id=1, source_target_pairs={{1,0},{2,1},{3,2},{4,3},{5,4},{6,5},{7,6},{0,7},{9,8},{10,9},{11,1... | collective-permute-start | bytes 884744 | tf_op jit(solution)/shard_map/ppermute | solution.py:289
  21.4 4.2 %collective-permute-done.1.n_ref = f32[3,12,16,128]{3,2,1,0:T(8,128)S(1)} collective-permute-done((f32[3,12,16,128]{3,2,1,0:T(8,128)}, f32[3,12,16,128]{3,2,1,0:T(8,128)S(1)}, u32[]{:S(2)}, u32[]{:S(2)}) %collective-permute-start.1) | collective-permute-done | bytes 294944 | tf_op jit(solution)/shard_map/ppermute | solution.py:289
  25.6 4.9 %collective-permute-done.p_ref = f32[3,12,16,128]{3,2,1,0:T(8,128)} collective-permute-done((f32[3,12,16,128]{3,2,1,0:T(8,128)}, f32[3,12,16,128]{3,2,1,0:T(8,128)}, u32[]{:S(2)}, u32[]{:S(2)}) %collective-permute-start) | collective-permute-done | bytes 294944 | tf_op jit(solution)/shard_map/ppermute | solution.py:288
  30.5 10.5 %shard_map.131 = (f32[3,12,128,128]{3,2,1,0:T(8,128)}, f32[1,12,128,128]{3,2,1,0:T(8,128)}, f32[1,12,16,128]{3,2,1,0:T(8,128)}, f32[1,12,16,128]{3,2,1,0:T(8,128)}) custom-call(f32[3,12,128,128]{3,2,1,0:T(8,128)} %pad_maximum_fusion.u_ref, f32[3,12,16,128]{3,2,1,0:T(8,128)} %collective-permute-done.p_ref, f32[3,12,16,128]{3,2,1,0:T(8,128)} %copy-done.4, ...), custom_call_target="tpu_custom_call" | custom-call | flops 1822556160 | bytes 6488916 | tf_op jit(solution)/shard_map/pallas_call | solution.py:217
  50.3 5.9 %shard_map.132 = (f32[1,12,128,128]{3,2,1,0:T(8,128)}, f32[1,12,128,128]{3,2,1,0:T(8,128)}, f32[1,12,16,128]{3,2,1,0:T(8,128)}, f32[1,12,16,128]{3,2,1,0:T(8,128)}) custom-call(f32[1,12,128,128]{3,2,1,0:T(8,128)} %get-tuple-element.50.a1_ref.refs_0_, f32[1,12,16,128]{3,2,1,0:T(8,128)} %copy-done.10, f32[1,12,16,128]{3,2,1,0:T(8,128)} %copy-done.12, ...), custom_call_target="tpu_custom_call" | custom-call | flops 607518720 | bytes 5309268 | tf_op jit(solution)/shard_map/pallas_call | solution.py:217
  56.5 4.4 %collective-permute-start.5 = (f32[1,12,16,128]{3,2,1,0:T(8,128)}, f32[1,12,16,128]{3,2,1,0:T(8,128)S(1)}, u32[]{:S(2)}, u32[]{:S(2)}) collective-permute-start(f32[1,12,16,128]{3,2,1,0:T(8,128)} %get-tuple-element.57), channel_id=1, source_target_pairs={{1,0},{2,1},{3,2},{4,3},{5,4},{6,5},{7,6},{0,7},{9,8},{10,9},{11,1... | collective-permute-start | bytes 294920 | tf_op jit(solution)/shard_map/ppermute | solution.py:289
  62.1 4.8 %shard_map.133 = (f32[1,12,64,128]{3,2,1,0:T(8,128)}, f32[1,12,64,128]{3,2,1,0:T(8,128)}) custom-call(f32[3,12,128,128]{3,2,1,0:T(8,128)} %pad_maximum_fusion.u_ref, f32[3,12,16,128]{3,2,1,0:T(8,128)} %collective-permute-done.p_ref, f32[3,12,16,128]{3,2,1,0:T(8,128)} %copy-done.4, f32[64,128]{1,0:T(8,128)} %constant.28.clone.r_ref.refs_11_, ...), custom_call_target="tpu_custom_call" | custom-call | flops 228261888 | bytes 3867988 | tf_op jit(solution)/shard_map/pallas_call | solution.py:217
  67.6 6.6 %shard_map.134 = (f32[12,64,128]{2,1,0:T(8,128)}, f32[12,64,128]{2,1,0:T(8,128)}) custom-call(f32[1,12,128,128]{3,2,1,0:T(8,128)} %get-tuple-element.54.a2_ref.refs_1_, f32[1,12,16,128]{3,2,1,0:T(8,128)} %copy-done.13, f32[1,12,16,128]{3,2,1,0:T(8,128)} %copy-done.14, f32[256,128]{1,0:T(8,128)} %constant.26.clone.l_ref, f32[128,128]{1,0:T(8,128)} %constant.25.clone.x_ref, ...), custom_call_target="tpu_custom_call" | custom-call | flops 607518720 | bytes 5538644 | tf_op jit(solution)/shard_map/pallas_call | solution.py:217
  80.5 4.2 %collective-permute-done.6 = f32[12,8,128]{2,1,0:T(8,128)S(1)} collective-permute-done((f32[12,8,128]{2,1,0:T(8,128)S(1)}, f32[12,8,128]{2,1,0:T(8,128)S(1)}, u32[]{:S(2)}, u32[]{:S(2)}) %collective-permute-start.6) | collective-permute-done | bytes 49184 | tf_op jit(solution)/shard_map/ppermute | solution.py:288
  84.7 8.2 %all-gather.5.cloned.1.call-done = f32[48,64,128]{2,1,0:T(8,128)} async-done(((f32[12,64,128]{2,1,0:T(8,128)}), f32[48,64,128]{2,1,0:T(8,128)}) %all-gather.5.cloned.1.call-update) | async-done | bytes 1572880 | tf_op jit(solution)/shard_map/all_gather | solution.py:502
  97.1 4.0 %collective-permute-start.9 = (f32[1,12,8,128]{3,2,1,0:T(8,128)}, f32[1,12,8,128]{3,2,1,0:T(8,128)S(1)}, u32[]{:S(2)}, u32[]{:S(2)}) collective-permute-start(f32[1,12,8,128]{3,2,1,0:T(8,128)} %get-tuple-element.64), channel_id=1, source_target_pairs={{1,0},{2,1},{3,2},{4,3},{5,4},{6,5},{7,6},{0,7},{9,8},{10,9},{11,1... | collective-permute-start | bytes 147464 | tf_op jit(solution)/shard_map/ppermute | solution.py:289
  104.0 3.5 %shard_map.136 = (f32[1,12,64,128]{3,2,1,0:T(8,128)}, f32[1,12,8,128]{3,2,1,0:T(8,128)}, f32[1,12,8,128]{3,2,1,0:T(8,128)}) custom-call(f32[1,12,64,128]{3,2,1,0:T(8,128)} %get-tuple-element.62.w_ref.refs_5_, f32[1,12,8,128]{3,2,1,0:T(8,128)} %copy-done.20, f32[1,12,8,128]{3,2,1,0:T(8,128)} %copy-done.25, f32[128,64]{1,0:T(8,128)} %constant.27.clone.l_ref, ...), custom_call_target="tpu_custom_call" | custom-call | flops 228261888 | bytes 2655060 | tf_op jit(solution)/shard_map/pallas_call | solution.py:217
  108.0 4.3 %collective-permute-start.11 = (f32[1,12,8,128]{3,2,1,0:T(8,128)}, f32[1,12,8,128]{3,2,1,0:T(8,128)S(1)}, u32[]{:S(2)}, u32[]{:S(2)}) collective-permute-start(f32[1,12,8,128]{3,2,1,0:T(8,128)} %get-tuple-element.67), channel_id=1, source_target_pairs={{1,0},{2,1},{3,2},{4,3},{5,4},{6,5},{7,6},{0,7},{9,8},{10,9},{11,1... | collective-permute-start | bytes 147464 | tf_op jit(solution)/shard_map/ppermute | solution.py:289
  115.2 3.6 %shard_map.137 = (f32[1,12,64,128]{3,2,1,0:T(8,128)}, f32[1,12,8,128]{3,2,1,0:T(8,128)}, f32[1,12,8,128]{3,2,1,0:T(8,128)}) custom-call(f32[1,12,64,128]{3,2,1,0:T(8,128)} %get-tuple-element.65.w_ref.refs_6_, f32[1,12,8,128]{3,2,1,0:T(8,128)} %copy-done.21, f32[1,12,8,128]{3,2,1,0:T(8,128)} %copy-done.26, f32[128,64]{1,0:T(8,128)} %constant.27.clone.l_ref, ...), custom_call_target="tpu_custom_call" | custom-call | flops 228261888 | bytes 2655060 | tf_op jit(solution)/shard_map/pallas_call | solution.py:217
  118.8 4.8 %collective-permute-start.13 = (f32[1,12,8,128]{3,2,1,0:T(8,128)}, f32[1,12,8,128]{3,2,1,0:T(8,128)S(1)}, u32[]{:S(2)}, u32[]{:S(2)}) collective-permute-start(f32[1,12,8,128]{3,2,1,0:T(8,128)} %get-tuple-element.70), channel_id=1, source_target_pairs={{1,0},{2,1},{3,2},{4,3},{5,4},{6,5},{7,6},{0,7},{9,8},{10,9},{11,1... | collective-permute-start | bytes 147464 | tf_op jit(solution)/shard_map/ppermute | solution.py:289
  126.4 3.5 %shard_map.138 = (f32[1,12,64,128]{3,2,1,0:T(8,128)}, f32[1,12,8,128]{3,2,1,0:T(8,128)}, f32[1,12,8,128]{3,2,1,0:T(8,128)}) custom-call(f32[1,12,64,128]{3,2,1,0:T(8,128)} %get-tuple-element.68.w_ref.refs_7_, f32[1,12,8,128]{3,2,1,0:T(8,128)} %copy-done.18, f32[1,12,8,128]{3,2,1,0:T(8,128)} %copy-done.22, f32[128,64]{1,0:T(8,128)} %constant.27.clone.l_ref, ...), custom_call_target="tpu_custom_call" | custom-call | flops 228261888 | bytes 2655060 | tf_op jit(solution)/shard_map/pallas_call | solution.py:217
  130.9 6.7 %shard_map.139 = (f32[3,12,128,128]{3,2,1,0:T(8,128)}, f32[3,12,16,128]{3,2,1,0:T(8,128)}, f32[3,12,16,128]{3,2,1,0:T(8,128)}) custom-call(f32[1,12,128,128]{3,2,1,0:T(8,128)} %get-tuple-element.50.a1_ref.refs_0_, f32[1,12,128,128]{3,2,1,0:T(8,128)} %get-tuple-element.54.a2_ref.refs_1_, f32[1,12,64,128]{3,2,1,0:T(8,128)} %get-tuple-element.55.refs_2_, ...), custom_call_target="tpu_custom_call" | custom-call | flops 603979776 | bytes 8912904 | tf_op jit(solution)/shard_map/pallas_call | solution.py:217
  137.6 4.8 %collective-permute-start.16 = (f32[3,12,16,128]{3,2,1,0:T(8,128)}, f32[3,12,16,128]{3,2,1,0:T(8,128)S(1)}, u32[]{:S(2)}, u32[]{:S(2)}) collective-permute-start(f32[3,12,16,128]{3,2,1,0:T(8,128)} %get-tuple-element.74), channel_id=1, source_target_pairs={{1,0},{2,1},{3,2},{4,3},{5,4},{6,5},{7,6},{0,7},{9,8},{10,9},{11,1... | collective-permute-start | bytes 884744 | tf_op jit(solution)/shard_map/ppermute | solution.py:289
  142.3 5.3 %collective-permute-done.15.p_ref = f32[3,12,16,128]{3,2,1,0:T(8,128)S(1)} collective-permute-done((f32[3,12,16,128]{3,2,1,0:T(8,128)}, f32[3,12,16,128]{3,2,1,0:T(8,128)S(1)}, u32[]{:S(2)}, u32[]{:S(2)}) %collective-permute-start.15) | collective-permute-done | bytes 294944 | tf_op jit(solution)/shard_map/ppermute | solution.py:288
  150.5 10.5 %shard_map.140 = (f32[3,12,128,128]{3,2,1,0:T(8,128)}, f32[1,12,128,128]{3,2,1,0:T(8,128)}, f32[1,12,16,128]{3,2,1,0:T(8,128)}, f32[1,12,16,128]{3,2,1,0:T(8,128)}) custom-call(f32[3,12,128,128]{3,2,1,0:T(8,128)} %get-tuple-element.72.u_ref, f32[3,12,16,128]{3,2,1,0:T(8,128)} %copy-done.5, f32[3,12,16,128]{3,2,1,0:T(8,128)} %copy-done.6, ...), custom_call_target="tpu_custom_call" | custom-call | flops 1822556160 | bytes 6488916 | tf_op jit(solution)/shard_map/pallas_call | solution.py:217
  161.4 4.4 %collective-permute-start.18 = (f32[1,12,16,128]{3,2,1,0:T(8,128)}, f32[1,12,16,128]{3,2,1,0:T(8,128)S(1)}, u32[]{:S(2)}, u32[]{:S(2)}) collective-permute-start(f32[1,12,16,128]{3,2,1,0:T(8,128)} %get-tuple-element.77), channel_id=1, source_target_pairs={{1,0},{2,1},{3,2},{4,3},{5,4},{6,5},{7,6},{0,7},{9,8},{10,9},{11,1... | collective-permute-start | bytes 294920 | tf_op jit(solution)/shard_map/ppermute | solution.py:289
  169.2 5.9 %shard_map.141 = (f32[1,12,128,128]{3,2,1,0:T(8,128)}, f32[1,12,128,128]{3,2,1,0:T(8,128)}, f32[1,12,16,128]{3,2,1,0:T(8,128)}, f32[1,12,16,128]{3,2,1,0:T(8,128)}) custom-call(f32[1,12,128,128]{3,2,1,0:T(8,128)} %get-tuple-element.75.a1_ref, f32[1,12,16,128]{3,2,1,0:T(8,128)} %copy-done.9, f32[1,12,16,128]{3,2,1,0:T(8,128)} %copy-done.11, ...), custom_call_target="tpu_custom_call" | custom-call | flops 607518720 | bytes 5309268 | tf_op jit(solution)/shard_map/pallas_call | solution.py:217
  175.1 4.9 %collective-permute-start.20 = (f32[1,12,16,128]{3,2,1,0:T(8,128)}, f32[1,12,16,128]{3,2,1,0:T(8,128)S(1)}, u32[]{:S(2)}, u32[]{:S(2)}) collective-permute-start(f32[1,12,16,128]{3,2,1,0:T(8,128)} %get-tuple-element.81), channel_id=1, source_target_pairs={{1,0},{2,1},{3,2},{4,3},{5,4},{6,5},{7,6},{0,7},{9,8},{10,9},{11,1... | collective-permute-start | bytes 294920 | tf_op jit(solution)/shard_map/ppermute | solution.py:289
  180.0 4.8 %shard_map.142 = (f32[1,12,64,128]{3,2,1,0:T(8,128)}, f32[1,12,64,128]{3,2,1,0:T(8,128)}) custom-call(f32[3,12,128,128]{3,2,1,0:T(8,128)} %get-tuple-element.72.u_ref, f32[3,12,16,128]{3,2,1,0:T(8,128)} %copy-done.5, f32[3,12,16,128]{3,2,1,0:T(8,128)} %copy-done.6, f32[64,128]{1,0:T(8,128)} %constant.28.clone.r_ref.refs_11_, f32[8,16]{1,0:T(8,128)} %constant.30.clone.rp_ref, ...), custom_call_target="tpu_custom_call" | custom-call | flops 228261888 | bytes 3867988 | tf_op jit(solution)/shard_map/pallas_call | solution.py:217
  185.4 6.6 %shard_map.143 = (f32[12,64,128]{2,1,0:T(8,128)}, f32[12,64,128]{2,1,0:T(8,128)}) custom-call(f32[1,12,128,128]{3,2,1,0:T(8,128)} %get-tuple-element.79.a2_ref.refs_0_, f32[1,12,16,128]{3,2,1,0:T(8,128)} %copy-done.15, f32[1,12,16,128]{3,2,1,0:T(8,128)} %copy-done.16, f32[256,128]{1,0:T(8,128)} %constant.26.clone.l_ref, f32[128,128]{1,0:T(8,128)} %constant.25.clone.x_ref, ...), custom_call_target="tpu_custom_call" | custom-call | flops 607518720 | bytes 5538644 | tf_op jit(solution)/shard_map/pallas_call | solution.py:217
  192.0 21.7 %all-gather.7.cloned.1.call-done = f32[48,64,128]{2,1,0:T(8,128)} async-done(((f32[12,64,128]{2,1,0:T(8,128)}), f32[48,64,128]{2,1,0:T(8,128)}) %all-gather.7.cloned.1.call-update) | async-done | bytes 1572880 | tf_op jit(solution)/shard_map/all_gather | solution.py:502
  213.6 3.5 %shard_map.144 = (f32[1,12,64,128]{3,2,1,0:T(8,128)}, f32[1,12,8,128]{3,2,1,0:T(8,128)}, f32[1,12,8,128]{3,2,1,0:T(8,128)}) custom-call(f32[1,12,64,128]{3,2,1,0:T(8,128)} %bitcast.35, f32[1,12,8,128]{3,2,1,0:T(8,128)} %bitcast.43, f32[1,12,8,128]{3,2,1,0:T(8,128)} %bitcast.41, f32[128,64]{1,0:T(8,128)} %constant.27.clone.l_ref, ...), custom_call_target="tpu_custom_call" | custom-call | flops 228261888 | bytes 2655060 | tf_op jit(solution)/shard_map/pallas_call | solution.py:217
  224.8 3.5 %shard_map.145 = (f32[1,12,64,128]{3,2,1,0:T(8,128)}, f32[1,12,8,128]{3,2,1,0:T(8,128)}, f32[1,12,8,128]{3,2,1,0:T(8,128)}) custom-call(f32[1,12,64,128]{3,2,1,0:T(8,128)} %get-tuple-element.86.w_ref.refs_3_, f32[1,12,8,128]{3,2,1,0:T(8,128)} %copy-done.23, f32[1,12,8,128]{3,2,1,0:T(8,128)} %copy-done.27, f32[128,64]{1,0:T(8,128)} %constant.27.clone.l_ref, ...), custom_call_target="tpu_custom_call" | custom-call | flops 228261888 | bytes 2655060 | tf_op jit(solution)/shard_map/pallas_call | solution.py:217
  229.5 3.6 %collective-permute-start.24 = (f32[1,12,8,128]{3,2,1,0:T(8,128)}, f32[1,12,8,128]{3,2,1,0:T(8,128)S(1)}, u32[]{:S(2)}, u32[]{:S(2)}) collective-permute-start(f32[1,12,8,128]{3,2,1,0:T(8,128)} %get-tuple-element.91), channel_id=1, source_target_pairs={{1,0},{2,1},{3,2},{4,3},{5,4},{6,5},{7,6},{0,7},{9,8},{10,9},{11,1... | collective-permute-start | bytes 147464 | tf_op jit(solution)/shard_map/ppermute | solution.py:289
  236.0 3.5 %shard_map.146 = (f32[1,12,64,128]{3,2,1,0:T(8,128)}, f32[1,12,8,128]{3,2,1,0:T(8,128)}, f32[1,12,8,128]{3,2,1,0:T(8,128)}) custom-call(f32[1,12,64,128]{3,2,1,0:T(8,128)} %get-tuple-element.89.w_ref.refs_4_, f32[1,12,8,128]{3,2,1,0:T(8,128)} %copy-done.24, f32[1,12,8,128]{3,2,1,0:T(8,128)} %copy-done.28, f32[128,64]{1,0:T(8,128)} %constant.27.clone.l_ref, ...), custom_call_target="tpu_custom_call" | custom-call | flops 228261888 | bytes 2655060 | tf_op jit(solution)/shard_map/pallas_call | solution.py:217
  239.7 4.6 %collective-permute-start.26 = (f32[1,12,8,128]{3,2,1,0:T(8,128)}, f32[1,12,8,128]{3,2,1,0:T(8,128)S(1)}, u32[]{:S(2)}, u32[]{:S(2)}) collective-permute-start(f32[1,12,8,128]{3,2,1,0:T(8,128)} %get-tuple-element.94), channel_id=1, source_target_pairs={{1,0},{2,1},{3,2},{4,3},{5,4},{6,5},{7,6},{0,7},{9,8},{10,9},{11,1... | collective-permute-start | bytes 147464 | tf_op jit(solution)/shard_map/ppermute | solution.py:289
  247.2 3.5 %shard_map.147 = (f32[1,12,64,128]{3,2,1,0:T(8,128)}, f32[1,12,8,128]{3,2,1,0:T(8,128)}, f32[1,12,8,128]{3,2,1,0:T(8,128)}) custom-call(f32[1,12,64,128]{3,2,1,0:T(8,128)} %get-tuple-element.92.w_ref.refs_5_, f32[1,12,8,128]{3,2,1,0:T(8,128)} %copy-done.17, f32[1,12,8,128]{3,2,1,0:T(8,128)} %copy-done.19, f32[128,64]{1,0:T(8,128)} %constant.27.clone.l_ref, ...), custom_call_target="tpu_custom_call" | custom-call | flops 228261888 | bytes 2655060 | tf_op jit(solution)/shard_map/pallas_call | solution.py:217
  (122 shorter events, 65.5 us)
Async XLA Ops:
  7.2 85.7 %all-gather.5.cloned.1.call-start = ((), (), s32[]{:S(2)}) async-start(), calls=%async_computation | async-start | bytes 1966080 | tf_op jit(solution)/shard_map/all_gather | solution.py:502
  11.9 13.7 %collective-permute-start.1 = (f32[3,12,16,128]{3,2,1,0:T(8,128)}, f32[3,12,16,128]{3,2,1,0:T(8,128)S(1)}, u32[]{:S(2)}, u32[]{:S(2)}) collective-permute-start(f32[3,12,16,128]{3,2,1,0:T(8,128)} %get-tuple-element.98), channel_id=1, source_target_pairs={{1,0},{2,1},{3,2},{4,3},{5,4},{6,5},{7,6},{0,7},{9,8},{10,9},{11,1... | collective-permute-start | bytes 884744 | tf_op jit(solution)/shard_map/ppermute | solution.py:289
  17.9 12.6 %collective-permute-start = (f32[3,12,16,128]{3,2,1,0:T(8,128)}, f32[3,12,16,128]{3,2,1,0:T(8,128)}, u32[]{:S(2)}, u32[]{:S(2)}) collective-permute-start(f32[3,12,16,128]{3,2,1,0:T(8,128)} %get-tuple-element.99), channel_id=1, source_target_pairs={{0,1},{1,2},{2,3},{3,4},{4,5},{5,6},{6,7},{7,0},{8,9},{9,10},{10,1... | collective-permute-start | bytes 884744 | tf_op jit(solution)/shard_map/ppermute | solution.py:288
  41.0 7.6 %collective-permute-start.2 = (f32[1,12,16,128]{3,2,1,0:T(8,128)}, f32[1,12,16,128]{3,2,1,0:T(8,128)S(1)}, u32[]{:S(2)}, u32[]{:S(2)}) collective-permute-start(f32[1,12,16,128]{3,2,1,0:T(8,128)} %get-tuple-element.51), channel_id=1, source_target_pairs={{0,1},{1,2},{2,3},{3,4},{4,5},{5,6},{6,7},{7,0},{8,9},{9,10},{10,1... | collective-permute-start | bytes 294920 | tf_op jit(solution)/shard_map/ppermute | solution.py:288
  42.8 6.9 %collective-permute-start.3 = (f32[1,12,16,128]{3,2,1,0:T(8,128)}, f32[1,12,16,128]{3,2,1,0:T(8,128)S(1)}, u32[]{:S(2)}, u32[]{:S(2)}) collective-permute-start(f32[1,12,16,128]{3,2,1,0:T(8,128)} %get-tuple-element.52), channel_id=1, source_target_pairs={{1,0},{2,1},{3,2},{4,3},{5,4},{6,5},{7,6},{0,7},{9,8},{10,9},{11,1... | collective-permute-start | bytes 294920 | tf_op jit(solution)/shard_map/ppermute | solution.py:289
  56.2 10.7 %collective-permute-start.4 = (f32[1,12,16,128]{3,2,1,0:T(8,128)}, f32[1,12,16,128]{3,2,1,0:T(8,128)S(1)}, u32[]{:S(2)}, u32[]{:S(2)}) collective-permute-start(f32[1,12,16,128]{3,2,1,0:T(8,128)} %get-tuple-element.56), channel_id=1, source_target_pairs={{0,1},{1,2},{2,3},{3,4},{4,5},{5,6},{6,7},{7,0},{8,9},{9,10},{10,1... | collective-permute-start | bytes 294920 | tf_op jit(solution)/shard_map/ppermute | solution.py:288
  56.5 10.4 %collective-permute-start.5 = (f32[1,12,16,128]{3,2,1,0:T(8,128)}, f32[1,12,16,128]{3,2,1,0:T(8,128)S(1)}, u32[]{:S(2)}, u32[]{:S(2)}) collective-permute-start(f32[1,12,16,128]{3,2,1,0:T(8,128)} %get-tuple-element.57), channel_id=1, source_target_pairs={{1,0},{2,1},{3,2},{4,3},{5,4},{6,5},{7,6},{0,7},{9,8},{10,9},{11,1... | collective-permute-start | bytes 294920 | tf_op jit(solution)/shard_map/ppermute | solution.py:289
  67.6 8.2 %copy-start.29 = (f32[8,16,1,1]{1,0,3,2:T(8,128)S(1)}, f32[8,16,1,1]{1,0,3,2:T(8,128)}, u32[]{:S(2)}) copy-start(f32[8,16,1,1]{1,0,3,2:T(8,128)} %constant.32) | copy-start | bytes 1540
  74.2 139.4 %all-gather.7.cloned.1.call-start = ((), (), s32[]{:S(2)}) async-start(), calls=%async_computation.1 | async-start | bytes 1966080 | tf_op jit(solution)/shard_map/all_gather | solution.py:502
  74.3 55.7 %collective-permute-start.14 = (f32[1,12,128,128]{3,2,1,0:T(8,128)S(1)}, f32[1,12,128,128]{3,2,1,0:T(8,128)S(1)}, u32[]{:S(2)}, u32[]{:S(2)}) collective-permute-start(f32[1,12,128,128]{3,2,1,0:T(8,128)S(1)} %copy-done.2), channel_id=1, source_target_pairs={{0,8},{8,16},{16,24},{1,9},{9,17},{17,25},{2,10},{10,18},{18,26},{... | collective-permute-start | bytes 2359304 | tf_op jit(solution)/shard_map/ppermute | solution.py:505
  76.3 16.6 %copy-start = (f32[8,12,8,128]{3,0,2,1:T(8,128)}, f32[8,12,8,128]{3,0,2,1:T(8,128)S(1)}, u32[]{:S(2)}) copy-start(f32[8,12,8,128]{3,0,2,1:T(8,128)S(1)} %fusion.3) | copy-start | bytes 1179652
  76.3 4.1 %collective-permute-start.7 = (f32[12,8,128]{2,1,0:T(8,128)S(1)}, f32[12,8,128]{2,1,0:T(8,128)S(1)}, u32[]{:S(2)}, u32[]{:S(2)}) collective-permute-start(f32[12,8,128]{2,1,0:T(8,128)S(1)} %get-tuple-element.100), channel_id=1, source_target_pairs={{1,0},{2,1},{3,2},{4,3},{5,4},{6,5},{7,6},{0,7},{9,8},{10,9},{11,1... | collective-permute-start | bytes 147464 | tf_op jit(solution)/shard_map/ppermute | solution.py:289
  77.9 6.8 %collective-permute-start.6 = (f32[12,8,128]{2,1,0:T(8,128)S(1)}, f32[12,8,128]{2,1,0:T(8,128)S(1)}, u32[]{:S(2)}, u32[]{:S(2)}) collective-permute-start(f32[12,8,128]{2,1,0:T(8,128)S(1)} %get-tuple-element.101), channel_id=1, source_target_pairs={{0,1},{1,2},{2,3},{3,4},{4,5},{5,6},{6,7},{7,0},{8,9},{9,10},{10,1... | collective-permute-start | bytes 147464 | tf_op jit(solution)/shard_map/ppermute | solution.py:288
  80.5 12.4 %copy-start.7 = (f32[12,8,128]{2,1,0:T(8,128)}, f32[12,8,128]{2,1,0:T(8,128)S(1)}, u32[]{:S(2)}) copy-start(f32[12,8,128]{2,1,0:T(8,128)S(1)} %collective-permute-done.7) | copy-start | bytes 147460
  96.4 7.0 %collective-permute-start.8 = (f32[1,12,8,128]{3,2,1,0:T(8,128)}, f32[1,12,8,128]{3,2,1,0:T(8,128)S(1)}, u32[]{:S(2)}, u32[]{:S(2)}) collective-permute-start(f32[1,12,8,128]{3,2,1,0:T(8,128)} %get-tuple-element.63), channel_id=1, source_target_pairs={{0,1},{1,2},{2,3},{3,4},{4,5},{5,6},{6,7},{7,0},{8,9},{9,10},{10,1... | collective-permute-start | bytes 147464 | tf_op jit(solution)/shard_map/ppermute | solution.py:288
  97.1 6.3 %collective-permute-start.9 = (f32[1,12,8,128]{3,2,1,0:T(8,128)}, f32[1,12,8,128]{3,2,1,0:T(8,128)S(1)}, u32[]{:S(2)}, u32[]{:S(2)}) collective-permute-start(f32[1,12,8,128]{3,2,1,0:T(8,128)} %get-tuple-element.64), channel_id=1, source_target_pairs={{1,0},{2,1},{3,2},{4,3},{5,4},{6,5},{7,6},{0,7},{9,8},{10,9},{11,1... | collective-permute-start | bytes 147464 | tf_op jit(solution)/shard_map/ppermute | solution.py:289
  107.6 7.0 %collective-permute-start.10 = (f32[1,12,8,128]{3,2,1,0:T(8,128)}, f32[1,12,8,128]{3,2,1,0:T(8,128)S(1)}, u32[]{:S(2)}, u32[]{:S(2)}) collective-permute-start(f32[1,12,8,128]{3,2,1,0:T(8,128)} %get-tuple-element.66), channel_id=1, source_target_pairs={{0,1},{1,2},{2,3},{3,4},{4,5},{5,6},{6,7},{7,0},{8,9},{9,10},{10,1... | collective-permute-start | bytes 147464 | tf_op jit(solution)/shard_map/ppermute | solution.py:288
  108.0 6.6 %collective-permute-start.11 = (f32[1,12,8,128]{3,2,1,0:T(8,128)}, f32[1,12,8,128]{3,2,1,0:T(8,128)S(1)}, u32[]{:S(2)}, u32[]{:S(2)}) collective-permute-start(f32[1,12,8,128]{3,2,1,0:T(8,128)} %get-tuple-element.67), channel_id=1, source_target_pairs={{1,0},{2,1},{3,2},{4,3},{5,4},{6,5},{7,6},{0,7},{9,8},{10,9},{11,1... | collective-permute-start | bytes 147464 | tf_op jit(solution)/shard_map/ppermute | solution.py:289
  118.8 7.0 %collective-permute-start.12 = (f32[1,12,8,128]{3,2,1,0:T(8,128)}, f32[1,12,8,128]{3,2,1,0:T(8,128)S(1)}, u32[]{:S(2)}, u32[]{:S(2)}) collective-permute-start(f32[1,12,8,128]{3,2,1,0:T(8,128)} %get-tuple-element.69), channel_id=1, source_target_pairs={{0,1},{1,2},{2,3},{3,4},{4,5},{5,6},{6,7},{7,0},{8,9},{9,10},{10,1... | collective-permute-start | bytes 147464 | tf_op jit(solution)/shard_map/ppermute | solution.py:288
  118.8 7.0 %collective-permute-start.13 = (f32[1,12,8,128]{3,2,1,0:T(8,128)}, f32[1,12,8,128]{3,2,1,0:T(8,128)S(1)}, u32[]{:S(2)}, u32[]{:S(2)}) collective-permute-start(f32[1,12,8,128]{3,2,1,0:T(8,128)} %get-tuple-element.70), channel_id=1, source_target_pairs={{1,0},{2,1},{3,2},{4,3},{5,4},{6,5},{7,6},{0,7},{9,8},{10,9},{11,1... | collective-permute-start | bytes 147464 | tf_op jit(solution)/shard_map/ppermute | solution.py:289
  137.6 10.1 %collective-permute-start.15 = (f32[3,12,16,128]{3,2,1,0:T(8,128)}, f32[3,12,16,128]{3,2,1,0:T(8,128)S(1)}, u32[]{:S(2)}, u32[]{:S(2)}) collective-permute-start(f32[3,12,16,128]{3,2,1,0:T(8,128)} %get-tuple-element.73), channel_id=1, source_target_pairs={{0,1},{1,2},{2,3},{3,4},{4,5},{5,6},{6,7},{7,0},{8,9},{9,10},{10,1... | collective-permute-start | bytes 884744 | tf_op jit(solution)/shard_map/ppermute | solution.py:288
  137.6 12.2 %collective-permute-start.16 = (f32[3,12,16,128]{3,2,1,0:T(8,128)}, f32[3,12,16,128]{3,2,1,0:T(8,128)S(1)}, u32[]{:S(2)}, u32[]{:S(2)}) collective-permute-start(f32[3,12,16,128]{3,2,1,0:T(8,128)} %get-tuple-element.74), channel_id=1, source_target_pairs={{1,0},{2,1},{3,2},{4,3},{5,4},{6,5},{7,6},{0,7},{9,8},{10,9},{11,1... | collective-permute-start | bytes 884744 | tf_op jit(solution)/shard_map/ppermute | solution.py:289
  161.0 7.5 %collective-permute-start.17 = (f32[1,12,16,128]{3,2,1,0:T(8,128)}, f32[1,12,16,128]{3,2,1,0:T(8,128)S(1)}, u32[]{:S(2)}, u32[]{:S(2)}) collective-permute-start(f32[1,12,16,128]{3,2,1,0:T(8,128)} %get-tuple-element.76), channel_id=1, source_target_pairs={{0,1},{1,2},{2,3},{3,4},{4,5},{5,6},{6,7},{7,0},{8,9},{9,10},{10,1... | collective-permute-start | bytes 294920 | tf_op jit(solution)/shard_map/ppermute | solution.py:288
  161.4 7.1 %collective-permute-start.18 = (f32[1,12,16,128]{3,2,1,0:T(8,128)}, f32[1,12,16,128]{3,2,1,0:T(8,128)S(1)}, u32[]{:S(2)}, u32[]{:S(2)}) collective-permute-start(f32[1,12,16,128]{3,2,1,0:T(8,128)} %get-tuple-element.77), channel_id=1, source_target_pairs={{1,0},{2,1},{3,2},{4,3},{5,4},{6,5},{7,6},{0,7},{9,8},{10,9},{11,1... | collective-permute-start | bytes 294920 | tf_op jit(solution)/shard_map/ppermute | solution.py:289
  175.1 9.6 %collective-permute-start.19 = (f32[1,12,16,128]{3,2,1,0:T(8,128)}, f32[1,12,16,128]{3,2,1,0:T(8,128)S(1)}, u32[]{:S(2)}, u32[]{:S(2)}) collective-permute-start(f32[1,12,16,128]{3,2,1,0:T(8,128)} %get-tuple-element.80), channel_id=1, source_target_pairs={{0,1},{1,2},{2,3},{3,4},{4,5},{5,6},{6,7},{7,0},{8,9},{9,10},{10,1... | collective-permute-start | bytes 294920 | tf_op jit(solution)/shard_map/ppermute | solution.py:288
  175.1 9.6 %collective-permute-start.20 = (f32[1,12,16,128]{3,2,1,0:T(8,128)}, f32[1,12,16,128]{3,2,1,0:T(8,128)S(1)}, u32[]{:S(2)}, u32[]{:S(2)}) collective-permute-start(f32[1,12,16,128]{3,2,1,0:T(8,128)} %get-tuple-element.81), channel_id=1, source_target_pairs={{1,0},{2,1},{3,2},{4,3},{5,4},{6,5},{7,6},{0,7},{9,8},{10,9},{11,1... | collective-permute-start | bytes 294920 | tf_op jit(solution)/shard_map/ppermute | solution.py:289
  217.2 7.0 %collective-permute-start.21 = (f32[1,12,8,128]{3,2,1,0:T(8,128)}, f32[1,12,8,128]{3,2,1,0:T(8,128)S(1)}, u32[]{:S(2)}, u32[]{:S(2)}) collective-permute-start(f32[1,12,8,128]{3,2,1,0:T(8,128)} %get-tuple-element.87), channel_id=1, source_target_pairs={{0,1},{1,2},{2,3},{3,4},{4,5},{5,6},{6,7},{7,0},{8,9},{9,10},{10,1... | collective-permute-start | bytes 147464 | tf_op jit(solution)/shard_map/ppermute | solution.py:288
  218.6 5.5 %collective-permute-start.22 = (f32[1,12,8,128]{3,2,1,0:T(8,128)}, f32[1,12,8,128]{3,2,1,0:T(8,128)S(1)}, u32[]{:S(2)}, u32[]{:S(2)}) collective-permute-start(f32[1,12,8,128]{3,2,1,0:T(8,128)} %get-tuple-element.88), channel_id=1, source_target_pairs={{1,0},{2,1},{3,2},{4,3},{5,4},{6,5},{7,6},{0,7},{9,8},{10,9},{11,1... | collective-permute-start | bytes 147464 | tf_op jit(solution)/shard_map/ppermute | solution.py:289
  228.3 7.0 %collective-permute-start.23 = (f32[1,12,8,128]{3,2,1,0:T(8,128)}, f32[1,12,8,128]{3,2,1,0:T(8,128)S(1)}, u32[]{:S(2)}, u32[]{:S(2)}) collective-permute-start(f32[1,12,8,128]{3,2,1,0:T(8,128)} %get-tuple-element.90), channel_id=1, source_target_pairs={{0,1},{1,2},{2,3},{3,4},{4,5},{5,6},{6,7},{7,0},{8,9},{9,10},{10,1... | collective-permute-start | bytes 147464 | tf_op jit(solution)/shard_map/ppermute | solution.py:288
  229.5 5.9 %collective-permute-start.24 = (f32[1,12,8,128]{3,2,1,0:T(8,128)}, f32[1,12,8,128]{3,2,1,0:T(8,128)S(1)}, u32[]{:S(2)}, u32[]{:S(2)}) collective-permute-start(f32[1,12,8,128]{3,2,1,0:T(8,128)} %get-tuple-element.91), channel_id=1, source_target_pairs={{1,0},{2,1},{3,2},{4,3},{5,4},{6,5},{7,6},{0,7},{9,8},{10,9},{11,1... | collective-permute-start | bytes 147464 | tf_op jit(solution)/shard_map/ppermute | solution.py:289
  239.5 7.0 %collective-permute-start.25 = (f32[1,12,8,128]{3,2,1,0:T(8,128)}, f32[1,12,8,128]{3,2,1,0:T(8,128)S(1)}, u32[]{:S(2)}, u32[]{:S(2)}) collective-permute-start(f32[1,12,8,128]{3,2,1,0:T(8,128)} %get-tuple-element.93), channel_id=1, source_target_pairs={{0,1},{1,2},{2,3},{3,4},{4,5},{5,6},{6,7},{7,0},{8,9},{9,10},{10,1... | collective-permute-start | bytes 147464 | tf_op jit(solution)/shard_map/ppermute | solution.py:288
  239.7 6.9 %collective-permute-start.26 = (f32[1,12,8,128]{3,2,1,0:T(8,128)}, f32[1,12,8,128]{3,2,1,0:T(8,128)S(1)}, u32[]{:S(2)}, u32[]{:S(2)}) collective-permute-start(f32[1,12,8,128]{3,2,1,0:T(8,128)} %get-tuple-element.94), channel_id=1, source_target_pairs={{1,0},{2,1},{3,2},{4,3},{5,4},{6,5},{7,6},{0,7},{9,8},{10,9},{11,1... | collective-permute-start | bytes 147464 | tf_op jit(solution)/shard_map/ppermute | solution.py:289
  (29 other events, 54.3 us)
Sparse Core Ops, SparseCore 0:
  74.3 18.5 all-gather.4
  192.1 21.4 all-gather.6

commit v10 on v9

--- a/solution.py
+++ b/solution.py
@@ -369,6 +369,18 @@
 
         lax.fori_loop(0, fields, body, 0)
 
+    def plain_kernel(w_ref, p_ref, n_ref, l_ref, x_ref, zc_ref, rx_ref, ra_ref, en_ref,
+                     out_ref, s_ref):
+        tendency_into(out_ref, w_ref, p_ref, n_ref, l_ref, x_ref, zc_ref, rx_ref, ra_ref,
+                      en_ref, s_ref, coarse_elem)
+
+    def first_kernel(w_ref, g_ref, rint_ref, out_ref, h_ref, t_ref):
+        for f in range(fields):
+            value = w_ref[0, f] + STEP * g_ref[0, f] + rint_ref[0, 0, f]
+            out_ref[0, f] = value
+            h_ref[0, f] = value[:coarse_rows]
+            t_ref[0, f] = value[coarse_span - coarse_rows:]
+
     def pick(sec_ref, w_refs, f, offset):
         value = w_refs[offset][0, f]
         for n in range(1, sections):
@@ -454,6 +466,15 @@
         )
 
     hop_pairs = [(d, d + 1) for d in range(sections - 1)]
+    (start_tendency,) = call(
+        plain_kernel,
+        (coarse_start[None], start_halo[0][None], start_halo[1][None], lop_coarse, xt)
+        + coarse_scalars,
+        (False,) * 5 + scalar_kinds,
+        (coarse_one,),
+        [coarse_scratch(1)],
+        *coarse_cost,
+    )
     where_now = section.astype(jnp.int32).reshape(1)
 
     fine_end = None
@@ -507,7 +528,20 @@
         w_halo = (start_halo[0][None], start_halo[1][None])
         chain = [w]
         for n in range(sections):
-            w, head, tail = coarse_step(w, w_halo, rint_all, n)
+            if n == 0:
+                w, head, tail = call(
+                    first_kernel,
+                    (w, start_tendency, rint_all),
+                    (False,) * 3,
+                    (coarse_one, plane_one, plane_one),
+                    [],
+                    4 * fields * coarse_span * columns, 0,
+                    blocks={2: pl.BlockSpec((1, 1, fields, coarse_span, columns),
+                                            lambda i: (0, 0, 0, 0, 0),
+                                            memory_space=pltpu.VMEM)},
+                )
+            else:
+                w, head, tail = coarse_step(w, w_halo, rint_all, n)
             chain.append(w)
             if n + 1 < sections:
                 w_halo = swap(head, tail)

time: 262 us -> 259 us (0.989)
  waiting for transfers between devices: 72.8 us -> 68.9 us
    all_gather x2, waiting for transfers between devices: 29.8 us -> 25.9 us  [per_device(): rint_all = lax.all_gather(rint[None], 'tm')]
    pallas_call x18 -> x19, Pallas kernels: 94 us -> 94.4 us  [call(): pl.pallas_call(kernel, out_shape=outs, in_specs=[blocks[i] if blocks is n...]
  transfers between devices with their start and end apart: 29 -> 29, of which waited for: 17 -> 17; matrix products, arithmetic and copies ran while one was open for 2% -> 2% of each run, Pallas kernels for 9% -> 10%
where the time goes in v10:
time: 259 us; the launch traced here: 258 us
  Pallas kernels  94.4 us (36%)
  waiting for transfers between devices  68.9 us (27%)
  starting transfers between devices  62.1 us (24%)
  local copies, waits for them, and re-layouts  15.5 us (6%)
  between operations  14.3 us (6%)
    pallas_call x19, Pallas kernels, call(): pl.pallas_call(kernel, out_shape=outs, in_specs=[blocks[i] if blocks is n...  94.4 us
    ppermute x13, starting transfers between devices, swap(): lax.ppermute(head, 'space', [((i + 1) % space_n, i) for i in range(space_...  53.6 us
    ppermute x13, waiting for transfers between devices, swap(): lax.ppermute(tail, 'space', [(i, (i + 1) % space_n) for i in range(space_...  33.5 us
    all_gather x2, waiting for transfers between devices, per_device(): rint_all = lax.all_gather(rint[None], 'tm')  25.9 us
    ppermute x13, waiting for transfers between devices, swap(): lax.ppermute(head, 'space', [((i + 1) % space_n, i) for i in range(space_...  9.42 us
    unnamed x65, local copies, waits for them, and re-layouts  9.35 us
    ppermute x13, starting transfers between devices, swap(): lax.ppermute(tail, 'space', [(i, (i + 1) % space_n) for i in range(space_...  6.92 us
  transfers between devices with their start and end apart: 29, of which 17 were waited for; matrix products, arithmetic and copies ran while one was open for 2% of the time, Pallas kernels for 10%

profile of v10, /device:TPU:0, one launch (start us, length us, event | category | flops | bytes accessed | tf_op | source)
XLA Modules:
  0.0 258.2 jit_solution(6777835415531579686)
XLA Ops:
  11.9 6.0 %collective-permute-start.1 = (f32[3,12,16,128]{3,2,1,0:T(8,128)}, f32[3,12,16,128]{3,2,1,0:T(8,128)S(1)}, u32[]{:S(2)}, u32[]{:S(2)}) collective-permute-start(f32[3,12,16,128]{3,2,1,0:T(8,128)} %get-tuple-element.98), channel_id=1, source_target_pairs={{1,0},{2,1},{3,2},{4,3},{5,4},{6,5},{7,6},{0,7},{9,8},{10,9},{11,1... | collective-permute-start | bytes 884744 | tf_op jit(solution)/shard_map/ppermute | solution.py:289
  21.4 4.2 %collective-permute-done.1.n_ref = f32[3,12,16,128]{3,2,1,0:T(8,128)S(1)} collective-permute-done((f32[3,12,16,128]{3,2,1,0:T(8,128)}, f32[3,12,16,128]{3,2,1,0:T(8,128)S(1)}, u32[]{:S(2)}, u32[]{:S(2)}) %collective-permute-start.1) | collective-permute-done | bytes 294944 | tf_op jit(solution)/shard_map/ppermute | solution.py:289
  25.6 4.9 %collective-permute-done.p_ref = f32[3,12,16,128]{3,2,1,0:T(8,128)} collective-permute-done((f32[3,12,16,128]{3,2,1,0:T(8,128)}, f32[3,12,16,128]{3,2,1,0:T(8,128)}, u32[]{:S(2)}, u32[]{:S(2)}) %collective-permute-start) | collective-permute-done | bytes 294944 | tf_op jit(solution)/shard_map/ppermute | solution.py:288
  30.5 10.5 %shard_map.131 = (f32[3,12,128,128]{3,2,1,0:T(8,128)}, f32[1,12,128,128]{3,2,1,0:T(8,128)}, f32[1,12,16,128]{3,2,1,0:T(8,128)}, f32[1,12,16,128]{3,2,1,0:T(8,128)}) custom-call(f32[3,12,128,128]{3,2,1,0:T(8,128)} %pad_maximum_fusion.u_ref, f32[3,12,16,128]{3,2,1,0:T(8,128)} %collective-permute-done.p_ref, f32[3,12,16,128]{3,2,1,0:T(8,128)} %copy-done.4, ...), custom_call_target="tpu_custom_call" | custom-call | flops 1822556160 | bytes 6488916 | tf_op jit(solution)/shard_map/pallas_call | solution.py:217
  50.3 5.9 %shard_map.132 = (f32[1,12,128,128]{3,2,1,0:T(8,128)}, f32[1,12,128,128]{3,2,1,0:T(8,128)}, f32[1,12,16,128]{3,2,1,0:T(8,128)}, f32[1,12,16,128]{3,2,1,0:T(8,128)}) custom-call(f32[1,12,128,128]{3,2,1,0:T(8,128)} %get-tuple-element.50.a1_ref.refs_0_, f32[1,12,16,128]{3,2,1,0:T(8,128)} %copy-done.8, f32[1,12,16,128]{3,2,1,0:T(8,128)} %copy-done.10, ...), custom_call_target="tpu_custom_call" | custom-call | flops 607518720 | bytes 5309268 | tf_op jit(solution)/shard_map/pallas_call | solution.py:217
  56.5 4.4 %collective-permute-start.5 = (f32[1,12,16,128]{3,2,1,0:T(8,128)}, f32[1,12,16,128]{3,2,1,0:T(8,128)S(1)}, u32[]{:S(2)}, u32[]{:S(2)}) collective-permute-start(f32[1,12,16,128]{3,2,1,0:T(8,128)} %get-tuple-element.57), channel_id=1, source_target_pairs={{1,0},{2,1},{3,2},{4,3},{5,4},{6,5},{7,6},{0,7},{9,8},{10,9},{11,1... | collective-permute-start | bytes 294920 | tf_op jit(solution)/shard_map/ppermute | solution.py:289
  62.1 4.8 %shard_map.133 = (f32[1,12,64,128]{3,2,1,0:T(8,128)}, f32[1,12,64,128]{3,2,1,0:T(8,128)}) custom-call(f32[3,12,128,128]{3,2,1,0:T(8,128)} %pad_maximum_fusion.u_ref, f32[3,12,16,128]{3,2,1,0:T(8,128)} %collective-permute-done.p_ref, f32[3,12,16,128]{3,2,1,0:T(8,128)} %copy-done.4, f32[64,128]{1,0:T(8,128)} %constant.28.clone.r_ref.refs_11_, ...), custom_call_target="tpu_custom_call" | custom-call | flops 228261888 | bytes 3867988 | tf_op jit(solution)/shard_map/pallas_call | solution.py:217
  67.6 6.6 %shard_map.134 = (f32[12,64,128]{2,1,0:T(8,128)}, f32[12,64,128]{2,1,0:T(8,128)}) custom-call(f32[1,12,128,128]{3,2,1,0:T(8,128)} %get-tuple-element.54.a2_ref.refs_1_, f32[1,12,16,128]{3,2,1,0:T(8,128)} %copy-done.11, f32[1,12,16,128]{3,2,1,0:T(8,128)} %copy-done.12, f32[256,128]{1,0:T(8,128)} %constant.26.clone.l_ref, f32[128,128]{1,0:T(8,128)} %constant.25.clone.x_ref, ...), custom_call_target="tpu_custom_call" | custom-call | flops 607518720 | bytes 5538644 | tf_op jit(solution)/shard_map/pallas_call | solution.py:217
  80.5 4.2 %collective-permute-done.6 = f32[12,8,128]{2,1,0:T(8,128)S(1)} collective-permute-done((f32[12,8,128]{2,1,0:T(8,128)S(1)}, f32[12,8,128]{2,1,0:T(8,128)S(1)}, u32[]{:S(2)}, u32[]{:S(2)}) %collective-permute-start.6) | collective-permute-done | bytes 49184 | tf_op jit(solution)/shard_map/ppermute | solution.py:288
  88.6 4.3 %all-gather.5.cloned.1.call-done = f32[48,64,128]{2,1,0:T(8,128)} async-done(((f32[12,64,128]{2,1,0:T(8,128)}), f32[48,64,128]{2,1,0:T(8,128)}) %all-gather.5.cloned.1.call-update) | async-done | bytes 1572880 | tf_op jit(solution)/shard_map/all_gather | solution.py:523
  95.7 4.0 %collective-permute-start.9 = (f32[1,12,8,128]{3,2,1,0:T(8,128)}, f32[1,12,8,128]{3,2,1,0:T(8,128)S(1)}, u32[]{:S(2)}, u32[]{:S(2)}) collective-permute-start(f32[1,12,8,128]{3,2,1,0:T(8,128)} %get-tuple-element.64), channel_id=1, source_target_pairs={{1,0},{2,1},{3,2},{4,3},{5,4},{6,5},{7,6},{0,7},{9,8},{10,9},{11,1... | collective-permute-start | bytes 147464 | tf_op jit(solution)/shard_map/ppermute | solution.py:289
  102.6 3.5 %shard_map.137 = (f32[1,12,64,128]{3,2,1,0:T(8,128)}, f32[1,12,8,128]{3,2,1,0:T(8,128)}, f32[1,12,8,128]{3,2,1,0:T(8,128)}) custom-call(f32[1,12,64,128]{3,2,1,0:T(8,128)} %get-tuple-element.62.w_ref.refs_5_, f32[1,12,8,128]{3,2,1,0:T(8,128)} %copy-done.20, f32[1,12,8,128]{3,2,1,0:T(8,128)} %copy-done.25, f32[128,64]{1,0:T(8,128)} %constant.27.clone.l_ref, ...), custom_call_target="tpu_custom_call" | custom-call | flops 228261888 | bytes 2655060 | tf_op jit(solution)/shard_map/pallas_call | solution.py:217
  106.5 4.4 %collective-permute-start.11 = (f32[1,12,8,128]{3,2,1,0:T(8,128)}, f32[1,12,8,128]{3,2,1,0:T(8,128)S(1)}, u32[]{:S(2)}, u32[]{:S(2)}) collective-permute-start(f32[1,12,8,128]{3,2,1,0:T(8,128)} %get-tuple-element.67), channel_id=1, source_target_pairs={{1,0},{2,1},{3,2},{4,3},{5,4},{6,5},{7,6},{0,7},{9,8},{10,9},{11,1... | collective-permute-start | bytes 147464 | tf_op jit(solution)/shard_map/ppermute | solution.py:289
  113.7 3.6 %shard_map.138 = (f32[1,12,64,128]{3,2,1,0:T(8,128)}, f32[1,12,8,128]{3,2,1,0:T(8,128)}, f32[1,12,8,128]{3,2,1,0:T(8,128)}) custom-call(f32[1,12,64,128]{3,2,1,0:T(8,128)} %get-tuple-element.65.w_ref.refs_6_, f32[1,12,8,128]{3,2,1,0:T(8,128)} %copy-done.21, f32[1,12,8,128]{3,2,1,0:T(8,128)} %copy-done.26, f32[128,64]{1,0:T(8,128)} %constant.27.clone.l_ref, ...), custom_call_target="tpu_custom_call" | custom-call | flops 228261888 | bytes 2655060 | tf_op jit(solution)/shard_map/pallas_call | solution.py:217
  117.3 4.8 %collective-permute-start.13 = (f32[1,12,8,128]{3,2,1,0:T(8,128)}, f32[1,12,8,128]{3,2,1,0:T(8,128)S(1)}, u32[]{:S(2)}, u32[]{:S(2)}) collective-permute-start(f32[1,12,8,128]{3,2,1,0:T(8,128)} %get-tuple-element.70), channel_id=1, source_target_pairs={{1,0},{2,1},{3,2},{4,3},{5,4},{6,5},{7,6},{0,7},{9,8},{10,9},{11,1... | collective-permute-start | bytes 147464 | tf_op jit(solution)/shard_map/ppermute | solution.py:289
  125.0 3.6 %shard_map.139 = (f32[1,12,64,128]{3,2,1,0:T(8,128)}, f32[1,12,8,128]{3,2,1,0:T(8,128)}, f32[1,12,8,128]{3,2,1,0:T(8,128)}) custom-call(f32[1,12,64,128]{3,2,1,0:T(8,128)} %get-tuple-element.68.w_ref.refs_7_, f32[1,12,8,128]{3,2,1,0:T(8,128)} %copy-done.18, f32[1,12,8,128]{3,2,1,0:T(8,128)} %copy-done.22, f32[128,64]{1,0:T(8,128)} %constant.27.clone.l_ref, ...), custom_call_target="tpu_custom_call" | custom-call | flops 228261888 | bytes 2655060 | tf_op jit(solution)/shard_map/pallas_call | solution.py:217
  129.4 6.7 %shard_map.140 = (f32[3,12,128,128]{3,2,1,0:T(8,128)}, f32[3,12,16,128]{3,2,1,0:T(8,128)}, f32[3,12,16,128]{3,2,1,0:T(8,128)}) custom-call(f32[1,12,128,128]{3,2,1,0:T(8,128)} %get-tuple-element.50.a1_ref.refs_0_, f32[1,12,128,128]{3,2,1,0:T(8,128)} %get-tuple-element.54.a2_ref.refs_1_, f32[1,12,64,128]{3,2,1,0:T(8,128)} %get-tuple-element.55.refs_2_, ...), custom_call_target="tpu_custom_call" | custom-call | flops 603979776 | bytes 8912904 | tf_op jit(solution)/shard_map/pallas_call | solution.py:217
  136.1 4.7 %collective-permute-start.16 = (f32[3,12,16,128]{3,2,1,0:T(8,128)}, f32[3,12,16,128]{3,2,1,0:T(8,128)S(1)}, u32[]{:S(2)}, u32[]{:S(2)}) collective-permute-start(f32[3,12,16,128]{3,2,1,0:T(8,128)} %get-tuple-element.74), channel_id=1, source_target_pairs={{1,0},{2,1},{3,2},{4,3},{5,4},{6,5},{7,6},{0,7},{9,8},{10,9},{11,1... | collective-permute-start | bytes 884744 | tf_op jit(solution)/shard_map/ppermute | solution.py:289
  140.9 5.3 %collective-permute-done.15.p_ref = f32[3,12,16,128]{3,2,1,0:T(8,128)S(1)} collective-permute-done((f32[3,12,16,128]{3,2,1,0:T(8,128)}, f32[3,12,16,128]{3,2,1,0:T(8,128)S(1)}, u32[]{:S(2)}, u32[]{:S(2)}) %collective-permute-start.15) | collective-permute-done | bytes 294944 | tf_op jit(solution)/shard_map/ppermute | solution.py:288
  149.0 10.5 %shard_map.141 = (f32[3,12,128,128]{3,2,1,0:T(8,128)}, f32[1,12,128,128]{3,2,1,0:T(8,128)}, f32[1,12,16,128]{3,2,1,0:T(8,128)}, f32[1,12,16,128]{3,2,1,0:T(8,128)}) custom-call(f32[3,12,128,128]{3,2,1,0:T(8,128)} %get-tuple-element.72.u_ref, f32[3,12,16,128]{3,2,1,0:T(8,128)} %copy-done.5, f32[3,12,16,128]{3,2,1,0:T(8,128)} %copy-done.6, ...), custom_call_target="tpu_custom_call" | custom-call | flops 1822556160 | bytes 6488916 | tf_op jit(solution)/shard_map/pallas_call | solution.py:217
  159.9 4.4 %collective-permute-start.18 = (f32[1,12,16,128]{3,2,1,0:T(8,128)}, f32[1,12,16,128]{3,2,1,0:T(8,128)S(1)}, u32[]{:S(2)}, u32[]{:S(2)}) collective-permute-start(f32[1,12,16,128]{3,2,1,0:T(8,128)} %get-tuple-element.77), channel_id=1, source_target_pairs={{1,0},{2,1},{3,2},{4,3},{5,4},{6,5},{7,6},{0,7},{9,8},{10,9},{11,1... | collective-permute-start | bytes 294920 | tf_op jit(solution)/shard_map/ppermute | solution.py:289
  167.7 5.9 %shard_map.142 = (f32[1,12,128,128]{3,2,1,0:T(8,128)}, f32[1,12,128,128]{3,2,1,0:T(8,128)}, f32[1,12,16,128]{3,2,1,0:T(8,128)}, f32[1,12,16,128]{3,2,1,0:T(8,128)}) custom-call(f32[1,12,128,128]{3,2,1,0:T(8,128)} %get-tuple-element.75.a1_ref, f32[1,12,16,128]{3,2,1,0:T(8,128)} %copy-done.7, f32[1,12,16,128]{3,2,1,0:T(8,128)} %copy-done.9, ...), custom_call_target="tpu_custom_call" | custom-call | flops 607518720 | bytes 5309268 | tf_op jit(solution)/shard_map/pallas_call | solution.py:217
  173.7 4.9 %collective-permute-start.20 = (f32[1,12,16,128]{3,2,1,0:T(8,128)}, f32[1,12,16,128]{3,2,1,0:T(8,128)S(1)}, u32[]{:S(2)}, u32[]{:S(2)}) collective-permute-start(f32[1,12,16,128]{3,2,1,0:T(8,128)} %get-tuple-element.81), channel_id=1, source_target_pairs={{1,0},{2,1},{3,2},{4,3},{5,4},{6,5},{7,6},{0,7},{9,8},{10,9},{11,1... | collective-permute-start | bytes 294920 | tf_op jit(solution)/shard_map/ppermute | solution.py:289
  178.5 4.8 %shard_map.143 = (f32[1,12,64,128]{3,2,1,0:T(8,128)}, f32[1,12,64,128]{3,2,1,0:T(8,128)}) custom-call(f32[3,12,128,128]{3,2,1,0:T(8,128)} %get-tuple-element.72.u_ref, f32[3,12,16,128]{3,2,1,0:T(8,128)} %copy-done.5, f32[3,12,16,128]{3,2,1,0:T(8,128)} %copy-done.6, f32[64,128]{1,0:T(8,128)} %constant.28.clone.r_ref.refs_11_, f32[8,16]{1,0:T(8,128)} %constant.30.clone.rp_ref, ...), custom_call_target="tpu_custom_call" | custom-call | flops 228261888 | bytes 3867988 | tf_op jit(solution)/shard_map/pallas_call | solution.py:217
  184.0 6.6 %shard_map.144 = (f32[12,64,128]{2,1,0:T(8,128)}, f32[12,64,128]{2,1,0:T(8,128)}) custom-call(f32[1,12,128,128]{3,2,1,0:T(8,128)} %get-tuple-element.79.a2_ref.refs_0_, f32[1,12,16,128]{3,2,1,0:T(8,128)} %copy-done.13, f32[1,12,16,128]{3,2,1,0:T(8,128)} %copy-done.14, f32[256,128]{1,0:T(8,128)} %constant.26.clone.l_ref, f32[128,128]{1,0:T(8,128)} %constant.25.clone.x_ref, ...), custom_call_target="tpu_custom_call" | custom-call | flops 607518720 | bytes 5538644 | tf_op jit(solution)/shard_map/pallas_call | solution.py:217
  190.6 21.7 %all-gather.7.cloned.1.call-done = f32[48,64,128]{2,1,0:T(8,128)} async-done(((f32[12,64,128]{2,1,0:T(8,128)}), f32[48,64,128]{2,1,0:T(8,128)}) %all-gather.7.cloned.1.call-update) | async-done | bytes 1572880 | tf_op jit(solution)/shard_map/all_gather | solution.py:523
  221.9 3.5 %shard_map.146 = (f32[1,12,64,128]{3,2,1,0:T(8,128)}, f32[1,12,8,128]{3,2,1,0:T(8,128)}, f32[1,12,8,128]{3,2,1,0:T(8,128)}) custom-call(f32[1,12,64,128]{3,2,1,0:T(8,128)} %get-tuple-element.86.w_ref.refs_3_, f32[1,12,8,128]{3,2,1,0:T(8,128)} %copy-done.23, f32[1,12,8,128]{3,2,1,0:T(8,128)} %copy-done.27, f32[128,64]{1,0:T(8,128)} %constant.27.clone.l_ref, ...), custom_call_target="tpu_custom_call" | custom-call | flops 228261888 | bytes 2655060 | tf_op jit(solution)/shard_map/pallas_call | solution.py:217
  226.6 3.6 %collective-permute-start.24 = (f32[1,12,8,128]{3,2,1,0:T(8,128)}, f32[1,12,8,128]{3,2,1,0:T(8,128)S(1)}, u32[]{:S(2)}, u32[]{:S(2)}) collective-permute-start(f32[1,12,8,128]{3,2,1,0:T(8,128)} %get-tuple-element.91), channel_id=1, source_target_pairs={{1,0},{2,1},{3,2},{4,3},{5,4},{6,5},{7,6},{0,7},{9,8},{10,9},{11,1... | collective-permute-start | bytes 147464 | tf_op jit(solution)/shard_map/ppermute | solution.py:289
  233.1 3.5 %shard_map.147 = (f32[1,12,64,128]{3,2,1,0:T(8,128)}, f32[1,12,8,128]{3,2,1,0:T(8,128)}, f32[1,12,8,128]{3,2,1,0:T(8,128)}) custom-call(f32[1,12,64,128]{3,2,1,0:T(8,128)} %get-tuple-element.89.w_ref.refs_4_, f32[1,12,8,128]{3,2,1,0:T(8,128)} %copy-done.24, f32[1,12,8,128]{3,2,1,0:T(8,128)} %copy-done.28, f32[128,64]{1,0:T(8,128)} %constant.27.clone.l_ref, ...), custom_call_target="tpu_custom_call" | custom-call | flops 228261888 | bytes 2655060 | tf_op jit(solution)/shard_map/pallas_call | solution.py:217
  236.8 4.6 %collective-permute-start.26 = (f32[1,12,8,128]{3,2,1,0:T(8,128)}, f32[1,12,8,128]{3,2,1,0:T(8,128)S(1)}, u32[]{:S(2)}, u32[]{:S(2)}) collective-permute-start(f32[1,12,8,128]{3,2,1,0:T(8,128)} %get-tuple-element.94), channel_id=1, source_target_pairs={{1,0},{2,1},{3,2},{4,3},{5,4},{6,5},{7,6},{0,7},{9,8},{10,9},{11,1... | collective-permute-start | bytes 147464 | tf_op jit(solution)/shard_map/ppermute | solution.py:289
  244.3 3.5 %shard_map.148 = (f32[1,12,64,128]{3,2,1,0:T(8,128)}, f32[1,12,8,128]{3,2,1,0:T(8,128)}, f32[1,12,8,128]{3,2,1,0:T(8,128)}) custom-call(f32[1,12,64,128]{3,2,1,0:T(8,128)} %get-tuple-element.92.w_ref.refs_5_, f32[1,12,8,128]{3,2,1,0:T(8,128)} %copy-done.17, f32[1,12,8,128]{3,2,1,0:T(8,128)} %copy-done.19, f32[128,64]{1,0:T(8,128)} %constant.27.clone.l_ref, ...), custom_call_target="tpu_custom_call" | custom-call | flops 228261888 | bytes 2655060 | tf_op jit(solution)/shard_map/pallas_call | solution.py:217
  247.8 3.5 %shard_map.149 = (f32[1,12,128,128]{3,2,1,0:T(8,128)}, f32[1,12,64,128]{3,2,1,0:T(8,128)}) custom-call(f32[1,12,128,128]{3,2,1,0:T(8,128)} %get-tuple-element.79.a2_ref.refs_0_, f32[12,64,128]{2,1,0:T(8,128)} %get-tuple-element.84.refs_1_, f32[1,12,64,128]{3,2,1,0:T(8,128)} %bitcast.35, f32[1,12,64,128]{3,2,1,0:T(8,128)} %get-tuple-element.86.w_ref.refs_3_, ...), custom_call_target="tpu_custom_call" | custom-call | flops 150994944 | bytes 4358148 | tf_op jit(solution)/shard_map/pallas_call | solution.py:217
  (123 shorter events, 66.5 us)
Async XLA Ops:
  7.2 85.7 %all-gather.5.cloned.1.call-start = ((), (), s32[]{:S(2)}) async-start(), calls=%async_computation | async-start | bytes 1966080 | tf_op jit(solution)/shard_map/all_gather | solution.py:523
  10.9 7.0 %copy-start.31 = (f32[3,12]{1,0:T(4,128)S(1)}, f32[3,12]{1,0:T(4,128)}, u32[]{:S(2)}) copy-start(f32[3,12]{1,0:T(4,128)} %param.14) | copy-start | bytes 436
  11.9 13.7 %collective-permute-start.1 = (f32[3,12,16,128]{3,2,1,0:T(8,128)}, f32[3,12,16,128]{3,2,1,0:T(8,128)S(1)}, u32[]{:S(2)}, u32[]{:S(2)}) collective-permute-start(f32[3,12,16,128]{3,2,1,0:T(8,128)} %get-tuple-element.98), channel_id=1, source_target_pairs={{1,0},{2,1},{3,2},{4,3},{5,4},{6,5},{7,6},{0,7},{9,8},{10,9},{11,1... | collective-permute-start | bytes 884744 | tf_op jit(solution)/shard_map/ppermute | solution.py:289
  17.9 12.6 %collective-permute-start = (f32[3,12,16,128]{3,2,1,0:T(8,128)}, f32[3,12,16,128]{3,2,1,0:T(8,128)}, u32[]{:S(2)}, u32[]{:S(2)}) collective-permute-start(f32[3,12,16,128]{3,2,1,0:T(8,128)} %get-tuple-element.99), channel_id=1, source_target_pairs={{0,1},{1,2},{2,3},{3,4},{4,5},{5,6},{6,7},{7,0},{8,9},{9,10},{10,1... | collective-permute-start | bytes 884744 | tf_op jit(solution)/shard_map/ppermute | solution.py:288
  41.0 7.6 %collective-permute-start.2 = (f32[1,12,16,128]{3,2,1,0:T(8,128)}, f32[1,12,16,128]{3,2,1,0:T(8,128)S(1)}, u32[]{:S(2)}, u32[]{:S(2)}) collective-permute-start(f32[1,12,16,128]{3,2,1,0:T(8,128)} %get-tuple-element.51), channel_id=1, source_target_pairs={{0,1},{1,2},{2,3},{3,4},{4,5},{5,6},{6,7},{7,0},{8,9},{9,10},{10,1... | collective-permute-start | bytes 294920 | tf_op jit(solution)/shard_map/ppermute | solution.py:288
  42.8 6.9 %collective-permute-start.3 = (f32[1,12,16,128]{3,2,1,0:T(8,128)}, f32[1,12,16,128]{3,2,1,0:T(8,128)S(1)}, u32[]{:S(2)}, u32[]{:S(2)}) collective-permute-start(f32[1,12,16,128]{3,2,1,0:T(8,128)} %get-tuple-element.52), channel_id=1, source_target_pairs={{1,0},{2,1},{3,2},{4,3},{5,4},{6,5},{7,6},{0,7},{9,8},{10,9},{11,1... | collective-permute-start | bytes 294920 | tf_op jit(solution)/shard_map/ppermute | solution.py:289
  56.2 10.7 %collective-permute-start.4 = (f32[1,12,16,128]{3,2,1,0:T(8,128)}, f32[1,12,16,128]{3,2,1,0:T(8,128)S(1)}, u32[]{:S(2)}, u32[]{:S(2)}) collective-permute-start(f32[1,12,16,128]{3,2,1,0:T(8,128)} %get-tuple-element.56), channel_id=1, source_target_pairs={{0,1},{1,2},{2,3},{3,4},{4,5},{5,6},{6,7},{7,0},{8,9},{9,10},{10,1... | collective-permute-start | bytes 294920 | tf_op jit(solution)/shard_map/ppermute | solution.py:288
  56.5 10.4 %collective-permute-start.5 = (f32[1,12,16,128]{3,2,1,0:T(8,128)}, f32[1,12,16,128]{3,2,1,0:T(8,128)S(1)}, u32[]{:S(2)}, u32[]{:S(2)}) collective-permute-start(f32[1,12,16,128]{3,2,1,0:T(8,128)} %get-tuple-element.57), channel_id=1, source_target_pairs={{1,0},{2,1},{3,2},{4,3},{5,4},{6,5},{7,6},{0,7},{9,8},{10,9},{11,1... | collective-permute-start | bytes 294920 | tf_op jit(solution)/shard_map/ppermute | solution.py:289
  67.6 8.2 %copy-start.29 = (f32[8,16,1,1]{1,0,3,2:T(8,128)S(1)}, f32[8,16,1,1]{1,0,3,2:T(8,128)}, u32[]{:S(2)}) copy-start(f32[8,16,1,1]{1,0,3,2:T(8,128)} %constant.32) | copy-start | bytes 1540
  74.2 138.0 %all-gather.7.cloned.1.call-start = ((), (), s32[]{:S(2)}) async-start(), calls=%async_computation.1 | async-start | bytes 1966080 | tf_op jit(solution)/shard_map/all_gather | solution.py:523
  74.3 54.3 %collective-permute-start.14 = (f32[1,12,128,128]{3,2,1,0:T(8,128)S(1)}, f32[1,12,128,128]{3,2,1,0:T(8,128)S(1)}, u32[]{:S(2)}, u32[]{:S(2)}) collective-permute-start(f32[1,12,128,128]{3,2,1,0:T(8,128)S(1)} %copy-done.2), channel_id=1, source_target_pairs={{0,8},{8,16},{16,24},{1,9},{9,17},{17,25},{2,10},{10,18},{18,26},{... | collective-permute-start | bytes 2359304 | tf_op jit(solution)/shard_map/ppermute | solution.py:526
  76.3 8.4 %copy-start = (f32[8,12,8,128]{3,0,2,1:T(8,128)}, f32[8,12,8,128]{3,0,2,1:T(8,128)S(1)}, u32[]{:S(2)}) copy-start(f32[8,12,8,128]{3,0,2,1:T(8,128)S(1)} %fusion.3) | copy-start | bytes 1179652
  76.3 4.1 %collective-permute-start.7 = (f32[12,8,128]{2,1,0:T(8,128)S(1)}, f32[12,8,128]{2,1,0:T(8,128)S(1)}, u32[]{:S(2)}, u32[]{:S(2)}) collective-permute-start(f32[12,8,128]{2,1,0:T(8,128)S(1)} %get-tuple-element.100), channel_id=1, source_target_pairs={{1,0},{2,1},{3,2},{4,3},{5,4},{6,5},{7,6},{0,7},{9,8},{10,9},{11,1... | collective-permute-start | bytes 147464 | tf_op jit(solution)/shard_map/ppermute | solution.py:289
  77.9 6.8 %collective-permute-start.6 = (f32[12,8,128]{2,1,0:T(8,128)S(1)}, f32[12,8,128]{2,1,0:T(8,128)S(1)}, u32[]{:S(2)}, u32[]{:S(2)}) collective-permute-start(f32[12,8,128]{2,1,0:T(8,128)S(1)} %get-tuple-element.101), channel_id=1, source_target_pairs={{0,1},{1,2},{2,3},{3,4},{4,5},{5,6},{6,7},{7,0},{8,9},{9,10},{10,1... | collective-permute-start | bytes 147464 | tf_op jit(solution)/shard_map/ppermute | solution.py:288
  94.9 7.0 %collective-permute-start.8 = (f32[1,12,8,128]{3,2,1,0:T(8,128)}, f32[1,12,8,128]{3,2,1,0:T(8,128)S(1)}, u32[]{:S(2)}, u32[]{:S(2)}) collective-permute-start(f32[1,12,8,128]{3,2,1,0:T(8,128)} %get-tuple-element.63), channel_id=1, source_target_pairs={{0,1},{1,2},{2,3},{3,4},{4,5},{5,6},{6,7},{7,0},{8,9},{9,10},{10,1... | collective-permute-start | bytes 147464 | tf_op jit(solution)/shard_map/ppermute | solution.py:288
  95.7 6.3 %collective-permute-start.9 = (f32[1,12,8,128]{3,2,1,0:T(8,128)}, f32[1,12,8,128]{3,2,1,0:T(8,128)S(1)}, u32[]{:S(2)}, u32[]{:S(2)}) collective-permute-start(f32[1,12,8,128]{3,2,1,0:T(8,128)} %get-tuple-element.64), channel_id=1, source_target_pairs={{1,0},{2,1},{3,2},{4,3},{5,4},{6,5},{7,6},{0,7},{9,8},{10,9},{11,1... | collective-permute-start | bytes 147464 | tf_op jit(solution)/shard_map/ppermute | solution.py:289
  106.1 7.0 %collective-permute-start.10 = (f32[1,12,8,128]{3,2,1,0:T(8,128)}, f32[1,12,8,128]{3,2,1,0:T(8,128)S(1)}, u32[]{:S(2)}, u32[]{:S(2)}) collective-permute-start(f32[1,12,8,128]{3,2,1,0:T(8,128)} %get-tuple-element.66), channel_id=1, source_target_pairs={{0,1},{1,2},{2,3},{3,4},{4,5},{5,6},{6,7},{7,0},{8,9},{9,10},{10,1... | collective-permute-start | bytes 147464 | tf_op jit(solution)/shard_map/ppermute | solution.py:288
  106.5 6.6 %collective-permute-start.11 = (f32[1,12,8,128]{3,2,1,0:T(8,128)}, f32[1,12,8,128]{3,2,1,0:T(8,128)S(1)}, u32[]{:S(2)}, u32[]{:S(2)}) collective-permute-start(f32[1,12,8,128]{3,2,1,0:T(8,128)} %get-tuple-element.67), channel_id=1, source_target_pairs={{1,0},{2,1},{3,2},{4,3},{5,4},{6,5},{7,6},{0,7},{9,8},{10,9},{11,1... | collective-permute-start | bytes 147464 | tf_op jit(solution)/shard_map/ppermute | solution.py:289
  117.3 7.0 %collective-permute-start.12 = (f32[1,12,8,128]{3,2,1,0:T(8,128)}, f32[1,12,8,128]{3,2,1,0:T(8,128)S(1)}, u32[]{:S(2)}, u32[]{:S(2)}) collective-permute-start(f32[1,12,8,128]{3,2,1,0:T(8,128)} %get-tuple-element.69), channel_id=1, source_target_pairs={{0,1},{1,2},{2,3},{3,4},{4,5},{5,6},{6,7},{7,0},{8,9},{9,10},{10,1... | collective-permute-start | bytes 147464 | tf_op jit(solution)/shard_map/ppermute | solution.py:288
  117.3 7.0 %collective-permute-start.13 = (f32[1,12,8,128]{3,2,1,0:T(8,128)}, f32[1,12,8,128]{3,2,1,0:T(8,128)S(1)}, u32[]{:S(2)}, u32[]{:S(2)}) collective-permute-start(f32[1,12,8,128]{3,2,1,0:T(8,128)} %get-tuple-element.70), channel_id=1, source_target_pairs={{1,0},{2,1},{3,2},{4,3},{5,4},{6,5},{7,6},{0,7},{9,8},{10,9},{11,1... | collective-permute-start | bytes 147464 | tf_op jit(solution)/shard_map/ppermute | solution.py:289
  136.1 10.1 %collective-permute-start.15 = (f32[3,12,16,128]{3,2,1,0:T(8,128)}, f32[3,12,16,128]{3,2,1,0:T(8,128)S(1)}, u32[]{:S(2)}, u32[]{:S(2)}) collective-permute-start(f32[3,12,16,128]{3,2,1,0:T(8,128)} %get-tuple-element.73), channel_id=1, source_target_pairs={{0,1},{1,2},{2,3},{3,4},{4,5},{5,6},{6,7},{7,0},{8,9},{9,10},{10,1... | collective-permute-start | bytes 884744 | tf_op jit(solution)/shard_map/ppermute | solution.py:288
  136.1 12.2 %collective-permute-start.16 = (f32[3,12,16,128]{3,2,1,0:T(8,128)}, f32[3,12,16,128]{3,2,1,0:T(8,128)S(1)}, u32[]{:S(2)}, u32[]{:S(2)}) collective-permute-start(f32[3,12,16,128]{3,2,1,0:T(8,128)} %get-tuple-element.74), channel_id=1, source_target_pairs={{1,0},{2,1},{3,2},{4,3},{5,4},{6,5},{7,6},{0,7},{9,8},{10,9},{11,1... | collective-permute-start | bytes 884744 | tf_op jit(solution)/shard_map/ppermute | solution.py:289
  159.5 7.5 %collective-permute-start.17 = (f32[1,12,16,128]{3,2,1,0:T(8,128)}, f32[1,12,16,128]{3,2,1,0:T(8,128)S(1)}, u32[]{:S(2)}, u32[]{:S(2)}) collective-permute-start(f32[1,12,16,128]{3,2,1,0:T(8,128)} %get-tuple-element.76), channel_id=1, source_target_pairs={{0,1},{1,2},{2,3},{3,4},{4,5},{5,6},{6,7},{7,0},{8,9},{9,10},{10,1... | collective-permute-start | bytes 294920 | tf_op jit(solution)/shard_map/ppermute | solution.py:288
  159.9 7.1 %collective-permute-start.18 = (f32[1,12,16,128]{3,2,1,0:T(8,128)}, f32[1,12,16,128]{3,2,1,0:T(8,128)S(1)}, u32[]{:S(2)}, u32[]{:S(2)}) collective-permute-start(f32[1,12,16,128]{3,2,1,0:T(8,128)} %get-tuple-element.77), channel_id=1, source_target_pairs={{1,0},{2,1},{3,2},{4,3},{5,4},{6,5},{7,6},{0,7},{9,8},{10,9},{11,1... | collective-permute-start | bytes 294920 | tf_op jit(solution)/shard_map/ppermute | solution.py:289
  173.7 9.6 %collective-permute-start.19 = (f32[1,12,16,128]{3,2,1,0:T(8,128)}, f32[1,12,16,128]{3,2,1,0:T(8,128)S(1)}, u32[]{:S(2)}, u32[]{:S(2)}) collective-permute-start(f32[1,12,16,128]{3,2,1,0:T(8,128)} %get-tuple-element.80), channel_id=1, source_target_pairs={{0,1},{1,2},{2,3},{3,4},{4,5},{5,6},{6,7},{7,0},{8,9},{9,10},{10,1... | collective-permute-start | bytes 294920 | tf_op jit(solution)/shard_map/ppermute | solution.py:288
  173.7 9.6 %collective-permute-start.20 = (f32[1,12,16,128]{3,2,1,0:T(8,128)}, f32[1,12,16,128]{3,2,1,0:T(8,128)S(1)}, u32[]{:S(2)}, u32[]{:S(2)}) collective-permute-start(f32[1,12,16,128]{3,2,1,0:T(8,128)} %get-tuple-element.81), channel_id=1, source_target_pairs={{1,0},{2,1},{3,2},{4,3},{5,4},{6,5},{7,6},{0,7},{9,8},{10,9},{11,1... | collective-permute-start | bytes 294920 | tf_op jit(solution)/shard_map/ppermute | solution.py:289
  214.3 7.0 %collective-permute-start.21 = (f32[1,12,8,128]{3,2,1,0:T(8,128)}, f32[1,12,8,128]{3,2,1,0:T(8,128)S(1)}, u32[]{:S(2)}, u32[]{:S(2)}) collective-permute-start(f32[1,12,8,128]{3,2,1,0:T(8,128)} %get-tuple-element.87), channel_id=1, source_target_pairs={{0,1},{1,2},{2,3},{3,4},{4,5},{5,6},{6,7},{7,0},{8,9},{9,10},{10,1... | collective-permute-start | bytes 147464 | tf_op jit(solution)/shard_map/ppermute | solution.py:288
  215.8 5.5 %collective-permute-start.22 = (f32[1,12,8,128]{3,2,1,0:T(8,128)}, f32[1,12,8,128]{3,2,1,0:T(8,128)S(1)}, u32[]{:S(2)}, u32[]{:S(2)}) collective-permute-start(f32[1,12,8,128]{3,2,1,0:T(8,128)} %get-tuple-element.88), channel_id=1, source_target_pairs={{1,0},{2,1},{3,2},{4,3},{5,4},{6,5},{7,6},{0,7},{9,8},{10,9},{11,1... | collective-permute-start | bytes 147464 | tf_op jit(solution)/shard_map/ppermute | solution.py:289
  225.5 7.0 %collective-permute-start.23 = (f32[1,12,8,128]{3,2,1,0:T(8,128)}, f32[1,12,8,128]{3,2,1,0:T(8,128)S(1)}, u32[]{:S(2)}, u32[]{:S(2)}) collective-permute-start(f32[1,12,8,128]{3,2,1,0:T(8,128)} %get-tuple-element.90), channel_id=1, source_target_pairs={{0,1},{1,2},{2,3},{3,4},{4,5},{5,6},{6,7},{7,0},{8,9},{9,10},{10,1... | collective-permute-start | bytes 147464 | tf_op jit(solution)/shard_map/ppermute | solution.py:288
  226.6 5.9 %collective-permute-start.24 = (f32[1,12,8,128]{3,2,1,0:T(8,128)}, f32[1,12,8,128]{3,2,1,0:T(8,128)S(1)}, u32[]{:S(2)}, u32[]{:S(2)}) collective-permute-start(f32[1,12,8,128]{3,2,1,0:T(8,128)} %get-tuple-element.91), channel_id=1, source_target_pairs={{1,0},{2,1},{3,2},{4,3},{5,4},{6,5},{7,6},{0,7},{9,8},{10,9},{11,1... | collective-permute-start | bytes 147464 | tf_op jit(solution)/shard_map/ppermute | solution.py:289
  236.6 7.0 %collective-permute-start.25 = (f32[1,12,8,128]{3,2,1,0:T(8,128)}, f32[1,12,8,128]{3,2,1,0:T(8,128)S(1)}, u32[]{:S(2)}, u32[]{:S(2)}) collective-permute-start(f32[1,12,8,128]{3,2,1,0:T(8,128)} %get-tuple-element.93), channel_id=1, source_target_pairs={{0,1},{1,2},{2,3},{3,4},{4,5},{5,6},{6,7},{7,0},{8,9},{9,10},{10,1... | collective-permute-start | bytes 147464 | tf_op jit(solution)/shard_map/ppermute | solution.py:288
  236.8 6.9 %collective-permute-start.26 = (f32[1,12,8,128]{3,2,1,0:T(8,128)}, f32[1,12,8,128]{3,2,1,0:T(8,128)S(1)}, u32[]{:S(2)}, u32[]{:S(2)}) collective-permute-start(f32[1,12,8,128]{3,2,1,0:T(8,128)} %get-tuple-element.94), channel_id=1, source_target_pairs={{1,0},{2,1},{3,2},{4,3},{5,4},{6,5},{7,6},{0,7},{9,8},{10,9},{11,1... | collective-permute-start | bytes 147464 | tf_op jit(solution)/shard_map/ppermute | solution.py:289
  (29 other events, 43.9 us)
Sparse Core Ops, SparseCore 0:
  74.3 18.4 all-gather.4
  190.7 21.4 all-gather.6

commit v11 on v10

--- a/solution.py
+++ b/solution.py
@@ -369,9 +369,14 @@
 
         lax.fori_loop(0, fields, body, 0)
 
-    def plain_kernel(w_ref, p_ref, n_ref, l_ref, x_ref, zc_ref, rx_ref, ra_ref, en_ref,
-                     out_ref, s_ref):
-        tendency_into(out_ref, w_ref, p_ref, n_ref, l_ref, x_ref, zc_ref, rx_ref, ra_ref,
+    def plain_kernel(w_ref, p_ref, n_ref, rp_ref, l_ref, x_ref, zc_ref, rx_ref, ra_ref, en_ref,
+                     out_ref, bp_ref, bn_ref, s_ref):
+        last = p_ref.shape[0] - 1
+        for dst, src_ref in ((bp_ref, p_ref), (bn_ref, n_ref)):
+            wide = dot(rp_ref[...], lanes([src_ref[last, f] for f in range(fields)]))
+            for f, part in enumerate(unlanes(wide, columns)):
+                dst[0, f] = part
+        tendency_into(out_ref, w_ref, bp_ref, bn_ref, l_ref, x_ref, zc_ref, rx_ref, ra_ref,
                       en_ref, s_ref, coarse_elem)
 
     def first_kernel(w_ref, g_ref, rint_ref, out_ref, h_ref, t_ref):
@@ -443,7 +448,6 @@
     nodes = jnp.concatenate([jnp.where(section == 0, u_flat, nodes[0])[None], nodes[1:]], axis=0)
     coarse_start = jnp.einsum("cy,fzyx->fzcx", restrict_plane,
                               u_start, precision=HIGHEST).reshape(fields, coarse_span, columns)
-    start_halo = halo(coarse_start, coarse_rows)
 
     coarse_one = jax.ShapeDtypeStruct((1, fields, coarse_span, columns), f32)
     plane_one = jax.ShapeDtypeStruct((1, fields, coarse_rows, columns), f32)
@@ -466,13 +470,17 @@
         )
 
     hop_pairs = [(d, d + 1) for d in range(sections - 1)]
+    first_head = jnp.concatenate([nodes[:, :, :rows], u_flat[None, :, :rows]])
+    first_tail = jnp.concatenate([nodes[:, :, span - rows:], u_flat[None, :, span - rows:]])
+    first_prev, first_next = swap(first_head, first_tail)
     (start_tendency,) = call(
         plain_kernel,
-        (coarse_start[None], start_halo[0][None], start_halo[1][None], lop_coarse, xt)
+        (coarse_start[None], first_prev, first_next, restrict_plane, lop_coarse, xt)
         + coarse_scalars,
-        (False,) * 5 + scalar_kinds,
+        (False,) * 6 + scalar_kinds,
         (coarse_one,),
-        [coarse_scratch(1)],
+        [pltpu.VMEM((1, fields, coarse_rows, columns), f32),
+         pltpu.VMEM((1, fields, coarse_rows, columns), f32), coarse_scratch(1)],
         *coarse_cost,
     )
     where_now = section.astype(jnp.int32).reshape(1)
@@ -481,7 +489,7 @@
     coarse_end = None
     for iteration in range(ITERS):
         if iteration == 0:
-            node_prev, node_next = halo(nodes, rows)
+            node_prev, node_next = first_prev, first_next
         else:
             node_prev, node_next = swap(node_head, node_tail)
         f_all, a1, a1_head, a1_tail = call(
@@ -525,7 +533,7 @@
         if not last:
             a2_handed = lax.ppermute(a2, "tm", hop_pairs)
         w = coarse_start[None]
-        w_halo = (start_halo[0][None], start_halo[1][None])
+        w_halo = None
         chain = [w]
         for n in range(sections):
             if n == 0:

time: 259 us -> 265 us (1.023)
  waiting for transfers between devices: 68.9 us -> 73.4 us
    all_gather x2, waiting for transfers between devices: 25.9 us -> 34.3 us  [per_device(): rint_all = lax.all_gather(rint[None], 'tm')]
    ppermute x13 -> x12, waiting for transfers between devices: 9.42 us -> 5.11 us  [swap(): lax.ppermute(head, 'space', [((i + 1) % space_n, i) for i in range(space_...]
    ppermute x13 -> x12, starting transfers between devices: 53.6 us -> 50.9 us  [swap(): lax.ppermute(head, 'space', [((i + 1) % space_n, i) for i in range(space_...]
    ppermute x13 -> x12, starting transfers between devices: 6.92 us -> 7.56 us  [swap(): lax.ppermute(tail, 'space', [(i, (i + 1) % space_n) for i in range(space_...]
    unnamed x65 -> x71, local copies, waits for them, and re-layouts: 9.35 us -> 8.8 us
    ppermute x13 -> x12, waiting for transfers between devices: 33.5 us -> 34 us  [swap(): lax.ppermute(tail, 'space', [(i, (i + 1) % space_n) for i in range(space_...]
  transfers between devices with their start and end apart: 29 -> 27, of which waited for: 17 -> 14; matrix products, arithmetic and copies ran while one was open for 2% -> 3% of each run, Pallas kernels for 10% -> 10%
where the time goes in v11:
time: 265 us; the launch traced here: 264 us
  Pallas kernels  94.9 us (36%)
  waiting for transfers between devices  73.4 us (28%)
  starting transfers between devices  60.1 us (23%)
  local copies, waits for them, and re-layouts  16.2 us (6%)
  between operations  14.3 us (5%)
  other arithmetic  3.88 us (1%)
    pallas_call x19, Pallas kernels, call(): pl.pallas_call(kernel, out_shape=outs, in_specs=[blocks[i] if blocks is n...  94.9 us
    ppermute x12, starting transfers between devices, swap(): lax.ppermute(head, 'space', [((i + 1) % space_n, i) for i in range(space_...  50.9 us
    all_gather x2, waiting for transfers between devices, per_device(): rint_all = lax.all_gather(rint[None], 'tm')  34.3 us
    ppermute x12, waiting for transfers between devices, swap(): lax.ppermute(tail, 'space', [(i, (i + 1) % space_n) for i in range(space_...  34 us
    unnamed x71, local copies, waits for them, and re-layouts  8.8 us
    ppermute x12, starting transfers between devices, swap(): lax.ppermute(tail, 'space', [(i, (i + 1) % space_n) for i in range(space_...  7.56 us
  transfers between devices with their start and end apart: 27, of which 14 were waited for; matrix products, arithmetic and copies ran while one was open for 3% of the time, Pallas kernels for 10%

profile of v11, /device:TPU:0, one launch (start us, length us, event | category | flops | bytes accessed | tf_op | source)
XLA Modules:
  0.0 264.0 jit_solution(3166612072373976179)
XLA Ops:
  24.1 9.6 %collective-permute-done.p_ref = f32[4,12,16,128]{3,2,1,0:T(8,128)S(1)} collective-permute-done((f32[4,12,16,128]{3,2,1,0:T(8,128)}, f32[4,12,16,128]{3,2,1,0:T(8,128)S(1)}, u32[]{:S(2)}, u32[]{:S(2)}) %collective-permute-start) | collective-permute-done | bytes 393248 | tf_op jit(solution)/shard_map/ppermute | solution.py:288
  36.7 10.5 %shard_map.131 = (f32[3,12,128,128]{3,2,1,0:T(8,128)}, f32[1,12,128,128]{3,2,1,0:T(8,128)}, f32[1,12,16,128]{3,2,1,0:T(8,128)}, f32[1,12,16,128]{3,2,1,0:T(8,128)}) custom-call(f32[3,12,128,128]{3,2,1,0:T(8,128)} %pad_maximum_fusion.u_ref, f32[4,12,16,128]{3,2,1,0:T(8,128)} %copy-done.2, f32[4,12,16,128]{3,2,1,0:T(8,128)} %collective-permute-done.1.n_ref, ...), custom_call_target="tpu_custom_call" | custom-call | flops 1822556160 | bytes 6685524 | tf_op jit(solution)/shard_map/pallas_call | solution.py:217
  47.5 4.6 %collective-permute-start.3 = (f32[1,12,16,128]{3,2,1,0:T(8,128)}, f32[1,12,16,128]{3,2,1,0:T(8,128)S(1)}, u32[]{:S(2)}, u32[]{:S(2)}) collective-permute-start(f32[1,12,16,128]{3,2,1,0:T(8,128)} %get-tuple-element.52), channel_id=1, source_target_pairs={{1,0},{2,1},{3,2},{4,3},{5,4},{6,5},{7,6},{0,7},{9,8},{10,9},{11,1... | collective-permute-start | bytes 294920 | tf_op jit(solution)/shard_map/ppermute | solution.py:289
  55.5 6.0 %shard_map.132 = (f32[1,12,128,128]{3,2,1,0:T(8,128)}, f32[1,12,128,128]{3,2,1,0:T(8,128)}, f32[1,12,16,128]{3,2,1,0:T(8,128)}, f32[1,12,16,128]{3,2,1,0:T(8,128)}) custom-call(f32[1,12,128,128]{3,2,1,0:T(8,128)} %get-tuple-element.50.a1_ref.refs_0_, f32[1,12,16,128]{3,2,1,0:T(8,128)} %copy-done.8, f32[1,12,16,128]{3,2,1,0:T(8,128)} %copy-done.10, ...), custom_call_target="tpu_custom_call" | custom-call | flops 607518720 | bytes 5309268 | tf_op jit(solution)/shard_map/pallas_call | solution.py:217
  61.6 4.6 %collective-permute-start.5 = (f32[1,12,16,128]{3,2,1,0:T(8,128)}, f32[1,12,16,128]{3,2,1,0:T(8,128)S(1)}, u32[]{:S(2)}, u32[]{:S(2)}) collective-permute-start(f32[1,12,16,128]{3,2,1,0:T(8,128)} %get-tuple-element.57), channel_id=1, source_target_pairs={{1,0},{2,1},{3,2},{4,3},{5,4},{6,5},{7,6},{0,7},{9,8},{10,9},{11,1... | collective-permute-start | bytes 294920 | tf_op jit(solution)/shard_map/ppermute | solution.py:289
  67.4 4.9 %shard_map.133 = (f32[1,12,64,128]{3,2,1,0:T(8,128)}, f32[1,12,64,128]{3,2,1,0:T(8,128)}) custom-call(f32[3,12,128,128]{3,2,1,0:T(8,128)} %pad_maximum_fusion.u_ref, f32[4,12,16,128]{3,2,1,0:T(8,128)} %copy-done.2, f32[4,12,16,128]{3,2,1,0:T(8,128)} %collective-permute-done.1.n_ref, f32[64,128]{1,0:T(8,128)} %constant.28.clone.r_ref.refs_11_, ...), custom_call_target="tpu_custom_call" | custom-call | flops 228261888 | bytes 4064596 | tf_op jit(solution)/shard_map/pallas_call | solution.py:217
  73.0 6.6 %shard_map.134 = (f32[12,64,128]{2,1,0:T(8,128)}, f32[12,64,128]{2,1,0:T(8,128)}) custom-call(f32[1,12,128,128]{3,2,1,0:T(8,128)} %get-tuple-element.54.a2_ref.refs_1_, f32[1,12,16,128]{3,2,1,0:T(8,128)} %copy-done.11, f32[1,12,16,128]{3,2,1,0:T(8,128)} %copy-done.13, f32[256,128]{1,0:T(8,128)} %constant.26.clone.l_ref, f32[128,128]{1,0:T(8,128)} %constant.25.clone.x_ref, ...), custom_call_target="tpu_custom_call" | custom-call | flops 607518720 | bytes 5538644 | tf_op jit(solution)/shard_map/pallas_call | solution.py:217
  82.5 3.7 %shard_map.135.g_ref = f32[1,12,64,128]{3,2,1,0:T(8,128)} custom-call(f32[1,12,64,128]{3,2,1,0:T(8,128)} %convolution_bitcast_fusion.w_ref.refs_4_.refs_2_, f32[4,12,16,128]{3,2,1,0:T(8,128)} %copy-done.2, f32[4,12,16,128]{3,2,1,0:T(8,128)} %collective-permute-done.1.n_ref, f32[8,16]{1,0:T(8,128)} %constant.30.clone.rp_ref, f32[128,64]{1,0:T(8,128)} %constant.27.clone.l_ref, ...), custom_call_target="tpu_custom_call" | custom-call | flops 228261888 | bytes 1672532 | tf_op jit(solution)/shard_map/pallas_call | solution.py:217
  86.2 12.6 %all-gather.5.cloned.1.call-done = f32[48,64,128]{2,1,0:T(8,128)} async-done(((f32[12,64,128]{2,1,0:T(8,128)}), f32[48,64,128]{2,1,0:T(8,128)}) %all-gather.5.cloned.1.call-update) | async-done | bytes 1572880 | tf_op jit(solution)/shard_map/all_gather | solution.py:531
  101.6 4.0 %collective-permute-start.7 = (f32[1,12,8,128]{3,2,1,0:T(8,128)}, f32[1,12,8,128]{3,2,1,0:T(8,128)S(1)}, u32[]{:S(2)}, u32[]{:S(2)}) collective-permute-start(f32[1,12,8,128]{3,2,1,0:T(8,128)} %get-tuple-element.64), channel_id=1, source_target_pairs={{1,0},{2,1},{3,2},{4,3},{5,4},{6,5},{7,6},{0,7},{9,8},{10,9},{11,1... | collective-permute-start | bytes 147464 | tf_op jit(solution)/shard_map/ppermute | solution.py:289
  108.5 3.5 %shard_map.137 = (f32[1,12,64,128]{3,2,1,0:T(8,128)}, f32[1,12,8,128]{3,2,1,0:T(8,128)}, f32[1,12,8,128]{3,2,1,0:T(8,128)}) custom-call(f32[1,12,64,128]{3,2,1,0:T(8,128)} %get-tuple-element.62.w_ref.refs_5_, f32[1,12,8,128]{3,2,1,0:T(8,128)} %copy-done.18, f32[1,12,8,128]{3,2,1,0:T(8,128)} %copy-done.23, f32[128,64]{1,0:T(8,128)} %constant.27.clone.l_ref, ...), custom_call_target="tpu_custom_call" | custom-call | flops 228261888 | bytes 2655060 | tf_op jit(solution)/shard_map/pallas_call | solution.py:217
  112.5 4.3 %collective-permute-start.9 = (f32[1,12,8,128]{3,2,1,0:T(8,128)}, f32[1,12,8,128]{3,2,1,0:T(8,128)S(1)}, u32[]{:S(2)}, u32[]{:S(2)}) collective-permute-start(f32[1,12,8,128]{3,2,1,0:T(8,128)} %get-tuple-element.67), channel_id=1, source_target_pairs={{1,0},{2,1},{3,2},{4,3},{5,4},{6,5},{7,6},{0,7},{9,8},{10,9},{11,1... | collective-permute-start | bytes 147464 | tf_op jit(solution)/shard_map/ppermute | solution.py:289
  119.7 3.5 %shard_map.138 = (f32[1,12,64,128]{3,2,1,0:T(8,128)}, f32[1,12,8,128]{3,2,1,0:T(8,128)}, f32[1,12,8,128]{3,2,1,0:T(8,128)}) custom-call(f32[1,12,64,128]{3,2,1,0:T(8,128)} %get-tuple-element.65.w_ref.refs_6_, f32[1,12,8,128]{3,2,1,0:T(8,128)} %copy-done.19, f32[1,12,8,128]{3,2,1,0:T(8,128)} %copy-done.24, f32[128,64]{1,0:T(8,128)} %constant.27.clone.l_ref, ...), custom_call_target="tpu_custom_call" | custom-call | flops 228261888 | bytes 2655060 | tf_op jit(solution)/shard_map/pallas_call | solution.py:217
  123.2 4.8 %collective-permute-start.11 = (f32[1,12,8,128]{3,2,1,0:T(8,128)}, f32[1,12,8,128]{3,2,1,0:T(8,128)S(1)}, u32[]{:S(2)}, u32[]{:S(2)}) collective-permute-start(f32[1,12,8,128]{3,2,1,0:T(8,128)} %get-tuple-element.70), channel_id=1, source_target_pairs={{1,0},{2,1},{3,2},{4,3},{5,4},{6,5},{7,6},{0,7},{9,8},{10,9},{11,1... | collective-permute-start | bytes 147464 | tf_op jit(solution)/shard_map/ppermute | solution.py:289
  130.9 3.5 %shard_map.139 = (f32[1,12,64,128]{3,2,1,0:T(8,128)}, f32[1,12,8,128]{3,2,1,0:T(8,128)}, f32[1,12,8,128]{3,2,1,0:T(8,128)}) custom-call(f32[1,12,64,128]{3,2,1,0:T(8,128)} %get-tuple-element.68.w_ref.refs_7_, f32[1,12,8,128]{3,2,1,0:T(8,128)} %copy-done.16, f32[1,12,8,128]{3,2,1,0:T(8,128)} %copy-done.20, f32[128,64]{1,0:T(8,128)} %constant.27.clone.l_ref, ...), custom_call_target="tpu_custom_call" | custom-call | flops 228261888 | bytes 2655060 | tf_op jit(solution)/shard_map/pallas_call | solution.py:217
  135.3 6.7 %shard_map.140 = (f32[3,12,128,128]{3,2,1,0:T(8,128)}, f32[3,12,16,128]{3,2,1,0:T(8,128)}, f32[3,12,16,128]{3,2,1,0:T(8,128)}) custom-call(f32[1,12,128,128]{3,2,1,0:T(8,128)} %get-tuple-element.50.a1_ref.refs_0_, f32[1,12,128,128]{3,2,1,0:T(8,128)} %get-tuple-element.54.a2_ref.refs_1_, f32[1,12,64,128]{3,2,1,0:T(8,128)} %get-tuple-element.55.refs_2_, ...), custom_call_target="tpu_custom_call" | custom-call | flops 603979776 | bytes 8912904 | tf_op jit(solution)/shard_map/pallas_call | solution.py:217
  142.0 4.8 %collective-permute-start.14 = (f32[3,12,16,128]{3,2,1,0:T(8,128)}, f32[3,12,16,128]{3,2,1,0:T(8,128)S(1)}, u32[]{:S(2)}, u32[]{:S(2)}) collective-permute-start(f32[3,12,16,128]{3,2,1,0:T(8,128)} %get-tuple-element.74), channel_id=1, source_target_pairs={{1,0},{2,1},{3,2},{4,3},{5,4},{6,5},{7,6},{0,7},{9,8},{10,9},{11,1... | collective-permute-start | bytes 884744 | tf_op jit(solution)/shard_map/ppermute | solution.py:289
  146.7 5.3 %collective-permute-done.13.p_ref = f32[3,12,16,128]{3,2,1,0:T(8,128)S(1)} collective-permute-done((f32[3,12,16,128]{3,2,1,0:T(8,128)}, f32[3,12,16,128]{3,2,1,0:T(8,128)S(1)}, u32[]{:S(2)}, u32[]{:S(2)}) %collective-permute-start.13) | collective-permute-done | bytes 294944 | tf_op jit(solution)/shard_map/ppermute | solution.py:288
  154.9 10.5 %shard_map.141 = (f32[3,12,128,128]{3,2,1,0:T(8,128)}, f32[1,12,128,128]{3,2,1,0:T(8,128)}, f32[1,12,16,128]{3,2,1,0:T(8,128)}, f32[1,12,16,128]{3,2,1,0:T(8,128)}) custom-call(f32[3,12,128,128]{3,2,1,0:T(8,128)} %get-tuple-element.72.u_ref, f32[3,12,16,128]{3,2,1,0:T(8,128)} %copy-done.5, f32[3,12,16,128]{3,2,1,0:T(8,128)} %copy-done.6, ...), custom_call_target="tpu_custom_call" | custom-call | flops 1822556160 | bytes 6488916 | tf_op jit(solution)/shard_map/pallas_call | solution.py:217
  165.7 4.4 %collective-permute-start.16 = (f32[1,12,16,128]{3,2,1,0:T(8,128)}, f32[1,12,16,128]{3,2,1,0:T(8,128)S(1)}, u32[]{:S(2)}, u32[]{:S(2)}) collective-permute-start(f32[1,12,16,128]{3,2,1,0:T(8,128)} %get-tuple-element.77), channel_id=1, source_target_pairs={{1,0},{2,1},{3,2},{4,3},{5,4},{6,5},{7,6},{0,7},{9,8},{10,9},{11,1... | collective-permute-start | bytes 294920 | tf_op jit(solution)/shard_map/ppermute | solution.py:289
  173.6 5.9 %shard_map.142 = (f32[1,12,128,128]{3,2,1,0:T(8,128)}, f32[1,12,128,128]{3,2,1,0:T(8,128)}, f32[1,12,16,128]{3,2,1,0:T(8,128)}, f32[1,12,16,128]{3,2,1,0:T(8,128)}) custom-call(f32[1,12,128,128]{3,2,1,0:T(8,128)} %get-tuple-element.75.a1_ref, f32[1,12,16,128]{3,2,1,0:T(8,128)} %copy-done.7, f32[1,12,16,128]{3,2,1,0:T(8,128)} %copy-done.9, ...), custom_call_target="tpu_custom_call" | custom-call | flops 607518720 | bytes 5309268 | tf_op jit(solution)/shard_map/pallas_call | solution.py:217
  179.5 4.8 %collective-permute-start.18 = (f32[1,12,16,128]{3,2,1,0:T(8,128)}, f32[1,12,16,128]{3,2,1,0:T(8,128)S(1)}, u32[]{:S(2)}, u32[]{:S(2)}) collective-permute-start(f32[1,12,16,128]{3,2,1,0:T(8,128)} %get-tuple-element.81), channel_id=1, source_target_pairs={{1,0},{2,1},{3,2},{4,3},{5,4},{6,5},{7,6},{0,7},{9,8},{10,9},{11,1... | collective-permute-start | bytes 294920 | tf_op jit(solution)/shard_map/ppermute | solution.py:289
  184.3 4.8 %shard_map.143 = (f32[1,12,64,128]{3,2,1,0:T(8,128)}, f32[1,12,64,128]{3,2,1,0:T(8,128)}) custom-call(f32[3,12,128,128]{3,2,1,0:T(8,128)} %get-tuple-element.72.u_ref, f32[3,12,16,128]{3,2,1,0:T(8,128)} %copy-done.5, f32[3,12,16,128]{3,2,1,0:T(8,128)} %copy-done.6, f32[64,128]{1,0:T(8,128)} %constant.28.clone.r_ref.refs_11_, f32[8,16]{1,0:T(8,128)} %constant.30.clone.rp_ref, ...), custom_call_target="tpu_custom_call" | custom-call | flops 228261888 | bytes 3867988 | tf_op jit(solution)/shard_map/pallas_call | solution.py:217
  189.8 6.6 %shard_map.144 = (f32[12,64,128]{2,1,0:T(8,128)}, f32[12,64,128]{2,1,0:T(8,128)}) custom-call(f32[1,12,128,128]{3,2,1,0:T(8,128)} %get-tuple-element.79.a2_ref.refs_0_, f32[1,12,16,128]{3,2,1,0:T(8,128)} %copy-done.12, f32[1,12,16,128]{3,2,1,0:T(8,128)} %copy-done.14, f32[256,128]{1,0:T(8,128)} %constant.26.clone.l_ref, f32[128,128]{1,0:T(8,128)} %constant.25.clone.x_ref, ...), custom_call_target="tpu_custom_call" | custom-call | flops 607518720 | bytes 5538644 | tf_op jit(solution)/shard_map/pallas_call | solution.py:217
  196.4 21.7 %all-gather.7.cloned.1.call-done = f32[48,64,128]{2,1,0:T(8,128)} async-done(((f32[12,64,128]{2,1,0:T(8,128)}), f32[48,64,128]{2,1,0:T(8,128)}) %all-gather.7.cloned.1.call-update) | async-done | bytes 1572880 | tf_op jit(solution)/shard_map/all_gather | solution.py:531
  221.6 3.2 %collective-permute-start.20 = (f32[1,12,8,128]{3,2,1,0:T(8,128)}, f32[1,12,8,128]{3,2,1,0:T(8,128)S(1)}, u32[]{:S(2)}, u32[]{:S(2)}) collective-permute-start(f32[1,12,8,128]{3,2,1,0:T(8,128)} %get-tuple-element.88), channel_id=1, source_target_pairs={{1,0},{2,1},{3,2},{4,3},{5,4},{6,5},{7,6},{0,7},{9,8},{10,9},{11,1... | collective-permute-start | bytes 147464 | tf_op jit(solution)/shard_map/ppermute | solution.py:289
  227.8 3.5 %shard_map.146 = (f32[1,12,64,128]{3,2,1,0:T(8,128)}, f32[1,12,8,128]{3,2,1,0:T(8,128)}, f32[1,12,8,128]{3,2,1,0:T(8,128)}) custom-call(f32[1,12,64,128]{3,2,1,0:T(8,128)} %get-tuple-element.86.w_ref.refs_3_, f32[1,12,8,128]{3,2,1,0:T(8,128)} %copy-done.21, f32[1,12,8,128]{3,2,1,0:T(8,128)} %copy-done.25, f32[128,64]{1,0:T(8,128)} %constant.27.clone.l_ref, ...), custom_call_target="tpu_custom_call" | custom-call | flops 228261888 | bytes 2655060 | tf_op jit(solution)/shard_map/pallas_call | solution.py:217
  232.4 3.6 %collective-permute-start.22 = (f32[1,12,8,128]{3,2,1,0:T(8,128)}, f32[1,12,8,128]{3,2,1,0:T(8,128)S(1)}, u32[]{:S(2)}, u32[]{:S(2)}) collective-permute-start(f32[1,12,8,128]{3,2,1,0:T(8,128)} %get-tuple-element.91), channel_id=1, source_target_pairs={{1,0},{2,1},{3,2},{4,3},{5,4},{6,5},{7,6},{0,7},{9,8},{10,9},{11,1... | collective-permute-start | bytes 147464 | tf_op jit(solution)/shard_map/ppermute | solution.py:289
  238.9 3.5 %shard_map.147 = (f32[1,12,64,128]{3,2,1,0:T(8,128)}, f32[1,12,8,128]{3,2,1,0:T(8,128)}, f32[1,12,8,128]{3,2,1,0:T(8,128)}) custom-call(f32[1,12,64,128]{3,2,1,0:T(8,128)} %get-tuple-element.89.w_ref.refs_4_, f32[1,12,8,128]{3,2,1,0:T(8,128)} %copy-done.22, f32[1,12,8,128]{3,2,1,0:T(8,128)} %copy-done.26, f32[128,64]{1,0:T(8,128)} %constant.27.clone.l_ref, ...), custom_call_target="tpu_custom_call" | custom-call | flops 228261888 | bytes 2655060 | tf_op jit(solution)/shard_map/pallas_call | solution.py:217
  242.6 4.6 %collective-permute-start.24 = (f32[1,12,8,128]{3,2,1,0:T(8,128)}, f32[1,12,8,128]{3,2,1,0:T(8,128)S(1)}, u32[]{:S(2)}, u32[]{:S(2)}) collective-permute-start(f32[1,12,8,128]{3,2,1,0:T(8,128)} %get-tuple-element.94), channel_id=1, source_target_pairs={{1,0},{2,1},{3,2},{4,3},{5,4},{6,5},{7,6},{0,7},{9,8},{10,9},{11,1... | collective-permute-start | bytes 147464 | tf_op jit(solution)/shard_map/ppermute | solution.py:289
  250.1 3.5 %shard_map.148 = (f32[1,12,64,128]{3,2,1,0:T(8,128)}, f32[1,12,8,128]{3,2,1,0:T(8,128)}, f32[1,12,8,128]{3,2,1,0:T(8,128)}) custom-call(f32[1,12,64,128]{3,2,1,0:T(8,128)} %get-tuple-element.92.w_ref.refs_5_, f32[1,12,8,128]{3,2,1,0:T(8,128)} %copy-done.15, f32[1,12,8,128]{3,2,1,0:T(8,128)} %copy-done.17, f32[128,64]{1,0:T(8,128)} %constant.27.clone.l_ref, ...), custom_call_target="tpu_custom_call" | custom-call | flops 228261888 | bytes 2655060 | tf_op jit(solution)/shard_map/pallas_call | solution.py:217
  253.7 3.5 %shard_map.149 = (f32[1,12,128,128]{3,2,1,0:T(8,128)}, f32[1,12,64,128]{3,2,1,0:T(8,128)}) custom-call(f32[1,12,128,128]{3,2,1,0:T(8,128)} %get-tuple-element.79.a2_ref.refs_0_, f32[12,64,128]{2,1,0:T(8,128)} %get-tuple-element.84.refs_1_, f32[1,12,64,128]{3,2,1,0:T(8,128)} %convolution_bitcast_fusion.w_ref.refs_4_.refs_2_, ...), custom_call_target="tpu_custom_call" | custom-call | flops 150994944 | bytes 4358148 | tf_op jit(solution)/shard_map/pallas_call | solution.py:217
  (127 shorter events, 61.8 us)
Async XLA Ops:
  7.2 91.7 %all-gather.5.cloned.1.call-start = ((), (), s32[]{:S(2)}) async-start(), calls=%async_computation | async-start | bytes 1966080 | tf_op jit(solution)/shard_map/all_gather | solution.py:531
  12.5 21.2 %collective-permute-start = (f32[4,12,16,128]{3,2,1,0:T(8,128)}, f32[4,12,16,128]{3,2,1,0:T(8,128)S(1)}, u32[]{:S(2)}, u32[]{:S(2)}) collective-permute-start(f32[4,12,16,128]{3,2,1,0:T(8,128)} %pad_maximum_fusion.1), channel_id=1, source_target_pairs={{0,1},{1,2},{2,3},{3,4},{4,5},{5,6},{6,7},{7,0},{8,9},{9,10},{10,1... | collective-permute-start | bytes 1179656 | tf_op jit(solution)/shard_map/ppermute | solution.py:288
  16.3 20.4 %collective-permute-start.1 = (f32[4,12,16,128]{3,2,1,0:T(8,128)}, f32[4,12,16,128]{3,2,1,0:T(8,128)}, u32[]{:S(2)}, u32[]{:S(2)}) collective-permute-start(f32[4,12,16,128]{3,2,1,0:T(8,128)} %pad_maximum_fusion.2), channel_id=1, source_target_pairs={{1,0},{2,1},{3,2},{4,3},{5,4},{6,5},{7,6},{0,7},{9,8},{10,9},{11,1... | collective-permute-start | bytes 1179656 | tf_op jit(solution)/shard_map/ppermute | solution.py:289
  47.2 19.0 %copy-start.27 = (f32[1,12]{1,0:T(1,128)S(1)}, f32[1,12]{1,0:T(1,128)}, u32[]{:S(2)}) copy-start(f32[1,12]{1,0:T(1,128)} %get-tuple-element.105) | copy-start | bytes 148
  47.2 19.0 %copy-start.28 = (f32[1,12]{1,0:T(1,128)S(1)}, f32[1,12]{1,0:T(1,128)}, u32[]{:S(2)}) copy-start(f32[1,12]{1,0:T(1,128)} %get-tuple-element.113) | copy-start | bytes 148
  47.2 19.0 %copy-start.29 = (f32[1,12]{1,0:T(1,128)S(1)}, f32[1,12]{1,0:T(1,128)}, u32[]{:S(2)}) copy-start(f32[1,12]{1,0:T(1,128)} %get-tuple-element.115) | copy-start | bytes 148
  47.2 19.0 %copy-start.33 = (f32[1,12]{1,0:T(1,128)S(1)}, f32[1,12]{1,0:T(1,128)}, u32[]{:S(2)}) copy-start(f32[1,12]{1,0:T(1,128)} %get-tuple-element.102) | copy-start | bytes 148
  47.3 19.0 %copy-start.34 = (f32[1,12]{1,0:T(1,128)S(1)}, f32[1,12]{1,0:T(1,128)}, u32[]{:S(2)}) copy-start(f32[1,12]{1,0:T(1,128)} %get-tuple-element.116) | copy-start | bytes 148
  47.3 7.6 %collective-permute-start.2 = (f32[1,12,16,128]{3,2,1,0:T(8,128)}, f32[1,12,16,128]{3,2,1,0:T(8,128)S(1)}, u32[]{:S(2)}, u32[]{:S(2)}) collective-permute-start(f32[1,12,16,128]{3,2,1,0:T(8,128)} %get-tuple-element.51), channel_id=1, source_target_pairs={{0,1},{1,2},{2,3},{3,4},{4,5},{5,6},{6,7},{7,0},{8,9},{9,10},{10,1... | collective-permute-start | bytes 294920 | tf_op jit(solution)/shard_map/ppermute | solution.py:288
  47.5 7.4 %collective-permute-start.3 = (f32[1,12,16,128]{3,2,1,0:T(8,128)}, f32[1,12,16,128]{3,2,1,0:T(8,128)S(1)}, u32[]{:S(2)}, u32[]{:S(2)}) collective-permute-start(f32[1,12,16,128]{3,2,1,0:T(8,128)} %get-tuple-element.52), channel_id=1, source_target_pairs={{1,0},{2,1},{3,2},{4,3},{5,4},{6,5},{7,6},{0,7},{9,8},{10,9},{11,1... | collective-permute-start | bytes 294920 | tf_op jit(solution)/shard_map/ppermute | solution.py:289
  61.5 10.8 %collective-permute-start.4 = (f32[1,12,16,128]{3,2,1,0:T(8,128)}, f32[1,12,16,128]{3,2,1,0:T(8,128)S(1)}, u32[]{:S(2)}, u32[]{:S(2)}) collective-permute-start(f32[1,12,16,128]{3,2,1,0:T(8,128)} %get-tuple-element.56), channel_id=1, source_target_pairs={{0,1},{1,2},{2,3},{3,4},{4,5},{5,6},{6,7},{7,0},{8,9},{9,10},{10,1... | collective-permute-start | bytes 294920 | tf_op jit(solution)/shard_map/ppermute | solution.py:288
  61.6 10.8 %collective-permute-start.5 = (f32[1,12,16,128]{3,2,1,0:T(8,128)}, f32[1,12,16,128]{3,2,1,0:T(8,128)S(1)}, u32[]{:S(2)}, u32[]{:S(2)}) collective-permute-start(f32[1,12,16,128]{3,2,1,0:T(8,128)} %get-tuple-element.57), channel_id=1, source_target_pairs={{1,0},{2,1},{3,2},{4,3},{5,4},{6,5},{7,6},{0,7},{9,8},{10,9},{11,1... | collective-permute-start | bytes 294920 | tf_op jit(solution)/shard_map/ppermute | solution.py:289
  79.6 138.4 %all-gather.7.cloned.1.call-start = ((), (), s32[]{:S(2)}) async-start(), calls=%async_computation.1 | async-start | bytes 1966080 | tf_op jit(solution)/shard_map/all_gather | solution.py:531
  79.7 54.7 %collective-permute-start.12 = (f32[1,12,128,128]{3,2,1,0:T(8,128)S(1)}, f32[1,12,128,128]{3,2,1,0:T(8,128)S(1)}, u32[]{:S(2)}, u32[]{:S(2)}) collective-permute-start(f32[1,12,128,128]{3,2,1,0:T(8,128)S(1)} %copy-done.1), channel_id=1, source_target_pairs={{0,8},{8,16},{16,24},{1,9},{9,17},{17,25},{2,10},{10,18},{18,26},{... | collective-permute-start | bytes 2359304 | tf_op jit(solution)/shard_map/ppermute | solution.py:534
  100.9 7.0 %collective-permute-start.6 = (f32[1,12,8,128]{3,2,1,0:T(8,128)}, f32[1,12,8,128]{3,2,1,0:T(8,128)S(1)}, u32[]{:S(2)}, u32[]{:S(2)}) collective-permute-start(f32[1,12,8,128]{3,2,1,0:T(8,128)} %get-tuple-element.63), channel_id=1, source_target_pairs={{0,1},{1,2},{2,3},{3,4},{4,5},{5,6},{6,7},{7,0},{8,9},{9,10},{10,1... | collective-permute-start | bytes 147464 | tf_op jit(solution)/shard_map/ppermute | solution.py:288
  101.6 6.3 %collective-permute-start.7 = (f32[1,12,8,128]{3,2,1,0:T(8,128)}, f32[1,12,8,128]{3,2,1,0:T(8,128)S(1)}, u32[]{:S(2)}, u32[]{:S(2)}) collective-permute-start(f32[1,12,8,128]{3,2,1,0:T(8,128)} %get-tuple-element.64), channel_id=1, source_target_pairs={{1,0},{2,1},{3,2},{4,3},{5,4},{6,5},{7,6},{0,7},{9,8},{10,9},{11,1... | collective-permute-start | bytes 147464 | tf_op jit(solution)/shard_map/ppermute | solution.py:289
  112.1 7.0 %collective-permute-start.8 = (f32[1,12,8,128]{3,2,1,0:T(8,128)}, f32[1,12,8,128]{3,2,1,0:T(8,128)S(1)}, u32[]{:S(2)}, u32[]{:S(2)}) collective-permute-start(f32[1,12,8,128]{3,2,1,0:T(8,128)} %get-tuple-element.66), channel_id=1, source_target_pairs={{0,1},{1,2},{2,3},{3,4},{4,5},{5,6},{6,7},{7,0},{8,9},{9,10},{10,1... | collective-permute-start | bytes 147464 | tf_op jit(solution)/shard_map/ppermute | solution.py:288
  112.5 6.6 %collective-permute-start.9 = (f32[1,12,8,128]{3,2,1,0:T(8,128)}, f32[1,12,8,128]{3,2,1,0:T(8,128)S(1)}, u32[]{:S(2)}, u32[]{:S(2)}) collective-permute-start(f32[1,12,8,128]{3,2,1,0:T(8,128)} %get-tuple-element.67), channel_id=1, source_target_pairs={{1,0},{2,1},{3,2},{4,3},{5,4},{6,5},{7,6},{0,7},{9,8},{10,9},{11,1... | collective-permute-start | bytes 147464 | tf_op jit(solution)/shard_map/ppermute | solution.py:289
  123.2 7.0 %collective-permute-start.10 = (f32[1,12,8,128]{3,2,1,0:T(8,128)}, f32[1,12,8,128]{3,2,1,0:T(8,128)S(1)}, u32[]{:S(2)}, u32[]{:S(2)}) collective-permute-start(f32[1,12,8,128]{3,2,1,0:T(8,128)} %get-tuple-element.69), channel_id=1, source_target_pairs={{0,1},{1,2},{2,3},{3,4},{4,5},{5,6},{6,7},{7,0},{8,9},{9,10},{10,1... | collective-permute-start | bytes 147464 | tf_op jit(solution)/shard_map/ppermute | solution.py:288
  123.2 7.0 %collective-permute-start.11 = (f32[1,12,8,128]{3,2,1,0:T(8,128)}, f32[1,12,8,128]{3,2,1,0:T(8,128)S(1)}, u32[]{:S(2)}, u32[]{:S(2)}) collective-permute-start(f32[1,12,8,128]{3,2,1,0:T(8,128)} %get-tuple-element.70), channel_id=1, source_target_pairs={{1,0},{2,1},{3,2},{4,3},{5,4},{6,5},{7,6},{0,7},{9,8},{10,9},{11,1... | collective-permute-start | bytes 147464 | tf_op jit(solution)/shard_map/ppermute | solution.py:289
  142.0 10.1 %collective-permute-start.13 = (f32[3,12,16,128]{3,2,1,0:T(8,128)}, f32[3,12,16,128]{3,2,1,0:T(8,128)S(1)}, u32[]{:S(2)}, u32[]{:S(2)}) collective-permute-start(f32[3,12,16,128]{3,2,1,0:T(8,128)} %get-tuple-element.73), channel_id=1, source_target_pairs={{0,1},{1,2},{2,3},{3,4},{4,5},{5,6},{6,7},{7,0},{8,9},{9,10},{10,1... | collective-permute-start | bytes 884744 | tf_op jit(solution)/shard_map/ppermute | solution.py:288
  142.0 12.2 %collective-permute-start.14 = (f32[3,12,16,128]{3,2,1,0:T(8,128)}, f32[3,12,16,128]{3,2,1,0:T(8,128)S(1)}, u32[]{:S(2)}, u32[]{:S(2)}) collective-permute-start(f32[3,12,16,128]{3,2,1,0:T(8,128)} %get-tuple-element.74), channel_id=1, source_target_pairs={{1,0},{2,1},{3,2},{4,3},{5,4},{6,5},{7,6},{0,7},{9,8},{10,9},{11,1... | collective-permute-start | bytes 884744 | tf_op jit(solution)/shard_map/ppermute | solution.py:289
  165.4 7.5 %collective-permute-start.15 = (f32[1,12,16,128]{3,2,1,0:T(8,128)}, f32[1,12,16,128]{3,2,1,0:T(8,128)S(1)}, u32[]{:S(2)}, u32[]{:S(2)}) collective-permute-start(f32[1,12,16,128]{3,2,1,0:T(8,128)} %get-tuple-element.76), channel_id=1, source_target_pairs={{0,1},{1,2},{2,3},{3,4},{4,5},{5,6},{6,7},{7,0},{8,9},{9,10},{10,1... | collective-permute-start | bytes 294920 | tf_op jit(solution)/shard_map/ppermute | solution.py:288
  165.7 7.1 %collective-permute-start.16 = (f32[1,12,16,128]{3,2,1,0:T(8,128)}, f32[1,12,16,128]{3,2,1,0:T(8,128)S(1)}, u32[]{:S(2)}, u32[]{:S(2)}) collective-permute-start(f32[1,12,16,128]{3,2,1,0:T(8,128)} %get-tuple-element.77), channel_id=1, source_target_pairs={{1,0},{2,1},{3,2},{4,3},{5,4},{6,5},{7,6},{0,7},{9,8},{10,9},{11,1... | collective-permute-start | bytes 294920 | tf_op jit(solution)/shard_map/ppermute | solution.py:289
  179.5 9.6 %collective-permute-start.17 = (f32[1,12,16,128]{3,2,1,0:T(8,128)}, f32[1,12,16,128]{3,2,1,0:T(8,128)S(1)}, u32[]{:S(2)}, u32[]{:S(2)}) collective-permute-start(f32[1,12,16,128]{3,2,1,0:T(8,128)} %get-tuple-element.80), channel_id=1, source_target_pairs={{0,1},{1,2},{2,3},{3,4},{4,5},{5,6},{6,7},{7,0},{8,9},{9,10},{10,1... | collective-permute-start | bytes 294920 | tf_op jit(solution)/shard_map/ppermute | solution.py:288
  179.5 9.6 %collective-permute-start.18 = (f32[1,12,16,128]{3,2,1,0:T(8,128)}, f32[1,12,16,128]{3,2,1,0:T(8,128)S(1)}, u32[]{:S(2)}, u32[]{:S(2)}) collective-permute-start(f32[1,12,16,128]{3,2,1,0:T(8,128)} %get-tuple-element.81), channel_id=1, source_target_pairs={{1,0},{2,1},{3,2},{4,3},{5,4},{6,5},{7,6},{0,7},{9,8},{10,9},{11,1... | collective-permute-start | bytes 294920 | tf_op jit(solution)/shard_map/ppermute | solution.py:289
  220.1 7.0 %collective-permute-start.19 = (f32[1,12,8,128]{3,2,1,0:T(8,128)}, f32[1,12,8,128]{3,2,1,0:T(8,128)S(1)}, u32[]{:S(2)}, u32[]{:S(2)}) collective-permute-start(f32[1,12,8,128]{3,2,1,0:T(8,128)} %get-tuple-element.87), channel_id=1, source_target_pairs={{0,1},{1,2},{2,3},{3,4},{4,5},{5,6},{6,7},{7,0},{8,9},{9,10},{10,1... | collective-permute-start | bytes 147464 | tf_op jit(solution)/shard_map/ppermute | solution.py:288
  221.6 5.5 %collective-permute-start.20 = (f32[1,12,8,128]{3,2,1,0:T(8,128)}, f32[1,12,8,128]{3,2,1,0:T(8,128)S(1)}, u32[]{:S(2)}, u32[]{:S(2)}) collective-permute-start(f32[1,12,8,128]{3,2,1,0:T(8,128)} %get-tuple-element.88), channel_id=1, source_target_pairs={{1,0},{2,1},{3,2},{4,3},{5,4},{6,5},{7,6},{0,7},{9,8},{10,9},{11,1... | collective-permute-start | bytes 147464 | tf_op jit(solution)/shard_map/ppermute | solution.py:289
  231.3 7.0 %collective-permute-start.21 = (f32[1,12,8,128]{3,2,1,0:T(8,128)}, f32[1,12,8,128]{3,2,1,0:T(8,128)S(1)}, u32[]{:S(2)}, u32[]{:S(2)}) collective-permute-start(f32[1,12,8,128]{3,2,1,0:T(8,128)} %get-tuple-element.90), channel_id=1, source_target_pairs={{0,1},{1,2},{2,3},{3,4},{4,5},{5,6},{6,7},{7,0},{8,9},{9,10},{10,1... | collective-permute-start | bytes 147464 | tf_op jit(solution)/shard_map/ppermute | solution.py:288
  232.4 5.9 %collective-permute-start.22 = (f32[1,12,8,128]{3,2,1,0:T(8,128)}, f32[1,12,8,128]{3,2,1,0:T(8,128)S(1)}, u32[]{:S(2)}, u32[]{:S(2)}) collective-permute-start(f32[1,12,8,128]{3,2,1,0:T(8,128)} %get-tuple-element.91), channel_id=1, source_target_pairs={{1,0},{2,1},{3,2},{4,3},{5,4},{6,5},{7,6},{0,7},{9,8},{10,9},{11,1... | collective-permute-start | bytes 147464 | tf_op jit(solution)/shard_map/ppermute | solution.py:289
  242.5 7.0 %collective-permute-start.23 = (f32[1,12,8,128]{3,2,1,0:T(8,128)}, f32[1,12,8,128]{3,2,1,0:T(8,128)S(1)}, u32[]{:S(2)}, u32[]{:S(2)}) collective-permute-start(f32[1,12,8,128]{3,2,1,0:T(8,128)} %get-tuple-element.93), channel_id=1, source_target_pairs={{0,1},{1,2},{2,3},{3,4},{4,5},{5,6},{6,7},{7,0},{8,9},{9,10},{10,1... | collective-permute-start | bytes 147464 | tf_op jit(solution)/shard_map/ppermute | solution.py:288
  242.6 6.8 %collective-permute-start.24 = (f32[1,12,8,128]{3,2,1,0:T(8,128)}, f32[1,12,8,128]{3,2,1,0:T(8,128)S(1)}, u32[]{:S(2)}, u32[]{:S(2)}) collective-permute-start(f32[1,12,8,128]{3,2,1,0:T(8,128)} %get-tuple-element.94), channel_id=1, source_target_pairs={{1,0},{2,1},{3,2},{4,3},{5,4},{6,5},{7,6},{0,7},{9,8},{10,9},{11,1... | collective-permute-start | bytes 147464 | tf_op jit(solution)/shard_map/ppermute | solution.py:289
  (30 other events, 57.2 us)
Sparse Core Ops, SparseCore 0:
  79.7 19.0 all-gather.4
  196.5 21.5 all-gather.6

commit v12 on v10

--- a/solution.py
+++ b/solution.py
@@ -127,6 +127,20 @@
     rows = prev_ref.shape[2]
     planes = span // rows
     f32 = jnp.float32
+    y_lift = 28.0 if y_elem == len(FINE_NODES) else 6.0
+    lifts = (28.0, y_lift, 28.0)
+
+    class Speeds:
+        def __getitem__(self, key):
+            k, f = key
+            if k < 3:
+                return -cf_ref[k, f]
+            d = (k - 3) // 2
+            if (k - 3) % 2 == 0:
+                return lifts[d] * jnp.maximum(cf_ref[d, f], 0.0)
+            return lifts[d] * jnp.maximum(-cf_ref[d, f], 0.0)
+
+    speeds = Speeds()
     row = lax.broadcasted_iota(jnp.int32, (span, columns), 0)
     lane = lax.broadcasted_iota(jnp.int32, (span, columns), 1)
     yy = row % rows
@@ -147,31 +161,31 @@
             for f in range(fields):
                 v = v_ref[b, f]
                 cols = slice(f * columns, (f + 1) * columns)
-                t = (cf_ref[0, f] * xd_ref[b, f] + cf_ref[1, f] * yz_ref[b, :span, cols]
-                     + cf_ref[2, f] * yz_ref[b, span:, cols])
+                t = (speeds[0, f] * xd_ref[b, f] + speeds[1, f] * yz_ref[b, :span, cols]
+                     + speeds[2, f] * yz_ref[b, span:, cols])
                 before_x = pltpu.roll(v, 1, 1)
                 after_x = pltpu.roll(v, columns - 1, 1)
-                t = t + jnp.where(x_first, cf_ref[3, f] * (before_x - v), 0.0)
-                t = t + jnp.where(x_last, cf_ref[4, f] * (after_x - v), 0.0)
+                t = t + jnp.where(x_first, speeds[3, f] * (before_x - v), 0.0)
+                t = t + jnp.where(x_last, speeds[4, f] * (after_x - v), 0.0)
                 before_y = jnp.where(yy == 0, pltpu.roll(v, span - rows + 1, 0),
                                      pltpu.roll(v, 1, 0))
                 after_y = jnp.where(yy == rows - 1, pltpu.roll(v, rows - 1, 0),
                                     pltpu.roll(v, span - 1, 0))
-                t = t + jnp.where(y_first, cf_ref[5, f] * (before_y - v), 0.0)
-                t = t + jnp.where(y_last, cf_ref[6, f] * (after_y - v), 0.0)
+                t = t + jnp.where(y_first, speeds[5, f] * (before_y - v), 0.0)
+                t = t + jnp.where(y_last, speeds[6, f] * (after_y - v), 0.0)
                 if planes > 8:
                     before_z = pltpu.roll(v, rows, 0)
                     after_z = pltpu.roll(v, span - rows, 0)
-                    t = t + jnp.where(z_first & (zz > 0), cf_ref[7, f] * before_z, 0.0)
-                    t = t + jnp.where(z_last & (zz < planes - 1), cf_ref[8, f] * after_z, 0.0)
-                t = t - jnp.where(z_first, cf_ref[7, f] * v, 0.0)
-                t = t - jnp.where(z_last, cf_ref[8, f] * v, 0.0)
+                    t = t + jnp.where(z_first & (zz > 0), speeds[7, f] * before_z, 0.0)
+                    t = t + jnp.where(z_last & (zz < planes - 1), speeds[8, f] * after_z, 0.0)
+                t = t - jnp.where(z_first, speeds[7, f] * v, 0.0)
+                t = t - jnp.where(z_last, speeds[8, f] * v, 0.0)
                 out_ref[b, f] = t
                 out_ref[b, f, pl.ds(0, rows), :] = (
-                    out_ref[b, f, pl.ds(0, rows), :] + cf_ref[7, f] * prev_ref[b, f]
+                    out_ref[b, f, pl.ds(0, rows), :] + speeds[7, f] * prev_ref[b, f]
                 )
                 out_ref[b, f, pl.ds(span - rows, rows), :] = (
-                    out_ref[b, f, pl.ds(span - rows, rows), :] + cf_ref[8, f] * next_ref[b, f]
+                    out_ref[b, f, pl.ds(span - rows, rows), :] + speeds[8, f] * next_ref[b, f]
                 )
                 s_ref[b, f] = jnp.tanh(v)
 
@@ -270,8 +284,8 @@
     rmat = jnp.asarray(np.kron(np.eye(depth), restrict_rows), jnp.float32)
     pmat = jnp.asarray(np.kron(np.eye(depth), prolong_rows), jnp.float32)
     restrict_plane = jnp.asarray(restrict_rows, jnp.float32)
-    scalars = (cf_fine, reactions.astype(jnp.int32), rates, energies)
-    coarse_scalars = (cf_coarse, reactions.astype(jnp.int32), rates, energies)
+    scalars = (velocity, reactions, rates, energies)
+    coarse_scalars = scalars
     scalar_kinds = (True, True, True, True)
 
     space_n = lax.axis_size("space")

time: 259 us -> 259 us (level)
    unnamed x65 -> x63, local copies, waits for them, and re-layouts: 9.35 us -> 9.35 us
  transfers between devices with their start and end apart: 29 -> 29, of which waited for: 17 -> 17; matrix products, arithmetic and copies ran while one was open for 2% -> 1% of each run, Pallas kernels for 10% -> 10%
where the time goes in v12:
time: 259 us; the launch traced here: 258 us
  Pallas kernels  94.3 us (36%)
  waiting for transfers between devices  70.7 us (27%)
  starting transfers between devices  62.8 us (24%)
  between operations  14.3 us (6%)
  local copies, waits for them, and re-layouts  13 us (5%)
    pallas_call x19, Pallas kernels, call(): pl.pallas_call(kernel, out_shape=outs, in_specs=[blocks[i] if blocks is n...  94.3 us
    ppermute x13, starting transfers between devices, swap(): lax.ppermute(head, 'space', [((i + 1) % space_n, i) for i in range(space_...  54.8 us
    ppermute x13, waiting for transfers between devices, swap(): lax.ppermute(tail, 'space', [(i, (i + 1) % space_n) for i in range(space_...  34.3 us
    all_gather x2, waiting for transfers between devices, per_device(): rint_all = lax.all_gather(rint[None], 'tm')  26 us
    ppermute x13, waiting for transfers between devices, swap(): lax.ppermute(head, 'space', [((i + 1) % space_n, i) for i in range(space_...  10.3 us
    unnamed x63, local copies, waits for them, and re-layouts  9.35 us
    ppermute x13, starting transfers between devices, swap(): lax.ppermute(tail, 'space', [(i, (i + 1) % space_n) for i in range(space_...  6.42 us
  transfers between devices with their start and end apart: 29, of which 17 were waited for; matrix products, arithmetic and copies ran while one was open for 1% of the time, Pallas kernels for 10%

profile of v12, /device:TPU:0, one launch (start us, length us, event | category | flops | bytes accessed | tf_op | source)
XLA Modules:
  0.0 258.1 jit_solution(17472364467527281637)
XLA Ops:
  11.9 6.0 %collective-permute-start.1 = (f32[3,12,16,128]{3,2,1,0:T(8,128)}, f32[3,12,16,128]{3,2,1,0:T(8,128)S(1)}, u32[]{:S(2)}, u32[]{:S(2)}) collective-permute-start(f32[3,12,16,128]{3,2,1,0:T(8,128)} %get-tuple-element.98), channel_id=1, source_target_pairs={{1,0},{2,1},{3,2},{4,3},{5,4},{6,5},{7,6},{0,7},{9,8},{10,9},{11,1... | collective-permute-start | bytes 884744 | tf_op jit(solution)/shard_map/ppermute | solution.py:303
  20.2 5.4 %collective-permute-done.1.n_ref = f32[3,12,16,128]{3,2,1,0:T(8,128)S(1)} collective-permute-done((f32[3,12,16,128]{3,2,1,0:T(8,128)}, f32[3,12,16,128]{3,2,1,0:T(8,128)S(1)}, u32[]{:S(2)}, u32[]{:S(2)}) %collective-permute-start.1) | collective-permute-done | bytes 294944 | tf_op jit(solution)/shard_map/ppermute | solution.py:303
  25.6 4.9 %collective-permute-done.p_ref = f32[3,12,16,128]{3,2,1,0:T(8,128)} collective-permute-done((f32[3,12,16,128]{3,2,1,0:T(8,128)}, f32[3,12,16,128]{3,2,1,0:T(8,128)}, u32[]{:S(2)}, u32[]{:S(2)}) %collective-permute-start) | collective-permute-done | bytes 294944 | tf_op jit(solution)/shard_map/ppermute | solution.py:302
  30.5 10.5 %shard_map.131 = (f32[3,12,128,128]{3,2,1,0:T(8,128)}, f32[1,12,128,128]{3,2,1,0:T(8,128)}, f32[1,12,16,128]{3,2,1,0:T(8,128)}, f32[1,12,16,128]{3,2,1,0:T(8,128)}) custom-call(f32[3,12,128,128]{3,2,1,0:T(8,128)} %pad_maximum_fusion.u_ref, f32[3,12,16,128]{3,2,1,0:T(8,128)} %collective-permute-done.p_ref, f32[3,12,16,128]{3,2,1,0:T(8,128)} %copy-done.4, ...), custom_call_target="tpu_custom_call" | custom-call | flops 1822556160 | bytes 6488628 | tf_op jit(solution)/shard_map/pallas_call | solution.py:231
  50.3 6.0 %shard_map.132 = (f32[1,12,128,128]{3,2,1,0:T(8,128)}, f32[1,12,128,128]{3,2,1,0:T(8,128)}, f32[1,12,16,128]{3,2,1,0:T(8,128)}, f32[1,12,16,128]{3,2,1,0:T(8,128)}) custom-call(f32[1,12,128,128]{3,2,1,0:T(8,128)} %get-tuple-element.50.a1_ref.refs_0_, f32[1,12,16,128]{3,2,1,0:T(8,128)} %copy-done.8, f32[1,12,16,128]{3,2,1,0:T(8,128)} %copy-done.10, ...), custom_call_target="tpu_custom_call" | custom-call | flops 607518720 | bytes 5308980 | tf_op jit(solution)/shard_map/pallas_call | solution.py:231
  56.5 4.4 %collective-permute-start.5 = (f32[1,12,16,128]{3,2,1,0:T(8,128)}, f32[1,12,16,128]{3,2,1,0:T(8,128)S(1)}, u32[]{:S(2)}, u32[]{:S(2)}) collective-permute-start(f32[1,12,16,128]{3,2,1,0:T(8,128)} %get-tuple-element.57), channel_id=1, source_target_pairs={{1,0},{2,1},{3,2},{4,3},{5,4},{6,5},{7,6},{0,7},{9,8},{10,9},{11,1... | collective-permute-start | bytes 294920 | tf_op jit(solution)/shard_map/ppermute | solution.py:303
  60.9 4.8 %shard_map.133 = (f32[1,12,64,128]{3,2,1,0:T(8,128)}, f32[1,12,64,128]{3,2,1,0:T(8,128)}) custom-call(f32[3,12,128,128]{3,2,1,0:T(8,128)} %pad_maximum_fusion.u_ref, f32[3,12,16,128]{3,2,1,0:T(8,128)} %collective-permute-done.p_ref, f32[3,12,16,128]{3,2,1,0:T(8,128)} %copy-done.4, f32[64,128]{1,0:T(8,128)} %constant.22.clone.r_ref.refs_11_, ...), custom_call_target="tpu_custom_call" | custom-call | flops 228261888 | bytes 3867700 | tf_op jit(solution)/shard_map/pallas_call | solution.py:231
  66.4 6.6 %shard_map.134 = (f32[12,64,128]{2,1,0:T(8,128)}, f32[12,64,128]{2,1,0:T(8,128)}) custom-call(f32[1,12,128,128]{3,2,1,0:T(8,128)} %get-tuple-element.54.a2_ref.refs_1_, f32[1,12,16,128]{3,2,1,0:T(8,128)} %copy-done.13, f32[1,12,16,128]{3,2,1,0:T(8,128)} %copy-done.14, f32[256,128]{1,0:T(8,128)} %constant.20.clone.l_ref, f32[128,128]{1,0:T(8,128)} %constant.19.clone.x_ref, ...), custom_call_target="tpu_custom_call" | custom-call | flops 607518720 | bytes 5538356 | tf_op jit(solution)/shard_map/pallas_call | solution.py:231
  79.7 5.0 %collective-permute-done.6 = f32[12,8,128]{2,1,0:T(8,128)S(1)} collective-permute-done((f32[12,8,128]{2,1,0:T(8,128)S(1)}, f32[12,8,128]{2,1,0:T(8,128)S(1)}, u32[]{:S(2)}, u32[]{:S(2)}) %collective-permute-start.6) | collective-permute-done | bytes 49184 | tf_op jit(solution)/shard_map/ppermute | solution.py:302
  88.5 4.3 %all-gather.5.cloned.1.call-done = f32[48,64,128]{2,1,0:T(8,128)} async-done(((f32[12,64,128]{2,1,0:T(8,128)}), f32[48,64,128]{2,1,0:T(8,128)}) %all-gather.5.cloned.1.call-update) | async-done | bytes 1572880 | tf_op jit(solution)/shard_map/all_gather | solution.py:537
  95.7 4.0 %collective-permute-start.9 = (f32[1,12,8,128]{3,2,1,0:T(8,128)}, f32[1,12,8,128]{3,2,1,0:T(8,128)S(1)}, u32[]{:S(2)}, u32[]{:S(2)}) collective-permute-start(f32[1,12,8,128]{3,2,1,0:T(8,128)} %get-tuple-element.64), channel_id=1, source_target_pairs={{1,0},{2,1},{3,2},{4,3},{5,4},{6,5},{7,6},{0,7},{9,8},{10,9},{11,1... | collective-permute-start | bytes 147464 | tf_op jit(solution)/shard_map/ppermute | solution.py:303
  102.6 3.5 %shard_map.137 = (f32[1,12,64,128]{3,2,1,0:T(8,128)}, f32[1,12,8,128]{3,2,1,0:T(8,128)}, f32[1,12,8,128]{3,2,1,0:T(8,128)}) custom-call(f32[1,12,64,128]{3,2,1,0:T(8,128)} %get-tuple-element.62.w_ref.refs_5_, f32[1,12,8,128]{3,2,1,0:T(8,128)} %copy-done.20, f32[1,12,8,128]{3,2,1,0:T(8,128)} %copy-done.25, f32[128,64]{1,0:T(8,128)} %constant.21.clone.l_ref, ...), custom_call_target="tpu_custom_call" | custom-call | flops 228261888 | bytes 2654772 | tf_op jit(solution)/shard_map/pallas_call | solution.py:231
  106.5 4.4 %collective-permute-start.11 = (f32[1,12,8,128]{3,2,1,0:T(8,128)}, f32[1,12,8,128]{3,2,1,0:T(8,128)S(1)}, u32[]{:S(2)}, u32[]{:S(2)}) collective-permute-start(f32[1,12,8,128]{3,2,1,0:T(8,128)} %get-tuple-element.67), channel_id=1, source_target_pairs={{1,0},{2,1},{3,2},{4,3},{5,4},{6,5},{7,6},{0,7},{9,8},{10,9},{11,1... | collective-permute-start | bytes 147464 | tf_op jit(solution)/shard_map/ppermute | solution.py:303
  113.8 3.5 %shard_map.138 = (f32[1,12,64,128]{3,2,1,0:T(8,128)}, f32[1,12,8,128]{3,2,1,0:T(8,128)}, f32[1,12,8,128]{3,2,1,0:T(8,128)}) custom-call(f32[1,12,64,128]{3,2,1,0:T(8,128)} %get-tuple-element.65.w_ref.refs_6_, f32[1,12,8,128]{3,2,1,0:T(8,128)} %copy-done.21, f32[1,12,8,128]{3,2,1,0:T(8,128)} %copy-done.26, f32[128,64]{1,0:T(8,128)} %constant.21.clone.l_ref, ...), custom_call_target="tpu_custom_call" | custom-call | flops 228261888 | bytes 2654772 | tf_op jit(solution)/shard_map/pallas_call | solution.py:231
  117.3 4.8 %collective-permute-start.13 = (f32[1,12,8,128]{3,2,1,0:T(8,128)}, f32[1,12,8,128]{3,2,1,0:T(8,128)S(1)}, u32[]{:S(2)}, u32[]{:S(2)}) collective-permute-start(f32[1,12,8,128]{3,2,1,0:T(8,128)} %get-tuple-element.70), channel_id=1, source_target_pairs={{1,0},{2,1},{3,2},{4,3},{5,4},{6,5},{7,6},{0,7},{9,8},{10,9},{11,1... | collective-permute-start | bytes 147464 | tf_op jit(solution)/shard_map/ppermute | solution.py:303
  124.9 3.5 %shard_map.139 = (f32[1,12,64,128]{3,2,1,0:T(8,128)}, f32[1,12,8,128]{3,2,1,0:T(8,128)}, f32[1,12,8,128]{3,2,1,0:T(8,128)}) custom-call(f32[1,12,64,128]{3,2,1,0:T(8,128)} %get-tuple-element.68.w_ref.refs_7_, f32[1,12,8,128]{3,2,1,0:T(8,128)} %copy-done.18, f32[1,12,8,128]{3,2,1,0:T(8,128)} %copy-done.22, f32[128,64]{1,0:T(8,128)} %constant.21.clone.l_ref, ...), custom_call_target="tpu_custom_call" | custom-call | flops 228261888 | bytes 2654772 | tf_op jit(solution)/shard_map/pallas_call | solution.py:231
  129.4 6.7 %shard_map.140 = (f32[3,12,128,128]{3,2,1,0:T(8,128)}, f32[3,12,16,128]{3,2,1,0:T(8,128)}, f32[3,12,16,128]{3,2,1,0:T(8,128)}) custom-call(f32[1,12,128,128]{3,2,1,0:T(8,128)} %get-tuple-element.50.a1_ref.refs_0_, f32[1,12,128,128]{3,2,1,0:T(8,128)} %get-tuple-element.54.a2_ref.refs_1_, f32[1,12,64,128]{3,2,1,0:T(8,128)} %get-tuple-element.55.refs_2_, ...), custom_call_target="tpu_custom_call" | custom-call | flops 603979776 | bytes 8912904 | tf_op jit(solution)/shard_map/pallas_call | solution.py:231
  136.1 4.7 %collective-permute-start.16 = (f32[3,12,16,128]{3,2,1,0:T(8,128)}, f32[3,12,16,128]{3,2,1,0:T(8,128)S(1)}, u32[]{:S(2)}, u32[]{:S(2)}) collective-permute-start(f32[3,12,16,128]{3,2,1,0:T(8,128)} %get-tuple-element.74), channel_id=1, source_target_pairs={{1,0},{2,1},{3,2},{4,3},{5,4},{6,5},{7,6},{0,7},{9,8},{10,9},{11,1... | collective-permute-start | bytes 884744 | tf_op jit(solution)/shard_map/ppermute | solution.py:303
  140.8 5.3 %collective-permute-done.15.p_ref = f32[3,12,16,128]{3,2,1,0:T(8,128)S(1)} collective-permute-done((f32[3,12,16,128]{3,2,1,0:T(8,128)}, f32[3,12,16,128]{3,2,1,0:T(8,128)S(1)}, u32[]{:S(2)}, u32[]{:S(2)}) %collective-permute-start.15) | collective-permute-done | bytes 294944 | tf_op jit(solution)/shard_map/ppermute | solution.py:302
  149.0 10.5 %shard_map.141 = (f32[3,12,128,128]{3,2,1,0:T(8,128)}, f32[1,12,128,128]{3,2,1,0:T(8,128)}, f32[1,12,16,128]{3,2,1,0:T(8,128)}, f32[1,12,16,128]{3,2,1,0:T(8,128)}) custom-call(f32[3,12,128,128]{3,2,1,0:T(8,128)} %get-tuple-element.72.u_ref, f32[3,12,16,128]{3,2,1,0:T(8,128)} %copy-done.5, f32[3,12,16,128]{3,2,1,0:T(8,128)} %copy-done.6, ...), custom_call_target="tpu_custom_call" | custom-call | flops 1822556160 | bytes 6488628 | tf_op jit(solution)/shard_map/pallas_call | solution.py:231
  159.9 4.4 %collective-permute-start.18 = (f32[1,12,16,128]{3,2,1,0:T(8,128)}, f32[1,12,16,128]{3,2,1,0:T(8,128)S(1)}, u32[]{:S(2)}, u32[]{:S(2)}) collective-permute-start(f32[1,12,16,128]{3,2,1,0:T(8,128)} %get-tuple-element.77), channel_id=1, source_target_pairs={{1,0},{2,1},{3,2},{4,3},{5,4},{6,5},{7,6},{0,7},{9,8},{10,9},{11,1... | collective-permute-start | bytes 294920 | tf_op jit(solution)/shard_map/ppermute | solution.py:303
  167.7 6.0 %shard_map.142 = (f32[1,12,128,128]{3,2,1,0:T(8,128)}, f32[1,12,128,128]{3,2,1,0:T(8,128)}, f32[1,12,16,128]{3,2,1,0:T(8,128)}, f32[1,12,16,128]{3,2,1,0:T(8,128)}) custom-call(f32[1,12,128,128]{3,2,1,0:T(8,128)} %get-tuple-element.75.a1_ref, f32[1,12,16,128]{3,2,1,0:T(8,128)} %copy-done.7, f32[1,12,16,128]{3,2,1,0:T(8,128)} %copy-done.9, ...), custom_call_target="tpu_custom_call" | custom-call | flops 607518720 | bytes 5308980 | tf_op jit(solution)/shard_map/pallas_call | solution.py:231
  173.6 4.8 %collective-permute-start.20 = (f32[1,12,16,128]{3,2,1,0:T(8,128)}, f32[1,12,16,128]{3,2,1,0:T(8,128)S(1)}, u32[]{:S(2)}, u32[]{:S(2)}) collective-permute-start(f32[1,12,16,128]{3,2,1,0:T(8,128)} %get-tuple-element.81), channel_id=1, source_target_pairs={{1,0},{2,1},{3,2},{4,3},{5,4},{6,5},{7,6},{0,7},{9,8},{10,9},{11,1... | collective-permute-start | bytes 294920 | tf_op jit(solution)/shard_map/ppermute | solution.py:303
  178.5 4.8 %shard_map.143 = (f32[1,12,64,128]{3,2,1,0:T(8,128)}, f32[1,12,64,128]{3,2,1,0:T(8,128)}) custom-call(f32[3,12,128,128]{3,2,1,0:T(8,128)} %get-tuple-element.72.u_ref, f32[3,12,16,128]{3,2,1,0:T(8,128)} %copy-done.5, f32[3,12,16,128]{3,2,1,0:T(8,128)} %copy-done.6, f32[64,128]{1,0:T(8,128)} %constant.22.clone.r_ref.refs_11_, f32[8,16]{1,0:T(8,128)} %constant.24.clone.rp_ref, ...), custom_call_target="tpu_custom_call" | custom-call | flops 228261888 | bytes 3867700 | tf_op jit(solution)/shard_map/pallas_call | solution.py:231
  183.9 6.5 %shard_map.144 = (f32[12,64,128]{2,1,0:T(8,128)}, f32[12,64,128]{2,1,0:T(8,128)}) custom-call(f32[1,12,128,128]{3,2,1,0:T(8,128)} %get-tuple-element.79.a2_ref.refs_0_, f32[1,12,16,128]{3,2,1,0:T(8,128)} %copy-done.11, f32[1,12,16,128]{3,2,1,0:T(8,128)} %copy-done.12, f32[256,128]{1,0:T(8,128)} %constant.20.clone.l_ref, f32[128,128]{1,0:T(8,128)} %constant.19.clone.x_ref, ...), custom_call_target="tpu_custom_call" | custom-call | flops 607518720 | bytes 5538356 | tf_op jit(solution)/shard_map/pallas_call | solution.py:231
  190.5 21.7 %all-gather.7.cloned.1.call-done = f32[48,64,128]{2,1,0:T(8,128)} async-done(((f32[12,64,128]{2,1,0:T(8,128)}), f32[48,64,128]{2,1,0:T(8,128)}) %all-gather.7.cloned.1.call-update) | async-done | bytes 1572880 | tf_op jit(solution)/shard_map/all_gather | solution.py:537
  221.8 3.5 %shard_map.146 = (f32[1,12,64,128]{3,2,1,0:T(8,128)}, f32[1,12,8,128]{3,2,1,0:T(8,128)}, f32[1,12,8,128]{3,2,1,0:T(8,128)}) custom-call(f32[1,12,64,128]{3,2,1,0:T(8,128)} %get-tuple-element.86.w_ref.refs_3_, f32[1,12,8,128]{3,2,1,0:T(8,128)} %copy-done.23, f32[1,12,8,128]{3,2,1,0:T(8,128)} %copy-done.27, f32[128,64]{1,0:T(8,128)} %constant.21.clone.l_ref, ...), custom_call_target="tpu_custom_call" | custom-call | flops 228261888 | bytes 2654772 | tf_op jit(solution)/shard_map/pallas_call | solution.py:231
  226.5 3.6 %collective-permute-start.24 = (f32[1,12,8,128]{3,2,1,0:T(8,128)}, f32[1,12,8,128]{3,2,1,0:T(8,128)S(1)}, u32[]{:S(2)}, u32[]{:S(2)}) collective-permute-start(f32[1,12,8,128]{3,2,1,0:T(8,128)} %get-tuple-element.91), channel_id=1, source_target_pairs={{1,0},{2,1},{3,2},{4,3},{5,4},{6,5},{7,6},{0,7},{9,8},{10,9},{11,1... | collective-permute-start | bytes 147464 | tf_op jit(solution)/shard_map/ppermute | solution.py:303
  233.0 3.5 %shard_map.147 = (f32[1,12,64,128]{3,2,1,0:T(8,128)}, f32[1,12,8,128]{3,2,1,0:T(8,128)}, f32[1,12,8,128]{3,2,1,0:T(8,128)}) custom-call(f32[1,12,64,128]{3,2,1,0:T(8,128)} %get-tuple-element.89.w_ref.refs_4_, f32[1,12,8,128]{3,2,1,0:T(8,128)} %copy-done.24, f32[1,12,8,128]{3,2,1,0:T(8,128)} %copy-done.28, f32[128,64]{1,0:T(8,128)} %constant.21.clone.l_ref, ...), custom_call_target="tpu_custom_call" | custom-call | flops 228261888 | bytes 2654772 | tf_op jit(solution)/shard_map/pallas_call | solution.py:231
  236.7 4.6 %collective-permute-start.26 = (f32[1,12,8,128]{3,2,1,0:T(8,128)}, f32[1,12,8,128]{3,2,1,0:T(8,128)S(1)}, u32[]{:S(2)}, u32[]{:S(2)}) collective-permute-start(f32[1,12,8,128]{3,2,1,0:T(8,128)} %get-tuple-element.94), channel_id=1, source_target_pairs={{1,0},{2,1},{3,2},{4,3},{5,4},{6,5},{7,6},{0,7},{9,8},{10,9},{11,1... | collective-permute-start | bytes 147464 | tf_op jit(solution)/shard_map/ppermute | solution.py:303
  244.2 3.5 %shard_map.148 = (f32[1,12,64,128]{3,2,1,0:T(8,128)}, f32[1,12,8,128]{3,2,1,0:T(8,128)}, f32[1,12,8,128]{3,2,1,0:T(8,128)}) custom-call(f32[1,12,64,128]{3,2,1,0:T(8,128)} %get-tuple-element.92.w_ref.refs_5_, f32[1,12,8,128]{3,2,1,0:T(8,128)} %copy-done.17, f32[1,12,8,128]{3,2,1,0:T(8,128)} %copy-done.19, f32[128,64]{1,0:T(8,128)} %constant.21.clone.l_ref, ...), custom_call_target="tpu_custom_call" | custom-call | flops 228261888 | bytes 2654772 | tf_op jit(solution)/shard_map/pallas_call | solution.py:231
  247.7 3.5 %shard_map.149 = (f32[1,12,128,128]{3,2,1,0:T(8,128)}, f32[1,12,64,128]{3,2,1,0:T(8,128)}) custom-call(f32[1,12,128,128]{3,2,1,0:T(8,128)} %get-tuple-element.79.a2_ref.refs_0_, f32[12,64,128]{2,1,0:T(8,128)} %get-tuple-element.84.refs_1_, f32[1,12,64,128]{3,2,1,0:T(8,128)} %bitcast.35, f32[1,12,64,128]{3,2,1,0:T(8,128)} %get-tuple-element.86.w_ref.refs_3_, ...), custom_call_target="tpu_custom_call" | custom-call | flops 150994944 | bytes 4358148 | tf_op jit(solution)/shard_map/pallas_call | solution.py:231
  (117 shorter events, 64.4 us)
Async XLA Ops:
  7.2 85.7 %all-gather.5.cloned.1.call-start = ((), (), s32[]{:S(2)}) async-start(), calls=%async_computation | async-start | bytes 1966080 | tf_op jit(solution)/shard_map/all_gather | solution.py:537
  10.9 7.0 %copy-start.30 = (s32[21,3]{0,1:T(4,128)S(1)}, s32[21,3]{0,1:T(4,128)}, u32[]{:S(2)}) copy-start(s32[21,3]{0,1:T(4,128)} %param.17) | copy-start | bytes 760
  11.9 13.7 %collective-permute-start.1 = (f32[3,12,16,128]{3,2,1,0:T(8,128)}, f32[3,12,16,128]{3,2,1,0:T(8,128)S(1)}, u32[]{:S(2)}, u32[]{:S(2)}) collective-permute-start(f32[3,12,16,128]{3,2,1,0:T(8,128)} %get-tuple-element.98), channel_id=1, source_target_pairs={{1,0},{2,1},{3,2},{4,3},{5,4},{6,5},{7,6},{0,7},{9,8},{10,9},{11,1... | collective-permute-start | bytes 884744 | tf_op jit(solution)/shard_map/ppermute | solution.py:303
  17.9 12.6 %collective-permute-start = (f32[3,12,16,128]{3,2,1,0:T(8,128)}, f32[3,12,16,128]{3,2,1,0:T(8,128)}, u32[]{:S(2)}, u32[]{:S(2)}) collective-permute-start(f32[3,12,16,128]{3,2,1,0:T(8,128)} %get-tuple-element.99), channel_id=1, source_target_pairs={{0,1},{1,2},{2,3},{3,4},{4,5},{5,6},{6,7},{7,0},{8,9},{9,10},{10,1... | collective-permute-start | bytes 884744 | tf_op jit(solution)/shard_map/ppermute | solution.py:302
  41.0 7.6 %collective-permute-start.2 = (f32[1,12,16,128]{3,2,1,0:T(8,128)}, f32[1,12,16,128]{3,2,1,0:T(8,128)S(1)}, u32[]{:S(2)}, u32[]{:S(2)}) collective-permute-start(f32[1,12,16,128]{3,2,1,0:T(8,128)} %get-tuple-element.51), channel_id=1, source_target_pairs={{0,1},{1,2},{2,3},{3,4},{4,5},{5,6},{6,7},{7,0},{8,9},{9,10},{10,1... | collective-permute-start | bytes 294920 | tf_op jit(solution)/shard_map/ppermute | solution.py:302
  42.8 6.9 %collective-permute-start.3 = (f32[1,12,16,128]{3,2,1,0:T(8,128)}, f32[1,12,16,128]{3,2,1,0:T(8,128)S(1)}, u32[]{:S(2)}, u32[]{:S(2)}) collective-permute-start(f32[1,12,16,128]{3,2,1,0:T(8,128)} %get-tuple-element.52), channel_id=1, source_target_pairs={{1,0},{2,1},{3,2},{4,3},{5,4},{6,5},{7,6},{0,7},{9,8},{10,9},{11,1... | collective-permute-start | bytes 294920 | tf_op jit(solution)/shard_map/ppermute | solution.py:303
  56.2 9.5 %collective-permute-start.4 = (f32[1,12,16,128]{3,2,1,0:T(8,128)}, f32[1,12,16,128]{3,2,1,0:T(8,128)S(1)}, u32[]{:S(2)}, u32[]{:S(2)}) collective-permute-start(f32[1,12,16,128]{3,2,1,0:T(8,128)} %get-tuple-element.56), channel_id=1, source_target_pairs={{0,1},{1,2},{2,3},{3,4},{4,5},{5,6},{6,7},{7,0},{8,9},{9,10},{10,1... | collective-permute-start | bytes 294920 | tf_op jit(solution)/shard_map/ppermute | solution.py:302
  56.5 9.2 %collective-permute-start.5 = (f32[1,12,16,128]{3,2,1,0:T(8,128)}, f32[1,12,16,128]{3,2,1,0:T(8,128)S(1)}, u32[]{:S(2)}, u32[]{:S(2)}) collective-permute-start(f32[1,12,16,128]{3,2,1,0:T(8,128)} %get-tuple-element.57), channel_id=1, source_target_pairs={{1,0},{2,1},{3,2},{4,3},{5,4},{6,5},{7,6},{0,7},{9,8},{10,9},{11,1... | collective-permute-start | bytes 294920 | tf_op jit(solution)/shard_map/ppermute | solution.py:303
  66.4 8.2 %copy-start.29 = (f32[8,16,1,1]{1,0,3,2:T(8,128)S(1)}, f32[8,16,1,1]{1,0,3,2:T(8,128)}, u32[]{:S(2)}) copy-start(f32[8,16,1,1]{1,0,3,2:T(8,128)} %constant.26) | copy-start | bytes 1540
  73.0 139.1 %all-gather.7.cloned.1.call-start = ((), (), s32[]{:S(2)}) async-start(), calls=%async_computation.1 | async-start | bytes 1966080 | tf_op jit(solution)/shard_map/all_gather | solution.py:537
  73.1 55.4 %collective-permute-start.14 = (f32[1,12,128,128]{3,2,1,0:T(8,128)S(1)}, f32[1,12,128,128]{3,2,1,0:T(8,128)S(1)}, u32[]{:S(2)}, u32[]{:S(2)}) collective-permute-start(f32[1,12,128,128]{3,2,1,0:T(8,128)S(1)} %copy-done.2), channel_id=1, source_target_pairs={{0,8},{8,16},{16,24},{1,9},{9,17},{17,25},{2,10},{10,18},{18,26},{... | collective-permute-start | bytes 2359304 | tf_op jit(solution)/shard_map/ppermute | solution.py:540
  75.1 9.6 %copy-start = (f32[8,12,8,128]{3,0,2,1:T(8,128)}, f32[8,12,8,128]{3,0,2,1:T(8,128)S(1)}, u32[]{:S(2)}) copy-start(f32[8,12,8,128]{3,0,2,1:T(8,128)S(1)} %fusion.3) | copy-start | bytes 1179652
  75.1 4.5 %collective-permute-start.7 = (f32[12,8,128]{2,1,0:T(8,128)S(1)}, f32[12,8,128]{2,1,0:T(8,128)S(1)}, u32[]{:S(2)}, u32[]{:S(2)}) collective-permute-start(f32[12,8,128]{2,1,0:T(8,128)S(1)} %get-tuple-element.100), channel_id=1, source_target_pairs={{1,0},{2,1},{3,2},{4,3},{5,4},{6,5},{7,6},{0,7},{9,8},{10,9},{11,1... | collective-permute-start | bytes 147464 | tf_op jit(solution)/shard_map/ppermute | solution.py:303
  77.9 6.8 %collective-permute-start.6 = (f32[12,8,128]{2,1,0:T(8,128)S(1)}, f32[12,8,128]{2,1,0:T(8,128)S(1)}, u32[]{:S(2)}, u32[]{:S(2)}) collective-permute-start(f32[12,8,128]{2,1,0:T(8,128)S(1)} %get-tuple-element.101), channel_id=1, source_target_pairs={{0,1},{1,2},{2,3},{3,4},{4,5},{5,6},{6,7},{7,0},{8,9},{9,10},{10,1... | collective-permute-start | bytes 147464 | tf_op jit(solution)/shard_map/ppermute | solution.py:302
  94.9 7.0 %collective-permute-start.8 = (f32[1,12,8,128]{3,2,1,0:T(8,128)}, f32[1,12,8,128]{3,2,1,0:T(8,128)S(1)}, u32[]{:S(2)}, u32[]{:S(2)}) collective-permute-start(f32[1,12,8,128]{3,2,1,0:T(8,128)} %get-tuple-element.63), channel_id=1, source_target_pairs={{0,1},{1,2},{2,3},{3,4},{4,5},{5,6},{6,7},{7,0},{8,9},{9,10},{10,1... | collective-permute-start | bytes 147464 | tf_op jit(solution)/shard_map/ppermute | solution.py:302
  95.7 6.3 %collective-permute-start.9 = (f32[1,12,8,128]{3,2,1,0:T(8,128)}, f32[1,12,8,128]{3,2,1,0:T(8,128)S(1)}, u32[]{:S(2)}, u32[]{:S(2)}) collective-permute-start(f32[1,12,8,128]{3,2,1,0:T(8,128)} %get-tuple-element.64), channel_id=1, source_target_pairs={{1,0},{2,1},{3,2},{4,3},{5,4},{6,5},{7,6},{0,7},{9,8},{10,9},{11,1... | collective-permute-start | bytes 147464 | tf_op jit(solution)/shard_map/ppermute | solution.py:303
  106.1 7.0 %collective-permute-start.10 = (f32[1,12,8,128]{3,2,1,0:T(8,128)}, f32[1,12,8,128]{3,2,1,0:T(8,128)S(1)}, u32[]{:S(2)}, u32[]{:S(2)}) collective-permute-start(f32[1,12,8,128]{3,2,1,0:T(8,128)} %get-tuple-element.66), channel_id=1, source_target_pairs={{0,1},{1,2},{2,3},{3,4},{4,5},{5,6},{6,7},{7,0},{8,9},{9,10},{10,1... | collective-permute-start | bytes 147464 | tf_op jit(solution)/shard_map/ppermute | solution.py:302
  106.5 6.6 %collective-permute-start.11 = (f32[1,12,8,128]{3,2,1,0:T(8,128)}, f32[1,12,8,128]{3,2,1,0:T(8,128)S(1)}, u32[]{:S(2)}, u32[]{:S(2)}) collective-permute-start(f32[1,12,8,128]{3,2,1,0:T(8,128)} %get-tuple-element.67), channel_id=1, source_target_pairs={{1,0},{2,1},{3,2},{4,3},{5,4},{6,5},{7,6},{0,7},{9,8},{10,9},{11,1... | collective-permute-start | bytes 147464 | tf_op jit(solution)/shard_map/ppermute | solution.py:303
  117.3 7.0 %collective-permute-start.12 = (f32[1,12,8,128]{3,2,1,0:T(8,128)}, f32[1,12,8,128]{3,2,1,0:T(8,128)S(1)}, u32[]{:S(2)}, u32[]{:S(2)}) collective-permute-start(f32[1,12,8,128]{3,2,1,0:T(8,128)} %get-tuple-element.69), channel_id=1, source_target_pairs={{0,1},{1,2},{2,3},{3,4},{4,5},{5,6},{6,7},{7,0},{8,9},{9,10},{10,1... | collective-permute-start | bytes 147464 | tf_op jit(solution)/shard_map/ppermute | solution.py:302
  117.3 7.0 %collective-permute-start.13 = (f32[1,12,8,128]{3,2,1,0:T(8,128)}, f32[1,12,8,128]{3,2,1,0:T(8,128)S(1)}, u32[]{:S(2)}, u32[]{:S(2)}) collective-permute-start(f32[1,12,8,128]{3,2,1,0:T(8,128)} %get-tuple-element.70), channel_id=1, source_target_pairs={{1,0},{2,1},{3,2},{4,3},{5,4},{6,5},{7,6},{0,7},{9,8},{10,9},{11,1... | collective-permute-start | bytes 147464 | tf_op jit(solution)/shard_map/ppermute | solution.py:303
  136.1 10.1 %collective-permute-start.15 = (f32[3,12,16,128]{3,2,1,0:T(8,128)}, f32[3,12,16,128]{3,2,1,0:T(8,128)S(1)}, u32[]{:S(2)}, u32[]{:S(2)}) collective-permute-start(f32[3,12,16,128]{3,2,1,0:T(8,128)} %get-tuple-element.73), channel_id=1, source_target_pairs={{0,1},{1,2},{2,3},{3,4},{4,5},{5,6},{6,7},{7,0},{8,9},{9,10},{10,1... | collective-permute-start | bytes 884744 | tf_op jit(solution)/shard_map/ppermute | solution.py:302
  136.1 12.2 %collective-permute-start.16 = (f32[3,12,16,128]{3,2,1,0:T(8,128)}, f32[3,12,16,128]{3,2,1,0:T(8,128)S(1)}, u32[]{:S(2)}, u32[]{:S(2)}) collective-permute-start(f32[3,12,16,128]{3,2,1,0:T(8,128)} %get-tuple-element.74), channel_id=1, source_target_pairs={{1,0},{2,1},{3,2},{4,3},{5,4},{6,5},{7,6},{0,7},{9,8},{10,9},{11,1... | collective-permute-start | bytes 884744 | tf_op jit(solution)/shard_map/ppermute | solution.py:303
  159.5 7.5 %collective-permute-start.17 = (f32[1,12,16,128]{3,2,1,0:T(8,128)}, f32[1,12,16,128]{3,2,1,0:T(8,128)S(1)}, u32[]{:S(2)}, u32[]{:S(2)}) collective-permute-start(f32[1,12,16,128]{3,2,1,0:T(8,128)} %get-tuple-element.76), channel_id=1, source_target_pairs={{0,1},{1,2},{2,3},{3,4},{4,5},{5,6},{6,7},{7,0},{8,9},{9,10},{10,1... | collective-permute-start | bytes 294920 | tf_op jit(solution)/shard_map/ppermute | solution.py:302
  159.9 7.1 %collective-permute-start.18 = (f32[1,12,16,128]{3,2,1,0:T(8,128)}, f32[1,12,16,128]{3,2,1,0:T(8,128)S(1)}, u32[]{:S(2)}, u32[]{:S(2)}) collective-permute-start(f32[1,12,16,128]{3,2,1,0:T(8,128)} %get-tuple-element.77), channel_id=1, source_target_pairs={{1,0},{2,1},{3,2},{4,3},{5,4},{6,5},{7,6},{0,7},{9,8},{10,9},{11,1... | collective-permute-start | bytes 294920 | tf_op jit(solution)/shard_map/ppermute | solution.py:303
  173.6 9.6 %collective-permute-start.19 = (f32[1,12,16,128]{3,2,1,0:T(8,128)}, f32[1,12,16,128]{3,2,1,0:T(8,128)S(1)}, u32[]{:S(2)}, u32[]{:S(2)}) collective-permute-start(f32[1,12,16,128]{3,2,1,0:T(8,128)} %get-tuple-element.80), channel_id=1, source_target_pairs={{0,1},{1,2},{2,3},{3,4},{4,5},{5,6},{6,7},{7,0},{8,9},{9,10},{10,1... | collective-permute-start | bytes 294920 | tf_op jit(solution)/shard_map/ppermute | solution.py:302
  173.6 9.6 %collective-permute-start.20 = (f32[1,12,16,128]{3,2,1,0:T(8,128)}, f32[1,12,16,128]{3,2,1,0:T(8,128)S(1)}, u32[]{:S(2)}, u32[]{:S(2)}) collective-permute-start(f32[1,12,16,128]{3,2,1,0:T(8,128)} %get-tuple-element.81), channel_id=1, source_target_pairs={{1,0},{2,1},{3,2},{4,3},{5,4},{6,5},{7,6},{0,7},{9,8},{10,9},{11,1... | collective-permute-start | bytes 294920 | tf_op jit(solution)/shard_map/ppermute | solution.py:303
  214.2 7.0 %collective-permute-start.21 = (f32[1,12,8,128]{3,2,1,0:T(8,128)}, f32[1,12,8,128]{3,2,1,0:T(8,128)S(1)}, u32[]{:S(2)}, u32[]{:S(2)}) collective-permute-start(f32[1,12,8,128]{3,2,1,0:T(8,128)} %get-tuple-element.87), channel_id=1, source_target_pairs={{0,1},{1,2},{2,3},{3,4},{4,5},{5,6},{6,7},{7,0},{8,9},{9,10},{10,1... | collective-permute-start | bytes 147464 | tf_op jit(solution)/shard_map/ppermute | solution.py:302
  215.7 5.5 %collective-permute-start.22 = (f32[1,12,8,128]{3,2,1,0:T(8,128)}, f32[1,12,8,128]{3,2,1,0:T(8,128)S(1)}, u32[]{:S(2)}, u32[]{:S(2)}) collective-permute-start(f32[1,12,8,128]{3,2,1,0:T(8,128)} %get-tuple-element.88), channel_id=1, source_target_pairs={{1,0},{2,1},{3,2},{4,3},{5,4},{6,5},{7,6},{0,7},{9,8},{10,9},{11,1... | collective-permute-start | bytes 147464 | tf_op jit(solution)/shard_map/ppermute | solution.py:303
  225.4 7.0 %collective-permute-start.23 = (f32[1,12,8,128]{3,2,1,0:T(8,128)}, f32[1,12,8,128]{3,2,1,0:T(8,128)S(1)}, u32[]{:S(2)}, u32[]{:S(2)}) collective-permute-start(f32[1,12,8,128]{3,2,1,0:T(8,128)} %get-tuple-element.90), channel_id=1, source_target_pairs={{0,1},{1,2},{2,3},{3,4},{4,5},{5,6},{6,7},{7,0},{8,9},{9,10},{10,1... | collective-permute-start | bytes 147464 | tf_op jit(solution)/shard_map/ppermute | solution.py:302
  226.5 5.9 %collective-permute-start.24 = (f32[1,12,8,128]{3,2,1,0:T(8,128)}, f32[1,12,8,128]{3,2,1,0:T(8,128)S(1)}, u32[]{:S(2)}, u32[]{:S(2)}) collective-permute-start(f32[1,12,8,128]{3,2,1,0:T(8,128)} %get-tuple-element.91), channel_id=1, source_target_pairs={{1,0},{2,1},{3,2},{4,3},{5,4},{6,5},{7,6},{0,7},{9,8},{10,9},{11,1... | collective-permute-start | bytes 147464 | tf_op jit(solution)/shard_map/ppermute | solution.py:303
  236.6 7.0 %collective-permute-start.25 = (f32[1,12,8,128]{3,2,1,0:T(8,128)}, f32[1,12,8,128]{3,2,1,0:T(8,128)S(1)}, u32[]{:S(2)}, u32[]{:S(2)}) collective-permute-start(f32[1,12,8,128]{3,2,1,0:T(8,128)} %get-tuple-element.93), channel_id=1, source_target_pairs={{0,1},{1,2},{2,3},{3,4},{4,5},{5,6},{6,7},{7,0},{8,9},{9,10},{10,1... | collective-permute-start | bytes 147464 | tf_op jit(solution)/shard_map/ppermute | solution.py:302
  236.7 6.9 %collective-permute-start.26 = (f32[1,12,8,128]{3,2,1,0:T(8,128)}, f32[1,12,8,128]{3,2,1,0:T(8,128)S(1)}, u32[]{:S(2)}, u32[]{:S(2)}) collective-permute-start(f32[1,12,8,128]{3,2,1,0:T(8,128)} %get-tuple-element.94), channel_id=1, source_target_pairs={{1,0},{2,1},{3,2},{4,3},{5,4},{6,5},{7,6},{0,7},{9,8},{10,9},{11,1... | collective-permute-start | bytes 147464 | tf_op jit(solution)/shard_map/ppermute | solution.py:303
  (28 other events, 37.7 us)
Sparse Core Ops, SparseCore 0:
  73.1 19.6 all-gather.4
  190.6 21.4 all-gather.6

commit v13 on v10

--- a/solution.py
+++ b/solution.py
@@ -481,7 +481,13 @@
     coarse_end = None
     for iteration in range(ITERS):
         if iteration == 0:
-            node_prev, node_next = halo(nodes, rows)
+            first = guess[0]
+            plane_sets = []
+            for z in (0, depth - 1):
+                plane_sets.append(jnp.concatenate(
+                    [jnp.where(section == 0, u_start[:, z], first[0, :, z])[None], first[1:, :, z]]
+                ))
+            node_prev, node_next = swap(plane_sets[0], plane_sets[1])
         else:
             node_prev, node_next = swap(node_head, node_tail)
         f_all, a1, a1_head, a1_tail = call(

time: 259 us -> 260 us (level)
  waiting for transfers between devices: 68.9 us -> 65.4 us
  local copies, waits for them, and re-layouts: 15.5 us -> 18.3 us
    unnamed x65 -> x72, local copies, waits for them, and re-layouts: 9.35 us -> 13.6 us
  transfers between devices with their start and end apart: 29 -> 29, of which waited for: 17 -> 16; matrix products, arithmetic and copies ran while one was open for 2% -> 3% of each run, Pallas kernels for 10% -> 10%
where the time goes in v13:
time: 260 us; the launch traced here: 259 us
  Pallas kernels  94.5 us (36%)
  waiting for transfers between devices  65.4 us (25%)
  starting transfers between devices  62.1 us (24%)
  local copies, waits for them, and re-layouts  18.3 us (7%)
  between operations  14.3 us (6%)
  other arithmetic  4.1 us (2%)
    pallas_call x19, Pallas kernels, call(): pl.pallas_call(kernel, out_shape=outs, in_specs=[blocks[i] if blocks is n...  94.5 us
    ppermute x13, starting transfers between devices, swap(): lax.ppermute(head, 'space', [((i + 1) % space_n, i) for i in range(space_...  53 us
    ppermute x13, waiting for transfers between devices, swap(): lax.ppermute(tail, 'space', [(i, (i + 1) % space_n) for i in range(space_...  32.3 us
    all_gather x2, waiting for transfers between devices, per_device(): rint_all = lax.all_gather(rint[None], 'tm')  26.1 us
    unnamed x72, local copies, waits for them, and re-layouts  13.6 us
    ppermute x13, starting transfers between devices, swap(): lax.ppermute(tail, 'space', [(i, (i + 1) % space_n) for i in range(space_...  7.45 us
    ppermute x13, waiting for transfers between devices, swap(): lax.ppermute(head, 'space', [((i + 1) % space_n, i) for i in range(space_...  7.06 us
  transfers between devices with their start and end apart: 29, of which 16 were waited for; matrix products, arithmetic and copies ran while one was open for 3% of the time, Pallas kernels for 10%

profile of v13, /device:TPU:0, one launch (start us, length us, event | category | flops | bytes accessed | tf_op | source)
XLA Modules:
  0.0 259.2 jit_solution(2350452122054114578)
XLA Ops:
  25.0 3.3 %collective-permute-done.p_ref = f32[3,12,16,128]{3,2,1,0:T(8,128)} collective-permute-done((f32[3,12,16,128]{3,2,1,0:T(8,128)}, f32[3,12,16,128]{3,2,1,0:T(8,128)}, u32[]{:S(2)}, u32[]{:S(2)}) %collective-permute-start) | collective-permute-done | bytes 294944 | tf_op jit(solution)/shard_map/ppermute | solution.py:288
  31.9 10.5 %shard_map.131 = (f32[3,12,128,128]{3,2,1,0:T(8,128)}, f32[1,12,128,128]{3,2,1,0:T(8,128)}, f32[1,12,16,128]{3,2,1,0:T(8,128)}, f32[1,12,16,128]{3,2,1,0:T(8,128)}) custom-call(f32[3,12,128,128]{3,2,1,0:T(8,128)} %pad_maximum_fusion.u_ref, f32[3,12,16,128]{3,2,1,0:T(8,128)} %collective-permute-done.p_ref, f32[3,12,16,128]{3,2,1,0:T(8,128)} %copy-done.7, ...), custom_call_target="tpu_custom_call" | custom-call | flops 1822556160 | bytes 6488916 | tf_op jit(solution)/shard_map/pallas_call | solution.py:217
  42.4 4.7 %collective-permute-start.3 = (f32[1,12,16,128]{3,2,1,0:T(8,128)}, f32[1,12,16,128]{3,2,1,0:T(8,128)S(1)}, u32[]{:S(2)}, u32[]{:S(2)}) collective-permute-start(f32[1,12,16,128]{3,2,1,0:T(8,128)} %get-tuple-element.52), channel_id=1, source_target_pairs={{1,0},{2,1},{3,2},{4,3},{5,4},{6,5},{7,6},{0,7},{9,8},{10,9},{11,1... | collective-permute-start | bytes 294920 | tf_op jit(solution)/shard_map/ppermute | solution.py:289
  50.6 6.0 %shard_map.132 = (f32[1,12,128,128]{3,2,1,0:T(8,128)}, f32[1,12,128,128]{3,2,1,0:T(8,128)}, f32[1,12,16,128]{3,2,1,0:T(8,128)}, f32[1,12,16,128]{3,2,1,0:T(8,128)}) custom-call(f32[1,12,128,128]{3,2,1,0:T(8,128)} %get-tuple-element.50.a1_ref.refs_0_, f32[1,12,16,128]{3,2,1,0:T(8,128)} %copy-done.11, f32[1,12,16,128]{3,2,1,0:T(8,128)} %copy-done.13, ...), custom_call_target="tpu_custom_call" | custom-call | flops 607518720 | bytes 5309268 | tf_op jit(solution)/shard_map/pallas_call | solution.py:217
  56.7 4.6 %collective-permute-start.5 = (f32[1,12,16,128]{3,2,1,0:T(8,128)}, f32[1,12,16,128]{3,2,1,0:T(8,128)S(1)}, u32[]{:S(2)}, u32[]{:S(2)}) collective-permute-start(f32[1,12,16,128]{3,2,1,0:T(8,128)} %get-tuple-element.57), channel_id=1, source_target_pairs={{1,0},{2,1},{3,2},{4,3},{5,4},{6,5},{7,6},{0,7},{9,8},{10,9},{11,1... | collective-permute-start | bytes 294920 | tf_op jit(solution)/shard_map/ppermute | solution.py:289
  62.5 4.8 %shard_map.133 = (f32[1,12,64,128]{3,2,1,0:T(8,128)}, f32[1,12,64,128]{3,2,1,0:T(8,128)}) custom-call(f32[3,12,128,128]{3,2,1,0:T(8,128)} %pad_maximum_fusion.u_ref, f32[3,12,16,128]{3,2,1,0:T(8,128)} %collective-permute-done.p_ref, f32[3,12,16,128]{3,2,1,0:T(8,128)} %copy-done.7, f32[64,128]{1,0:T(8,128)} %constant.28.clone.r_ref.refs_11_, ...), custom_call_target="tpu_custom_call" | custom-call | flops 228261888 | bytes 3867988 | tf_op jit(solution)/shard_map/pallas_call | solution.py:217
  68.0 6.6 %shard_map.134 = (f32[12,64,128]{2,1,0:T(8,128)}, f32[12,64,128]{2,1,0:T(8,128)}) custom-call(f32[1,12,128,128]{3,2,1,0:T(8,128)} %get-tuple-element.54.a2_ref.refs_1_, f32[1,12,16,128]{3,2,1,0:T(8,128)} %copy-done.14, f32[1,12,16,128]{3,2,1,0:T(8,128)} %copy-done.15, f32[256,128]{1,0:T(8,128)} %constant.26.clone.l_ref, f32[128,128]{1,0:T(8,128)} %constant.25.clone.x_ref, ...), custom_call_target="tpu_custom_call" | custom-call | flops 607518720 | bytes 5538644 | tf_op jit(solution)/shard_map/pallas_call | solution.py:217
  80.9 4.7 %collective-permute-done.6 = f32[12,8,128]{2,1,0:T(8,128)S(1)} collective-permute-done((f32[12,8,128]{2,1,0:T(8,128)S(1)}, f32[12,8,128]{2,1,0:T(8,128)S(1)}, u32[]{:S(2)}, u32[]{:S(2)}) %collective-permute-start.6) | collective-permute-done | bytes 49184 | tf_op jit(solution)/shard_map/ppermute | solution.py:288
  86.2 3.3 %shard_map.135.g_ref = f32[1,12,64,128]{3,2,1,0:T(8,128)} custom-call(f32[1,12,64,128]{3,2,1,0:T(8,128)} %bitcast.57, f32[1,12,8,128]{3,2,1,0:T(8,128)} %bitcast.70, f32[1,12,8,128]{3,2,1,0:T(8,128)} %bitcast.69, f32[128,64]{1,0:T(8,128)} %constant.27.clone.l_ref, f32[128,128]{1,0:T(8,128)} %constant.25.clone.x_ref, f32[9,12]{1,0:T(8,128)} %concatenate.19.zc_ref, ...), custom_call_target="tpu_custom_call" | custom-call | flops 228261888 | bytes 983892 | tf_op jit(solution)/shard_map/pallas_call | solution.py:217
  89.5 4.4 %all-gather.5.cloned.1.call-done = f32[48,64,128]{2,1,0:T(8,128)} async-done(((f32[12,64,128]{2,1,0:T(8,128)}), f32[48,64,128]{2,1,0:T(8,128)}) %all-gather.5.cloned.1.call-update) | async-done | bytes 1572880 | tf_op jit(solution)/shard_map/all_gather | solution.py:529
  96.7 4.0 %collective-permute-start.9 = (f32[1,12,8,128]{3,2,1,0:T(8,128)}, f32[1,12,8,128]{3,2,1,0:T(8,128)S(1)}, u32[]{:S(2)}, u32[]{:S(2)}) collective-permute-start(f32[1,12,8,128]{3,2,1,0:T(8,128)} %get-tuple-element.64), channel_id=1, source_target_pairs={{1,0},{2,1},{3,2},{4,3},{5,4},{6,5},{7,6},{0,7},{9,8},{10,9},{11,1... | collective-permute-start | bytes 147464 | tf_op jit(solution)/shard_map/ppermute | solution.py:289
  103.5 3.5 %shard_map.137 = (f32[1,12,64,128]{3,2,1,0:T(8,128)}, f32[1,12,8,128]{3,2,1,0:T(8,128)}, f32[1,12,8,128]{3,2,1,0:T(8,128)}) custom-call(f32[1,12,64,128]{3,2,1,0:T(8,128)} %get-tuple-element.62.w_ref.refs_5_, f32[1,12,8,128]{3,2,1,0:T(8,128)} %copy-done.23, f32[1,12,8,128]{3,2,1,0:T(8,128)} %copy-done.28, f32[128,64]{1,0:T(8,128)} %constant.27.clone.l_ref, ...), custom_call_target="tpu_custom_call" | custom-call | flops 228261888 | bytes 2655060 | tf_op jit(solution)/shard_map/pallas_call | solution.py:217
  107.5 4.3 %collective-permute-start.11 = (f32[1,12,8,128]{3,2,1,0:T(8,128)}, f32[1,12,8,128]{3,2,1,0:T(8,128)S(1)}, u32[]{:S(2)}, u32[]{:S(2)}) collective-permute-start(f32[1,12,8,128]{3,2,1,0:T(8,128)} %get-tuple-element.67), channel_id=1, source_target_pairs={{1,0},{2,1},{3,2},{4,3},{5,4},{6,5},{7,6},{0,7},{9,8},{10,9},{11,1... | collective-permute-start | bytes 147464 | tf_op jit(solution)/shard_map/ppermute | solution.py:289
  114.7 3.5 %shard_map.138 = (f32[1,12,64,128]{3,2,1,0:T(8,128)}, f32[1,12,8,128]{3,2,1,0:T(8,128)}, f32[1,12,8,128]{3,2,1,0:T(8,128)}) custom-call(f32[1,12,64,128]{3,2,1,0:T(8,128)} %get-tuple-element.65.w_ref.refs_6_, f32[1,12,8,128]{3,2,1,0:T(8,128)} %copy-done.24, f32[1,12,8,128]{3,2,1,0:T(8,128)} %copy-done.29, f32[128,64]{1,0:T(8,128)} %constant.27.clone.l_ref, ...), custom_call_target="tpu_custom_call" | custom-call | flops 228261888 | bytes 2655060 | tf_op jit(solution)/shard_map/pallas_call | solution.py:217
  118.3 4.8 %collective-permute-start.13 = (f32[1,12,8,128]{3,2,1,0:T(8,128)}, f32[1,12,8,128]{3,2,1,0:T(8,128)S(1)}, u32[]{:S(2)}, u32[]{:S(2)}) collective-permute-start(f32[1,12,8,128]{3,2,1,0:T(8,128)} %get-tuple-element.70), channel_id=1, source_target_pairs={{1,0},{2,1},{3,2},{4,3},{5,4},{6,5},{7,6},{0,7},{9,8},{10,9},{11,1... | collective-permute-start | bytes 147464 | tf_op jit(solution)/shard_map/ppermute | solution.py:289
  125.9 3.6 %shard_map.139 = (f32[1,12,64,128]{3,2,1,0:T(8,128)}, f32[1,12,8,128]{3,2,1,0:T(8,128)}, f32[1,12,8,128]{3,2,1,0:T(8,128)}) custom-call(f32[1,12,64,128]{3,2,1,0:T(8,128)} %get-tuple-element.68.w_ref.refs_7_, f32[1,12,8,128]{3,2,1,0:T(8,128)} %copy-done.21, f32[1,12,8,128]{3,2,1,0:T(8,128)} %copy-done.25, f32[128,64]{1,0:T(8,128)} %constant.27.clone.l_ref, ...), custom_call_target="tpu_custom_call" | custom-call | flops 228261888 | bytes 2655060 | tf_op jit(solution)/shard_map/pallas_call | solution.py:217
  130.4 6.7 %shard_map.140 = (f32[3,12,128,128]{3,2,1,0:T(8,128)}, f32[3,12,16,128]{3,2,1,0:T(8,128)}, f32[3,12,16,128]{3,2,1,0:T(8,128)}) custom-call(f32[1,12,128,128]{3,2,1,0:T(8,128)} %get-tuple-element.50.a1_ref.refs_0_, f32[1,12,128,128]{3,2,1,0:T(8,128)} %get-tuple-element.54.a2_ref.refs_1_, f32[1,12,64,128]{3,2,1,0:T(8,128)} %get-tuple-element.55.refs_2_, ...), custom_call_target="tpu_custom_call" | custom-call | flops 603979776 | bytes 8912904 | tf_op jit(solution)/shard_map/pallas_call | solution.py:217
  137.1 4.7 %collective-permute-start.16 = (f32[3,12,16,128]{3,2,1,0:T(8,128)}, f32[3,12,16,128]{3,2,1,0:T(8,128)S(1)}, u32[]{:S(2)}, u32[]{:S(2)}) collective-permute-start(f32[3,12,16,128]{3,2,1,0:T(8,128)} %get-tuple-element.74), channel_id=1, source_target_pairs={{1,0},{2,1},{3,2},{4,3},{5,4},{6,5},{7,6},{0,7},{9,8},{10,9},{11,1... | collective-permute-start | bytes 884744 | tf_op jit(solution)/shard_map/ppermute | solution.py:289
  141.9 5.3 %collective-permute-done.15.p_ref = f32[3,12,16,128]{3,2,1,0:T(8,128)S(1)} collective-permute-done((f32[3,12,16,128]{3,2,1,0:T(8,128)}, f32[3,12,16,128]{3,2,1,0:T(8,128)S(1)}, u32[]{:S(2)}, u32[]{:S(2)}) %collective-permute-start.15) | collective-permute-done | bytes 294944 | tf_op jit(solution)/shard_map/ppermute | solution.py:288
  150.1 10.5 %shard_map.141 = (f32[3,12,128,128]{3,2,1,0:T(8,128)}, f32[1,12,128,128]{3,2,1,0:T(8,128)}, f32[1,12,16,128]{3,2,1,0:T(8,128)}, f32[1,12,16,128]{3,2,1,0:T(8,128)}) custom-call(f32[3,12,128,128]{3,2,1,0:T(8,128)} %get-tuple-element.72.u_ref, f32[3,12,16,128]{3,2,1,0:T(8,128)} %copy-done.8, f32[3,12,16,128]{3,2,1,0:T(8,128)} %copy-done.9, ...), custom_call_target="tpu_custom_call" | custom-call | flops 1822556160 | bytes 6488916 | tf_op jit(solution)/shard_map/pallas_call | solution.py:217
  160.9 4.4 %collective-permute-start.18 = (f32[1,12,16,128]{3,2,1,0:T(8,128)}, f32[1,12,16,128]{3,2,1,0:T(8,128)S(1)}, u32[]{:S(2)}, u32[]{:S(2)}) collective-permute-start(f32[1,12,16,128]{3,2,1,0:T(8,128)} %get-tuple-element.77), channel_id=1, source_target_pairs={{1,0},{2,1},{3,2},{4,3},{5,4},{6,5},{7,6},{0,7},{9,8},{10,9},{11,1... | collective-permute-start | bytes 294920 | tf_op jit(solution)/shard_map/ppermute | solution.py:289
  168.8 5.9 %shard_map.142 = (f32[1,12,128,128]{3,2,1,0:T(8,128)}, f32[1,12,128,128]{3,2,1,0:T(8,128)}, f32[1,12,16,128]{3,2,1,0:T(8,128)}, f32[1,12,16,128]{3,2,1,0:T(8,128)}) custom-call(f32[1,12,128,128]{3,2,1,0:T(8,128)} %get-tuple-element.75.a1_ref, f32[1,12,16,128]{3,2,1,0:T(8,128)} %copy-done.10, f32[1,12,16,128]{3,2,1,0:T(8,128)} %copy-done.12, ...), custom_call_target="tpu_custom_call" | custom-call | flops 607518720 | bytes 5309268 | tf_op jit(solution)/shard_map/pallas_call | solution.py:217
  174.7 4.8 %collective-permute-start.20 = (f32[1,12,16,128]{3,2,1,0:T(8,128)}, f32[1,12,16,128]{3,2,1,0:T(8,128)S(1)}, u32[]{:S(2)}, u32[]{:S(2)}) collective-permute-start(f32[1,12,16,128]{3,2,1,0:T(8,128)} %get-tuple-element.81), channel_id=1, source_target_pairs={{1,0},{2,1},{3,2},{4,3},{5,4},{6,5},{7,6},{0,7},{9,8},{10,9},{11,1... | collective-permute-start | bytes 294920 | tf_op jit(solution)/shard_map/ppermute | solution.py:289
  179.5 4.8 %shard_map.143 = (f32[1,12,64,128]{3,2,1,0:T(8,128)}, f32[1,12,64,128]{3,2,1,0:T(8,128)}) custom-call(f32[3,12,128,128]{3,2,1,0:T(8,128)} %get-tuple-element.72.u_ref, f32[3,12,16,128]{3,2,1,0:T(8,128)} %copy-done.8, f32[3,12,16,128]{3,2,1,0:T(8,128)} %copy-done.9, f32[64,128]{1,0:T(8,128)} %constant.28.clone.r_ref.refs_11_, f32[8,16]{1,0:T(8,128)} %constant.30.clone.rp_ref, ...), custom_call_target="tpu_custom_call" | custom-call | flops 228261888 | bytes 3867988 | tf_op jit(solution)/shard_map/pallas_call | solution.py:217
  185.0 6.5 %shard_map.144 = (f32[12,64,128]{2,1,0:T(8,128)}, f32[12,64,128]{2,1,0:T(8,128)}) custom-call(f32[1,12,128,128]{3,2,1,0:T(8,128)} %get-tuple-element.79.a2_ref.refs_0_, f32[1,12,16,128]{3,2,1,0:T(8,128)} %copy-done.16, f32[1,12,16,128]{3,2,1,0:T(8,128)} %copy-done.17, f32[256,128]{1,0:T(8,128)} %constant.26.clone.l_ref, f32[128,128]{1,0:T(8,128)} %constant.25.clone.x_ref, ...), custom_call_target="tpu_custom_call" | custom-call | flops 607518720 | bytes 5538644 | tf_op jit(solution)/shard_map/pallas_call | solution.py:217
  191.5 21.7 %all-gather.7.cloned.1.call-done = f32[48,64,128]{2,1,0:T(8,128)} async-done(((f32[12,64,128]{2,1,0:T(8,128)}), f32[48,64,128]{2,1,0:T(8,128)}) %all-gather.7.cloned.1.call-update) | async-done | bytes 1572880 | tf_op jit(solution)/shard_map/all_gather | solution.py:529
  222.9 3.5 %shard_map.146 = (f32[1,12,64,128]{3,2,1,0:T(8,128)}, f32[1,12,8,128]{3,2,1,0:T(8,128)}, f32[1,12,8,128]{3,2,1,0:T(8,128)}) custom-call(f32[1,12,64,128]{3,2,1,0:T(8,128)} %get-tuple-element.86.w_ref.refs_3_, f32[1,12,8,128]{3,2,1,0:T(8,128)} %copy-done.26, f32[1,12,8,128]{3,2,1,0:T(8,128)} %copy-done.30, f32[128,64]{1,0:T(8,128)} %constant.27.clone.l_ref, ...), custom_call_target="tpu_custom_call" | custom-call | flops 228261888 | bytes 2655060 | tf_op jit(solution)/shard_map/pallas_call | solution.py:217
  227.6 3.6 %collective-permute-start.24 = (f32[1,12,8,128]{3,2,1,0:T(8,128)}, f32[1,12,8,128]{3,2,1,0:T(8,128)S(1)}, u32[]{:S(2)}, u32[]{:S(2)}) collective-permute-start(f32[1,12,8,128]{3,2,1,0:T(8,128)} %get-tuple-element.91), channel_id=1, source_target_pairs={{1,0},{2,1},{3,2},{4,3},{5,4},{6,5},{7,6},{0,7},{9,8},{10,9},{11,1... | collective-permute-start | bytes 147464 | tf_op jit(solution)/shard_map/ppermute | solution.py:289
  234.1 3.5 %shard_map.147 = (f32[1,12,64,128]{3,2,1,0:T(8,128)}, f32[1,12,8,128]{3,2,1,0:T(8,128)}, f32[1,12,8,128]{3,2,1,0:T(8,128)}) custom-call(f32[1,12,64,128]{3,2,1,0:T(8,128)} %get-tuple-element.89.w_ref.refs_4_, f32[1,12,8,128]{3,2,1,0:T(8,128)} %copy-done.27, f32[1,12,8,128]{3,2,1,0:T(8,128)} %copy-done.31, f32[128,64]{1,0:T(8,128)} %constant.27.clone.l_ref, ...), custom_call_target="tpu_custom_call" | custom-call | flops 228261888 | bytes 2655060 | tf_op jit(solution)/shard_map/pallas_call | solution.py:217
  237.8 4.6 %collective-permute-start.26 = (f32[1,12,8,128]{3,2,1,0:T(8,128)}, f32[1,12,8,128]{3,2,1,0:T(8,128)S(1)}, u32[]{:S(2)}, u32[]{:S(2)}) collective-permute-start(f32[1,12,8,128]{3,2,1,0:T(8,128)} %get-tuple-element.94), channel_id=1, source_target_pairs={{1,0},{2,1},{3,2},{4,3},{5,4},{6,5},{7,6},{0,7},{9,8},{10,9},{11,1... | collective-permute-start | bytes 147464 | tf_op jit(solution)/shard_map/ppermute | solution.py:289
  245.3 3.5 %shard_map.148 = (f32[1,12,64,128]{3,2,1,0:T(8,128)}, f32[1,12,8,128]{3,2,1,0:T(8,128)}, f32[1,12,8,128]{3,2,1,0:T(8,128)}) custom-call(f32[1,12,64,128]{3,2,1,0:T(8,128)} %get-tuple-element.92.w_ref.refs_5_, f32[1,12,8,128]{3,2,1,0:T(8,128)} %copy-done.20, f32[1,12,8,128]{3,2,1,0:T(8,128)} %copy-done.22, f32[128,64]{1,0:T(8,128)} %constant.27.clone.l_ref, ...), custom_call_target="tpu_custom_call" | custom-call | flops 228261888 | bytes 2655060 | tf_op jit(solution)/shard_map/pallas_call | solution.py:217
  248.8 3.5 %shard_map.149 = (f32[1,12,128,128]{3,2,1,0:T(8,128)}, f32[1,12,64,128]{3,2,1,0:T(8,128)}) custom-call(f32[1,12,128,128]{3,2,1,0:T(8,128)} %get-tuple-element.79.a2_ref.refs_0_, f32[12,64,128]{2,1,0:T(8,128)} %get-tuple-element.84.refs_1_, f32[1,12,64,128]{3,2,1,0:T(8,128)} %bitcast.61, f32[1,12,64,128]{3,2,1,0:T(8,128)} %get-tuple-element.86.w_ref.refs_3_, ...), custom_call_target="tpu_custom_call" | custom-call | flops 150994944 | bytes 4358148 | tf_op jit(solution)/shard_map/pallas_call | solution.py:217
  (133 shorter events, 70.5 us)
Async XLA Ops:
  7.2 86.7 %all-gather.5.cloned.1.call-start = ((), (), s32[]{:S(2)}) async-start(), calls=%async_computation | async-start | bytes 1966080 | tf_op jit(solution)/shard_map/all_gather | solution.py:529
  12.4 15.9 %collective-permute-start = (f32[3,12,16,128]{3,2,1,0:T(8,128)}, f32[3,12,16,128]{3,2,1,0:T(8,128)}, u32[]{:S(2)}, u32[]{:S(2)}) collective-permute-start(f32[3,12,16,128]{3,2,1,0:T(8,128)} %pad_maximum_fusion.1), channel_id=1, source_target_pairs={{0,1},{1,2},{2,3},{3,4},{4,5},{5,6},{6,7},{7,0},{8,9},{9,10},{10,1... | collective-permute-start | bytes 884744 | tf_op jit(solution)/shard_map/ppermute | solution.py:288
  16.2 15.0 %collective-permute-start.1 = (f32[3,12,16,128]{3,2,1,0:T(8,128)}, f32[3,12,16,128]{3,2,1,0:T(8,128)S(1)}, u32[]{:S(2)}, u32[]{:S(2)}) collective-permute-start(f32[3,12,16,128]{3,2,1,0:T(8,128)} %pad_maximum_fusion.2), channel_id=1, source_target_pairs={{1,0},{2,1},{3,2},{4,3},{5,4},{6,5},{7,6},{0,7},{9,8},{10,9},{11,1... | collective-permute-start | bytes 884744 | tf_op jit(solution)/shard_map/ppermute | solution.py:289
  42.4 7.5 %collective-permute-start.2 = (f32[1,12,16,128]{3,2,1,0:T(8,128)}, f32[1,12,16,128]{3,2,1,0:T(8,128)S(1)}, u32[]{:S(2)}, u32[]{:S(2)}) collective-permute-start(f32[1,12,16,128]{3,2,1,0:T(8,128)} %get-tuple-element.51), channel_id=1, source_target_pairs={{0,1},{1,2},{2,3},{3,4},{4,5},{5,6},{6,7},{7,0},{8,9},{9,10},{10,1... | collective-permute-start | bytes 294920 | tf_op jit(solution)/shard_map/ppermute | solution.py:288
  42.4 7.5 %collective-permute-start.3 = (f32[1,12,16,128]{3,2,1,0:T(8,128)}, f32[1,12,16,128]{3,2,1,0:T(8,128)S(1)}, u32[]{:S(2)}, u32[]{:S(2)}) collective-permute-start(f32[1,12,16,128]{3,2,1,0:T(8,128)} %get-tuple-element.52), channel_id=1, source_target_pairs={{1,0},{2,1},{3,2},{4,3},{5,4},{6,5},{7,6},{0,7},{9,8},{10,9},{11,1... | collective-permute-start | bytes 294920 | tf_op jit(solution)/shard_map/ppermute | solution.py:289
  56.6 10.7 %collective-permute-start.4 = (f32[1,12,16,128]{3,2,1,0:T(8,128)}, f32[1,12,16,128]{3,2,1,0:T(8,128)S(1)}, u32[]{:S(2)}, u32[]{:S(2)}) collective-permute-start(f32[1,12,16,128]{3,2,1,0:T(8,128)} %get-tuple-element.56), channel_id=1, source_target_pairs={{0,1},{1,2},{2,3},{3,4},{4,5},{5,6},{6,7},{7,0},{8,9},{9,10},{10,1... | collective-permute-start | bytes 294920 | tf_op jit(solution)/shard_map/ppermute | solution.py:288
  56.7 10.6 %collective-permute-start.5 = (f32[1,12,16,128]{3,2,1,0:T(8,128)}, f32[1,12,16,128]{3,2,1,0:T(8,128)S(1)}, u32[]{:S(2)}, u32[]{:S(2)}) collective-permute-start(f32[1,12,16,128]{3,2,1,0:T(8,128)} %get-tuple-element.57), channel_id=1, source_target_pairs={{1,0},{2,1},{3,2},{4,3},{5,4},{6,5},{7,6},{0,7},{9,8},{10,9},{11,1... | collective-permute-start | bytes 294920 | tf_op jit(solution)/shard_map/ppermute | solution.py:289
  68.0 6.7 %copy-start.5 = (f32[1,12,128,128]{3,2,1,0:T(8,128)S(1)}, f32[1,12,128,128]{3,2,1,0:T(8,128)}, u32[]{:S(2)}) copy-start(f32[1,12,128,128]{3,2,1,0:T(8,128)} %get-tuple-element.54.a2_ref.refs_1_) | copy-start | bytes 2359300
  68.0 8.2 %copy-start.32 = (f32[8,16,1,1]{1,0,3,2:T(8,128)S(1)}, f32[8,16,1,1]{1,0,3,2:T(8,128)}, u32[]{:S(2)}) copy-start(f32[8,16,1,1]{1,0,3,2:T(8,128)} %constant.32) | copy-start | bytes 1540
  74.6 138.6 %all-gather.7.cloned.1.call-start = ((), (), s32[]{:S(2)}) async-start(), calls=%async_computation.1 | async-start | bytes 1966080 | tf_op jit(solution)/shard_map/all_gather | solution.py:529
  74.7 54.8 %collective-permute-start.14 = (f32[1,12,128,128]{3,2,1,0:T(8,128)S(1)}, f32[1,12,128,128]{3,2,1,0:T(8,128)S(1)}, u32[]{:S(2)}, u32[]{:S(2)}) collective-permute-start(f32[1,12,128,128]{3,2,1,0:T(8,128)S(1)} %copy-done.5), channel_id=1, source_target_pairs={{0,8},{8,16},{16,24},{1,9},{9,17},{17,25},{2,10},{10,18},{18,26},{... | collective-permute-start | bytes 2359304 | tf_op jit(solution)/shard_map/ppermute | solution.py:532
  76.7 8.8 %copy-start = (f32[8,12,8,128]{3,0,2,1:T(8,128)}, f32[8,12,8,128]{3,0,2,1:T(8,128)S(1)}, u32[]{:S(2)}) copy-start(f32[8,12,8,128]{3,0,2,1:T(8,128)S(1)} %fusion.3) | copy-start | bytes 1179652
  76.7 4.1 %collective-permute-start.7 = (f32[12,8,128]{2,1,0:T(8,128)S(1)}, f32[12,8,128]{2,1,0:T(8,128)S(1)}, u32[]{:S(2)}, u32[]{:S(2)}) collective-permute-start(f32[12,8,128]{2,1,0:T(8,128)S(1)} %get-tuple-element.102), channel_id=1, source_target_pairs={{1,0},{2,1},{3,2},{4,3},{5,4},{6,5},{7,6},{0,7},{9,8},{10,9},{11,1... | collective-permute-start | bytes 147464 | tf_op jit(solution)/shard_map/ppermute | solution.py:289
  78.8 6.8 %collective-permute-start.6 = (f32[12,8,128]{2,1,0:T(8,128)S(1)}, f32[12,8,128]{2,1,0:T(8,128)S(1)}, u32[]{:S(2)}, u32[]{:S(2)}) collective-permute-start(f32[12,8,128]{2,1,0:T(8,128)S(1)} %get-tuple-element.103), channel_id=1, source_target_pairs={{0,1},{1,2},{2,3},{3,4},{4,5},{5,6},{6,7},{7,0},{8,9},{9,10},{10,1... | collective-permute-start | bytes 147464 | tf_op jit(solution)/shard_map/ppermute | solution.py:288
  95.9 7.0 %collective-permute-start.8 = (f32[1,12,8,128]{3,2,1,0:T(8,128)}, f32[1,12,8,128]{3,2,1,0:T(8,128)S(1)}, u32[]{:S(2)}, u32[]{:S(2)}) collective-permute-start(f32[1,12,8,128]{3,2,1,0:T(8,128)} %get-tuple-element.63), channel_id=1, source_target_pairs={{0,1},{1,2},{2,3},{3,4},{4,5},{5,6},{6,7},{7,0},{8,9},{9,10},{10,1... | collective-permute-start | bytes 147464 | tf_op jit(solution)/shard_map/ppermute | solution.py:288
  96.7 6.3 %collective-permute-start.9 = (f32[1,12,8,128]{3,2,1,0:T(8,128)}, f32[1,12,8,128]{3,2,1,0:T(8,128)S(1)}, u32[]{:S(2)}, u32[]{:S(2)}) collective-permute-start(f32[1,12,8,128]{3,2,1,0:T(8,128)} %get-tuple-element.64), channel_id=1, source_target_pairs={{1,0},{2,1},{3,2},{4,3},{5,4},{6,5},{7,6},{0,7},{9,8},{10,9},{11,1... | collective-permute-start | bytes 147464 | tf_op jit(solution)/shard_map/ppermute | solution.py:289
  107.1 7.0 %collective-permute-start.10 = (f32[1,12,8,128]{3,2,1,0:T(8,128)}, f32[1,12,8,128]{3,2,1,0:T(8,128)S(1)}, u32[]{:S(2)}, u32[]{:S(2)}) collective-permute-start(f32[1,12,8,128]{3,2,1,0:T(8,128)} %get-tuple-element.66), channel_id=1, source_target_pairs={{0,1},{1,2},{2,3},{3,4},{4,5},{5,6},{6,7},{7,0},{8,9},{9,10},{10,1... | collective-permute-start | bytes 147464 | tf_op jit(solution)/shard_map/ppermute | solution.py:288
  107.5 6.6 %collective-permute-start.11 = (f32[1,12,8,128]{3,2,1,0:T(8,128)}, f32[1,12,8,128]{3,2,1,0:T(8,128)S(1)}, u32[]{:S(2)}, u32[]{:S(2)}) collective-permute-start(f32[1,12,8,128]{3,2,1,0:T(8,128)} %get-tuple-element.67), channel_id=1, source_target_pairs={{1,0},{2,1},{3,2},{4,3},{5,4},{6,5},{7,6},{0,7},{9,8},{10,9},{11,1... | collective-permute-start | bytes 147464 | tf_op jit(solution)/shard_map/ppermute | solution.py:289
  118.3 7.0 %collective-permute-start.12 = (f32[1,12,8,128]{3,2,1,0:T(8,128)}, f32[1,12,8,128]{3,2,1,0:T(8,128)S(1)}, u32[]{:S(2)}, u32[]{:S(2)}) collective-permute-start(f32[1,12,8,128]{3,2,1,0:T(8,128)} %get-tuple-element.69), channel_id=1, source_target_pairs={{0,1},{1,2},{2,3},{3,4},{4,5},{5,6},{6,7},{7,0},{8,9},{9,10},{10,1... | collective-permute-start | bytes 147464 | tf_op jit(solution)/shard_map/ppermute | solution.py:288
  118.3 7.0 %collective-permute-start.13 = (f32[1,12,8,128]{3,2,1,0:T(8,128)}, f32[1,12,8,128]{3,2,1,0:T(8,128)S(1)}, u32[]{:S(2)}, u32[]{:S(2)}) collective-permute-start(f32[1,12,8,128]{3,2,1,0:T(8,128)} %get-tuple-element.70), channel_id=1, source_target_pairs={{1,0},{2,1},{3,2},{4,3},{5,4},{6,5},{7,6},{0,7},{9,8},{10,9},{11,1... | collective-permute-start | bytes 147464 | tf_op jit(solution)/shard_map/ppermute | solution.py:289
  137.1 10.1 %collective-permute-start.15 = (f32[3,12,16,128]{3,2,1,0:T(8,128)}, f32[3,12,16,128]{3,2,1,0:T(8,128)S(1)}, u32[]{:S(2)}, u32[]{:S(2)}) collective-permute-start(f32[3,12,16,128]{3,2,1,0:T(8,128)} %get-tuple-element.73), channel_id=1, source_target_pairs={{0,1},{1,2},{2,3},{3,4},{4,5},{5,6},{6,7},{7,0},{8,9},{9,10},{10,1... | collective-permute-start | bytes 884744 | tf_op jit(solution)/shard_map/ppermute | solution.py:288
  137.1 12.2 %collective-permute-start.16 = (f32[3,12,16,128]{3,2,1,0:T(8,128)}, f32[3,12,16,128]{3,2,1,0:T(8,128)S(1)}, u32[]{:S(2)}, u32[]{:S(2)}) collective-permute-start(f32[3,12,16,128]{3,2,1,0:T(8,128)} %get-tuple-element.74), channel_id=1, source_target_pairs={{1,0},{2,1},{3,2},{4,3},{5,4},{6,5},{7,6},{0,7},{9,8},{10,9},{11,1... | collective-permute-start | bytes 884744 | tf_op jit(solution)/shard_map/ppermute | solution.py:289
  160.5 7.5 %collective-permute-start.17 = (f32[1,12,16,128]{3,2,1,0:T(8,128)}, f32[1,12,16,128]{3,2,1,0:T(8,128)S(1)}, u32[]{:S(2)}, u32[]{:S(2)}) collective-permute-start(f32[1,12,16,128]{3,2,1,0:T(8,128)} %get-tuple-element.76), channel_id=1, source_target_pairs={{0,1},{1,2},{2,3},{3,4},{4,5},{5,6},{6,7},{7,0},{8,9},{9,10},{10,1... | collective-permute-start | bytes 294920 | tf_op jit(solution)/shard_map/ppermute | solution.py:288
  160.9 7.1 %collective-permute-start.18 = (f32[1,12,16,128]{3,2,1,0:T(8,128)}, f32[1,12,16,128]{3,2,1,0:T(8,128)S(1)}, u32[]{:S(2)}, u32[]{:S(2)}) collective-permute-start(f32[1,12,16,128]{3,2,1,0:T(8,128)} %get-tuple-element.77), channel_id=1, source_target_pairs={{1,0},{2,1},{3,2},{4,3},{5,4},{6,5},{7,6},{0,7},{9,8},{10,9},{11,1... | collective-permute-start | bytes 294920 | tf_op jit(solution)/shard_map/ppermute | solution.py:289
  174.7 9.6 %collective-permute-start.19 = (f32[1,12,16,128]{3,2,1,0:T(8,128)}, f32[1,12,16,128]{3,2,1,0:T(8,128)S(1)}, u32[]{:S(2)}, u32[]{:S(2)}) collective-permute-start(f32[1,12,16,128]{3,2,1,0:T(8,128)} %get-tuple-element.80), channel_id=1, source_target_pairs={{0,1},{1,2},{2,3},{3,4},{4,5},{5,6},{6,7},{7,0},{8,9},{9,10},{10,1... | collective-permute-start | bytes 294920 | tf_op jit(solution)/shard_map/ppermute | solution.py:288
  174.7 9.6 %collective-permute-start.20 = (f32[1,12,16,128]{3,2,1,0:T(8,128)}, f32[1,12,16,128]{3,2,1,0:T(8,128)S(1)}, u32[]{:S(2)}, u32[]{:S(2)}) collective-permute-start(f32[1,12,16,128]{3,2,1,0:T(8,128)} %get-tuple-element.81), channel_id=1, source_target_pairs={{1,0},{2,1},{3,2},{4,3},{5,4},{6,5},{7,6},{0,7},{9,8},{10,9},{11,1... | collective-permute-start | bytes 294920 | tf_op jit(solution)/shard_map/ppermute | solution.py:289
  215.3 7.0 %collective-permute-start.21 = (f32[1,12,8,128]{3,2,1,0:T(8,128)}, f32[1,12,8,128]{3,2,1,0:T(8,128)S(1)}, u32[]{:S(2)}, u32[]{:S(2)}) collective-permute-start(f32[1,12,8,128]{3,2,1,0:T(8,128)} %get-tuple-element.87), channel_id=1, source_target_pairs={{0,1},{1,2},{2,3},{3,4},{4,5},{5,6},{6,7},{7,0},{8,9},{9,10},{10,1... | collective-permute-start | bytes 147464 | tf_op jit(solution)/shard_map/ppermute | solution.py:288
  216.8 5.5 %collective-permute-start.22 = (f32[1,12,8,128]{3,2,1,0:T(8,128)}, f32[1,12,8,128]{3,2,1,0:T(8,128)S(1)}, u32[]{:S(2)}, u32[]{:S(2)}) collective-permute-start(f32[1,12,8,128]{3,2,1,0:T(8,128)} %get-tuple-element.88), channel_id=1, source_target_pairs={{1,0},{2,1},{3,2},{4,3},{5,4},{6,5},{7,6},{0,7},{9,8},{10,9},{11,1... | collective-permute-start | bytes 147464 | tf_op jit(solution)/shard_map/ppermute | solution.py:289
  226.5 7.0 %collective-permute-start.23 = (f32[1,12,8,128]{3,2,1,0:T(8,128)}, f32[1,12,8,128]{3,2,1,0:T(8,128)S(1)}, u32[]{:S(2)}, u32[]{:S(2)}) collective-permute-start(f32[1,12,8,128]{3,2,1,0:T(8,128)} %get-tuple-element.90), channel_id=1, source_target_pairs={{0,1},{1,2},{2,3},{3,4},{4,5},{5,6},{6,7},{7,0},{8,9},{9,10},{10,1... | collective-permute-start | bytes 147464 | tf_op jit(solution)/shard_map/ppermute | solution.py:288
  227.6 5.9 %collective-permute-start.24 = (f32[1,12,8,128]{3,2,1,0:T(8,128)}, f32[1,12,8,128]{3,2,1,0:T(8,128)S(1)}, u32[]{:S(2)}, u32[]{:S(2)}) collective-permute-start(f32[1,12,8,128]{3,2,1,0:T(8,128)} %get-tuple-element.91), channel_id=1, source_target_pairs={{1,0},{2,1},{3,2},{4,3},{5,4},{6,5},{7,6},{0,7},{9,8},{10,9},{11,1... | collective-permute-start | bytes 147464 | tf_op jit(solution)/shard_map/ppermute | solution.py:289
  237.6 7.0 %collective-permute-start.25 = (f32[1,12,8,128]{3,2,1,0:T(8,128)}, f32[1,12,8,128]{3,2,1,0:T(8,128)S(1)}, u32[]{:S(2)}, u32[]{:S(2)}) collective-permute-start(f32[1,12,8,128]{3,2,1,0:T(8,128)} %get-tuple-element.93), channel_id=1, source_target_pairs={{0,1},{1,2},{2,3},{3,4},{4,5},{5,6},{6,7},{7,0},{8,9},{9,10},{10,1... | collective-permute-start | bytes 147464 | tf_op jit(solution)/shard_map/ppermute | solution.py:288
  237.8 6.9 %collective-permute-start.26 = (f32[1,12,8,128]{3,2,1,0:T(8,128)}, f32[1,12,8,128]{3,2,1,0:T(8,128)S(1)}, u32[]{:S(2)}, u32[]{:S(2)}) collective-permute-start(f32[1,12,8,128]{3,2,1,0:T(8,128)} %get-tuple-element.94), channel_id=1, source_target_pairs={{1,0},{2,1},{3,2},{4,3},{5,4},{6,5},{7,6},{0,7},{9,8},{10,9},{11,1... | collective-permute-start | bytes 147464 | tf_op jit(solution)/shard_map/ppermute | solution.py:289
  (32 other events, 43.6 us)
Sparse Core Ops, SparseCore 0:
  74.7 19.0 all-gather.4
  191.7 21.5 all-gather.6

commit v14 on v10

--- a/solution.py
+++ b/solution.py
@@ -285,8 +285,8 @@
         return swap(head, tail)
 
     def swap(head, tail):
+        nxt = lax.ppermute(head, "space", [((i + 1) % space_n, i) for i in range(space_n)])
         prev = lax.ppermute(tail, "space", [(i, (i + 1) % space_n) for i in range(space_n)])
-        nxt = lax.ppermute(head, "space", [((i + 1) % space_n, i) for i in range(space_n)])
         return prev, nxt
 
     f32 = jnp.float32

time: 259 us -> 259 us (level)
  no operation moved by 1% of the time
where the time goes in v14:
time: 259 us; the launch traced here: 258 us
  Pallas kernels  94.4 us (36%)
  waiting for transfers between devices  68.9 us (27%)
  starting transfers between devices  62.1 us (24%)
  local copies, waits for them, and re-layouts  15.4 us (6%)
  between operations  14.3 us (6%)
    pallas_call x19, Pallas kernels, call(): pl.pallas_call(kernel, out_shape=outs, in_specs=[blocks[i] if blocks is n...  94.4 us
    ppermute x13, starting transfers between devices, swap(): lax.ppermute(head, 'space', [((i + 1) % space_n, i) for i in range(space_...  53.6 us
    ppermute x13, waiting for transfers between devices, swap(): lax.ppermute(tail, 'space', [(i, (i + 1) % space_n) for i in range(space_...  33.5 us
    all_gather x2, waiting for transfers between devices, per_device(): rint_all = lax.all_gather(rint[None], 'tm')  25.9 us
    ppermute x13, waiting for transfers between devices, swap(): lax.ppermute(head, 'space', [((i + 1) % space_n, i) for i in range(space_...  9.42 us
    unnamed x65, local copies, waits for them, and re-layouts  9.35 us
    ppermute x13, starting transfers between devices, swap(): lax.ppermute(tail, 'space', [(i, (i + 1) % space_n) for i in range(space_...  6.93 us
  transfers between devices with their start and end apart: 29, of which 17 were waited for; matrix products, arithmetic and copies ran while one was open for 2% of the time, Pallas kernels for 10%

profile of v14, /device:TPU:0, one launch (start us, length us, event | category | flops | bytes accessed | tf_op | source)
XLA Modules:
  0.0 258.2 jit_solution(6777835415531579686)
XLA Ops:
  11.9 6.0 %collective-permute-start.1 = (f32[3,12,16,128]{3,2,1,0:T(8,128)}, f32[3,12,16,128]{3,2,1,0:T(8,128)S(1)}, u32[]{:S(2)}, u32[]{:S(2)}) collective-permute-start(f32[3,12,16,128]{3,2,1,0:T(8,128)} %get-tuple-element.98), channel_id=1, source_target_pairs={{1,0},{2,1},{3,2},{4,3},{5,4},{6,5},{7,6},{0,7},{9,8},{10,9},{11,1... | collective-permute-start | bytes 884744 | tf_op jit(solution)/shard_map/ppermute | solution.py:288
  21.4 4.2 %collective-permute-done.1.n_ref = f32[3,12,16,128]{3,2,1,0:T(8,128)S(1)} collective-permute-done((f32[3,12,16,128]{3,2,1,0:T(8,128)}, f32[3,12,16,128]{3,2,1,0:T(8,128)S(1)}, u32[]{:S(2)}, u32[]{:S(2)}) %collective-permute-start.1) | collective-permute-done | bytes 294944 | tf_op jit(solution)/shard_map/ppermute | solution.py:288
  25.6 4.9 %collective-permute-done.p_ref = f32[3,12,16,128]{3,2,1,0:T(8,128)} collective-permute-done((f32[3,12,16,128]{3,2,1,0:T(8,128)}, f32[3,12,16,128]{3,2,1,0:T(8,128)}, u32[]{:S(2)}, u32[]{:S(2)}) %collective-permute-start) | collective-permute-done | bytes 294944 | tf_op jit(solution)/shard_map/ppermute | solution.py:289
  30.5 10.5 %shard_map.131 = (f32[3,12,128,128]{3,2,1,0:T(8,128)}, f32[1,12,128,128]{3,2,1,0:T(8,128)}, f32[1,12,16,128]{3,2,1,0:T(8,128)}, f32[1,12,16,128]{3,2,1,0:T(8,128)}) custom-call(f32[3,12,128,128]{3,2,1,0:T(8,128)} %pad_maximum_fusion.u_ref, f32[3,12,16,128]{3,2,1,0:T(8,128)} %collective-permute-done.p_ref, f32[3,12,16,128]{3,2,1,0:T(8,128)} %copy-done.4, ...), custom_call_target="tpu_custom_call" | custom-call | flops 1822556160 | bytes 6488916 | tf_op jit(solution)/shard_map/pallas_call | solution.py:217
  50.3 5.9 %shard_map.132 = (f32[1,12,128,128]{3,2,1,0:T(8,128)}, f32[1,12,128,128]{3,2,1,0:T(8,128)}, f32[1,12,16,128]{3,2,1,0:T(8,128)}, f32[1,12,16,128]{3,2,1,0:T(8,128)}) custom-call(f32[1,12,128,128]{3,2,1,0:T(8,128)} %get-tuple-element.50.a1_ref.refs_0_, f32[1,12,16,128]{3,2,1,0:T(8,128)} %copy-done.8, f32[1,12,16,128]{3,2,1,0:T(8,128)} %copy-done.10, ...), custom_call_target="tpu_custom_call" | custom-call | flops 607518720 | bytes 5309268 | tf_op jit(solution)/shard_map/pallas_call | solution.py:217
  56.5 4.4 %collective-permute-start.5 = (f32[1,12,16,128]{3,2,1,0:T(8,128)}, f32[1,12,16,128]{3,2,1,0:T(8,128)S(1)}, u32[]{:S(2)}, u32[]{:S(2)}) collective-permute-start(f32[1,12,16,128]{3,2,1,0:T(8,128)} %get-tuple-element.57), channel_id=1, source_target_pairs={{1,0},{2,1},{3,2},{4,3},{5,4},{6,5},{7,6},{0,7},{9,8},{10,9},{11,1... | collective-permute-start | bytes 294920 | tf_op jit(solution)/shard_map/ppermute | solution.py:288
  62.1 4.8 %shard_map.133 = (f32[1,12,64,128]{3,2,1,0:T(8,128)}, f32[1,12,64,128]{3,2,1,0:T(8,128)}) custom-call(f32[3,12,128,128]{3,2,1,0:T(8,128)} %pad_maximum_fusion.u_ref, f32[3,12,16,128]{3,2,1,0:T(8,128)} %collective-permute-done.p_ref, f32[3,12,16,128]{3,2,1,0:T(8,128)} %copy-done.4, f32[64,128]{1,0:T(8,128)} %constant.28.clone.r_ref.refs_11_, ...), custom_call_target="tpu_custom_call" | custom-call | flops 228261888 | bytes 3867988 | tf_op jit(solution)/shard_map/pallas_call | solution.py:217
  67.6 6.6 %shard_map.134 = (f32[12,64,128]{2,1,0:T(8,128)}, f32[12,64,128]{2,1,0:T(8,128)}) custom-call(f32[1,12,128,128]{3,2,1,0:T(8,128)} %get-tuple-element.54.a2_ref.refs_1_, f32[1,12,16,128]{3,2,1,0:T(8,128)} %copy-done.11, f32[1,12,16,128]{3,2,1,0:T(8,128)} %copy-done.12, f32[256,128]{1,0:T(8,128)} %constant.26.clone.l_ref, f32[128,128]{1,0:T(8,128)} %constant.25.clone.x_ref, ...), custom_call_target="tpu_custom_call" | custom-call | flops 607518720 | bytes 5538644 | tf_op jit(solution)/shard_map/pallas_call | solution.py:217
  80.5 4.2 %collective-permute-done.6 = f32[12,8,128]{2,1,0:T(8,128)S(1)} collective-permute-done((f32[12,8,128]{2,1,0:T(8,128)S(1)}, f32[12,8,128]{2,1,0:T(8,128)S(1)}, u32[]{:S(2)}, u32[]{:S(2)}) %collective-permute-start.6) | collective-permute-done | bytes 49184 | tf_op jit(solution)/shard_map/ppermute | solution.py:289
  88.6 4.3 %all-gather.5.cloned.1.call-done = f32[48,64,128]{2,1,0:T(8,128)} async-done(((f32[12,64,128]{2,1,0:T(8,128)}), f32[48,64,128]{2,1,0:T(8,128)}) %all-gather.5.cloned.1.call-update) | async-done | bytes 1572880 | tf_op jit(solution)/shard_map/all_gather | solution.py:523
  95.7 4.0 %collective-permute-start.9 = (f32[1,12,8,128]{3,2,1,0:T(8,128)}, f32[1,12,8,128]{3,2,1,0:T(8,128)S(1)}, u32[]{:S(2)}, u32[]{:S(2)}) collective-permute-start(f32[1,12,8,128]{3,2,1,0:T(8,128)} %get-tuple-element.64), channel_id=1, source_target_pairs={{1,0},{2,1},{3,2},{4,3},{5,4},{6,5},{7,6},{0,7},{9,8},{10,9},{11,1... | collective-permute-start | bytes 147464 | tf_op jit(solution)/shard_map/ppermute | solution.py:288
  102.6 3.5 %shard_map.137 = (f32[1,12,64,128]{3,2,1,0:T(8,128)}, f32[1,12,8,128]{3,2,1,0:T(8,128)}, f32[1,12,8,128]{3,2,1,0:T(8,128)}) custom-call(f32[1,12,64,128]{3,2,1,0:T(8,128)} %get-tuple-element.62.w_ref.refs_5_, f32[1,12,8,128]{3,2,1,0:T(8,128)} %copy-done.20, f32[1,12,8,128]{3,2,1,0:T(8,128)} %copy-done.25, f32[128,64]{1,0:T(8,128)} %constant.27.clone.l_ref, ...), custom_call_target="tpu_custom_call" | custom-call | flops 228261888 | bytes 2655060 | tf_op jit(solution)/shard_map/pallas_call | solution.py:217
  106.5 4.3 %collective-permute-start.11 = (f32[1,12,8,128]{3,2,1,0:T(8,128)}, f32[1,12,8,128]{3,2,1,0:T(8,128)S(1)}, u32[]{:S(2)}, u32[]{:S(2)}) collective-permute-start(f32[1,12,8,128]{3,2,1,0:T(8,128)} %get-tuple-element.67), channel_id=1, source_target_pairs={{1,0},{2,1},{3,2},{4,3},{5,4},{6,5},{7,6},{0,7},{9,8},{10,9},{11,1... | collective-permute-start | bytes 147464 | tf_op jit(solution)/shard_map/ppermute | solution.py:288
  113.7 3.6 %shard_map.138 = (f32[1,12,64,128]{3,2,1,0:T(8,128)}, f32[1,12,8,128]{3,2,1,0:T(8,128)}, f32[1,12,8,128]{3,2,1,0:T(8,128)}) custom-call(f32[1,12,64,128]{3,2,1,0:T(8,128)} %get-tuple-element.65.w_ref.refs_6_, f32[1,12,8,128]{3,2,1,0:T(8,128)} %copy-done.21, f32[1,12,8,128]{3,2,1,0:T(8,128)} %copy-done.26, f32[128,64]{1,0:T(8,128)} %constant.27.clone.l_ref, ...), custom_call_target="tpu_custom_call" | custom-call | flops 228261888 | bytes 2655060 | tf_op jit(solution)/shard_map/pallas_call | solution.py:217
  117.3 4.8 %collective-permute-start.13 = (f32[1,12,8,128]{3,2,1,0:T(8,128)}, f32[1,12,8,128]{3,2,1,0:T(8,128)S(1)}, u32[]{:S(2)}, u32[]{:S(2)}) collective-permute-start(f32[1,12,8,128]{3,2,1,0:T(8,128)} %get-tuple-element.70), channel_id=1, source_target_pairs={{1,0},{2,1},{3,2},{4,3},{5,4},{6,5},{7,6},{0,7},{9,8},{10,9},{11,1... | collective-permute-start | bytes 147464 | tf_op jit(solution)/shard_map/ppermute | solution.py:288
  125.0 3.6 %shard_map.139 = (f32[1,12,64,128]{3,2,1,0:T(8,128)}, f32[1,12,8,128]{3,2,1,0:T(8,128)}, f32[1,12,8,128]{3,2,1,0:T(8,128)}) custom-call(f32[1,12,64,128]{3,2,1,0:T(8,128)} %get-tuple-element.68.w_ref.refs_7_, f32[1,12,8,128]{3,2,1,0:T(8,128)} %copy-done.18, f32[1,12,8,128]{3,2,1,0:T(8,128)} %copy-done.22, f32[128,64]{1,0:T(8,128)} %constant.27.clone.l_ref, ...), custom_call_target="tpu_custom_call" | custom-call | flops 228261888 | bytes 2655060 | tf_op jit(solution)/shard_map/pallas_call | solution.py:217
  129.4 6.7 %shard_map.140 = (f32[3,12,128,128]{3,2,1,0:T(8,128)}, f32[3,12,16,128]{3,2,1,0:T(8,128)}, f32[3,12,16,128]{3,2,1,0:T(8,128)}) custom-call(f32[1,12,128,128]{3,2,1,0:T(8,128)} %get-tuple-element.50.a1_ref.refs_0_, f32[1,12,128,128]{3,2,1,0:T(8,128)} %get-tuple-element.54.a2_ref.refs_1_, f32[1,12,64,128]{3,2,1,0:T(8,128)} %get-tuple-element.55.refs_2_, ...), custom_call_target="tpu_custom_call" | custom-call | flops 603979776 | bytes 8912904 | tf_op jit(solution)/shard_map/pallas_call | solution.py:217
  136.1 4.7 %collective-permute-start.16 = (f32[3,12,16,128]{3,2,1,0:T(8,128)}, f32[3,12,16,128]{3,2,1,0:T(8,128)S(1)}, u32[]{:S(2)}, u32[]{:S(2)}) collective-permute-start(f32[3,12,16,128]{3,2,1,0:T(8,128)} %get-tuple-element.74), channel_id=1, source_target_pairs={{1,0},{2,1},{3,2},{4,3},{5,4},{6,5},{7,6},{0,7},{9,8},{10,9},{11,1... | collective-permute-start | bytes 884744 | tf_op jit(solution)/shard_map/ppermute | solution.py:288
  140.9 5.3 %collective-permute-done.15.p_ref = f32[3,12,16,128]{3,2,1,0:T(8,128)S(1)} collective-permute-done((f32[3,12,16,128]{3,2,1,0:T(8,128)}, f32[3,12,16,128]{3,2,1,0:T(8,128)S(1)}, u32[]{:S(2)}, u32[]{:S(2)}) %collective-permute-start.15) | collective-permute-done | bytes 294944 | tf_op jit(solution)/shard_map/ppermute | solution.py:289
  149.0 10.5 %shard_map.141 = (f32[3,12,128,128]{3,2,1,0:T(8,128)}, f32[1,12,128,128]{3,2,1,0:T(8,128)}, f32[1,12,16,128]{3,2,1,0:T(8,128)}, f32[1,12,16,128]{3,2,1,0:T(8,128)}) custom-call(f32[3,12,128,128]{3,2,1,0:T(8,128)} %get-tuple-element.72.u_ref, f32[3,12,16,128]{3,2,1,0:T(8,128)} %copy-done.5, f32[3,12,16,128]{3,2,1,0:T(8,128)} %copy-done.6, ...), custom_call_target="tpu_custom_call" | custom-call | flops 1822556160 | bytes 6488916 | tf_op jit(solution)/shard_map/pallas_call | solution.py:217
  159.9 4.4 %collective-permute-start.18 = (f32[1,12,16,128]{3,2,1,0:T(8,128)}, f32[1,12,16,128]{3,2,1,0:T(8,128)S(1)}, u32[]{:S(2)}, u32[]{:S(2)}) collective-permute-start(f32[1,12,16,128]{3,2,1,0:T(8,128)} %get-tuple-element.77), channel_id=1, source_target_pairs={{1,0},{2,1},{3,2},{4,3},{5,4},{6,5},{7,6},{0,7},{9,8},{10,9},{11,1... | collective-permute-start | bytes 294920 | tf_op jit(solution)/shard_map/ppermute | solution.py:288
  167.7 5.9 %shard_map.142 = (f32[1,12,128,128]{3,2,1,0:T(8,128)}, f32[1,12,128,128]{3,2,1,0:T(8,128)}, f32[1,12,16,128]{3,2,1,0:T(8,128)}, f32[1,12,16,128]{3,2,1,0:T(8,128)}) custom-call(f32[1,12,128,128]{3,2,1,0:T(8,128)} %get-tuple-element.75.a1_ref, f32[1,12,16,128]{3,2,1,0:T(8,128)} %copy-done.7, f32[1,12,16,128]{3,2,1,0:T(8,128)} %copy-done.9, ...), custom_call_target="tpu_custom_call" | custom-call | flops 607518720 | bytes 5309268 | tf_op jit(solution)/shard_map/pallas_call | solution.py:217
  173.7 4.9 %collective-permute-start.20 = (f32[1,12,16,128]{3,2,1,0:T(8,128)}, f32[1,12,16,128]{3,2,1,0:T(8,128)S(1)}, u32[]{:S(2)}, u32[]{:S(2)}) collective-permute-start(f32[1,12,16,128]{3,2,1,0:T(8,128)} %get-tuple-element.81), channel_id=1, source_target_pairs={{1,0},{2,1},{3,2},{4,3},{5,4},{6,5},{7,6},{0,7},{9,8},{10,9},{11,1... | collective-permute-start | bytes 294920 | tf_op jit(solution)/shard_map/ppermute | solution.py:288
  178.5 4.8 %shard_map.143 = (f32[1,12,64,128]{3,2,1,0:T(8,128)}, f32[1,12,64,128]{3,2,1,0:T(8,128)}) custom-call(f32[3,12,128,128]{3,2,1,0:T(8,128)} %get-tuple-element.72.u_ref, f32[3,12,16,128]{3,2,1,0:T(8,128)} %copy-done.5, f32[3,12,16,128]{3,2,1,0:T(8,128)} %copy-done.6, f32[64,128]{1,0:T(8,128)} %constant.28.clone.r_ref.refs_11_, f32[8,16]{1,0:T(8,128)} %constant.30.clone.rp_ref, ...), custom_call_target="tpu_custom_call" | custom-call | flops 228261888 | bytes 3867988 | tf_op jit(solution)/shard_map/pallas_call | solution.py:217
  184.0 6.6 %shard_map.144 = (f32[12,64,128]{2,1,0:T(8,128)}, f32[12,64,128]{2,1,0:T(8,128)}) custom-call(f32[1,12,128,128]{3,2,1,0:T(8,128)} %get-tuple-element.79.a2_ref.refs_0_, f32[1,12,16,128]{3,2,1,0:T(8,128)} %copy-done.13, f32[1,12,16,128]{3,2,1,0:T(8,128)} %copy-done.14, f32[256,128]{1,0:T(8,128)} %constant.26.clone.l_ref, f32[128,128]{1,0:T(8,128)} %constant.25.clone.x_ref, ...), custom_call_target="tpu_custom_call" | custom-call | flops 607518720 | bytes 5538644 | tf_op jit(solution)/shard_map/pallas_call | solution.py:217
  190.6 21.7 %all-gather.7.cloned.1.call-done = f32[48,64,128]{2,1,0:T(8,128)} async-done(((f32[12,64,128]{2,1,0:T(8,128)}), f32[48,64,128]{2,1,0:T(8,128)}) %all-gather.7.cloned.1.call-update) | async-done | bytes 1572880 | tf_op jit(solution)/shard_map/all_gather | solution.py:523
  221.9 3.5 %shard_map.146 = (f32[1,12,64,128]{3,2,1,0:T(8,128)}, f32[1,12,8,128]{3,2,1,0:T(8,128)}, f32[1,12,8,128]{3,2,1,0:T(8,128)}) custom-call(f32[1,12,64,128]{3,2,1,0:T(8,128)} %get-tuple-element.86.w_ref.refs_3_, f32[1,12,8,128]{3,2,1,0:T(8,128)} %copy-done.23, f32[1,12,8,128]{3,2,1,0:T(8,128)} %copy-done.27, f32[128,64]{1,0:T(8,128)} %constant.27.clone.l_ref, ...), custom_call_target="tpu_custom_call" | custom-call | flops 228261888 | bytes 2655060 | tf_op jit(solution)/shard_map/pallas_call | solution.py:217
  226.6 3.6 %collective-permute-start.24 = (f32[1,12,8,128]{3,2,1,0:T(8,128)}, f32[1,12,8,128]{3,2,1,0:T(8,128)S(1)}, u32[]{:S(2)}, u32[]{:S(2)}) collective-permute-start(f32[1,12,8,128]{3,2,1,0:T(8,128)} %get-tuple-element.91), channel_id=1, source_target_pairs={{1,0},{2,1},{3,2},{4,3},{5,4},{6,5},{7,6},{0,7},{9,8},{10,9},{11,1... | collective-permute-start | bytes 147464 | tf_op jit(solution)/shard_map/ppermute | solution.py:288
  233.1 3.5 %shard_map.147 = (f32[1,12,64,128]{3,2,1,0:T(8,128)}, f32[1,12,8,128]{3,2,1,0:T(8,128)}, f32[1,12,8,128]{3,2,1,0:T(8,128)}) custom-call(f32[1,12,64,128]{3,2,1,0:T(8,128)} %get-tuple-element.89.w_ref.refs_4_, f32[1,12,8,128]{3,2,1,0:T(8,128)} %copy-done.24, f32[1,12,8,128]{3,2,1,0:T(8,128)} %copy-done.28, f32[128,64]{1,0:T(8,128)} %constant.27.clone.l_ref, ...), custom_call_target="tpu_custom_call" | custom-call | flops 228261888 | bytes 2655060 | tf_op jit(solution)/shard_map/pallas_call | solution.py:217
  236.8 4.6 %collective-permute-start.26 = (f32[1,12,8,128]{3,2,1,0:T(8,128)}, f32[1,12,8,128]{3,2,1,0:T(8,128)S(1)}, u32[]{:S(2)}, u32[]{:S(2)}) collective-permute-start(f32[1,12,8,128]{3,2,1,0:T(8,128)} %get-tuple-element.94), channel_id=1, source_target_pairs={{1,0},{2,1},{3,2},{4,3},{5,4},{6,5},{7,6},{0,7},{9,8},{10,9},{11,1... | collective-permute-start | bytes 147464 | tf_op jit(solution)/shard_map/ppermute | solution.py:288
  244.3 3.5 %shard_map.148 = (f32[1,12,64,128]{3,2,1,0:T(8,128)}, f32[1,12,8,128]{3,2,1,0:T(8,128)}, f32[1,12,8,128]{3,2,1,0:T(8,128)}) custom-call(f32[1,12,64,128]{3,2,1,0:T(8,128)} %get-tuple-element.92.w_ref.refs_5_, f32[1,12,8,128]{3,2,1,0:T(8,128)} %copy-done.17, f32[1,12,8,128]{3,2,1,0:T(8,128)} %copy-done.19, f32[128,64]{1,0:T(8,128)} %constant.27.clone.l_ref, ...), custom_call_target="tpu_custom_call" | custom-call | flops 228261888 | bytes 2655060 | tf_op jit(solution)/shard_map/pallas_call | solution.py:217
  247.8 3.5 %shard_map.149 = (f32[1,12,128,128]{3,2,1,0:T(8,128)}, f32[1,12,64,128]{3,2,1,0:T(8,128)}) custom-call(f32[1,12,128,128]{3,2,1,0:T(8,128)} %get-tuple-element.79.a2_ref.refs_0_, f32[12,64,128]{2,1,0:T(8,128)} %get-tuple-element.84.refs_1_, f32[1,12,64,128]{3,2,1,0:T(8,128)} %bitcast.35, f32[1,12,64,128]{3,2,1,0:T(8,128)} %get-tuple-element.86.w_ref.refs_3_, ...), custom_call_target="tpu_custom_call" | custom-call | flops 150994944 | bytes 4358148 | tf_op jit(solution)/shard_map/pallas_call | solution.py:217
  (123 shorter events, 66.5 us)
Async XLA Ops:
  7.2 85.7 %all-gather.5.cloned.1.call-start = ((), (), s32[]{:S(2)}) async-start(), calls=%async_computation | async-start | bytes 1966080 | tf_op jit(solution)/shard_map/all_gather | solution.py:523
  10.9 7.0 %copy-start.31 = (f32[3,12]{1,0:T(4,128)S(1)}, f32[3,12]{1,0:T(4,128)}, u32[]{:S(2)}) copy-start(f32[3,12]{1,0:T(4,128)} %param.14) | copy-start | bytes 436
  11.9 13.7 %collective-permute-start.1 = (f32[3,12,16,128]{3,2,1,0:T(8,128)}, f32[3,12,16,128]{3,2,1,0:T(8,128)S(1)}, u32[]{:S(2)}, u32[]{:S(2)}) collective-permute-start(f32[3,12,16,128]{3,2,1,0:T(8,128)} %get-tuple-element.98), channel_id=1, source_target_pairs={{1,0},{2,1},{3,2},{4,3},{5,4},{6,5},{7,6},{0,7},{9,8},{10,9},{11,1... | collective-permute-start | bytes 884744 | tf_op jit(solution)/shard_map/ppermute | solution.py:288
  17.9 12.6 %collective-permute-start = (f32[3,12,16,128]{3,2,1,0:T(8,128)}, f32[3,12,16,128]{3,2,1,0:T(8,128)}, u32[]{:S(2)}, u32[]{:S(2)}) collective-permute-start(f32[3,12,16,128]{3,2,1,0:T(8,128)} %get-tuple-element.99), channel_id=1, source_target_pairs={{0,1},{1,2},{2,3},{3,4},{4,5},{5,6},{6,7},{7,0},{8,9},{9,10},{10,1... | collective-permute-start | bytes 884744 | tf_op jit(solution)/shard_map/ppermute | solution.py:289
  41.0 7.6 %collective-permute-start.2 = (f32[1,12,16,128]{3,2,1,0:T(8,128)}, f32[1,12,16,128]{3,2,1,0:T(8,128)S(1)}, u32[]{:S(2)}, u32[]{:S(2)}) collective-permute-start(f32[1,12,16,128]{3,2,1,0:T(8,128)} %get-tuple-element.51), channel_id=1, source_target_pairs={{0,1},{1,2},{2,3},{3,4},{4,5},{5,6},{6,7},{7,0},{8,9},{9,10},{10,1... | collective-permute-start | bytes 294920 | tf_op jit(solution)/shard_map/ppermute | solution.py:289
  42.8 6.9 %collective-permute-start.3 = (f32[1,12,16,128]{3,2,1,0:T(8,128)}, f32[1,12,16,128]{3,2,1,0:T(8,128)S(1)}, u32[]{:S(2)}, u32[]{:S(2)}) collective-permute-start(f32[1,12,16,128]{3,2,1,0:T(8,128)} %get-tuple-element.52), channel_id=1, source_target_pairs={{1,0},{2,1},{3,2},{4,3},{5,4},{6,5},{7,6},{0,7},{9,8},{10,9},{11,1... | collective-permute-start | bytes 294920 | tf_op jit(solution)/shard_map/ppermute | solution.py:288
  56.2 10.7 %collective-permute-start.4 = (f32[1,12,16,128]{3,2,1,0:T(8,128)}, f32[1,12,16,128]{3,2,1,0:T(8,128)S(1)}, u32[]{:S(2)}, u32[]{:S(2)}) collective-permute-start(f32[1,12,16,128]{3,2,1,0:T(8,128)} %get-tuple-element.56), channel_id=1, source_target_pairs={{0,1},{1,2},{2,3},{3,4},{4,5},{5,6},{6,7},{7,0},{8,9},{9,10},{10,1... | collective-permute-start | bytes 294920 | tf_op jit(solution)/shard_map/ppermute | solution.py:289
  56.5 10.4 %collective-permute-start.5 = (f32[1,12,16,128]{3,2,1,0:T(8,128)}, f32[1,12,16,128]{3,2,1,0:T(8,128)S(1)}, u32[]{:S(2)}, u32[]{:S(2)}) collective-permute-start(f32[1,12,16,128]{3,2,1,0:T(8,128)} %get-tuple-element.57), channel_id=1, source_target_pairs={{1,0},{2,1},{3,2},{4,3},{5,4},{6,5},{7,6},{0,7},{9,8},{10,9},{11,1... | collective-permute-start | bytes 294920 | tf_op jit(solution)/shard_map/ppermute | solution.py:288
  67.6 8.2 %copy-start.29 = (f32[8,16,1,1]{1,0,3,2:T(8,128)S(1)}, f32[8,16,1,1]{1,0,3,2:T(8,128)}, u32[]{:S(2)}) copy-start(f32[8,16,1,1]{1,0,3,2:T(8,128)} %constant.32) | copy-start | bytes 1540
  74.2 138.0 %all-gather.7.cloned.1.call-start = ((), (), s32[]{:S(2)}) async-start(), calls=%async_computation.1 | async-start | bytes 1966080 | tf_op jit(solution)/shard_map/all_gather | solution.py:523
  74.3 54.3 %collective-permute-start.14 = (f32[1,12,128,128]{3,2,1,0:T(8,128)S(1)}, f32[1,12,128,128]{3,2,1,0:T(8,128)S(1)}, u32[]{:S(2)}, u32[]{:S(2)}) collective-permute-start(f32[1,12,128,128]{3,2,1,0:T(8,128)S(1)} %copy-done.2), channel_id=1, source_target_pairs={{0,8},{8,16},{16,24},{1,9},{9,17},{17,25},{2,10},{10,18},{18,26},{... | collective-permute-start | bytes 2359304 | tf_op jit(solution)/shard_map/ppermute | solution.py:526
  76.3 8.4 %copy-start = (f32[8,12,8,128]{3,0,2,1:T(8,128)}, f32[8,12,8,128]{3,0,2,1:T(8,128)S(1)}, u32[]{:S(2)}) copy-start(f32[8,12,8,128]{3,0,2,1:T(8,128)S(1)} %fusion.3) | copy-start | bytes 1179652
  76.3 4.1 %collective-permute-start.7 = (f32[12,8,128]{2,1,0:T(8,128)S(1)}, f32[12,8,128]{2,1,0:T(8,128)S(1)}, u32[]{:S(2)}, u32[]{:S(2)}) collective-permute-start(f32[12,8,128]{2,1,0:T(8,128)S(1)} %get-tuple-element.100), channel_id=1, source_target_pairs={{1,0},{2,1},{3,2},{4,3},{5,4},{6,5},{7,6},{0,7},{9,8},{10,9},{11,1... | collective-permute-start | bytes 147464 | tf_op jit(solution)/shard_map/ppermute | solution.py:288
  77.9 6.8 %collective-permute-start.6 = (f32[12,8,128]{2,1,0:T(8,128)S(1)}, f32[12,8,128]{2,1,0:T(8,128)S(1)}, u32[]{:S(2)}, u32[]{:S(2)}) collective-permute-start(f32[12,8,128]{2,1,0:T(8,128)S(1)} %get-tuple-element.101), channel_id=1, source_target_pairs={{0,1},{1,2},{2,3},{3,4},{4,5},{5,6},{6,7},{7,0},{8,9},{9,10},{10,1... | collective-permute-start | bytes 147464 | tf_op jit(solution)/shard_map/ppermute | solution.py:289
  94.9 7.0 %collective-permute-start.8 = (f32[1,12,8,128]{3,2,1,0:T(8,128)}, f32[1,12,8,128]{3,2,1,0:T(8,128)S(1)}, u32[]{:S(2)}, u32[]{:S(2)}) collective-permute-start(f32[1,12,8,128]{3,2,1,0:T(8,128)} %get-tuple-element.63), channel_id=1, source_target_pairs={{0,1},{1,2},{2,3},{3,4},{4,5},{5,6},{6,7},{7,0},{8,9},{9,10},{10,1... | collective-permute-start | bytes 147464 | tf_op jit(solution)/shard_map/ppermute | solution.py:289
  95.7 6.3 %collective-permute-start.9 = (f32[1,12,8,128]{3,2,1,0:T(8,128)}, f32[1,12,8,128]{3,2,1,0:T(8,128)S(1)}, u32[]{:S(2)}, u32[]{:S(2)}) collective-permute-start(f32[1,12,8,128]{3,2,1,0:T(8,128)} %get-tuple-element.64), channel_id=1, source_target_pairs={{1,0},{2,1},{3,2},{4,3},{5,4},{6,5},{7,6},{0,7},{9,8},{10,9},{11,1... | collective-permute-start | bytes 147464 | tf_op jit(solution)/shard_map/ppermute | solution.py:288
  106.1 7.0 %collective-permute-start.10 = (f32[1,12,8,128]{3,2,1,0:T(8,128)}, f32[1,12,8,128]{3,2,1,0:T(8,128)S(1)}, u32[]{:S(2)}, u32[]{:S(2)}) collective-permute-start(f32[1,12,8,128]{3,2,1,0:T(8,128)} %get-tuple-element.66), channel_id=1, source_target_pairs={{0,1},{1,2},{2,3},{3,4},{4,5},{5,6},{6,7},{7,0},{8,9},{9,10},{10,1... | collective-permute-start | bytes 147464 | tf_op jit(solution)/shard_map/ppermute | solution.py:289
  106.5 6.6 %collective-permute-start.11 = (f32[1,12,8,128]{3,2,1,0:T(8,128)}, f32[1,12,8,128]{3,2,1,0:T(8,128)S(1)}, u32[]{:S(2)}, u32[]{:S(2)}) collective-permute-start(f32[1,12,8,128]{3,2,1,0:T(8,128)} %get-tuple-element.67), channel_id=1, source_target_pairs={{1,0},{2,1},{3,2},{4,3},{5,4},{6,5},{7,6},{0,7},{9,8},{10,9},{11,1... | collective-permute-start | bytes 147464 | tf_op jit(solution)/shard_map/ppermute | solution.py:288
  117.3 7.0 %collective-permute-start.12 = (f32[1,12,8,128]{3,2,1,0:T(8,128)}, f32[1,12,8,128]{3,2,1,0:T(8,128)S(1)}, u32[]{:S(2)}, u32[]{:S(2)}) collective-permute-start(f32[1,12,8,128]{3,2,1,0:T(8,128)} %get-tuple-element.69), channel_id=1, source_target_pairs={{0,1},{1,2},{2,3},{3,4},{4,5},{5,6},{6,7},{7,0},{8,9},{9,10},{10,1... | collective-permute-start | bytes 147464 | tf_op jit(solution)/shard_map/ppermute | solution.py:289
  117.3 7.0 %collective-permute-start.13 = (f32[1,12,8,128]{3,2,1,0:T(8,128)}, f32[1,12,8,128]{3,2,1,0:T(8,128)S(1)}, u32[]{:S(2)}, u32[]{:S(2)}) collective-permute-start(f32[1,12,8,128]{3,2,1,0:T(8,128)} %get-tuple-element.70), channel_id=1, source_target_pairs={{1,0},{2,1},{3,2},{4,3},{5,4},{6,5},{7,6},{0,7},{9,8},{10,9},{11,1... | collective-permute-start | bytes 147464 | tf_op jit(solution)/shard_map/ppermute | solution.py:288
  136.1 10.1 %collective-permute-start.15 = (f32[3,12,16,128]{3,2,1,0:T(8,128)}, f32[3,12,16,128]{3,2,1,0:T(8,128)S(1)}, u32[]{:S(2)}, u32[]{:S(2)}) collective-permute-start(f32[3,12,16,128]{3,2,1,0:T(8,128)} %get-tuple-element.73), channel_id=1, source_target_pairs={{0,1},{1,2},{2,3},{3,4},{4,5},{5,6},{6,7},{7,0},{8,9},{9,10},{10,1... | collective-permute-start | bytes 884744 | tf_op jit(solution)/shard_map/ppermute | solution.py:289
  136.1 12.2 %collective-permute-start.16 = (f32[3,12,16,128]{3,2,1,0:T(8,128)}, f32[3,12,16,128]{3,2,1,0:T(8,128)S(1)}, u32[]{:S(2)}, u32[]{:S(2)}) collective-permute-start(f32[3,12,16,128]{3,2,1,0:T(8,128)} %get-tuple-element.74), channel_id=1, source_target_pairs={{1,0},{2,1},{3,2},{4,3},{5,4},{6,5},{7,6},{0,7},{9,8},{10,9},{11,1... | collective-permute-start | bytes 884744 | tf_op jit(solution)/shard_map/ppermute | solution.py:288
  159.5 7.5 %collective-permute-start.17 = (f32[1,12,16,128]{3,2,1,0:T(8,128)}, f32[1,12,16,128]{3,2,1,0:T(8,128)S(1)}, u32[]{:S(2)}, u32[]{:S(2)}) collective-permute-start(f32[1,12,16,128]{3,2,1,0:T(8,128)} %get-tuple-element.76), channel_id=1, source_target_pairs={{0,1},{1,2},{2,3},{3,4},{4,5},{5,6},{6,7},{7,0},{8,9},{9,10},{10,1... | collective-permute-start | bytes 294920 | tf_op jit(solution)/shard_map/ppermute | solution.py:289
  159.9 7.1 %collective-permute-start.18 = (f32[1,12,16,128]{3,2,1,0:T(8,128)}, f32[1,12,16,128]{3,2,1,0:T(8,128)S(1)}, u32[]{:S(2)}, u32[]{:S(2)}) collective-permute-start(f32[1,12,16,128]{3,2,1,0:T(8,128)} %get-tuple-element.77), channel_id=1, source_target_pairs={{1,0},{2,1},{3,2},{4,3},{5,4},{6,5},{7,6},{0,7},{9,8},{10,9},{11,1... | collective-permute-start | bytes 294920 | tf_op jit(solution)/shard_map/ppermute | solution.py:288
  173.7 9.6 %collective-permute-start.19 = (f32[1,12,16,128]{3,2,1,0:T(8,128)}, f32[1,12,16,128]{3,2,1,0:T(8,128)S(1)}, u32[]{:S(2)}, u32[]{:S(2)}) collective-permute-start(f32[1,12,16,128]{3,2,1,0:T(8,128)} %get-tuple-element.80), channel_id=1, source_target_pairs={{0,1},{1,2},{2,3},{3,4},{4,5},{5,6},{6,7},{7,0},{8,9},{9,10},{10,1... | collective-permute-start | bytes 294920 | tf_op jit(solution)/shard_map/ppermute | solution.py:289
  173.7 9.6 %collective-permute-start.20 = (f32[1,12,16,128]{3,2,1,0:T(8,128)}, f32[1,12,16,128]{3,2,1,0:T(8,128)S(1)}, u32[]{:S(2)}, u32[]{:S(2)}) collective-permute-start(f32[1,12,16,128]{3,2,1,0:T(8,128)} %get-tuple-element.81), channel_id=1, source_target_pairs={{1,0},{2,1},{3,2},{4,3},{5,4},{6,5},{7,6},{0,7},{9,8},{10,9},{11,1... | collective-permute-start | bytes 294920 | tf_op jit(solution)/shard_map/ppermute | solution.py:288
  214.3 7.0 %collective-permute-start.21 = (f32[1,12,8,128]{3,2,1,0:T(8,128)}, f32[1,12,8,128]{3,2,1,0:T(8,128)S(1)}, u32[]{:S(2)}, u32[]{:S(2)}) collective-permute-start(f32[1,12,8,128]{3,2,1,0:T(8,128)} %get-tuple-element.87), channel_id=1, source_target_pairs={{0,1},{1,2},{2,3},{3,4},{4,5},{5,6},{6,7},{7,0},{8,9},{9,10},{10,1... | collective-permute-start | bytes 147464 | tf_op jit(solution)/shard_map/ppermute | solution.py:289
  215.8 5.5 %collective-permute-start.22 = (f32[1,12,8,128]{3,2,1,0:T(8,128)}, f32[1,12,8,128]{3,2,1,0:T(8,128)S(1)}, u32[]{:S(2)}, u32[]{:S(2)}) collective-permute-start(f32[1,12,8,128]{3,2,1,0:T(8,128)} %get-tuple-element.88), channel_id=1, source_target_pairs={{1,0},{2,1},{3,2},{4,3},{5,4},{6,5},{7,6},{0,7},{9,8},{10,9},{11,1... | collective-permute-start | bytes 147464 | tf_op jit(solution)/shard_map/ppermute | solution.py:288
  225.5 7.0 %collective-permute-start.23 = (f32[1,12,8,128]{3,2,1,0:T(8,128)}, f32[1,12,8,128]{3,2,1,0:T(8,128)S(1)}, u32[]{:S(2)}, u32[]{:S(2)}) collective-permute-start(f32[1,12,8,128]{3,2,1,0:T(8,128)} %get-tuple-element.90), channel_id=1, source_target_pairs={{0,1},{1,2},{2,3},{3,4},{4,5},{5,6},{6,7},{7,0},{8,9},{9,10},{10,1... | collective-permute-start | bytes 147464 | tf_op jit(solution)/shard_map/ppermute | solution.py:289
  226.6 5.9 %collective-permute-start.24 = (f32[1,12,8,128]{3,2,1,0:T(8,128)}, f32[1,12,8,128]{3,2,1,0:T(8,128)S(1)}, u32[]{:S(2)}, u32[]{:S(2)}) collective-permute-start(f32[1,12,8,128]{3,2,1,0:T(8,128)} %get-tuple-element.91), channel_id=1, source_target_pairs={{1,0},{2,1},{3,2},{4,3},{5,4},{6,5},{7,6},{0,7},{9,8},{10,9},{11,1... | collective-permute-start | bytes 147464 | tf_op jit(solution)/shard_map/ppermute | solution.py:288
  236.6 7.0 %collective-permute-start.25 = (f32[1,12,8,128]{3,2,1,0:T(8,128)}, f32[1,12,8,128]{3,2,1,0:T(8,128)S(1)}, u32[]{:S(2)}, u32[]{:S(2)}) collective-permute-start(f32[1,12,8,128]{3,2,1,0:T(8,128)} %get-tuple-element.93), channel_id=1, source_target_pairs={{0,1},{1,2},{2,3},{3,4},{4,5},{5,6},{6,7},{7,0},{8,9},{9,10},{10,1... | collective-permute-start | bytes 147464 | tf_op jit(solution)/shard_map/ppermute | solution.py:289
  236.8 6.9 %collective-permute-start.26 = (f32[1,12,8,128]{3,2,1,0:T(8,128)}, f32[1,12,8,128]{3,2,1,0:T(8,128)S(1)}, u32[]{:S(2)}, u32[]{:S(2)}) collective-permute-start(f32[1,12,8,128]{3,2,1,0:T(8,128)} %get-tuple-element.94), channel_id=1, source_target_pairs={{1,0},{2,1},{3,2},{4,3},{5,4},{6,5},{7,6},{0,7},{9,8},{10,9},{11,1... | collective-permute-start | bytes 147464 | tf_op jit(solution)/shard_map/ppermute | solution.py:288
  (29 other events, 43.9 us)
Sparse Core Ops, SparseCore 0:
  74.3 18.4 all-gather.4
  190.7 21.4 all-gather.6

commit v15 on v10

--- a/solution.py
+++ b/solution.py
@@ -192,7 +192,7 @@
             out_ref[b, second] = out_ref[b, second] - progress
             return carry
 
-        lax.fori_loop(0, rx_ref.shape[0], reaction_body, 0)
+        lax.fori_loop(0, rx_ref.shape[0], reaction_body, 0, unroll=3)
 
 
 def vmem():

time: 259 us -> 256 us (0.988)
  Pallas kernels: 94.4 us -> 90.9 us
    pallas_call x19, Pallas kernels: 94.4 us -> 90.9 us  [call(): pl.pallas_call(kernel, out_shape=outs, in_specs=[blocks[i] if blocks is n...]
where the time goes in v15:
time: 256 us; the launch traced here: 255 us
  Pallas kernels  90.9 us (36%)
  waiting for transfers between devices  69.6 us (27%)
  starting transfers between devices  62.1 us (24%)
  local copies, waits for them, and re-layouts  15.4 us (6%)
  between operations  14.3 us (6%)
  other arithmetic  2.56 us (1%)
    pallas_call x19, Pallas kernels, call(): pl.pallas_call(kernel, out_shape=outs, in_specs=[blocks[i] if blocks is n...  90.9 us
    ppermute x13, starting transfers between devices, swap(): lax.ppermute(head, 'space', [((i + 1) % space_n, i) for i in range(space_...  54 us
    ppermute x13, waiting for transfers between devices, swap(): lax.ppermute(tail, 'space', [(i, (i + 1) % space_n) for i in range(space_...  33.6 us
    all_gather x2, waiting for transfers between devices, per_device(): rint_all = lax.all_gather(rint[None], 'tm')  26.3 us
    ppermute x13, waiting for transfers between devices, swap(): lax.ppermute(head, 'space', [((i + 1) % space_n, i) for i in range(space_...  9.64 us
    unnamed x65, local copies, waits for them, and re-layouts  9.35 us
    ppermute x13, starting transfers between devices, swap(): lax.ppermute(tail, 'space', [(i, (i + 1) % space_n) for i in range(space_...  6.53 us
  transfers between devices with their start and end apart: 29, of which 17 were waited for; matrix products, arithmetic and copies ran while one was open for 2% of the time, Pallas kernels for 10%

profile of v15, /device:TPU:0, one launch (start us, length us, event | category | flops | bytes accessed | tf_op | source)
XLA Modules:
  0.0 255.4 jit_solution(6918601142351225210)
XLA Ops:
  11.9 6.0 %collective-permute-start.1 = (f32[3,12,16,128]{3,2,1,0:T(8,128)}, f32[3,12,16,128]{3,2,1,0:T(8,128)S(1)}, u32[]{:S(2)}, u32[]{:S(2)}) collective-permute-start(f32[3,12,16,128]{3,2,1,0:T(8,128)} %get-tuple-element.98), channel_id=1, source_target_pairs={{1,0},{2,1},{3,2},{4,3},{5,4},{6,5},{7,6},{0,7},{9,8},{10,9},{11,1... | collective-permute-start | bytes 884744 | tf_op jit(solution)/shard_map/ppermute | solution.py:289
  21.4 4.2 %collective-permute-done.1.n_ref = f32[3,12,16,128]{3,2,1,0:T(8,128)S(1)} collective-permute-done((f32[3,12,16,128]{3,2,1,0:T(8,128)}, f32[3,12,16,128]{3,2,1,0:T(8,128)S(1)}, u32[]{:S(2)}, u32[]{:S(2)}) %collective-permute-start.1) | collective-permute-done | bytes 294944 | tf_op jit(solution)/shard_map/ppermute | solution.py:289
  25.6 4.9 %collective-permute-done.p_ref = f32[3,12,16,128]{3,2,1,0:T(8,128)} collective-permute-done((f32[3,12,16,128]{3,2,1,0:T(8,128)}, f32[3,12,16,128]{3,2,1,0:T(8,128)}, u32[]{:S(2)}, u32[]{:S(2)}) %collective-permute-start) | collective-permute-done | bytes 294944 | tf_op jit(solution)/shard_map/ppermute | solution.py:288
  30.5 9.9 %shard_map.131 = (f32[3,12,128,128]{3,2,1,0:T(8,128)}, f32[1,12,128,128]{3,2,1,0:T(8,128)}, f32[1,12,16,128]{3,2,1,0:T(8,128)}, f32[1,12,16,128]{3,2,1,0:T(8,128)}) custom-call(f32[3,12,128,128]{3,2,1,0:T(8,128)} %pad_maximum_fusion.u_ref, f32[3,12,16,128]{3,2,1,0:T(8,128)} %collective-permute-done.p_ref, f32[3,12,16,128]{3,2,1,0:T(8,128)} %copy-done.4, ...), custom_call_target="tpu_custom_call" | custom-call | flops 1822556160 | bytes 6488916 | tf_op jit(solution)/shard_map/pallas_call | solution.py:217
  49.7 5.7 %shard_map.132 = (f32[1,12,128,128]{3,2,1,0:T(8,128)}, f32[1,12,128,128]{3,2,1,0:T(8,128)}, f32[1,12,16,128]{3,2,1,0:T(8,128)}, f32[1,12,16,128]{3,2,1,0:T(8,128)}) custom-call(f32[1,12,128,128]{3,2,1,0:T(8,128)} %get-tuple-element.50.a1_ref.refs_0_, f32[1,12,16,128]{3,2,1,0:T(8,128)} %copy-done.8, f32[1,12,16,128]{3,2,1,0:T(8,128)} %copy-done.10, ...), custom_call_target="tpu_custom_call" | custom-call | flops 607518720 | bytes 5309268 | tf_op jit(solution)/shard_map/pallas_call | solution.py:217
  55.7 4.4 %collective-permute-start.5 = (f32[1,12,16,128]{3,2,1,0:T(8,128)}, f32[1,12,16,128]{3,2,1,0:T(8,128)S(1)}, u32[]{:S(2)}, u32[]{:S(2)}) collective-permute-start(f32[1,12,16,128]{3,2,1,0:T(8,128)} %get-tuple-element.57), channel_id=1, source_target_pairs={{1,0},{2,1},{3,2},{4,3},{5,4},{6,5},{7,6},{0,7},{9,8},{10,9},{11,1... | collective-permute-start | bytes 294920 | tf_op jit(solution)/shard_map/ppermute | solution.py:289
  61.4 4.6 %shard_map.133 = (f32[1,12,64,128]{3,2,1,0:T(8,128)}, f32[1,12,64,128]{3,2,1,0:T(8,128)}) custom-call(f32[3,12,128,128]{3,2,1,0:T(8,128)} %pad_maximum_fusion.u_ref, f32[3,12,16,128]{3,2,1,0:T(8,128)} %collective-permute-done.p_ref, f32[3,12,16,128]{3,2,1,0:T(8,128)} %copy-done.4, f32[64,128]{1,0:T(8,128)} %constant.28.clone.r_ref.refs_11_, ...), custom_call_target="tpu_custom_call" | custom-call | flops 228261888 | bytes 3867988 | tf_op jit(solution)/shard_map/pallas_call | solution.py:217
  66.6 6.4 %shard_map.134 = (f32[12,64,128]{2,1,0:T(8,128)}, f32[12,64,128]{2,1,0:T(8,128)}) custom-call(f32[1,12,128,128]{3,2,1,0:T(8,128)} %get-tuple-element.54.a2_ref.refs_1_, f32[1,12,16,128]{3,2,1,0:T(8,128)} %copy-done.11, f32[1,12,16,128]{3,2,1,0:T(8,128)} %copy-done.12, f32[256,128]{1,0:T(8,128)} %constant.26.clone.l_ref, f32[128,128]{1,0:T(8,128)} %constant.25.clone.x_ref, ...), custom_call_target="tpu_custom_call" | custom-call | flops 607518720 | bytes 5538644 | tf_op jit(solution)/shard_map/pallas_call | solution.py:217
  79.3 4.4 %collective-permute-done.6 = f32[12,8,128]{2,1,0:T(8,128)S(1)} collective-permute-done((f32[12,8,128]{2,1,0:T(8,128)S(1)}, f32[12,8,128]{2,1,0:T(8,128)S(1)}, u32[]{:S(2)}, u32[]{:S(2)}) %collective-permute-start.6) | collective-permute-done | bytes 49184 | tf_op jit(solution)/shard_map/ppermute | solution.py:288
  87.4 4.5 %all-gather.5.cloned.1.call-done = f32[48,64,128]{2,1,0:T(8,128)} async-done(((f32[12,64,128]{2,1,0:T(8,128)}), f32[48,64,128]{2,1,0:T(8,128)}) %all-gather.5.cloned.1.call-update) | async-done | bytes 1572880 | tf_op jit(solution)/shard_map/all_gather | solution.py:523
  94.7 4.0 %collective-permute-start.9 = (f32[1,12,8,128]{3,2,1,0:T(8,128)}, f32[1,12,8,128]{3,2,1,0:T(8,128)S(1)}, u32[]{:S(2)}, u32[]{:S(2)}) collective-permute-start(f32[1,12,8,128]{3,2,1,0:T(8,128)} %get-tuple-element.64), channel_id=1, source_target_pairs={{1,0},{2,1},{3,2},{4,3},{5,4},{6,5},{7,6},{0,7},{9,8},{10,9},{11,1... | collective-permute-start | bytes 147464 | tf_op jit(solution)/shard_map/ppermute | solution.py:289
  101.6 3.4 %shard_map.137 = (f32[1,12,64,128]{3,2,1,0:T(8,128)}, f32[1,12,8,128]{3,2,1,0:T(8,128)}, f32[1,12,8,128]{3,2,1,0:T(8,128)}) custom-call(f32[1,12,64,128]{3,2,1,0:T(8,128)} %get-tuple-element.62.w_ref.refs_5_, f32[1,12,8,128]{3,2,1,0:T(8,128)} %copy-done.20, f32[1,12,8,128]{3,2,1,0:T(8,128)} %copy-done.25, f32[128,64]{1,0:T(8,128)} %constant.27.clone.l_ref, ...), custom_call_target="tpu_custom_call" | custom-call | flops 228261888 | bytes 2655060 | tf_op jit(solution)/shard_map/pallas_call | solution.py:217
  105.4 4.4 %collective-permute-start.11 = (f32[1,12,8,128]{3,2,1,0:T(8,128)}, f32[1,12,8,128]{3,2,1,0:T(8,128)S(1)}, u32[]{:S(2)}, u32[]{:S(2)}) collective-permute-start(f32[1,12,8,128]{3,2,1,0:T(8,128)} %get-tuple-element.67), channel_id=1, source_target_pairs={{1,0},{2,1},{3,2},{4,3},{5,4},{6,5},{7,6},{0,7},{9,8},{10,9},{11,1... | collective-permute-start | bytes 147464 | tf_op jit(solution)/shard_map/ppermute | solution.py:289
  112.6 3.4 %shard_map.138 = (f32[1,12,64,128]{3,2,1,0:T(8,128)}, f32[1,12,8,128]{3,2,1,0:T(8,128)}, f32[1,12,8,128]{3,2,1,0:T(8,128)}) custom-call(f32[1,12,64,128]{3,2,1,0:T(8,128)} %get-tuple-element.65.w_ref.refs_6_, f32[1,12,8,128]{3,2,1,0:T(8,128)} %copy-done.21, f32[1,12,8,128]{3,2,1,0:T(8,128)} %copy-done.26, f32[128,64]{1,0:T(8,128)} %constant.27.clone.l_ref, ...), custom_call_target="tpu_custom_call" | custom-call | flops 228261888 | bytes 2655060 | tf_op jit(solution)/shard_map/pallas_call | solution.py:217
  116.0 4.8 %collective-permute-start.13 = (f32[1,12,8,128]{3,2,1,0:T(8,128)}, f32[1,12,8,128]{3,2,1,0:T(8,128)S(1)}, u32[]{:S(2)}, u32[]{:S(2)}) collective-permute-start(f32[1,12,8,128]{3,2,1,0:T(8,128)} %get-tuple-element.70), channel_id=1, source_target_pairs={{1,0},{2,1},{3,2},{4,3},{5,4},{6,5},{7,6},{0,7},{9,8},{10,9},{11,1... | collective-permute-start | bytes 147464 | tf_op jit(solution)/shard_map/ppermute | solution.py:289
  123.7 3.4 %shard_map.139 = (f32[1,12,64,128]{3,2,1,0:T(8,128)}, f32[1,12,8,128]{3,2,1,0:T(8,128)}, f32[1,12,8,128]{3,2,1,0:T(8,128)}) custom-call(f32[1,12,64,128]{3,2,1,0:T(8,128)} %get-tuple-element.68.w_ref.refs_7_, f32[1,12,8,128]{3,2,1,0:T(8,128)} %copy-done.18, f32[1,12,8,128]{3,2,1,0:T(8,128)} %copy-done.22, f32[128,64]{1,0:T(8,128)} %constant.27.clone.l_ref, ...), custom_call_target="tpu_custom_call" | custom-call | flops 228261888 | bytes 2655060 | tf_op jit(solution)/shard_map/pallas_call | solution.py:217
  128.0 6.7 %shard_map.140 = (f32[3,12,128,128]{3,2,1,0:T(8,128)}, f32[3,12,16,128]{3,2,1,0:T(8,128)}, f32[3,12,16,128]{3,2,1,0:T(8,128)}) custom-call(f32[1,12,128,128]{3,2,1,0:T(8,128)} %get-tuple-element.50.a1_ref.refs_0_, f32[1,12,128,128]{3,2,1,0:T(8,128)} %get-tuple-element.54.a2_ref.refs_1_, f32[1,12,64,128]{3,2,1,0:T(8,128)} %get-tuple-element.55.refs_2_, ...), custom_call_target="tpu_custom_call" | custom-call | flops 603979776 | bytes 8912904 | tf_op jit(solution)/shard_map/pallas_call | solution.py:217
  134.7 5.0 %collective-permute-start.16 = (f32[3,12,16,128]{3,2,1,0:T(8,128)}, f32[3,12,16,128]{3,2,1,0:T(8,128)S(1)}, u32[]{:S(2)}, u32[]{:S(2)}) collective-permute-start(f32[3,12,16,128]{3,2,1,0:T(8,128)} %get-tuple-element.74), channel_id=1, source_target_pairs={{1,0},{2,1},{3,2},{4,3},{5,4},{6,5},{7,6},{0,7},{9,8},{10,9},{11,1... | collective-permute-start | bytes 884744 | tf_op jit(solution)/shard_map/ppermute | solution.py:289
  139.6 5.1 %collective-permute-done.15.p_ref = f32[3,12,16,128]{3,2,1,0:T(8,128)S(1)} collective-permute-done((f32[3,12,16,128]{3,2,1,0:T(8,128)}, f32[3,12,16,128]{3,2,1,0:T(8,128)S(1)}, u32[]{:S(2)}, u32[]{:S(2)}) %collective-permute-start.15) | collective-permute-done | bytes 294944 | tf_op jit(solution)/shard_map/ppermute | solution.py:288
  147.8 9.9 %shard_map.141 = (f32[3,12,128,128]{3,2,1,0:T(8,128)}, f32[1,12,128,128]{3,2,1,0:T(8,128)}, f32[1,12,16,128]{3,2,1,0:T(8,128)}, f32[1,12,16,128]{3,2,1,0:T(8,128)}) custom-call(f32[3,12,128,128]{3,2,1,0:T(8,128)} %get-tuple-element.72.u_ref, f32[3,12,16,128]{3,2,1,0:T(8,128)} %copy-done.5, f32[3,12,16,128]{3,2,1,0:T(8,128)} %copy-done.6, ...), custom_call_target="tpu_custom_call" | custom-call | flops 1822556160 | bytes 6488916 | tf_op jit(solution)/shard_map/pallas_call | solution.py:217
  157.9 4.5 %collective-permute-start.18 = (f32[1,12,16,128]{3,2,1,0:T(8,128)}, f32[1,12,16,128]{3,2,1,0:T(8,128)S(1)}, u32[]{:S(2)}, u32[]{:S(2)}) collective-permute-start(f32[1,12,16,128]{3,2,1,0:T(8,128)} %get-tuple-element.77), channel_id=1, source_target_pairs={{1,0},{2,1},{3,2},{4,3},{5,4},{6,5},{7,6},{0,7},{9,8},{10,9},{11,1... | collective-permute-start | bytes 294920 | tf_op jit(solution)/shard_map/ppermute | solution.py:289
  165.9 5.8 %shard_map.142 = (f32[1,12,128,128]{3,2,1,0:T(8,128)}, f32[1,12,128,128]{3,2,1,0:T(8,128)}, f32[1,12,16,128]{3,2,1,0:T(8,128)}, f32[1,12,16,128]{3,2,1,0:T(8,128)}) custom-call(f32[1,12,128,128]{3,2,1,0:T(8,128)} %get-tuple-element.75.a1_ref, f32[1,12,16,128]{3,2,1,0:T(8,128)} %copy-done.7, f32[1,12,16,128]{3,2,1,0:T(8,128)} %copy-done.9, ...), custom_call_target="tpu_custom_call" | custom-call | flops 607518720 | bytes 5309268 | tf_op jit(solution)/shard_map/pallas_call | solution.py:217
  171.7 4.7 %collective-permute-start.20 = (f32[1,12,16,128]{3,2,1,0:T(8,128)}, f32[1,12,16,128]{3,2,1,0:T(8,128)S(1)}, u32[]{:S(2)}, u32[]{:S(2)}) collective-permute-start(f32[1,12,16,128]{3,2,1,0:T(8,128)} %get-tuple-element.81), channel_id=1, source_target_pairs={{1,0},{2,1},{3,2},{4,3},{5,4},{6,5},{7,6},{0,7},{9,8},{10,9},{11,1... | collective-permute-start | bytes 294920 | tf_op jit(solution)/shard_map/ppermute | solution.py:289
  176.4 4.6 %shard_map.143 = (f32[1,12,64,128]{3,2,1,0:T(8,128)}, f32[1,12,64,128]{3,2,1,0:T(8,128)}) custom-call(f32[3,12,128,128]{3,2,1,0:T(8,128)} %get-tuple-element.72.u_ref, f32[3,12,16,128]{3,2,1,0:T(8,128)} %copy-done.5, f32[3,12,16,128]{3,2,1,0:T(8,128)} %copy-done.6, f32[64,128]{1,0:T(8,128)} %constant.28.clone.r_ref.refs_11_, f32[8,16]{1,0:T(8,128)} %constant.30.clone.rp_ref, ...), custom_call_target="tpu_custom_call" | custom-call | flops 228261888 | bytes 3867988 | tf_op jit(solution)/shard_map/pallas_call | solution.py:217
  181.7 6.4 %shard_map.144 = (f32[12,64,128]{2,1,0:T(8,128)}, f32[12,64,128]{2,1,0:T(8,128)}) custom-call(f32[1,12,128,128]{3,2,1,0:T(8,128)} %get-tuple-element.79.a2_ref.refs_0_, f32[1,12,16,128]{3,2,1,0:T(8,128)} %copy-done.13, f32[1,12,16,128]{3,2,1,0:T(8,128)} %copy-done.14, f32[256,128]{1,0:T(8,128)} %constant.26.clone.l_ref, f32[128,128]{1,0:T(8,128)} %constant.25.clone.x_ref, ...), custom_call_target="tpu_custom_call" | custom-call | flops 607518720 | bytes 5538644 | tf_op jit(solution)/shard_map/pallas_call | solution.py:217
  188.1 21.8 %all-gather.7.cloned.1.call-done = f32[48,64,128]{2,1,0:T(8,128)} async-done(((f32[12,64,128]{2,1,0:T(8,128)}), f32[48,64,128]{2,1,0:T(8,128)}) %all-gather.7.cloned.1.call-update) | async-done | bytes 1572880 | tf_op jit(solution)/shard_map/all_gather | solution.py:523
  219.6 3.4 %shard_map.146 = (f32[1,12,64,128]{3,2,1,0:T(8,128)}, f32[1,12,8,128]{3,2,1,0:T(8,128)}, f32[1,12,8,128]{3,2,1,0:T(8,128)}) custom-call(f32[1,12,64,128]{3,2,1,0:T(8,128)} %get-tuple-element.86.w_ref.refs_3_, f32[1,12,8,128]{3,2,1,0:T(8,128)} %copy-done.23, f32[1,12,8,128]{3,2,1,0:T(8,128)} %copy-done.27, f32[128,64]{1,0:T(8,128)} %constant.27.clone.l_ref, ...), custom_call_target="tpu_custom_call" | custom-call | flops 228261888 | bytes 2655060 | tf_op jit(solution)/shard_map/pallas_call | solution.py:217
  224.1 3.6 %collective-permute-start.24 = (f32[1,12,8,128]{3,2,1,0:T(8,128)}, f32[1,12,8,128]{3,2,1,0:T(8,128)S(1)}, u32[]{:S(2)}, u32[]{:S(2)}) collective-permute-start(f32[1,12,8,128]{3,2,1,0:T(8,128)} %get-tuple-element.91), channel_id=1, source_target_pairs={{1,0},{2,1},{3,2},{4,3},{5,4},{6,5},{7,6},{0,7},{9,8},{10,9},{11,1... | collective-permute-start | bytes 147464 | tf_op jit(solution)/shard_map/ppermute | solution.py:289
  230.6 3.4 %shard_map.147 = (f32[1,12,64,128]{3,2,1,0:T(8,128)}, f32[1,12,8,128]{3,2,1,0:T(8,128)}, f32[1,12,8,128]{3,2,1,0:T(8,128)}) custom-call(f32[1,12,64,128]{3,2,1,0:T(8,128)} %get-tuple-element.89.w_ref.refs_4_, f32[1,12,8,128]{3,2,1,0:T(8,128)} %copy-done.24, f32[1,12,8,128]{3,2,1,0:T(8,128)} %copy-done.28, f32[128,64]{1,0:T(8,128)} %constant.27.clone.l_ref, ...), custom_call_target="tpu_custom_call" | custom-call | flops 228261888 | bytes 2655060 | tf_op jit(solution)/shard_map/pallas_call | solution.py:217
  234.1 4.6 %collective-permute-start.26 = (f32[1,12,8,128]{3,2,1,0:T(8,128)}, f32[1,12,8,128]{3,2,1,0:T(8,128)S(1)}, u32[]{:S(2)}, u32[]{:S(2)}) collective-permute-start(f32[1,12,8,128]{3,2,1,0:T(8,128)} %get-tuple-element.94), channel_id=1, source_target_pairs={{1,0},{2,1},{3,2},{4,3},{5,4},{6,5},{7,6},{0,7},{9,8},{10,9},{11,1... | collective-permute-start | bytes 147464 | tf_op jit(solution)/shard_map/ppermute | solution.py:289
  241.6 3.4 %shard_map.148 = (f32[1,12,64,128]{3,2,1,0:T(8,128)}, f32[1,12,8,128]{3,2,1,0:T(8,128)}, f32[1,12,8,128]{3,2,1,0:T(8,128)}) custom-call(f32[1,12,64,128]{3,2,1,0:T(8,128)} %get-tuple-element.92.w_ref.refs_5_, f32[1,12,8,128]{3,2,1,0:T(8,128)} %copy-done.17, f32[1,12,8,128]{3,2,1,0:T(8,128)} %copy-done.19, f32[128,64]{1,0:T(8,128)} %constant.27.clone.l_ref, ...), custom_call_target="tpu_custom_call" | custom-call | flops 228261888 | bytes 2655060 | tf_op jit(solution)/shard_map/pallas_call | solution.py:217
  245.0 3.5 %shard_map.149 = (f32[1,12,128,128]{3,2,1,0:T(8,128)}, f32[1,12,64,128]{3,2,1,0:T(8,128)}) custom-call(f32[1,12,128,128]{3,2,1,0:T(8,128)} %get-tuple-element.79.a2_ref.refs_0_, f32[12,64,128]{2,1,0:T(8,128)} %get-tuple-element.84.refs_1_, f32[1,12,64,128]{3,2,1,0:T(8,128)} %bitcast.35, f32[1,12,64,128]{3,2,1,0:T(8,128)} %get-tuple-element.86.w_ref.refs_3_, ...), custom_call_target="tpu_custom_call" | custom-call | flops 150994944 | bytes 4358148 | tf_op jit(solution)/shard_map/pallas_call | solution.py:217
  (123 shorter events, 66.4 us)
Async XLA Ops:
  7.2 84.8 %all-gather.5.cloned.1.call-start = ((), (), s32[]{:S(2)}) async-start(), calls=%async_computation | async-start | bytes 1966080 | tf_op jit(solution)/shard_map/all_gather | solution.py:523
  10.9 7.0 %copy-start.31 = (f32[3,12]{1,0:T(4,128)S(1)}, f32[3,12]{1,0:T(4,128)}, u32[]{:S(2)}) copy-start(f32[3,12]{1,0:T(4,128)} %param.14) | copy-start | bytes 436
  11.9 13.7 %collective-permute-start.1 = (f32[3,12,16,128]{3,2,1,0:T(8,128)}, f32[3,12,16,128]{3,2,1,0:T(8,128)S(1)}, u32[]{:S(2)}, u32[]{:S(2)}) collective-permute-start(f32[3,12,16,128]{3,2,1,0:T(8,128)} %get-tuple-element.98), channel_id=1, source_target_pairs={{1,0},{2,1},{3,2},{4,3},{5,4},{6,5},{7,6},{0,7},{9,8},{10,9},{11,1... | collective-permute-start | bytes 884744 | tf_op jit(solution)/shard_map/ppermute | solution.py:289
  17.9 12.6 %collective-permute-start = (f32[3,12,16,128]{3,2,1,0:T(8,128)}, f32[3,12,16,128]{3,2,1,0:T(8,128)}, u32[]{:S(2)}, u32[]{:S(2)}) collective-permute-start(f32[3,12,16,128]{3,2,1,0:T(8,128)} %get-tuple-element.99), channel_id=1, source_target_pairs={{0,1},{1,2},{2,3},{3,4},{4,5},{5,6},{6,7},{7,0},{8,9},{9,10},{10,1... | collective-permute-start | bytes 884744 | tf_op jit(solution)/shard_map/ppermute | solution.py:288
  40.4 7.6 %collective-permute-start.2 = (f32[1,12,16,128]{3,2,1,0:T(8,128)}, f32[1,12,16,128]{3,2,1,0:T(8,128)S(1)}, u32[]{:S(2)}, u32[]{:S(2)}) collective-permute-start(f32[1,12,16,128]{3,2,1,0:T(8,128)} %get-tuple-element.51), channel_id=1, source_target_pairs={{0,1},{1,2},{2,3},{3,4},{4,5},{5,6},{6,7},{7,0},{8,9},{9,10},{10,1... | collective-permute-start | bytes 294920 | tf_op jit(solution)/shard_map/ppermute | solution.py:288
  42.2 6.9 %collective-permute-start.3 = (f32[1,12,16,128]{3,2,1,0:T(8,128)}, f32[1,12,16,128]{3,2,1,0:T(8,128)S(1)}, u32[]{:S(2)}, u32[]{:S(2)}) collective-permute-start(f32[1,12,16,128]{3,2,1,0:T(8,128)} %get-tuple-element.52), channel_id=1, source_target_pairs={{1,0},{2,1},{3,2},{4,3},{5,4},{6,5},{7,6},{0,7},{9,8},{10,9},{11,1... | collective-permute-start | bytes 294920 | tf_op jit(solution)/shard_map/ppermute | solution.py:289
  55.4 10.5 %collective-permute-start.4 = (f32[1,12,16,128]{3,2,1,0:T(8,128)}, f32[1,12,16,128]{3,2,1,0:T(8,128)S(1)}, u32[]{:S(2)}, u32[]{:S(2)}) collective-permute-start(f32[1,12,16,128]{3,2,1,0:T(8,128)} %get-tuple-element.56), channel_id=1, source_target_pairs={{0,1},{1,2},{2,3},{3,4},{4,5},{5,6},{6,7},{7,0},{8,9},{9,10},{10,1... | collective-permute-start | bytes 294920 | tf_op jit(solution)/shard_map/ppermute | solution.py:288
  55.7 10.2 %collective-permute-start.5 = (f32[1,12,16,128]{3,2,1,0:T(8,128)}, f32[1,12,16,128]{3,2,1,0:T(8,128)S(1)}, u32[]{:S(2)}, u32[]{:S(2)}) collective-permute-start(f32[1,12,16,128]{3,2,1,0:T(8,128)} %get-tuple-element.57), channel_id=1, source_target_pairs={{1,0},{2,1},{3,2},{4,3},{5,4},{6,5},{7,6},{0,7},{9,8},{10,9},{11,1... | collective-permute-start | bytes 294920 | tf_op jit(solution)/shard_map/ppermute | solution.py:289
  66.6 8.0 %copy-start.29 = (f32[8,16,1,1]{1,0,3,2:T(8,128)S(1)}, f32[8,16,1,1]{1,0,3,2:T(8,128)}, u32[]{:S(2)}) copy-start(f32[8,16,1,1]{1,0,3,2:T(8,128)} %constant.32) | copy-start | bytes 1540
  73.1 136.8 %all-gather.7.cloned.1.call-start = ((), (), s32[]{:S(2)}) async-start(), calls=%async_computation.1 | async-start | bytes 1966080 | tf_op jit(solution)/shard_map/all_gather | solution.py:523
  73.1 53.9 %collective-permute-start.14 = (f32[1,12,128,128]{3,2,1,0:T(8,128)S(1)}, f32[1,12,128,128]{3,2,1,0:T(8,128)S(1)}, u32[]{:S(2)}, u32[]{:S(2)}) collective-permute-start(f32[1,12,128,128]{3,2,1,0:T(8,128)S(1)} %copy-done.2), channel_id=1, source_target_pairs={{0,8},{8,16},{16,24},{1,9},{9,17},{17,25},{2,10},{10,18},{18,26},{... | collective-permute-start | bytes 2359304 | tf_op jit(solution)/shard_map/ppermute | solution.py:526
  75.2 8.6 %copy-start = (f32[8,12,8,128]{3,0,2,1:T(8,128)}, f32[8,12,8,128]{3,0,2,1:T(8,128)S(1)}, u32[]{:S(2)}) copy-start(f32[8,12,8,128]{3,0,2,1:T(8,128)S(1)} %fusion.3) | copy-start | bytes 1179652
  75.2 4.1 %collective-permute-start.7 = (f32[12,8,128]{2,1,0:T(8,128)S(1)}, f32[12,8,128]{2,1,0:T(8,128)S(1)}, u32[]{:S(2)}, u32[]{:S(2)}) collective-permute-start(f32[12,8,128]{2,1,0:T(8,128)S(1)} %get-tuple-element.100), channel_id=1, source_target_pairs={{1,0},{2,1},{3,2},{4,3},{5,4},{6,5},{7,6},{0,7},{9,8},{10,9},{11,1... | collective-permute-start | bytes 147464 | tf_op jit(solution)/shard_map/ppermute | solution.py:289
  76.9 6.8 %collective-permute-start.6 = (f32[12,8,128]{2,1,0:T(8,128)S(1)}, f32[12,8,128]{2,1,0:T(8,128)S(1)}, u32[]{:S(2)}, u32[]{:S(2)}) collective-permute-start(f32[12,8,128]{2,1,0:T(8,128)S(1)} %get-tuple-element.101), channel_id=1, source_target_pairs={{0,1},{1,2},{2,3},{3,4},{4,5},{5,6},{6,7},{7,0},{8,9},{9,10},{10,1... | collective-permute-start | bytes 147464 | tf_op jit(solution)/shard_map/ppermute | solution.py:288
  94.0 7.0 %collective-permute-start.8 = (f32[1,12,8,128]{3,2,1,0:T(8,128)}, f32[1,12,8,128]{3,2,1,0:T(8,128)S(1)}, u32[]{:S(2)}, u32[]{:S(2)}) collective-permute-start(f32[1,12,8,128]{3,2,1,0:T(8,128)} %get-tuple-element.63), channel_id=1, source_target_pairs={{0,1},{1,2},{2,3},{3,4},{4,5},{5,6},{6,7},{7,0},{8,9},{9,10},{10,1... | collective-permute-start | bytes 147464 | tf_op jit(solution)/shard_map/ppermute | solution.py:288
  94.7 6.3 %collective-permute-start.9 = (f32[1,12,8,128]{3,2,1,0:T(8,128)}, f32[1,12,8,128]{3,2,1,0:T(8,128)S(1)}, u32[]{:S(2)}, u32[]{:S(2)}) collective-permute-start(f32[1,12,8,128]{3,2,1,0:T(8,128)} %get-tuple-element.64), channel_id=1, source_target_pairs={{1,0},{2,1},{3,2},{4,3},{5,4},{6,5},{7,6},{0,7},{9,8},{10,9},{11,1... | collective-permute-start | bytes 147464 | tf_op jit(solution)/shard_map/ppermute | solution.py:289
  105.0 7.0 %collective-permute-start.10 = (f32[1,12,8,128]{3,2,1,0:T(8,128)}, f32[1,12,8,128]{3,2,1,0:T(8,128)S(1)}, u32[]{:S(2)}, u32[]{:S(2)}) collective-permute-start(f32[1,12,8,128]{3,2,1,0:T(8,128)} %get-tuple-element.66), channel_id=1, source_target_pairs={{0,1},{1,2},{2,3},{3,4},{4,5},{5,6},{6,7},{7,0},{8,9},{9,10},{10,1... | collective-permute-start | bytes 147464 | tf_op jit(solution)/shard_map/ppermute | solution.py:288
  105.4 6.6 %collective-permute-start.11 = (f32[1,12,8,128]{3,2,1,0:T(8,128)}, f32[1,12,8,128]{3,2,1,0:T(8,128)S(1)}, u32[]{:S(2)}, u32[]{:S(2)}) collective-permute-start(f32[1,12,8,128]{3,2,1,0:T(8,128)} %get-tuple-element.67), channel_id=1, source_target_pairs={{1,0},{2,1},{3,2},{4,3},{5,4},{6,5},{7,6},{0,7},{9,8},{10,9},{11,1... | collective-permute-start | bytes 147464 | tf_op jit(solution)/shard_map/ppermute | solution.py:289
  116.0 7.0 %collective-permute-start.12 = (f32[1,12,8,128]{3,2,1,0:T(8,128)}, f32[1,12,8,128]{3,2,1,0:T(8,128)S(1)}, u32[]{:S(2)}, u32[]{:S(2)}) collective-permute-start(f32[1,12,8,128]{3,2,1,0:T(8,128)} %get-tuple-element.69), channel_id=1, source_target_pairs={{0,1},{1,2},{2,3},{3,4},{4,5},{5,6},{6,7},{7,0},{8,9},{9,10},{10,1... | collective-permute-start | bytes 147464 | tf_op jit(solution)/shard_map/ppermute | solution.py:288
  116.0 7.0 %collective-permute-start.13 = (f32[1,12,8,128]{3,2,1,0:T(8,128)}, f32[1,12,8,128]{3,2,1,0:T(8,128)S(1)}, u32[]{:S(2)}, u32[]{:S(2)}) collective-permute-start(f32[1,12,8,128]{3,2,1,0:T(8,128)} %get-tuple-element.70), channel_id=1, source_target_pairs={{1,0},{2,1},{3,2},{4,3},{5,4},{6,5},{7,6},{0,7},{9,8},{10,9},{11,1... | collective-permute-start | bytes 147464 | tf_op jit(solution)/shard_map/ppermute | solution.py:289
  134.7 10.1 %collective-permute-start.15 = (f32[3,12,16,128]{3,2,1,0:T(8,128)}, f32[3,12,16,128]{3,2,1,0:T(8,128)S(1)}, u32[]{:S(2)}, u32[]{:S(2)}) collective-permute-start(f32[3,12,16,128]{3,2,1,0:T(8,128)} %get-tuple-element.73), channel_id=1, source_target_pairs={{0,1},{1,2},{2,3},{3,4},{4,5},{5,6},{6,7},{7,0},{8,9},{9,10},{10,1... | collective-permute-start | bytes 884744 | tf_op jit(solution)/shard_map/ppermute | solution.py:288
  134.7 12.4 %collective-permute-start.16 = (f32[3,12,16,128]{3,2,1,0:T(8,128)}, f32[3,12,16,128]{3,2,1,0:T(8,128)S(1)}, u32[]{:S(2)}, u32[]{:S(2)}) collective-permute-start(f32[3,12,16,128]{3,2,1,0:T(8,128)} %get-tuple-element.74), channel_id=1, source_target_pairs={{1,0},{2,1},{3,2},{4,3},{5,4},{6,5},{7,6},{0,7},{9,8},{10,9},{11,1... | collective-permute-start | bytes 884744 | tf_op jit(solution)/shard_map/ppermute | solution.py:289
  157.7 7.5 %collective-permute-start.17 = (f32[1,12,16,128]{3,2,1,0:T(8,128)}, f32[1,12,16,128]{3,2,1,0:T(8,128)S(1)}, u32[]{:S(2)}, u32[]{:S(2)}) collective-permute-start(f32[1,12,16,128]{3,2,1,0:T(8,128)} %get-tuple-element.76), channel_id=1, source_target_pairs={{0,1},{1,2},{2,3},{3,4},{4,5},{5,6},{6,7},{7,0},{8,9},{9,10},{10,1... | collective-permute-start | bytes 294920 | tf_op jit(solution)/shard_map/ppermute | solution.py:288
  157.9 7.3 %collective-permute-start.18 = (f32[1,12,16,128]{3,2,1,0:T(8,128)}, f32[1,12,16,128]{3,2,1,0:T(8,128)S(1)}, u32[]{:S(2)}, u32[]{:S(2)}) collective-permute-start(f32[1,12,16,128]{3,2,1,0:T(8,128)} %get-tuple-element.77), channel_id=1, source_target_pairs={{1,0},{2,1},{3,2},{4,3},{5,4},{6,5},{7,6},{0,7},{9,8},{10,9},{11,1... | collective-permute-start | bytes 294920 | tf_op jit(solution)/shard_map/ppermute | solution.py:289
  171.7 9.3 %collective-permute-start.19 = (f32[1,12,16,128]{3,2,1,0:T(8,128)}, f32[1,12,16,128]{3,2,1,0:T(8,128)S(1)}, u32[]{:S(2)}, u32[]{:S(2)}) collective-permute-start(f32[1,12,16,128]{3,2,1,0:T(8,128)} %get-tuple-element.80), channel_id=1, source_target_pairs={{0,1},{1,2},{2,3},{3,4},{4,5},{5,6},{6,7},{7,0},{8,9},{9,10},{10,1... | collective-permute-start | bytes 294920 | tf_op jit(solution)/shard_map/ppermute | solution.py:288
  171.7 9.3 %collective-permute-start.20 = (f32[1,12,16,128]{3,2,1,0:T(8,128)}, f32[1,12,16,128]{3,2,1,0:T(8,128)S(1)}, u32[]{:S(2)}, u32[]{:S(2)}) collective-permute-start(f32[1,12,16,128]{3,2,1,0:T(8,128)} %get-tuple-element.81), channel_id=1, source_target_pairs={{1,0},{2,1},{3,2},{4,3},{5,4},{6,5},{7,6},{0,7},{9,8},{10,9},{11,1... | collective-permute-start | bytes 294920 | tf_op jit(solution)/shard_map/ppermute | solution.py:289
  212.0 7.0 %collective-permute-start.21 = (f32[1,12,8,128]{3,2,1,0:T(8,128)}, f32[1,12,8,128]{3,2,1,0:T(8,128)S(1)}, u32[]{:S(2)}, u32[]{:S(2)}) collective-permute-start(f32[1,12,8,128]{3,2,1,0:T(8,128)} %get-tuple-element.87), channel_id=1, source_target_pairs={{0,1},{1,2},{2,3},{3,4},{4,5},{5,6},{6,7},{7,0},{8,9},{9,10},{10,1... | collective-permute-start | bytes 147464 | tf_op jit(solution)/shard_map/ppermute | solution.py:288
  213.5 5.5 %collective-permute-start.22 = (f32[1,12,8,128]{3,2,1,0:T(8,128)}, f32[1,12,8,128]{3,2,1,0:T(8,128)S(1)}, u32[]{:S(2)}, u32[]{:S(2)}) collective-permute-start(f32[1,12,8,128]{3,2,1,0:T(8,128)} %get-tuple-element.88), channel_id=1, source_target_pairs={{1,0},{2,1},{3,2},{4,3},{5,4},{6,5},{7,6},{0,7},{9,8},{10,9},{11,1... | collective-permute-start | bytes 147464 | tf_op jit(solution)/shard_map/ppermute | solution.py:289
  223.0 7.0 %collective-permute-start.23 = (f32[1,12,8,128]{3,2,1,0:T(8,128)}, f32[1,12,8,128]{3,2,1,0:T(8,128)S(1)}, u32[]{:S(2)}, u32[]{:S(2)}) collective-permute-start(f32[1,12,8,128]{3,2,1,0:T(8,128)} %get-tuple-element.90), channel_id=1, source_target_pairs={{0,1},{1,2},{2,3},{3,4},{4,5},{5,6},{6,7},{7,0},{8,9},{9,10},{10,1... | collective-permute-start | bytes 147464 | tf_op jit(solution)/shard_map/ppermute | solution.py:288
  224.1 5.9 %collective-permute-start.24 = (f32[1,12,8,128]{3,2,1,0:T(8,128)}, f32[1,12,8,128]{3,2,1,0:T(8,128)S(1)}, u32[]{:S(2)}, u32[]{:S(2)}) collective-permute-start(f32[1,12,8,128]{3,2,1,0:T(8,128)} %get-tuple-element.91), channel_id=1, source_target_pairs={{1,0},{2,1},{3,2},{4,3},{5,4},{6,5},{7,6},{0,7},{9,8},{10,9},{11,1... | collective-permute-start | bytes 147464 | tf_op jit(solution)/shard_map/ppermute | solution.py:289
  234.0 7.0 %collective-permute-start.25 = (f32[1,12,8,128]{3,2,1,0:T(8,128)}, f32[1,12,8,128]{3,2,1,0:T(8,128)S(1)}, u32[]{:S(2)}, u32[]{:S(2)}) collective-permute-start(f32[1,12,8,128]{3,2,1,0:T(8,128)} %get-tuple-element.93), channel_id=1, source_target_pairs={{0,1},{1,2},{2,3},{3,4},{4,5},{5,6},{6,7},{7,0},{8,9},{9,10},{10,1... | collective-permute-start | bytes 147464 | tf_op jit(solution)/shard_map/ppermute | solution.py:288
  234.1 6.9 %collective-permute-start.26 = (f32[1,12,8,128]{3,2,1,0:T(8,128)}, f32[1,12,8,128]{3,2,1,0:T(8,128)S(1)}, u32[]{:S(2)}, u32[]{:S(2)}) collective-permute-start(f32[1,12,8,128]{3,2,1,0:T(8,128)} %get-tuple-element.94), channel_id=1, source_target_pairs={{1,0},{2,1},{3,2},{4,3},{5,4},{6,5},{7,6},{0,7},{9,8},{10,9},{11,1... | collective-permute-start | bytes 147464 | tf_op jit(solution)/shard_map/ppermute | solution.py:289
  (29 other events, 44.1 us)
Sparse Core Ops, SparseCore 0:
  73.2 18.6 all-gather.4
  188.2 21.6 all-gather.6
